TPU v7x, 32 devices: a whole 2x2x4 slice. The times are simulated.
32 devices in a mesh: tok: 8 (over z, x), grp: 4 (over y, core).
Axes of the slice: x: 2, y: 2, z: 4, core: 2. Of those that a mesh axis runs over, the one named last changes fastest.
Arguments:
- queries: bfloat16 [1536, 2048], P('tok', 'grp'), may hold values from -72 to 72
- new_keys: bfloat16 [1536, 2048], P('tok', 'grp'), may hold values from -8 to 8
- new_values: bfloat16 [1536, 2048], P('tok', 'grp'), may hold values from -6 to 6
- residual: bfloat16 [1536, 2048], P('tok', 'grp'), may hold values from -6 to 6
- w_out: bfloat16 [2048, 2048], P('grp'), may hold values from -0.125 to 0.125
- leaf_keys: bfloat16 [8, 512, 2048], P('tok', None, 'grp'), may hold values from -6 to 6
- leaf_values: bfloat16 [8, 512, 2048], P('tok', None, 'grp'), may hold values from -6 to 6
- upper_keys: bfloat16 [6, 1024, 2048], P(None, 'tok', 'grp'), may hold values from -8 to 8
- upper_values: bfloat16 [6, 1024, 2048], P(None, 'tok', 'grp'), may hold values from -6 to 6
- req_len: int32 [8], replicated, may hold values from 48 to 192, as said below
- leaf_mid: int32 [8], replicated, may hold values from 0 to 3
- mid_root: int32 [4], replicated, may hold values from 0 to 1, as said below
- upper_len: int32 [6], replicated, may hold values from 256 to 1024, as said below
- leaf_len: int32 [8], replicated, may hold values from 128 to 512, as said below
Outputs:
- hidden_out: bfloat16 [1536, 2048], P('tok', 'grp')
Inputs may be any that keep to these rules, and one draw needn't show every extreme that they name: `req_len`: some request has exactly 192 new tokens. `mid_root`: each root is the parent of 2 mids. `upper_len`: the first 2 entries are roots and equal 1024. `leaf_len`: some leaf has exactly 512 positions.
All inputs are finite; a program needn't handle non-finite values.
Results may differ from a plain program's by a relative error of at most 0.008.
Values may be sent and summed in bfloat16 or wider, within the bound.
No kernel may reach another device: no remote copies, remote signals or barrier semaphores. Data moves between devices by JAX's collectives and lax.ppermute only.
A program may use at most 64 MiB of HBM per device.

v0:
```python
import math

import jax
import jax.numpy as jnp
from jax import lax
from jax.sharding import PartitionSpec as P

HEAD_DIM = 128


NEG_FILL = -1e30


def partial_attention(query_rows, key_rows, values, allowed, head_count):
    head_width = query_rows.shape[1] // head_count
    query_heads = query_rows.reshape(query_rows.shape[0], head_count, head_width)
    key_heads = key_rows.reshape(key_rows.shape[0], head_count, head_width)
    value_heads = values.reshape(values.shape[0], head_count, head_width)
    scores = jnp.einsum(
        "qhd,khd->hqk", query_heads, key_heads, preferred_element_type=jnp.float32
    ) * head_width ** (-0.5)
    scores = jnp.where(allowed[None], scores, NEG_FILL)
    row_max = jnp.max(scores, axis=2)
    exp_scores = jnp.where(allowed[None], jnp.exp(scores - row_max[:, :, None]), 0.0)
    row_total = jnp.sum(exp_scores, axis=2)
    weighted = jnp.einsum(
        "hqk,khd->hqd",
        exp_scores.astype(jnp.bfloat16),
        value_heads,
        preferred_element_type=jnp.float32,
    )
    return (row_max, row_total, weighted)


def combine(earlier, latter):
    new_max = jnp.maximum(earlier[0], latter[0])
    earlier_scale = jnp.exp(earlier[0] - new_max)
    latter_scale = jnp.exp(latter[0] - new_max)
    return (
        new_max,
        earlier[1] * earlier_scale + latter[1] * latter_scale,
        earlier[2] * earlier_scale[:, :, None] + latter[2] * latter_scale[:, :, None],
    )


def node_attention(carry, query_rows, node_keys, node_values, node_len, head_count):
    node_rows = node_keys.shape[0]
    block = math.gcd(node_rows, 512)
    row_count = query_rows.shape[0]
    for start in range(0, node_rows, block):
        positions = start + jnp.arange(block, dtype=jnp.int32)
        allowed = jnp.broadcast_to((positions < node_len)[None, :], (row_count, block))
        piece_part = partial_attention(
            query_rows,
            node_keys[start : start + block],
            node_values[start : start + block],
            allowed,
            head_count,
        )
        carry = combine(carry, piece_part)
    return carry


def shards(
    queries,
    new_keys,
    new_values,
    residual,
    w_out,
    leaf_keys,
    leaf_values,
    upper_keys,
    upper_values,
    req_len,
    leaf_mid,
    mid_root,
    upper_len,
    leaf_len,
):
    dev_count = lax.axis_size("tok")
    my_index = lax.axis_index("tok")
    row_count = queries.shape[0]
    col_count = queries.shape[1]
    head_count = col_count // HEAD_DIM
    mid_count = mid_root.shape[0]
    node_count = upper_len.shape[0]
    root_count = node_count - mid_count
    owned = (jnp.arange(dev_count, dtype=jnp.int32) == my_index).astype(jnp.int32)
    my_length = jnp.sum(owned * req_len)
    my_mid = jnp.sum(owned * leaf_mid)
    my_leaf_len = jnp.sum(owned * leaf_len)
    my_root = jnp.sum((jnp.arange(mid_count) == my_mid).astype(jnp.int32) * mid_root)
    node_ids = jnp.arange(node_count)
    root_len = jnp.sum((node_ids == my_root).astype(jnp.int32) * upper_len)
    mid_len = jnp.sum((node_ids == root_count + my_mid).astype(jnp.int32) * upper_len)
    position = jnp.arange(row_count, dtype=jnp.int32)
    is_live = position < my_length
    leaf_count = leaf_keys.shape[1]
    local_keys = jnp.concatenate([leaf_keys[0], new_keys], axis=0)
    local_values = jnp.concatenate([leaf_values[0], new_values], axis=0)
    leaf_allowed = jnp.broadcast_to(
        (jnp.arange(leaf_count) < my_leaf_len)[None, :], (row_count, leaf_count)
    )
    new_allowed = (position[None, :] <= position[:, None]) & is_live[None, :]
    local_part = partial_attention(
        queries,
        local_keys,
        local_values,
        jnp.concatenate([leaf_allowed, new_allowed], axis=1),
        head_count,
    )
    gathered_keys, gathered_values = (
        lax.all_gather(upper_keys, "tok", axis=1, tiled=True),
        lax.all_gather(upper_values, "tok", axis=1, tiled=True),
    )
    merged = node_attention(
        local_part, queries, gathered_keys[my_root], gathered_values[my_root], root_len, head_count
    )
    merged = node_attention(
        merged,
        queries,
        gathered_keys[root_count + my_mid],
        gathered_values[root_count + my_mid],
        mid_len,
        head_count,
    )
    attended = (merged[2] / merged[1][:, :, None]).transpose(1, 0, 2).reshape(row_count, col_count)
    attention = jnp.where(is_live[:, None], attended, 0.0).astype(jnp.bfloat16)
    projected = jnp.dot(attention, w_out, preferred_element_type=jnp.float32)
    mixed = lax.psum_scatter(
        projected.astype(jnp.bfloat16), "grp", scatter_dimension=1, tiled=True
    ).astype(jnp.float32)
    return (residual.astype(jnp.float32) + mixed).astype(jnp.bfloat16)


def solution(mesh):
    in_specs = (
        P("tok", "grp"),
        P("tok", "grp"),
        P("tok", "grp"),
        P("tok", "grp"),
        P("grp", None),
        P("tok", None, "grp"),
        P("tok", None, "grp"),
        P(None, "tok", "grp"),
        P(None, "tok", "grp"),
        P(),
        P(),
        P(),
        P(),
        P(),
    )
    out_specs = P("tok", "grp")
    return jax.shard_map(shards, mesh=mesh, in_specs=in_specs, out_specs=out_specs, check_vma=False)
```

profile of v0, /device:TPU:0, one launch (start us, length us, event | category | flops | bytes accessed | tf_op | source)
XLA Modules:
  0.0 251.3 jit_solution(10677370438847150841)
XLA Ops:
  6.5 0.0 copy-start
  6.5 0.0 all-gather.3.cloned.1.call-start
  6.5 2.5 copy.27
  9.0 0.0 all-gather.3.cloned.1.call-update
  9.0 0.0 all-gather.5.cloned.1.call-start
  9.1 0.0 copy-done.12
  9.1 1.2 copy.30
  10.3 0.0 all-gather.5.cloned.1.call-update
  10.3 0.0 reduce-scatter.2.cloned.1.call-start
  10.4 0.0 copy-done.16
  10.4 0.6 select_reduce_fusion
  12.3 1.3 fusion.91
  14.9 0.2 copy.20
  15.1 0.0 copy-start.18
  15.1 0.0 copy-start.20
  15.1 0.0 copy-start.14
  15.1 1.0 copy.21
  16.2 1.3 copy.24
  17.4 0.3 copy.25
  18.3 0.6 iota_compare_fusion.3
  18.9 1.2 fusion.92
  20.2 0.6 iota_compare_fusion.1
  20.8 0.6 fusion.89
  21.4 0.7 fusion.90
  22.0 0.7 iota_compare_fusion.2
  22.7 0.6 select_reduce_fusion.2
  23.3 0.6 iota_compare_fusion.4
  24.0 0.1 pad_add_fusion
  24.1 1.0 copy_bitcast_fusion
  25.1 0.0 copy-done.9
  25.1 1.7 fusion
  26.9 1.4 copy-done.10
  28.3 0.9 fusion.1
  29.1 82.9 %all-gather.3.cloned.1.call-done = bf16[6,1024,512]{1,2,0:T(8,128)(2,1)} async-done(((bf16[6,128,512]{1,2,0:T(8,128)(2,1)}), bf16[6,1024,512]{1,2,0:T(8,128)(2,1)}) %all-gather.3.cloned.1.call-update) | async-done | bytes 6291472 | tf_op jit(solution)/shard_map/all_gather | solution.py:113
  112.1 1.7 constant_dynamic-slice_fusion.3
  113.7 0.5 bitcast_reduce_fusion
  114.2 0.5 fusion.17
  114.7 0.5 bitcast_reduce_fusion.1
  115.2 0.1 copy-done.3
  115.3 0.5 fusion.15
  115.9 0.5 bitcast_reduce_fusion.2
  116.3 0.2 copy-done.5
  116.5 0.5 fusion.13
  117.0 0.5 bitcast_reduce_fusion.3
  117.5 0.2 copy-done.1
  117.7 1.1 copy-done.7
  118.9 0.5 fusion.11
  119.4 92.8 %all-gather.5.cloned.1.call-done = bf16[6,1024,512]{1,2,0:T(8,128)(2,1)} async-done(((bf16[6,128,512]{1,2,0:T(8,128)(2,1)}), bf16[6,1024,512]{1,2,0:T(8,128)(2,1)}) %all-gather.5.cloned.1.call-update) | async-done | bytes 6291472 | tf_op jit(solution)/shard_map/all_gather | solution.py:114
  212.3 1.8 constant_dynamic-slice_fusion.4
  214.1 0.3 copy-done.6
  214.3 0.5 fusion.22
  214.8 0.7 copy-done.8
  215.5 0.5 fusion.24
  216.0 0.6 copy-done.11
  216.6 1.0 fusion.31
  217.5 0.4 copy-done.2
  218.0 0.6 fusion.32
  218.5 0.8 copy-done.4
  219.4 0.5 fusion.30
  219.9 0.0 copy-start.15
  219.9 1.5 convolution_convert_fusion
  221.4 0.0 reduce-scatter.2.cloned.1.call-update
  221.4 21.6 %reduce-scatter.2.cloned.1.call-done = bf16[192,512]{1,0:T(8,128)(2,1)} async-done(((bf16[192,2048]{1,0:T(8,128)(2,1)}), bf16[192,512]{1,0:T(8,128)(2,1)}) %reduce-scatter.2.cloned.1.call-update) | async-done | bytes 196624 | tf_op jit(solution)/shard_map/reduce_scatter | solution.py:130
  243.1 1.7 add_convert_fusion
  (28 shorter events, 0.1 us)
Async XLA Ops:
  6.5 213.3 %copy-start = (bf16[512,2048]{1,0:T(8,128)(2,1)S(1)}, bf16[512,2048]{1,0:T(8,128)(2,1)}, u32[]{:S(2)}) copy-start(bf16[512,2048]{1,0:T(8,128)(2,1)} %param.18) | copy-start | bytes 6291460
  6.5 2.6 %copy-start.12 = (bf16[6,128,512]{2,1,0:T(8,128)(2,1)S(1)}, bf16[6,128,512]{2,1,0:T(8,128)(2,1)}, u32[]{:S(2)}) copy-start(bf16[6,128,512]{2,1,0:T(8,128)(2,1)} %param.22) | copy-start | bytes 2359300
  6.5 105.5 %all-gather.3.cloned.1.call-start = ((), (), s32[]{:S(2)}) async-start(), calls=%async_computation.1 | async-start | bytes 7077888 | tf_op jit(solution)/shard_map/all_gather | solution.py:113
  9.0 1.3 copy-start.16
  9.0 1.4 copy-start.17
  9.0 3.3 %copy-start.19 = (s32[4]{0:T(128)S(1)}, s32[4]{0:T(128)}, u32[]{:S(2)}) copy-start(s32[4]{0:T(128)} %param.25) | copy-start | bytes 52
  9.0 5.8 %copy-start.13 = (bf16[1,512,512]{2,1,0:T(8,128)(2,1)S(1)}, bf16[1,512,512]{2,1,0:T(8,128)(2,1)}, u32[]{:S(2)}) copy-start(bf16[1,512,512]{2,1,0:T(8,128)(2,1)} %param.19) | copy-start | bytes 1572868
  9.0 203.2 %all-gather.5.cloned.1.call-start = ((), (), s32[]{:S(2)}) async-start(), calls=%async_computation.2 | async-start | bytes 7077888 | tf_op jit(solution)/shard_map/all_gather | solution.py:114
  10.3 232.8 %reduce-scatter.2.cloned.1.call-start = ((), (), s32[]{:S(2)}) async-start(), calls=%async_computation.3 | async-start | bytes 983040 | tf_op jit(solution)/shard_map/reduce_scatter | solution.py:130
  15.1 3.9 %copy-start.18 = (s32[6]{0:T(128)S(1)}, s32[6]{0:T(128)}, u32[]{:S(2)}) copy-start(s32[6]{0:T(128)} %param.26) | copy-start | bytes 76
  15.1 7.6 %copy-start.20 = (s32[8]{0:T(128)S(1)}, s32[8]{0:T(128)}, u32[]{:S(2)}) copy-start(s32[8]{0:T(128)} %param.23) | copy-start | bytes 100
  15.1 9.0 %copy-start.14 = (bf16[192,512]{1,0:T(8,128)(2,1)S(1)}, bf16[192,512]{1,0:T(8,128)(2,1)}, u32[]{:S(2)}) copy-start(bf16[192,512]{1,0:T(8,128)(2,1)} %param.15) | copy-start | bytes 589828
  16.2 8.9 %copy-start.9 = (bf16[192,512]{1,0:T(8,128)(2,1)S(1)}, bf16[192,512]{1,0:T(8,128)(2,1)}, u32[]{:S(2)}) copy-start(bf16[192,512]{1,0:T(8,128)(2,1)} %param.14) | copy-start | bytes 589828
  26.8 1.4 copy-start.10
  114.2 1.2 copy-start.3
  115.3 1.2 copy-start.5
  116.5 1.2 copy-start.1
  117.7 1.1 copy-start.7
  212.3 2.0 copy-start.6
  214.0 1.5 copy-start.8
  214.8 1.8 copy-start.11
  216.6 1.4 copy-start.2
  218.0 1.4 copy-start.4
  219.9 23.2 %copy-start.15 = (bf16[192,512]{1,0:T(8,128)(2,1)S(1)}, bf16[192,512]{1,0:T(8,128)(2,1)}, u32[]{:S(2)}) copy-start(bf16[192,512]{1,0:T(8,128)(2,1)} %param.17) | copy-start | bytes 589828
Sparse Core Ops, SparseCore 0:
  9.4 102.6 all-gather.2
  114.1 98.1 all-gather.4
  221.6 21.4 reduce-scatter.1
where the time goes:
time: 252 us; the launch traced here: 251 us
  waiting for transfers between devices  197 us (78%)
  local copies, waits for them, and re-layouts  16.9 us (7%)
  between operations  16.5 us (7%)
  other arithmetic  12.3 us (5%)
  matrix products  8.03 us (3%)
    all_gather x1, waiting for transfers between devices, shards(): lax.all_gather(upper_values, 'tok', axis=1, tiled=True)  92.8 us
    all_gather x1, waiting for transfers between devices, shards(): lax.all_gather(upper_keys, 'tok', axis=1, tiled=True)  82.9 us
    reduce_scatter x1, waiting for transfers between devices, shards(): lax.psum_scatter(projected.astype(jnp.bfloat16), 'grp', scatter_dimension...  21.6 us
    unnamed x46, local copies, waits for them, and re-layouts  11.2 us
  transfers between devices with their start and end apart: 3, of which 3 were waited for; matrix products, arithmetic and copies ran while one was open for 8% of the time, Pallas kernels for 0%

commit v1 on v0

--- a/solution.py
+++ b/solution.py
@@ -1,5 +1,3 @@
-import math
-
 import jax
 import jax.numpy as jnp
 from jax import lax
@@ -43,24 +41,6 @@
     )
 
 
-def node_attention(carry, query_rows, node_keys, node_values, node_len, head_count):
-    node_rows = node_keys.shape[0]
-    block = math.gcd(node_rows, 512)
-    row_count = query_rows.shape[0]
-    for start in range(0, node_rows, block):
-        positions = start + jnp.arange(block, dtype=jnp.int32)
-        allowed = jnp.broadcast_to((positions < node_len)[None, :], (row_count, block))
-        piece_part = partial_attention(
-            query_rows,
-            node_keys[start : start + block],
-            node_values[start : start + block],
-            allowed,
-            head_count,
-        )
-        carry = combine(carry, piece_part)
-    return carry
-
-
 def shards(
     queries,
     new_keys,
@@ -85,6 +65,16 @@
     mid_count = mid_root.shape[0]
     node_count = upper_len.shape[0]
     root_count = node_count - mid_count
+    chunk = upper_keys.shape[1]
+
+    dest_mid = leaf_mid.astype(jnp.int32)
+    dest_root = jnp.take(mid_root, dest_mid).astype(jnp.int32)
+    dest_nodes = jnp.stack([dest_root, root_count + dest_mid], axis=1)
+    send_keys = jnp.take(upper_keys, dest_nodes, axis=0)
+    send_values = jnp.take(upper_values, dest_nodes, axis=0)
+    recv_keys = lax.all_to_all(send_keys, "tok", 0, 0, tiled=True)
+    recv_values = lax.all_to_all(send_values, "tok", 0, 0, tiled=True)
+
     owned = (jnp.arange(dev_count, dtype=jnp.int32) == my_index).astype(jnp.int32)
     my_length = jnp.sum(owned * req_len)
     my_mid = jnp.sum(owned * leaf_mid)
@@ -109,21 +99,21 @@
         jnp.concatenate([leaf_allowed, new_allowed], axis=1),
         head_count,
     )
-    gathered_keys, gathered_values = (
-        lax.all_gather(upper_keys, "tok", axis=1, tiled=True),
-        lax.all_gather(upper_values, "tok", axis=1, tiled=True),
+
+    upper_pos = (
+        jnp.arange(dev_count, dtype=jnp.int32)[:, None, None] * chunk
+        + jnp.arange(chunk, dtype=jnp.int32)[None, None, :]
     )
-    merged = node_attention(
-        local_part, queries, gathered_keys[my_root], gathered_values[my_root], root_len, head_count
-    )
-    merged = node_attention(
-        merged,
+    upper_limit = jnp.stack([root_len, mid_len])[None, :, None]
+    upper_ok = (upper_pos < upper_limit).reshape(-1)
+    upper_part = partial_attention(
         queries,
-        gathered_keys[root_count + my_mid],
-        gathered_values[root_count + my_mid],
-        mid_len,
+        recv_keys.reshape(-1, col_count),
+        recv_values.reshape(-1, col_count),
+        jnp.broadcast_to(upper_ok[None, :], (row_count, upper_ok.shape[0])),
         head_count,
     )
+    merged = combine(local_part, upper_part)
     attended = (merged[2] / merged[1][:, :, None]).transpose(1, 0, 2).reshape(row_count, col_count)
     attention = jnp.where(is_live[:, None], attended, 0.0).astype(jnp.bfloat16)
     projected = jnp.dot(attention, w_out, preferred_element_type=jnp.float32)

time: 252 us -> 172 us (0.68)
  waiting for transfers between devices: 197 us -> 95.2 us
  starting transfers between devices: 0.09 us -> 11.8 us
  other arithmetic: 12.3 us -> 17 us
  matrix products: 8.03 us -> 12.5 us
  local copies, waits for them, and re-layouts: 16.9 us -> 20.2 us
    all_gather x2 -> x0, waiting for transfers between devices: 176 us -> none  [the longest x1 92.8 us: shards(): lax.all_gather(upper_values, 'tok', axis=1, tiled=True)]
    all_to_all x0 -> x2, waiting for transfers between devices: none -> 72.7 us  [the longest x1 45.1 us: shards(): recv_keys = lax.all_to_all(send_keys, 'tok', 0, 0, tiled=True)]
    all_to_all x0 -> x2, starting transfers between devices: none -> 11.7 us  [the longest x1 7.38 us: shards(): recv_keys = lax.all_to_all(send_keys, 'tok', 0, 0, tiled=True)]
    another operation x0 -> x2, local copies, waits for them, and re-layouts: none -> 8.04 us  [the longest x1 4.02 us: partial_attention(): key_heads = key_rows.reshape(key_rows.shape[0], head_count, head_width)]
    unnamed x46 -> x28, local copies, waits for them, and re-layouts: 11.2 us -> 4 us
    gather x0 -> x3, local copies, waits for them, and re-layouts: none -> 6.55 us  [the longest x1 3.17 us: shards(): send_keys = jnp.take(upper_keys, dest_nodes, axis=0)]
    select_n x0 -> x2, other arithmetic: none -> 5.54 us  [the longest x1 4.73 us: shards(): send_keys = jnp.take(upper_keys, dest_nodes, axis=0)]
    slice x2 -> x0, local copies, waits for them, and re-layouts: 3.42 us -> none  [the longest x1 1.77 us: node_attention(): node_values[start:start + block]]
  transfers between devices with their start and end apart: 3 -> 3, of which waited for: 3 -> 3; matrix products, arithmetic and copies ran while one was open for 8% -> 12% of each run, Pallas kernels for 0% -> 0%
where the time goes in v1:
time: 172 us; the launch traced here: 171 us
  waiting for transfers between devices  95.2 us (55%)
  local copies, waits for them, and re-layouts  20.2 us (12%)
  other arithmetic  17 us (10%)
  between operations  14.3 us (8%)
  matrix products  12.5 us (7%)
  starting transfers between devices  11.8 us (7%)
    all_to_all x1, waiting for transfers between devices, shards(): recv_keys = lax.all_to_all(send_keys, 'tok', 0, 0, tiled=True)  45.1 us
    all_to_all x1, waiting for transfers between devices, shards(): recv_values = lax.all_to_all(send_values, 'tok', 0, 0, tiled=True)  27.7 us
    reduce_scatter x1, waiting for transfers between devices, shards(): lax.psum_scatter(projected.astype(jnp.bfloat16), 'grp', scatter_dimension...  22.5 us
    all_to_all x1, starting transfers between devices, shards(): recv_keys = lax.all_to_all(send_keys, 'tok', 0, 0, tiled=True)  7.38 us
    dot_general x2, matrix products, partial_attention(): jnp.einsum('hqk,khd->hqd', exp_scores.astype(jnp.bfloat16), value_heads,...  6.34 us
    select_n x1, other arithmetic, shards(): send_keys = jnp.take(upper_keys, dest_nodes, axis=0)  4.73 us
    dot_general x2, matrix products, partial_attention(): jnp.einsum('qhd,khd->hqk', query_heads, key_heads, preferred_element_type...  4.66 us
    all_to_all x1, starting transfers between devices, shards(): recv_values = lax.all_to_all(send_values, 'tok', 0, 0, tiled=True)  4.36 us
  transfers between devices with their start and end apart: 3, of which 3 were waited for; matrix products, arithmetic and copies ran while one was open for 12% of the time, Pallas kernels for 0%

profile of v1, /device:TPU:0, one launch (start us, length us, event | category | flops | bytes accessed | tf_op | source)
XLA Modules:
  0.0 171.1 jit_solution(13336882417145120249)
XLA Ops:
  6.5 0.0 copy-start
  6.5 0.8 compare_select_fusion.1
  7.4 0.0 copy-start.3
  7.4 1.4 gather_fusion
  8.7 1.3 select_reduce_fusion
  10.1 0.1 copy.29
  10.2 0.1 reshape.141
  10.2 0.1 copy.28
  10.3 3.2 %gather_fusion.1 = bf16[16,128,512]{2,1,0:T(8,128)(2,1)} fusion(bf16[6,128,512]{2,1,0:T(8,128)(2,1)} %param.23, s32[1024]{0:T(1024)S(1)} %pad_clamp_fusion), kind=kCustom, calls=%fused_computation.clone | custom fusion | bytes 4194368 | tf_op jit(solution)/shard_map/jit(_take)/gather | solution.py:73
  13.5 0.0 copy-done.3
  13.5 2.0 %gather_fusion.2 = bf16[16,128,512]{2,1,0:T(8,128)(2,1)} fusion(bf16[6,128,512]{2,1,0:T(8,128)(2,1)S(1)} %copy-done.3, s32[1024]{0:T(1024)S(1)} %pad_clamp_fusion), kind=kCustom, calls=%fused_computation.1.clone | custom fusion | bytes 4194368 | tf_op jit(solution)/shard_map/jit(_take)/gather | solution.py:74
  15.5 4.7 %broadcast_select_fusion.1 = (bf16[8,2,128,512]{3,2,1,0:T(8,128)(2,1)}, bf16[8,2,128,512]{3,2,1,0:T(8,128)(2,1)}) fusion(bf16[8,2,128,512]{3,2,1,0:T(8,128)(2,1)} %bitcast.107, pred[8,2]{1,0:T(8,128)(4,1)S(1)} %copy.28, bf16[8,2,128,512]{3,2,1,0:T(8,128)(2,1)} %bitcast.108), kind=kLoop, calls=%fused_computation.20 | loop fusion | flops 2097152 | bytes 8388624 | tf_op jit(solution)/shard_map/jit(_take)/select_n | solution.py:73
  20.2 0.0 copy-start.1
  20.2 7.4 %all-to-all-start = ((bf16[8,2,128,512]{3,2,1,0:T(8,128)(2,1)}), bf16[8,2,128,512]{3,2,1,0:T(8,128)(2,1)}, u32[]{:S(2)}, u32[]{:S(2)}) async-start(bf16[8,2,128,512]{3,2,1,0:T(8,128)(2,1)} %get-tuple-element.13), calls=%async_computation | async-start | bytes 4194304 | tf_op jit(solution)/shard_map/all_to_all | solution.py:75
  27.6 0.0 copy-start.6
  28.3 0.0 copy-done.1
  28.4 1.3 fusion.52
  29.7 0.0 copy-done.10
  29.7 1.2 fusion.53
  30.9 45.1 %all-to-all-done = bf16[8,2,128,512]{3,2,1,0:T(8,128)(2,1)} async-done(((bf16[8,2,128,512]{3,2,1,0:T(8,128)(2,1)}), bf16[8,2,128,512]{3,2,1,0:T(8,128)(2,1)}, u32[]{:S(2)}, u32[]{:S(2)}) %all-to-all-start) | async-done | bytes 2097184 | tf_op jit(solution)/shard_map/all_to_all | solution.py:75
  76.0 4.4 %all-to-all-start.1 = ((bf16[8,2,128,512]{3,2,1,0:T(8,128)(2,1)}), bf16[8,2,128,512]{3,2,1,0:T(8,128)(2,1)}, u32[]{:S(2)}, u32[]{:S(2)}) async-start(bf16[8,2,128,512]{3,2,1,0:T(8,128)(2,1)} %get-tuple-element.14), calls=%async_computation.1 | async-start | bytes 4194304 | tf_op jit(solution)/shard_map/all_to_all | solution.py:76
  80.3 0.0 copy-start.12
  80.4 0.0 copy-start.7
  80.4 0.0 reduce-scatter.2.cloned.1.call-start
  80.4 1.4 pad_add_fusion.1
  81.8 0.1 iota_add_fusion
  81.9 0.1 broadcast_compare_fusion
  82.0 0.0 copy-done.6
  82.0 0.0 copy-start.8
  82.0 0.2 copy.21
  82.2 1.0 copy.22
  83.2 1.3 copy.25
  84.5 0.3 copy.26
  84.7 0.6 iota_compare_fusion.1
  85.3 0.0 copy-done.12
  85.4 0.6 select_reduce_fusion.2
  86.0 0.6 iota_compare_fusion.2
  86.7 0.1 pad_add_fusion
  86.7 0.0 copy-done.7
  86.8 0.0 copy-done.8
  86.8 1.8 %fusion.11 = (f32[4,192]{1,0:T(4,128)S(1)}, f32[4,704,192]{1,2,0:T(8,128)S(1)}) fusion(pred[192,704]{1,0:T(8,128)(4,1)S(1)} %pad_add_fusion, bf16[192,4,128]{2,0,1:T(8,128)(2,1)S(1)} %copy_bitcast_fusion.1, bf16[512,4,128]{2,0,1:T(8,128)(2,1)} %copy.22, bf16[192,512]{1,0:T(8,128)(2,1)} %param.16), kind=kOutput, calls=%fused_computation.21 | convolution fusion | flops 141475072 | bytes 3218432 | tf_op jit(solution)/shard_map/qhd,khd->hqk/dot_general | solution.py:17
  88.6 0.0 copy-start.4
  88.6 1.4 copy-done.4
  90.0 0.9 fusion.12
  90.9 0.0 copy-start.11
  90.9 4.0 %reshape_reshape.6 = bf16[2048,4,128]{2,1,0:T(4,128)(2,1)} reshape(bf16[8,2,128,512]{3,2,1,0:T(8,128)(2,1)} %all-to-all-done) | data formatting | bytes 4194304 | tf_op jit(solution)/shard_map/reshape;reshape | solution.py:15
  94.9 0.0 copy-done.11
  94.9 2.9 %bitcast_reduce_fusion = (f32[4,192]{1,0:T(4,128)S(1)}, f32[4,2048,192]{1,2,0:T(8,128)S(1)}) fusion(pred[2048]{0:T(1024)(128)(4,1)S(1)} %lt.58, bf16[2048,4,128]{2,1,0:T(4,128)(2,1)} %reshape_reshape.6, bf16[192,512]{1,0:T(8,128)(2,1)S(1)} %copy-done.11), kind=kOutput, calls=%fused_computation.4 | convolution fusion | flops 407371008 | bytes 8590336 | tf_op jit(solution)/shard_map/qhd,khd->hqk/dot_general | solution.py:17
  97.8 0.0 copy-start.2
  97.8 1.6 fusion.2
  99.4 1.1 copy-done.2
  100.5 27.7 %all-to-all-done.1 = bf16[8,2,128,512]{3,2,1,0:T(8,128)(2,1)} async-done(((bf16[8,2,128,512]{3,2,1,0:T(8,128)(2,1)}), bf16[8,2,128,512]{3,2,1,0:T(8,128)(2,1)}, u32[]{:S(2)}, u32[]{:S(2)}) %all-to-all-start.1) | async-done | bytes 2097184 | tf_op jit(solution)/shard_map/all_to_all | solution.py:76
  128.2 4.0 %reshape_reshape.7 = bf16[2048,4,128]{2,1,0:T(4,128)(2,1)} reshape(bf16[8,2,128,512]{3,2,1,0:T(8,128)(2,1)} %all-to-all-done.1) | data formatting | bytes 4194304 | tf_op jit(solution)/shard_map/reshape;reshape | solution.py:16
  132.2 0.0 copy-start.5
  132.2 5.4 %fusion.23 = f32[192,4,128]{2,0,1:T(8,128)S(1)} fusion(bf16[2048,4,128]{2,1,0:T(4,128)(2,1)} %reshape_reshape.7, f32[4,2048,192]{1,2,0:T(8,128)} %copy-done.2, f32[4,192]{1,0:T(4,128)S(1)} %get-tuple-element.18, pred[2048]{0:T(1024)(128)(4,1)S(1)} %lt.58, f32[192,4]{0,1:T(4,128)S(1)} %get-tuple-element.10), kind=kOutput, calls=%fused_computation.30 | convolution fusion | flops 410615808 | bytes 8790016 | tf_op jit(solution)/shard_map/hqk,khd->hqd/dot_general | solution.py:24
  137.6 0.0 copy-done.5
  137.6 0.9 fusion.17
  138.5 0.0 copy-done
  138.5 0.0 copy-start.9
  138.5 1.5 convolution_convert_fusion
  140.0 0.0 reduce-scatter.2.cloned.1.call-update
  140.1 22.5 %reduce-scatter.2.cloned.1.call-done = bf16[192,512]{1,0:T(8,128)(2,1)} async-done(((bf16[192,2048]{1,0:T(8,128)(2,1)}), bf16[192,512]{1,0:T(8,128)(2,1)}) %reduce-scatter.2.cloned.1.call-update) | async-done | bytes 196624 | tf_op jit(solution)/shard_map/reduce_scatter | solution.py:120
  162.6 0.0 copy-done.9
  162.6 1.7 add_convert_fusion
  (11 shorter events, 0.2 us)
Async XLA Ops:
  6.5 132.0 %copy-start = (bf16[512,2048]{1,0:T(8,128)(2,1)S(1)}, bf16[512,2048]{1,0:T(8,128)(2,1)}, u32[]{:S(2)}) copy-start(bf16[512,2048]{1,0:T(8,128)(2,1)} %param.20) | copy-start | bytes 6291460
  7.4 6.2 %copy-start.3 = (bf16[6,128,512]{2,1,0:T(8,128)(2,1)S(1)}, bf16[6,128,512]{2,1,0:T(8,128)(2,1)}, u32[]{:S(2)}) copy-start(bf16[6,128,512]{2,1,0:T(8,128)(2,1)} %param.24) | copy-start | bytes 2359300
  20.2 8.1 %copy-start.1 = (s32[4]{0:T(128)S(1)}, s32[4]{0:T(128)}, u32[]{:S(2)}) copy-start(s32[4]{0:T(128)} %param.27) | copy-start | bytes 52
  20.2 9.4 %copy-start.10 = (s32[6]{0:T(128)S(1)}, s32[6]{0:T(128)}, u32[]{:S(2)}) copy-start(s32[6]{0:T(128)} %param.28) | copy-start | bytes 76
  20.2 55.7 %all-to-all-start = ((bf16[8,2,128,512]{3,2,1,0:T(8,128)(2,1)}), bf16[8,2,128,512]{3,2,1,0:T(8,128)(2,1)}, u32[]{:S(2)}, u32[]{:S(2)}) async-start(bf16[8,2,128,512]{3,2,1,0:T(8,128)(2,1)} %get-tuple-element.13), calls=%async_computation | async-start | bytes 4194304 | tf_op jit(solution)/shard_map/all_to_all | solution.py:75
  27.6 54.3 %copy-start.6 = (bf16[1,512,512]{2,1,0:T(8,128)(2,1)S(1)}, bf16[1,512,512]{2,1,0:T(8,128)(2,1)}, u32[]{:S(2)}) copy-start(bf16[1,512,512]{2,1,0:T(8,128)(2,1)} %param.21) | copy-start | bytes 1572868
  76.0 52.2 %all-to-all-start.1 = ((bf16[8,2,128,512]{3,2,1,0:T(8,128)(2,1)}), bf16[8,2,128,512]{3,2,1,0:T(8,128)(2,1)}, u32[]{:S(2)}, u32[]{:S(2)}) async-start(bf16[8,2,128,512]{3,2,1,0:T(8,128)(2,1)} %get-tuple-element.14), calls=%async_computation.1 | async-start | bytes 4194304 | tf_op jit(solution)/shard_map/all_to_all | solution.py:76
  80.3 5.0 %copy-start.12 = (s32[8]{0:T(128)S(1)}, s32[8]{0:T(128)}, u32[]{:S(2)}) copy-start(s32[8]{0:T(128)} %param.25) | copy-start | bytes 100
  80.4 6.4 %copy-start.7 = (bf16[192,512]{1,0:T(8,128)(2,1)S(1)}, bf16[192,512]{1,0:T(8,128)(2,1)}, u32[]{:S(2)}) copy-start(bf16[192,512]{1,0:T(8,128)(2,1)} %param.17) | copy-start | bytes 589828
  80.4 82.2 %reduce-scatter.2.cloned.1.call-start = ((), (), s32[]{:S(2)}) async-start(), calls=%async_computation.3 | async-start | bytes 983040 | tf_op jit(solution)/shard_map/reduce_scatter | solution.py:120
  82.0 4.8 %copy-start.8 = (bf16[192,512]{1,0:T(8,128)(2,1)S(1)}, bf16[192,512]{1,0:T(8,128)(2,1)}, u32[]{:S(2)}) copy-start(bf16[192,512]{1,0:T(8,128)(2,1)} %param.18) | copy-start | bytes 589828
  88.6 1.4 copy-start.4
  90.9 4.0 %copy-start.11 = (bf16[192,512]{1,0:T(8,128)(2,1)S(1)}, bf16[192,512]{1,0:T(8,128)(2,1)}, u32[]{:S(2)}) copy-start(bf16[192,512]{1,0:T(8,128)(2,1)} %param.16) | copy-start | bytes 589828
  97.8 2.7 %copy-start.2 = (f32[4,2048,192]{1,2,0:T(8,128)}, f32[4,2048,192]{1,2,0:T(8,128)S(1)}, u32[]{:S(2)}) copy-start(f32[4,2048,192]{1,2,0:T(8,128)S(1)} %get-tuple-element.19) | copy-start | bytes 18874372
  132.2 5.4 %copy-start.5 = (f32[4,704,192]{1,2,0:T(8,128)S(1)}, f32[4,704,192]{1,2,0:T(8,128)}, u32[]{:S(2)}) copy-start(f32[4,704,192]{1,2,0:T(8,128)} %copy-done.4) | copy-start | bytes 6488068
  138.5 24.1 %copy-start.9 = (bf16[192,512]{1,0:T(8,128)(2,1)S(1)}, bf16[192,512]{1,0:T(8,128)(2,1)}, u32[]{:S(2)}) copy-start(bf16[192,512]{1,0:T(8,128)(2,1)} %param.19) | copy-start | bytes 589828
Sparse Core Ops, SparseCore 0:
  140.2 22.3 reduce-scatter.1

commit v2 on v1

--- a/solution.py
+++ b/solution.py
@@ -11,34 +11,38 @@
 
 def partial_attention(query_rows, key_rows, values, allowed, head_count):
     head_width = query_rows.shape[1] // head_count
-    query_heads = query_rows.reshape(query_rows.shape[0], head_count, head_width)
-    key_heads = key_rows.reshape(key_rows.shape[0], head_count, head_width)
-    value_heads = values.reshape(values.shape[0], head_count, head_width)
-    scores = jnp.einsum(
-        "qhd,khd->hqk", query_heads, key_heads, preferred_element_type=jnp.float32
-    ) * head_width ** (-0.5)
-    scores = jnp.where(allowed[None], scores, NEG_FILL)
-    row_max = jnp.max(scores, axis=2)
-    exp_scores = jnp.where(allowed[None], jnp.exp(scores - row_max[:, :, None]), 0.0)
-    row_total = jnp.sum(exp_scores, axis=2)
-    weighted = jnp.einsum(
-        "hqk,khd->hqd",
-        exp_scores.astype(jnp.bfloat16),
-        value_heads,
-        preferred_element_type=jnp.float32,
-    )
-    return (row_max, row_total, weighted)
+    parts = []
+    for head in range(head_count):
+        cols = slice(head * head_width, (head + 1) * head_width)
+        scores = lax.dot_general(
+            query_rows[:, cols],
+            key_rows[:, cols],
+            (((1,), (1,)), ((), ())),
+            preferred_element_type=jnp.float32,
+        ) * head_width ** (-0.5)
+        scores = jnp.where(allowed, scores, NEG_FILL)
+        row_max = jnp.max(scores, axis=1, keepdims=True)
+        exp_scores = jnp.where(allowed, jnp.exp(scores - row_max), 0.0)
+        row_total = jnp.sum(exp_scores, axis=1, keepdims=True)
+        weighted = jnp.dot(
+            exp_scores.astype(jnp.bfloat16),
+            values[:, cols],
+            preferred_element_type=jnp.float32,
+        )
+        parts.append((row_max, row_total, weighted))
+    return parts
 
 
 def combine(earlier, latter):
-    new_max = jnp.maximum(earlier[0], latter[0])
-    earlier_scale = jnp.exp(earlier[0] - new_max)
-    latter_scale = jnp.exp(latter[0] - new_max)
-    return (
-        new_max,
-        earlier[1] * earlier_scale + latter[1] * latter_scale,
-        earlier[2] * earlier_scale[:, :, None] + latter[2] * latter_scale[:, :, None],
-    )
+    merged = []
+    for (max_a, total_a, sum_a), (max_b, total_b, sum_b) in zip(earlier, latter):
+        new_max = jnp.maximum(max_a, max_b)
+        scale_a = jnp.exp(max_a - new_max)
+        scale_b = jnp.exp(max_b - new_max)
+        merged.append(
+            (new_max, total_a * scale_a + total_b * scale_b, sum_a * scale_a + sum_b * scale_b)
+        )
+    return merged
 
 
 def shards(
@@ -70,10 +74,16 @@
     dest_mid = leaf_mid.astype(jnp.int32)
     dest_root = jnp.take(mid_root, dest_mid).astype(jnp.int32)
     dest_nodes = jnp.stack([dest_root, root_count + dest_mid], axis=1)
-    send_keys = jnp.take(upper_keys, dest_nodes, axis=0)
-    send_values = jnp.take(upper_values, dest_nodes, axis=0)
-    recv_keys = lax.all_to_all(send_keys, "tok", 0, 0, tiled=True)
-    recv_values = lax.all_to_all(send_values, "tok", 0, 0, tiled=True)
+    send = jnp.concatenate(
+        [
+            upper_keys.at[dest_nodes].get(mode="promise_in_bounds"),
+            upper_values.at[dest_nodes].get(mode="promise_in_bounds"),
+        ],
+        axis=1,
+    )
+    received = lax.all_to_all(send, "tok", 0, 0, tiled=True)
+    recv_keys = received[:, :2]
+    recv_values = received[:, 2:]
 
     owned = (jnp.arange(dev_count, dtype=jnp.int32) == my_index).astype(jnp.int32)
     my_length = jnp.sum(owned * req_len)
@@ -110,11 +120,11 @@
         queries,
         recv_keys.reshape(-1, col_count),
         recv_values.reshape(-1, col_count),
-        jnp.broadcast_to(upper_ok[None, :], (row_count, upper_ok.shape[0])),
+        upper_ok[None, :],
         head_count,
     )
     merged = combine(local_part, upper_part)
-    attended = (merged[2] / merged[1][:, :, None]).transpose(1, 0, 2).reshape(row_count, col_count)
+    attended = jnp.concatenate([part[2] / part[1] for part in merged], axis=1)
     attention = jnp.where(is_live[:, None], attended, 0.0).astype(jnp.bfloat16)
     projected = jnp.dot(attention, w_out, preferred_element_type=jnp.float32)
     mixed = lax.psum_scatter(

time: 172 us -> 163 us (0.948)
  waiting for transfers between devices: 95.2 us -> 106 us
  local copies, waits for them, and re-layouts: 20.2 us -> 9.67 us
  starting transfers between devices: 11.8 us -> 7.43 us
  matrix products: 12.5 us -> 8.72 us
    all_to_all x2 -> x1, waiting for transfers between devices: 72.7 us -> 83.6 us  [shards(): received = lax.all_to_all(send, 'tok', 0, 0, tiled=True)]
    another operation x2 -> x0, local copies, waits for them, and re-layouts: 8.04 us -> none  [the longest x1 4.02 us: partial_attention(): key_heads = key_rows.reshape(key_rows.shape[0], head_count, head_width)]
    select_n x1, other arithmetic: 4.73 us -> 0.01 us  [shards(): upper_keys.at[dest_nodes].get(mode='promise_in_bounds')]
    concatenate x1, other arithmetic: 0.05 us -> 4.51 us  [shards(): jnp.concatenate([upper_keys.at[dest_nodes].get(mode='promise_in_bounds'),...]
    all_to_all x2 -> x1, starting transfers between devices: 11.7 us -> 7.4 us  [shards(): received = lax.all_to_all(send, 'tok', 0, 0, tiled=True)]
    dot_general x4 -> x16, matrix products: 11 us -> 7.19 us  [the longest x8 4.12 us: partial_attention(): lax.dot_general(query_rows[:, cols], key_rows[:, cols], (((1,), (1,)), ((...]
    unnamed x28 -> x38, local copies, waits for them, and re-layouts: 4 us -> 0.44 us
    slice x0 -> x1, local copies, waits for them, and re-layouts: none -> 2.49 us  [shards(): recv_values = received[:, 2:]]
  transfers between devices with their start and end apart: 3 -> 2, of which waited for: 3 -> 2; matrix products, arithmetic and copies ran while one was open for 12% -> 5% of each run, Pallas kernels for 0% -> 0%
where the time goes in v2:
time: 163 us; the launch traced here: 162 us
  waiting for transfers between devices  106 us (65%)
  other arithmetic  16.1 us (10%)
  between operations  14.4 us (9%)
  local copies, waits for them, and re-layouts  9.67 us (6%)
  matrix products  8.72 us (5%)
  starting transfers between devices  7.43 us (5%)
    all_to_all x1, waiting for transfers between devices, shards(): received = lax.all_to_all(send, 'tok', 0, 0, tiled=True)  83.6 us
    reduce_scatter x1, waiting for transfers between devices, shards(): lax.psum_scatter(projected.astype(jnp.bfloat16), 'grp', scatter_dimension...  22.5 us
    all_to_all x1, starting transfers between devices, shards(): received = lax.all_to_all(send, 'tok', 0, 0, tiled=True)  7.4 us
    concatenate x1, other arithmetic, shards(): jnp.concatenate([upper_keys.at[dest_nodes].get(mode='promise_in_bounds'),...  4.51 us
    dot_general x8, matrix products, partial_attention(): lax.dot_general(query_rows[:, cols], key_rows[:, cols], (((1,), (1,)), ((...  4.12 us
  transfers between devices with their start and end apart: 2, of which 2 were waited for; matrix products, arithmetic and copies ran while one was open for 5% of the time, Pallas kernels for 0%

profile of v2, /device:TPU:0, one launch (start us, length us, event | category | flops | bytes accessed | tf_op | source)
XLA Modules:
  0.0 162.4 jit_solution(9761047829950386952)
XLA Ops:
  6.5 0.0 copy-start
  6.5 0.8 compare_select_fusion.1
  7.4 1.3 gather_fusion
  8.6 1.3 fusion.110
  10.0 0.1 copy.16
  10.0 0.1 reshape.299
  10.1 3.2 %gather_fusion.1 = bf16[16,128,512]{2,1,0:T(8,128)(2,1)} fusion(bf16[6,128,512]{2,1,0:T(8,128)(2,1)} %param.21, s32[1024]{0:T(1024)S(1)} %pad_clamp_fusion), kind=kCustom, calls=%fused_computation.1 | custom fusion | bytes 4194368 | tf_op jit(solution)/shard_map/gather | solution.py:79
  13.4 0.0 copy-done.3
  13.4 2.0 %gather_fusion.2 = bf16[16,128,512]{2,1,0:T(8,128)(2,1)} fusion(bf16[6,128,512]{2,1,0:T(8,128)(2,1)S(1)} %copy-done.3, s32[1024]{0:T(1024)S(1)} %pad_clamp_fusion), kind=kCustom, calls=%fused_computation.2 | custom fusion | bytes 4194368 | tf_op jit(solution)/shard_map/gather | solution.py:80
  15.4 4.5 %pad_maximum_fusion = bf16[8,4,128,512]{3,2,1,0:T(8,128)(2,1)} fusion(bf16[8,2,128,512]{3,2,1,0:T(8,128)(2,1)} %bitcast.32, bf16[8,2,128,512]{3,2,1,0:T(8,128)(2,1)} %bitcast.31), kind=kLoop, calls=%fused_computation.3 | loop fusion | flops 2097152 | bytes 8388608 | tf_op jit(solution)/shard_map/concatenate | solution.py:77
  19.9 0.0 copy-start.2
  19.9 0.0 copy-start.4
  19.9 0.0 copy-start.12
  19.9 7.4 %all-to-all-start = ((bf16[8,4,128,512]{3,2,1,0:T(8,128)(2,1)}), bf16[8,4,128,512]{3,2,1,0:T(8,128)(2,1)}, u32[]{:S(2)}, u32[]{:S(2)}) async-start(bf16[8,4,128,512]{3,2,1,0:T(8,128)(2,1)} %pad_maximum_fusion), calls=%async_computation | async-start | bytes 8388608 | tf_op jit(solution)/shard_map/all_to_all | solution.py:84
  27.3 0.0 reduce-scatter.2.cloned.1.call-start
  28.0 0.0 copy-done.1
  28.1 1.3 fusion.107
  29.3 0.0 copy-done.16
  29.3 1.2 fusion.108
  30.5 1.3 pad_add_fusion.1
  31.9 0.1 iota_add_fusion
  31.9 0.1 broadcast_compare_fusion
  32.0 0.0 copy-done.17
  32.0 0.0 copy-done.18
  32.0 0.6 select_reduce_fusion.1
  32.7 0.6 iota_compare_fusion.1
  33.4 0.6 iota_compare_fusion.2
  34.0 0.0 copy-done.2
  34.0 0.0 copy-done.4
  34.0 0.0 copy-done.12
  34.0 0.3 fusion.143
  34.3 0.0 copy-start.9
  34.4 0.3 fusion.144
  34.7 0.0 copy-start.7
  34.7 0.3 fusion.145
  35.1 0.0 copy-start.5
  35.1 1.2 fusion.138
  36.3 0.0 copy-done.9
  36.3 0.8 fusion.52
  37.1 83.6 %all-to-all-done = bf16[8,4,128,512]{3,2,1,0:T(8,128)(2,1)} async-done(((bf16[8,4,128,512]{3,2,1,0:T(8,128)(2,1)}), bf16[8,4,128,512]{3,2,1,0:T(8,128)(2,1)}, u32[]{:S(2)}, u32[]{:S(2)}) %all-to-all-start) | async-done | bytes 4194336 | tf_op jit(solution)/shard_map/all_to_all | solution.py:84
  120.6 2.5 %fusion.137 = (bf16[8,2,128,512]{3,2,1,0:T(8,128)(2,1)S(1)}, bf16[8,2,128,512]{3,2,1,0:T(8,128)(2,1)S(1)}) fusion(bf16[8,4,128,512]{3,2,1,0:T(8,128)(2,1)} %all-to-all-done), kind=kLoop, calls=%fused_computation.192 | loop fusion | bytes 8388608 | tf_op jit(solution)/shard_map/slice | solution.py:86
  123.1 0.0 copy-done.13
  123.1 0.5 fusion.139
  123.6 0.5 fusion.140
  124.1 0.5 fusion.141
  124.6 0.5 fusion.142
  125.0 0.0 copy-start.11
  125.0 0.0 copy-start.14
  125.1 1.2 fusion.4
  126.3 0.3 convolution_multiply_fusion.15
  126.6 0.0 copy-done.8
  126.7 0.3 convolution_multiply_fusion.13
  127.0 0.4 copy-done.6
  127.4 0.3 convolution_multiply_fusion.11
  127.7 0.3 convolution_multiply_fusion.9
  128.1 0.4 fusion.27
  128.5 0.4 fusion.25
  128.9 0.4 fusion.23
  129.4 0.4 fusion.21
  129.8 0.0 copy-start.15
  129.9 1.5 convolution_convert_fusion
  131.4 0.0 reduce-scatter.2.cloned.1.call-update
  131.4 22.5 %reduce-scatter.2.cloned.1.call-done = bf16[192,512]{1,0:T(8,128)(2,1)} async-done(((bf16[192,2048]{1,0:T(8,128)(2,1)}), bf16[192,512]{1,0:T(8,128)(2,1)}) %reduce-scatter.2.cloned.1.call-update) | async-done | bytes 196624 | tf_op jit(solution)/shard_map/reduce_scatter | solution.py:130
  153.9 1.7 %add_convert_fusion = bf16[192,512]{1,0:T(8,128)(2,1)} fusion(bf16[192,512]{1,0:T(8,128)(2,1)} %reduce-scatter.2.cloned.1.call-done, bf16[192,512]{1,0:T(8,128)(2,1)S(1)} %copy-done.15), kind=kLoop, calls=%fused_computation.100 | loop fusion | flops 393216 | bytes 589824 | tf_op jit(solution)/shard_map/convert_element_type | solution.py:133
  (27 shorter events, 0.2 us)
Async XLA Ops:
  6.5 123.3 %copy-start = (bf16[512,2048]{1,0:T(8,128)(2,1)S(1)}, bf16[512,2048]{1,0:T(8,128)(2,1)}, u32[]{:S(2)}) copy-start(bf16[512,2048]{1,0:T(8,128)(2,1)} %param.18) | copy-start | bytes 6291460
  10.1 3.2 %copy-start.3 = (bf16[6,128,512]{2,1,0:T(8,128)(2,1)S(1)}, bf16[6,128,512]{2,1,0:T(8,128)(2,1)}, u32[]{:S(2)}) copy-start(bf16[6,128,512]{2,1,0:T(8,128)(2,1)} %param.22) | copy-start | bytes 2359300
  19.9 8.2 %copy-start.1 = (s32[4]{0:T(128)S(1)}, s32[4]{0:T(128)}, u32[]{:S(2)}) copy-start(s32[4]{0:T(128)} %param.25) | copy-start | bytes 52
  19.9 9.4 %copy-start.16 = (s32[6]{0:T(128)S(1)}, s32[6]{0:T(128)}, u32[]{:S(2)}) copy-start(s32[6]{0:T(128)} %param.26) | copy-start | bytes 76
  19.9 12.1 %copy-start.17 = (s32[8]{0:T(128)S(1)}, s32[8]{0:T(128)}, u32[]{:S(2)}) copy-start(s32[8]{0:T(128)} %param.27) | copy-start | bytes 100
  19.9 12.1 %copy-start.18 = (s32[8]{0:T(128)S(1)}, s32[8]{0:T(128)}, u32[]{:S(2)}) copy-start(s32[8]{0:T(128)} %param.23) | copy-start | bytes 100
  19.9 14.1 %copy-start.2 = (bf16[1,512,512]{2,1,0:T(8,128)(2,1)S(1)}, bf16[1,512,512]{2,1,0:T(8,128)(2,1)}, u32[]{:S(2)}) copy-start(bf16[1,512,512]{2,1,0:T(8,128)(2,1)} %param.19) | copy-start | bytes 1572868
  19.9 14.1 %copy-start.4 = (bf16[192,512]{1,0:T(8,128)(2,1)S(1)}, bf16[192,512]{1,0:T(8,128)(2,1)}, u32[]{:S(2)}) copy-start(bf16[192,512]{1,0:T(8,128)(2,1)} %param.15) | copy-start | bytes 589828
  19.9 14.1 %copy-start.12 = (bf16[192,512]{1,0:T(8,128)(2,1)S(1)}, bf16[192,512]{1,0:T(8,128)(2,1)}, u32[]{:S(2)}) copy-start(bf16[192,512]{1,0:T(8,128)(2,1)} %param.14) | copy-start | bytes 589828
  19.9 100.7 %all-to-all-start = ((bf16[8,4,128,512]{3,2,1,0:T(8,128)(2,1)}), bf16[8,4,128,512]{3,2,1,0:T(8,128)(2,1)}, u32[]{:S(2)}, u32[]{:S(2)}) async-start(bf16[8,4,128,512]{3,2,1,0:T(8,128)(2,1)} %pad_maximum_fusion), calls=%async_computation | async-start | bytes 8388608 | tf_op jit(solution)/shard_map/all_to_all | solution.py:84
  27.3 126.6 %reduce-scatter.2.cloned.1.call-start = ((), (), s32[]{:S(2)}) async-start(), calls=%async_computation.2 | async-start | bytes 983040 | tf_op jit(solution)/shard_map/reduce_scatter | solution.py:130
  34.3 1.9 %copy-start.9 = (f32[192,704]{1,0:T(8,128)}, f32[192,704]{1,0:T(8,128)S(1)}, u32[]{:S(2)}) copy-start(f32[192,704]{1,0:T(8,128)S(1)} %get-tuple-element.43) | copy-start | bytes 1622020
  34.7 1.6 copy-start.7
  35.1 1.2 copy-start.5
  37.1 86.1 %copy-start.13 = (bf16[192,512]{1,0:T(8,128)(2,1)S(1)}, bf16[192,512]{1,0:T(8,128)(2,1)}, u32[]{:S(2)}) copy-start(bf16[192,512]{1,0:T(8,128)(2,1)} %param.14) | copy-start | bytes 589828
  125.0 1.3 copy-start.10
  125.0 1.3 copy-start.11
  125.0 1.3 copy-start.14
  125.1 1.6 copy-start.8
  126.2 1.1 copy-start.6
  129.8 24.1 %copy-start.15 = (bf16[192,512]{1,0:T(8,128)(2,1)S(1)}, bf16[192,512]{1,0:T(8,128)(2,1)}, u32[]{:S(2)}) copy-start(bf16[192,512]{1,0:T(8,128)(2,1)} %param.17) | copy-start | bytes 589828
Sparse Core Ops, SparseCore 0:
  131.5 22.3 reduce-scatter.1

commit v3 on v2

--- a/solution.py
+++ b/solution.py
@@ -66,24 +66,11 @@
     row_count = queries.shape[0]
     col_count = queries.shape[1]
     head_count = col_count // HEAD_DIM
+    head_width = col_count // head_count
     mid_count = mid_root.shape[0]
     node_count = upper_len.shape[0]
     root_count = node_count - mid_count
     chunk = upper_keys.shape[1]
-
-    dest_mid = leaf_mid.astype(jnp.int32)
-    dest_root = jnp.take(mid_root, dest_mid).astype(jnp.int32)
-    dest_nodes = jnp.stack([dest_root, root_count + dest_mid], axis=1)
-    send = jnp.concatenate(
-        [
-            upper_keys.at[dest_nodes].get(mode="promise_in_bounds"),
-            upper_values.at[dest_nodes].get(mode="promise_in_bounds"),
-        ],
-        axis=1,
-    )
-    received = lax.all_to_all(send, "tok", 0, 0, tiled=True)
-    recv_keys = received[:, :2]
-    recv_values = received[:, 2:]
 
     owned = (jnp.arange(dev_count, dtype=jnp.int32) == my_index).astype(jnp.int32)
     my_length = jnp.sum(owned * req_len)
@@ -102,14 +89,47 @@
         (jnp.arange(leaf_count) < my_leaf_len)[None, :], (row_count, leaf_count)
     )
     new_allowed = (position[None, :] <= position[:, None]) & is_live[None, :]
-    local_part = partial_attention(
-        queries,
-        local_keys,
-        local_values,
-        jnp.concatenate([leaf_allowed, new_allowed], axis=1),
-        head_count,
-    )
-
+    local_allowed = jnp.concatenate([leaf_allowed, new_allowed], axis=1)
+
+    if dev_count * row_count * col_count * 4 <= (8 << 20):
+        merged = query_plan(
+            queries, local_keys, local_values, local_allowed, upper_keys, upper_values,
+            leaf_mid, mid_root, upper_len, head_count, my_index, root_count, chunk,
+        )
+    else:
+        merged = node_plan(
+            queries, local_keys, local_values, local_allowed, upper_keys, upper_values,
+            leaf_mid, mid_root, root_len, mid_len, head_count, root_count, chunk,
+        )
+    attended = jnp.concatenate([part[2] / part[1] for part in merged], axis=1)
+    attention = jnp.where(is_live[:, None], attended, 0.0).astype(jnp.bfloat16)
+    projected = jnp.dot(attention, w_out, preferred_element_type=jnp.float32)
+    mixed = lax.psum_scatter(
+        projected.astype(jnp.bfloat16), "grp", scatter_dimension=1, tiled=True
+    ).astype(jnp.float32)
+    return (residual.astype(jnp.float32) + mixed).astype(jnp.bfloat16)
+
+
+def node_plan(
+    queries, local_keys, local_values, local_allowed, upper_keys, upper_values,
+    leaf_mid, mid_root, root_len, mid_len, head_count, root_count, chunk,
+):
+    dev_count = lax.axis_size("tok")
+    col_count = queries.shape[1]
+    dest_mid = leaf_mid.astype(jnp.int32)
+    dest_root = jnp.take(mid_root, dest_mid).astype(jnp.int32)
+    dest_nodes = jnp.stack([dest_root, root_count + dest_mid], axis=1)
+    send = jnp.concatenate(
+        [
+            upper_keys.at[dest_nodes].get(mode="promise_in_bounds"),
+            upper_values.at[dest_nodes].get(mode="promise_in_bounds"),
+        ],
+        axis=1,
+    )
+    received = lax.all_to_all(send, "tok", 0, 0, tiled=True)
+    recv_keys = received[:, :2]
+    recv_values = received[:, 2:]
+    local_part = partial_attention(queries, local_keys, local_values, local_allowed, head_count)
     upper_pos = (
         jnp.arange(dev_count, dtype=jnp.int32)[:, None, None] * chunk
         + jnp.arange(chunk, dtype=jnp.int32)[None, None, :]
@@ -123,14 +143,86 @@
         upper_ok[None, :],
         head_count,
     )
-    merged = combine(local_part, upper_part)
-    attended = jnp.concatenate([part[2] / part[1] for part in merged], axis=1)
-    attention = jnp.where(is_live[:, None], attended, 0.0).astype(jnp.bfloat16)
-    projected = jnp.dot(attention, w_out, preferred_element_type=jnp.float32)
-    mixed = lax.psum_scatter(
-        projected.astype(jnp.bfloat16), "grp", scatter_dimension=1, tiled=True
-    ).astype(jnp.float32)
-    return (residual.astype(jnp.float32) + mixed).astype(jnp.bfloat16)
+    return combine(local_part, upper_part)
+
+
+def query_plan(
+    queries, local_keys, local_values, local_allowed, upper_keys, upper_values,
+    leaf_mid, mid_root, upper_len, head_count, my_index, root_count, chunk,
+):
+    dev_count = lax.axis_size("tok")
+    row_count = queries.shape[0]
+    col_count = queries.shape[1]
+    head_width = col_count // head_count
+    node_count = upper_keys.shape[0]
+    scale = head_width ** (-0.5)
+    all_queries = lax.all_gather(queries, "tok", axis=0, tiled=True)
+    req_mid = leaf_mid.astype(jnp.int32)
+    req_root = jnp.take(mid_root, req_mid).astype(jnp.int32)
+    node_ids = jnp.arange(node_count, dtype=jnp.int32)
+    node_used = (node_ids[None, :] == req_root[:, None]) | (
+        node_ids[None, :] == root_count + req_mid[:, None]
+    )
+    pos_ok = (my_index * chunk + jnp.arange(chunk, dtype=jnp.int32))[None, :] < upper_len[:, None]
+    seen = (node_used[:, :, None] & pos_ok[None, :, :]).reshape(dev_count, 1, node_count * chunk)
+    flat_keys = upper_keys.reshape(node_count * chunk, col_count)
+    flat_values = upper_values.reshape(node_count * chunk, col_count)
+
+    upper_scores = []
+    local_scores = []
+    maxima = []
+    for head in range(head_count):
+        cols = slice(head * head_width, (head + 1) * head_width)
+        scores = lax.dot_general(
+            all_queries[:, cols], flat_keys[:, cols], (((1,), (1,)), ((), ())),
+            preferred_element_type=jnp.float32,
+        ) * scale
+        scores = jnp.where(seen, scores.reshape(dev_count, row_count, -1), NEG_FILL)
+        upper_max = jnp.max(scores, axis=2)
+        own = lax.dynamic_slice_in_dim(upper_max, my_index, 1, axis=0)
+        mine = lax.dot_general(
+            queries[:, cols], local_keys[:, cols], (((1,), (1,)), ((), ())),
+            preferred_element_type=jnp.float32,
+        ) * scale
+        mine = jnp.where(local_allowed, mine, NEG_FILL)
+        own = jnp.maximum(own, jnp.max(mine, axis=1)[None, :])
+        maxima.append(lax.dynamic_update_slice_in_dim(upper_max, own, my_index, axis=0))
+        upper_scores.append(scores)
+        local_scores.append(mine)
+    row_max = lax.pmax(jnp.stack(maxima, axis=2), "tok")
+    sums = []
+    totals = []
+    for head in range(head_count):
+        cols = slice(head * head_width, (head + 1) * head_width)
+        head_max = row_max[:, :, head : head + 1]
+        exps = jnp.where(seen, jnp.exp(upper_scores[head] - head_max), 0.0)
+        totals.append(jnp.sum(exps, axis=2))
+        sums.append(
+            jnp.dot(
+                exps.reshape(dev_count * row_count, -1).astype(jnp.bfloat16),
+                flat_values[:, cols],
+                preferred_element_type=jnp.float32,
+            )
+        )
+    upper_sum, upper_total = lax.psum_scatter(
+        (jnp.concatenate(sums, axis=1), jnp.stack(totals, axis=2).reshape(dev_count * row_count, head_count)),
+        "tok",
+        scatter_dimension=0,
+        tiled=True,
+    )
+    own_max = lax.dynamic_index_in_dim(row_max, my_index, axis=0, keepdims=False)
+    merged = []
+    for head in range(head_count):
+        cols = slice(head * head_width, (head + 1) * head_width)
+        exps = jnp.where(
+            local_allowed, jnp.exp(local_scores[head] - own_max[:, head : head + 1]), 0.0
+        )
+        total = jnp.sum(exps, axis=1, keepdims=True) + upper_total[:, head : head + 1]
+        weighted = jnp.dot(
+            exps.astype(jnp.bfloat16), local_values[:, cols], preferred_element_type=jnp.float32
+        ) + upper_sum[:, cols]
+        merged.append((None, total, weighted))
+    return merged
 
 
 def solution(mesh):

time: 163 us -> 300 us (1.84)
  waiting for transfers between devices: 106 us -> 180 us
  blocking collectives: 0 us -> 35 us
  matrix products: 8.72 us -> 38.8 us
  starting transfers between devices: 7.43 us -> 0.12 us
  local copies, waits for them, and re-layouts: 9.67 us -> 15.6 us
    all_to_all x1 -> x0, waiting for transfers between devices: 83.6 us -> none  [shards(): received = lax.all_to_all(send, 'tok', 0, 0, tiled=True)]
    reduce_scatter x0 -> x1, waiting for transfers between devices: none -> 73.3 us  [query_plan(): lax.psum_scatter((jnp.concatenate(sums, axis=1), jnp.stack(totals, axis=2...]
    unnamed x1 -> x5, waiting for transfers between devices: 0.02 us -> 51.1 us
    pmax x0 -> x1, blocking collectives: none -> 35 us  [query_plan(): row_max = lax.pmax(jnp.stack(maxima, axis=2), 'tok')]
    all_gather x0 -> x1, waiting for transfers between devices: none -> 33.2 us  [query_plan(): all_queries = lax.all_gather(queries, 'tok', axis=0, tiled=True)]
    dot_general x16, matrix products: 7.19 us -> 36.7 us  [the longest x4 15 us: query_plan(): jnp.dot(exps.reshape(dev_count * row_count, -1).astype(jnp.bfloat16), fla...]
    unnamed x38 -> x65, local copies, waits for them, and re-layouts: 0.44 us -> 9.09 us
    all_to_all x1 -> x0, starting transfers between devices: 7.4 us -> none  [shards(): received = lax.all_to_all(send, 'tok', 0, 0, tiled=True)]
  transfers between devices with their start and end apart: 2 -> 4, of which waited for: 2 -> 4; matrix products, arithmetic and copies ran while one was open for 5% -> 10% of each run, Pallas kernels for 0% -> 0%
where the time goes in v3:
time: 300 us; the launch traced here: 299 us
  waiting for transfers between devices  180 us (60%)
  matrix products  38.8 us (13%)
  blocking collectives  35 us (12%)
  other arithmetic  16 us (5%)
  local copies, waits for them, and re-layouts  15.6 us (5%)
  between operations  13.7 us (5%)
    reduce_scatter x1, waiting for transfers between devices, query_plan(): lax.psum_scatter((jnp.concatenate(sums, axis=1), jnp.stack(totals, axis=2...  73.3 us
    unnamed x5, waiting for transfers between devices  51.1 us
    pmax x1, blocking collectives, query_plan(): row_max = lax.pmax(jnp.stack(maxima, axis=2), 'tok')  35 us
    all_gather x1, waiting for transfers between devices, query_plan(): all_queries = lax.all_gather(queries, 'tok', axis=0, tiled=True)  33.2 us
    reduce_scatter x1, waiting for transfers between devices, shards(): lax.psum_scatter(projected.astype(jnp.bfloat16), 'grp', scatter_dimension...  22.5 us
    dot_general x4, matrix products, query_plan(): jnp.dot(exps.reshape(dev_count * row_count, -1).astype(jnp.bfloat16), fla...  15 us
    unnamed x65, local copies, waits for them, and re-layouts  9.09 us
    dot_general x4, matrix products, query_plan(): lax.dot_general(all_queries[:, cols], flat_keys[:, cols], (((1,), (1,)),...  8.22 us
  transfers between devices with their start and end apart: 4, of which 4 were waited for; matrix products, arithmetic and copies ran while one was open for 10% of the time, Pallas kernels for 0%

profile of v3, /device:TPU:0, one launch (start us, length us, event | category | flops | bytes accessed | tf_op | source)
XLA Modules:
  0.0 299.4 jit_solution(17973138903810217957)
XLA Ops:
  6.5 0.7 all-gather.2.cloned.1.call-update
  7.3 0.0 reduce-scatter.12.cloned.1.call-start
  7.3 0.7 compare_select_fusion
  8.0 1.3 gather_fusion
  9.3 0.7 broadcast_reduce_fusion
  10.0 0.7 and_select_fusion
  10.7 0.1 bitcast_and_fusion
  10.8 0.3 broadcast_in_dim.119
  11.1 1.3 copy.27
  12.4 1.4 fusion.100
  13.8 0.6 iota_compare_fusion.3
  14.5 0.7 iota_compare_fusion.4
  15.2 2.0 fusion.134
  17.1 2.0 fusion.133
  19.2 2.0 fusion.132
  21.1 2.0 fusion.131
  23.1 33.2 %all-gather.2.cloned.1.call-done = bf16[1536,512]{1,0:T(8,128)(2,1)} async-done(((bf16[192,512]{1,0:T(8,128)(2,1)}), bf16[1536,512]{1,0:T(8,128)(2,1)}) %all-gather.2.cloned.1.call-update) | async-done | bytes 1572880 | tf_op jit(solution)/shard_map/all_gather | solution.py:159
  56.3 2.0 fusion.40
  58.3 0.8 fusion.42
  59.1 0.8 fusion.44
  59.9 0.5 copy-done.1
  60.4 1.4 copy-done.2
  61.9 4.7 %fusion = (f32[1536]{0:T(1024)S(1)}, f32[1536]{0:T(1024)S(1)}, f32[1536]{0:T(1024)S(1)}, f32[1536]{0:T(1024)S(1)}, f32[1536,768]{0,1:T(8,128)}) fusion(pred[1536,768]{0,1:T(32,128)(4,1)S(1)} %copy.27, f32[1536,768]{0,1:T(8,128)S(1)} %fusion.40, f32[1536,768]{0,1:T(8,128)S(1)} %fusion.42, f32[1536,768]{0,1:T(8,128)S(1)} %fusion.44, ...), kind=kOutput, calls=%fused_computation.9 | convolution fusion | flops 316139520 | bytes 20668416 | tf_op jit(solution)/shard_map/dot_general | solution.py:176
  66.6 0.1 reduce_max.81
  66.6 0.1 stack.38
  66.7 0.1 reduce_max.84
  66.8 0.1 stack.40
  66.9 0.1 reduce_max.87
  66.9 0.1 stack.42
  67.0 0.1 reduce_max.90
  67.1 0.1 stack.44
  67.4 35.0 %pmax.7 = f32[8,192,4]{1,0,2:T(8,128)S(1)} all-reduce(f32[8,192,4]{1,0,2:T(8,128)S(1)} %pad_maximum_fusion.5), channel_id=1, replica_groups=mesh['tok'=8,'grp'=4] {'tok'}, use_global_device_ids=true, to_apply=%region_10.11 | all-reduce | flops 6144 | bytes 49152 | tf_op jit(solution)/shard_map/pmax | solution.py:192
  102.4 0.1 sub.100
  102.5 0.1 sub.91
  102.6 0.1 sub.94
  102.6 0.1 sub.97
  102.7 4.9 %fusion.16 = f32[1536,128]{0,1:T(8,128)S(1)} fusion(pred[1536,768]{0,1:T(32,128)(4,1)} %copy-done.4, f32[1536,768]{0,1:T(8,128)} %copy-done.3, f32[1536]{0:T(1024)S(1)} %sub.94, bf16[768,512]{1,0:T(8,128)(2,1)} %bitcast.111), kind=kOutput, calls=%fused_computation.25 | convolution fusion | flops 307888128 | bytes 6887424 | tf_op jit(solution)/shard_map/dot_general | solution.py:201
  107.7 2.3 fusion.14
  110.0 5.4 %fusion.18 = f32[1536,128]{0,1:T(8,128)} fusion(pred[1536,768]{0,1:T(32,128)(4,1)S(1)} %copy-done.5, f32[1536,768]{0,1:T(8,128)} %get-tuple-element.31, f32[1536]{0:T(1024)S(1)} %sub.91, bf16[768,512]{1,0:T(8,128)(2,1)S(1)} %bitcast.113), kind=kOutput, calls=%fused_computation.26 | convolution fusion | flops 307888128 | bytes 6889472 | tf_op jit(solution)/shard_map/dot_general | solution.py:201
  115.5 4.7 %fusion.4 = (f32[1536]{0:T(1024)S(1)}, f32[1536]{0:T(1024)S(1)}, f32[1536]{0:T(1024)S(1)}, f32[1536]{0:T(1024)S(1)}) fusion(pred[1536,768]{0,1:T(32,128)(4,1)S(1)} %copy-done.5, f32[1536,768]{0,1:T(8,128)S(1)} %bitcast.80, f32[1536]{0:T(1024)S(1)} %sub.91, f32[1536]{0:T(1024)S(1)} %sub.100, f32[1536,768]{0,1:T(8,128)S(1)} %bitcast.74, f32[1536]{0:T(1024)S(1)} %sub.97, ...), kind=kLoop, calls=%fused_computation.14 | loop fusion | flops 23586816 | bytes 20103168 | tf_op jit(solution)/shard_map/reduce_sum | solution.py:199
  120.2 2.3 fusion.12
  122.6 1.2 copy.45
  123.8 0.0 reduce-scatter.12.cloned.1.call-update
  123.8 0.0 reduce-scatter.10.cloned.1.call-start
  123.9 3.5 %pad_maximum_fusion = f32[1536,512]{0,1:T(8,128)} fusion(f32[1536,128]{0,1:T(8,128)} %fusion.12, f32[1536,128]{0,1:T(8,128)} %fusion.14, f32[1536,128]{0,1:T(8,128)S(1)} %fusion.16, f32[1536,128]{0,1:T(8,128)} %fusion.18), kind=kLoop, calls=%fused_computation.13 | loop fusion | flops 2359296 | bytes 6291456 | tf_op jit(solution)/shard_map/concatenate | solution.py:208
  127.4 3.7 %copy.43 = f32[1536,512]{1,0:T(8,128)} copy(f32[1536,512]{0,1:T(8,128)} %pad_maximum_fusion) | data formatting | bytes 6291456
  131.1 0.0 reduce-scatter.10.cloned.1.call-update
  131.1 0.0 reduce-scatter.8.cloned.1.call-start
  131.3 2.0 fusion.32
  133.3 50.3 %reduce-scatter.12.cloned.1.call-done = f32[192,4]{1,0:T(8,128)} async-done(((f32[1536,4]{1,0:T(8,128)}), f32[192,4]{1,0:T(8,128)}) %reduce-scatter.12.cloned.1.call-update) | async-done | bytes 3088
  183.6 1.8 fusion.128
  185.4 1.0 copy.48
  186.4 1.0 copy.49
  187.4 0.1 copy.50
  187.5 0.1 copy.51
  187.6 73.3 %reduce-scatter.10.cloned.1.call-done = f32[192,512]{1,0:T(8,128)} async-done(((f32[1536,512]{1,0:T(8,128)}), f32[192,512]{1,0:T(8,128)}) %reduce-scatter.10.cloned.1.call-update) | async-done | bytes 393232 | tf_op jit(solution)/shard_map/reduce_scatter | solution.py:207
  260.9 1.5 fusion.28
  262.4 1.5 fusion.29
  263.9 1.3 fusion.30
  265.3 1.2 fusion.31
  266.5 2.1 convolution_convert_fusion
  268.6 0.0 reduce-scatter.8.cloned.1.call-update
  268.6 22.5 %reduce-scatter.8.cloned.1.call-done = bf16[192,512]{1,0:T(8,128)(2,1)} async-done(((bf16[192,2048]{1,0:T(8,128)(2,1)}), bf16[192,512]{1,0:T(8,128)(2,1)}) %reduce-scatter.8.cloned.1.call-update) | async-done | bytes 196624 | tf_op jit(solution)/shard_map/reduce_scatter | solution.py:107
  291.2 1.7 add_convert_fusion
  (89 shorter events, 0.5 us)
Async XLA Ops:
  6.5 260.0 %copy-start = (bf16[512,2048]{1,0:T(8,128)(2,1)S(1)}, bf16[512,2048]{1,0:T(8,128)(2,1)}, u32[]{:S(2)}) copy-start(bf16[512,2048]{1,0:T(8,128)(2,1)} %param.18) | copy-start | bytes 6291460
  6.5 10.6 %copy-start.7 = (bf16[192,512]{1,0:T(8,128)(2,1)S(1)}, bf16[192,512]{1,0:T(8,128)(2,1)}, u32[]{:S(2)}) copy-start(bf16[192,512]{1,0:T(8,128)(2,1)} %param.15) | copy-start | bytes 589828
  6.5 49.8 %all-gather.2.cloned.1.call-start = ((), (), s32[]{:S(2)}) async-start(), calls=%async_computation.3 | async-start | bytes 1769472 | tf_op jit(solution)/shard_map/all_gather | solution.py:159
  7.3 176.3 %reduce-scatter.12.cloned.1.call-start = ((), (), s32[]{:S(2)}) async-start(), calls=%async_computation.6 | async-start | bytes 884736
  12.4 47.5 %copy-start.4 = (pred[1536,768]{0,1:T(32,128)(4,1)}, pred[1536,768]{0,1:T(32,128)(4,1)S(1)}, u32[]{:S(2)}) copy-start(pred[1536,768]{0,1:T(32,128)(4,1)S(1)} %copy.27) | copy-start | bytes 3538948
  15.1 4.0 %copy-start.17 = (pred[192]{0:T(512)(128)(4,1)}, pred[192]{0:T(512)(128)(4,1)S(1)}, u32[]{:S(2)}) copy-start(pred[192]{0:T(512)(128)(4,1)S(1)} %iota_compare_fusion.4) | copy-start | bytes 580
  56.3 2.0 copy-start.6
  56.3 2.0 copy-start.10
  58.3 2.1 copy-start.1
  59.1 2.8 copy-start.2
  61.9 4.7 %copy-start.3 = (f32[1536,768]{0,1:T(8,128)}, f32[1536,768]{0,1:T(8,128)S(1)}, u32[]{:S(2)}) copy-start(f32[1536,768]{0,1:T(8,128)S(1)} %fusion.44) | copy-start | bytes 14155780
  102.4 5.2 %slice-start.2 = ((s8[4718592]{0:T(1024)(128)(4,1)}), s8[524288]{0:T(1024)(128)(4,1)S(1)}, s32[]{:S(2)}) async-start(s8[4718592]{0:T(1024)(128)(4,1)} %bitcast.75), calls=%async_computation.9 | async-start | bytes 1048576
  102.7 5.0 %slice-start.3 = ((s8[4718592]{0:T(1024)(128)(4,1)}), s8[4194304]{0:T(1024)(128)(4,1)S(1)}, s32[]{:S(2)}) async-start(s8[4718592]{0:T(1024)(128)(4,1)} %bitcast.75), calls=%async_computation.10 | async-start | bytes 8388608
  102.7 5.0 %copy-start.5 = (pred[1536,768]{0,1:T(32,128)(4,1)S(1)}, pred[1536,768]{0,1:T(32,128)(4,1)}, u32[]{:S(2)}) copy-start(pred[1536,768]{0,1:T(32,128)(4,1)} %copy-done.4) | copy-start | bytes 3538948
  102.7 5.0 %copy-start.18 = (bf16[6,128,512]{2,1,0:T(8,128)(2,1)S(1)}, bf16[6,128,512]{2,1,0:T(8,128)(2,1)}, u32[]{:S(2)}) copy-start(bf16[6,128,512]{2,1,0:T(8,128)(2,1)} %param.22) | copy-start | bytes 2359300
  107.7 7.8 %slice-start = ((s8[4718592]{0:T(1024)(128)(4,1)}), s8[4194304]{0:T(1024)(128)(4,1)S(1)}, s32[]{:S(2)}) async-start(s8[4718592]{0:T(1024)(128)(4,1)} %bitcast.73), calls=%async_computation.7 | async-start | bytes 8388608
  107.7 7.8 %slice-start.4 = ((s8[4718592]{0:T(1024)(128)(4,1)}), s8[4194304]{0:T(1024)(128)(4,1)S(1)}, s32[]{:S(2)}) async-start(s8[4718592]{0:T(1024)(128)(4,1)} %bitcast.77), calls=%async_computation.11 | async-start | bytes 8388608
  107.7 7.8 %slice-start.6 = ((s8[4718592]{0:T(1024)(128)(4,1)}), s8[4194304]{0:T(1024)(128)(4,1)S(1)}, s32[]{:S(2)}) async-start(s8[4718592]{0:T(1024)(128)(4,1)} %bitcast.79), calls=%async_computation.13 | async-start | bytes 8388608
  110.0 5.4 %slice-start.1 = ((s8[4718592]{0:T(1024)(128)(4,1)}), s8[524288]{0:T(1024)(128)(4,1)S(1)}, s32[]{:S(2)}) async-start(s8[4718592]{0:T(1024)(128)(4,1)} %bitcast.73), calls=%async_computation.8 | async-start | bytes 1048576
  110.0 5.5 %slice-start.5 = ((s8[4718592]{0:T(1024)(128)(4,1)}), s8[524288]{0:T(1024)(128)(4,1)S(1)}, s32[]{:S(2)}) async-start(s8[4718592]{0:T(1024)(128)(4,1)} %bitcast.77), calls=%async_computation.12 | async-start | bytes 1048576
  110.0 5.5 %slice-start.7 = ((s8[4718592]{0:T(1024)(128)(4,1)}), s8[524288]{0:T(1024)(128)(4,1)S(1)}, s32[]{:S(2)}) async-start(s8[4718592]{0:T(1024)(128)(4,1)} %bitcast.79), calls=%async_computation.14 | async-start | bytes 1048576
  123.8 137.0 %reduce-scatter.10.cloned.1.call-start = ((), (), s32[]{:S(2)}) async-start(), calls=%async_computation.5 | async-start | bytes 3538944 | tf_op jit(solution)/shard_map/reduce_scatter | solution.py:207
  127.4 3.9 %copy-start.8 = (f32[192,704]{1,0:T(8,128)S(1)}, f32[192,704]{1,0:T(8,128)}, u32[]{:S(2)}) copy-start(f32[192,704]{1,0:T(8,128)} %get-tuple-element.33) | copy-start | bytes 1622020
  127.4 3.9 %copy-start.9 = (f32[192,704]{1,0:T(8,128)S(1)}, f32[192,704]{1,0:T(8,128)}, u32[]{:S(2)}) copy-start(f32[192,704]{1,0:T(8,128)} %get-tuple-element.35) | copy-start | bytes 1622020
  131.1 160.1 %reduce-scatter.8.cloned.1.call-start = ((), (), s32[]{:S(2)}) async-start(), calls=%async_computation.4 | async-start | bytes 983040 | tf_op jit(solution)/shard_map/reduce_scatter | solution.py:107
  131.2 2.0 copy-start.12
  131.2 2.0 copy-start.14
  131.2 2.0 copy-start.15
  131.2 2.0 copy-start.16
  187.5 77.7 %copy-start.13 = (f32[192,1]{0,1:T(1,128)S(1)}, f32[192,1]{0,1:T(1,128)}, u32[]{:S(2)}) copy-start(f32[192,1]{0,1:T(1,128)} %copy-done.12) | copy-start | bytes 2308
  260.8 4.4 %copy-start.19 = (bf16[1,512,512]{2,1,0:T(8,128)(2,1)S(1)}, bf16[1,512,512]{2,1,0:T(8,128)(2,1)}, u32[]{:S(2)}) copy-start(bf16[1,512,512]{2,1,0:T(8,128)(2,1)} %param.20) | copy-start | bytes 1572868
  260.9 4.4 %copy-start.20 = (bf16[192,512]{1,0:T(8,128)(2,1)S(1)}, bf16[192,512]{1,0:T(8,128)(2,1)}, u32[]{:S(2)}) copy-start(bf16[192,512]{1,0:T(8,128)(2,1)} %param.16) | copy-start | bytes 589828
  262.4 28.8 %copy-start.11 = (bf16[192,512]{1,0:T(8,128)(2,1)S(1)}, bf16[192,512]{1,0:T(8,128)(2,1)}, u32[]{:S(2)}) copy-start(bf16[192,512]{1,0:T(8,128)(2,1)} %param.17) | copy-start | bytes 589828
Sparse Core Ops, SparseCore 0:
  9.5 46.7 all-gather.1
  123.9 59.5 reduce-scatter.11
  187.6 73.2 reduce-scatter.9
  268.8 22.3 reduce-scatter.7

commit v4 on v2

--- a/solution.py
+++ b/solution.py
@@ -1,6 +1,8 @@
 import jax
 import jax.numpy as jnp
 from jax import lax
+from jax.experimental import pallas as pl
+from jax.experimental.pallas import tpu as pltpu
 from jax.sharding import PartitionSpec as P
 
 HEAD_DIM = 128
@@ -43,6 +45,72 @@
             (new_max, total_a * scale_a + total_b * scale_b, sum_a * scale_a + sum_b * scale_b)
         )
     return merged
+
+
+def gather_nodes(dest_nodes, upper_keys, upper_values):
+    dest_count = dest_nodes.shape[0]
+    chunk, cols = upper_keys.shape[1], upper_keys.shape[2]
+
+    def kernel(nodes_ref, keys_ref, values_ref, out_ref, sems):
+        def copies(dest):
+            found = []
+            for slot in range(2):
+                node = nodes_ref[dest, slot]
+                found.append(
+                    pltpu.make_async_copy(
+                        keys_ref.at[node], out_ref.at[dest, slot], sems.at[dest, slot]
+                    )
+                )
+                found.append(
+                    pltpu.make_async_copy(
+                        values_ref.at[node], out_ref.at[dest, 2 + slot], sems.at[dest, 2 + slot]
+                    )
+                )
+            return found
+
+        def start(dest, carry):
+            for copy in copies(dest):
+                copy.start()
+            return carry
+
+        def wait(dest, carry):
+            for copy in copies(dest):
+                copy.wait()
+            return carry
+
+        lax.fori_loop(0, dest_count, start, 0)
+        lax.fori_loop(0, dest_count, wait, 0)
+
+    return pl.pallas_call(
+        kernel,
+        out_shape=jax.ShapeDtypeStruct((dest_count, 4, chunk, cols), upper_keys.dtype),
+        grid_spec=pltpu.PrefetchScalarGridSpec(
+            num_scalar_prefetch=1,
+            grid=(1,),
+            in_specs=[pl.BlockSpec(memory_space=pl.ANY), pl.BlockSpec(memory_space=pl.ANY)],
+            out_specs=pl.BlockSpec(memory_space=pl.ANY),
+            scratch_shapes=[pltpu.SemaphoreType.DMA((dest_count, 4))],
+        ),
+    )(dest_nodes, upper_keys, upper_values)
+
+
+def sum_over_grp(projected):
+    size = lax.axis_size("grp")
+    index = lax.axis_index("grp")
+    block = projected.shape[1] // size
+    kept = projected
+    step = size // 2
+    while step >= 1:
+        width = step * block
+        lower = (index & step) == 0
+        keep = jnp.where(lower, kept[:, :width], kept[:, width:])
+        give = jnp.where(lower, kept[:, width:], kept[:, :width])
+        if step == size // 2:
+            give = give.astype(jnp.bfloat16)
+        pairs = [(g, g ^ step) for g in range(size)]
+        kept = keep + lax.ppermute(give, "grp", pairs).astype(jnp.float32)
+        step //= 2
+    return kept
 
 
 def shards(
@@ -74,13 +142,7 @@
     dest_mid = leaf_mid.astype(jnp.int32)
     dest_root = jnp.take(mid_root, dest_mid).astype(jnp.int32)
     dest_nodes = jnp.stack([dest_root, root_count + dest_mid], axis=1)
-    send = jnp.concatenate(
-        [
-            upper_keys.at[dest_nodes].get(mode="promise_in_bounds"),
-            upper_values.at[dest_nodes].get(mode="promise_in_bounds"),
-        ],
-        axis=1,
-    )
+    send = gather_nodes(dest_nodes, upper_keys, upper_values)
     received = lax.all_to_all(send, "tok", 0, 0, tiled=True)
     recv_keys = received[:, :2]
     recv_values = received[:, 2:]
@@ -127,9 +189,7 @@
     attended = jnp.concatenate([part[2] / part[1] for part in merged], axis=1)
     attention = jnp.where(is_live[:, None], attended, 0.0).astype(jnp.bfloat16)
     projected = jnp.dot(attention, w_out, preferred_element_type=jnp.float32)
-    mixed = lax.psum_scatter(
-        projected.astype(jnp.bfloat16), "grp", scatter_dimension=1, tiled=True
-    ).astype(jnp.float32)
+    mixed = sum_over_grp(projected)
     return (residual.astype(jnp.float32) + mixed).astype(jnp.bfloat16)
 
 

time: 163 us -> 260 us (1.60)
  Pallas kernels: 0 us -> 129 us
  between operations: 14.4 us -> 0.99 us
  waiting for transfers between devices: 106 us -> 93.6 us
  other arithmetic: 16.1 us -> 12.3 us
  local copies, waits for them, and re-layouts: 9.67 us -> 6.09 us
    pallas_call x0 -> x1, Pallas kernels: none -> 129 us  [gather_nodes(): pl.pallas_call(kernel, out_shape=jax.ShapeDtypeStruct((dest_count, 4, chu...]
    reduce_scatter x1 -> x0, waiting for transfers between devices: 22.5 us -> none  [shards(): lax.psum_scatter(projected.astype(jnp.bfloat16), 'grp', scatter_dimension...]
    ppermute x0 -> x2, waiting for transfers between devices: none -> 9.9 us  [sum_over_grp(): kept = keep + lax.ppermute(give, 'grp', pairs).astype(jnp.float32)]
    gather x2 -> x0, local copies, waits for them, and re-layouts: 5.24 us -> none  [the longest x1 3.23 us: shards(): upper_keys.at[dest_nodes].get(mode='promise_in_bounds')]
    concatenate x1 -> x0, other arithmetic: 4.51 us -> none  [shards(): jnp.concatenate([upper_keys.at[dest_nodes].get(mode='promise_in_bounds'),...]
  transfers between devices with their start and end apart: 2 -> 3, of which waited for: 2 -> 3; matrix products, arithmetic and copies ran while one was open for 5% -> 3% of each run, Pallas kernels for 0% -> 0%
where the time goes in v4:
time: 260 us; the launch traced here: 259 us
  Pallas kernels  129 us (50%)
  waiting for transfers between devices  93.6 us (36%)
  other arithmetic  12.3 us (5%)
  starting transfers between devices  9.05 us (3%)
  matrix products  7.84 us (3%)
  local copies, waits for them, and re-layouts  6.09 us (2%)
    pallas_call x1, Pallas kernels, gather_nodes(): pl.pallas_call(kernel, out_shape=jax.ShapeDtypeStruct((dest_count, 4, chu...  129 us
    all_to_all x1, waiting for transfers between devices, shards(): received = lax.all_to_all(send, 'tok', 0, 0, tiled=True)  83.7 us
    ppermute x2, waiting for transfers between devices, sum_over_grp(): kept = keep + lax.ppermute(give, 'grp', pairs).astype(jnp.float32)  9.9 us
    all_to_all x1, starting transfers between devices, shards(): received = lax.all_to_all(send, 'tok', 0, 0, tiled=True)  7.4 us
  transfers between devices with their start and end apart: 3, of which 3 were waited for; matrix products, arithmetic and copies ran while one was open for 3% of the time, Pallas kernels for 0%

profile of v4, /device:TPU:0, one launch (start us, length us, event | category | flops | bytes accessed | tf_op | source)
XLA Modules:
  0.0 259.1 jit_solution(15452820931628024158)
XLA Ops:
  0.0 0.0 copy-start
  0.0 0.8 compare_select_fusion
  0.8 1.3 gather_fusion
  2.1 1.3 fusion.111
  3.4 0.7 copy.19.nodes_ref
  4.1 129.2 %shard_map.136 = bf16[8,4,128,512]{3,2,1,0:T(8,128)(2,1)} custom-call(s32[8,2]{1,0:T(8,128)} %copy.19.nodes_ref, bf16[6,128,512]{2,1,0:T(8,128)(2,1)} %keys_ref.1, bf16[6,128,512]{2,1,0:T(8,128)(2,1)} %values_ref.1), custom_call_target="tpu_custom_call" | custom-call | tf_op jit(solution)/shard_map/pallas_call | solution.py:84
  133.2 0.0 copy-start.1
  133.3 0.0 copy-start.16
  133.3 0.0 copy-start.17
  133.3 0.0 copy-start.18
  133.3 0.0 copy-start.3
  133.3 0.0 copy-start.4
  133.3 0.0 copy-start.12
  133.3 7.4 %all-to-all-start = ((bf16[8,4,128,512]{3,2,1,0:T(8,128)(2,1)}), bf16[8,4,128,512]{3,2,1,0:T(8,128)(2,1)}, u32[]{:S(2)}, u32[]{:S(2)}) async-start(bf16[8,4,128,512]{3,2,1,0:T(8,128)(2,1)} %shard_map.136), calls=%async_computation | async-start | bytes 8388608 | tf_op jit(solution)/shard_map/all_to_all | solution.py:146
  141.3 0.0 copy-done.1
  141.3 1.2 fusion.108
  142.5 0.0 copy-done.16
  142.5 1.3 fusion.109
  143.8 1.3 pad_add_fusion.2
  145.1 0.1 iota_add_fusion
  145.2 0.1 broadcast_compare_fusion
  145.3 0.0 copy-done.17
  145.3 0.0 copy-done.18
  145.3 0.6 select_reduce_fusion.1
  145.9 0.6 iota_compare_fusion.1
  146.6 0.6 iota_compare_fusion.2
  147.2 0.0 copy-done.3
  147.2 0.0 copy-done.4
  147.2 0.0 copy-done.12
  147.2 0.3 fusion.144
  147.6 0.3 fusion.145
  147.9 0.3 fusion.146
  148.3 1.2 fusion.139
  149.5 0.8 fusion.52
  150.3 83.7 %all-to-all-done = bf16[8,4,128,512]{3,2,1,0:T(8,128)(2,1)} async-done(((bf16[8,4,128,512]{3,2,1,0:T(8,128)(2,1)}), bf16[8,4,128,512]{3,2,1,0:T(8,128)(2,1)}, u32[]{:S(2)}, u32[]{:S(2)}) %all-to-all-start) | async-done | bytes 4194336 | tf_op jit(solution)/shard_map/all_to_all | solution.py:146
  234.0 2.5 fusion.138
  236.5 0.0 copy-done.13
  236.5 0.5 fusion.140
  237.0 0.5 fusion.141
  237.5 0.5 fusion.142
  237.9 0.5 fusion.143
  238.4 0.0 copy-start.11
  238.4 0.0 copy-start.14
  238.5 1.2 fusion.4
  239.7 0.3 convolution_multiply_fusion.15
  240.0 0.3 convolution_multiply_fusion.13
  240.4 0.4 copy-done.6
  240.8 0.3 convolution_multiply_fusion.11
  241.1 0.3 convolution_multiply_fusion.9
  241.4 0.4 fusion.27
  241.9 0.4 fusion.25
  242.3 0.4 fusion.23
  242.8 0.4 fusion.21
  243.2 0.0 copy-done
  243.2 0.6 fusion.73
  243.9 1.1 copy-done.2
  245.0 0.1 select_convert_fusion
  245.1 1.6 collective-permute-start
  246.7 8.2 %collective-permute-done = bf16[192,1024]{1,0:T(8,128)(2,1)S(1)} collective-permute-done((bf16[192,1024]{1,0:T(8,128)(2,1)S(1)}, bf16[192,1024]{1,0:T(8,128)(2,1)S(1)}, u32[]{:S(2)}, u32[]{:S(2)}) %collective-permute-start) | collective-permute-done | bytes 393248 | tf_op jit(solution)/shard_map/ppermute | solution.py:111
  254.9 1.5 convert_add_fusion
  256.4 0.1 slice_select_fusion
  256.5 0.1 collective-permute-start.1
  256.6 1.7 collective-permute-done.1
  258.3 0.8 add_convert_fusion
  (27 shorter events, 0.2 us)
Async XLA Ops:
  0.0 243.2 %copy-start = (bf16[512,2048]{1,0:T(8,128)(2,1)S(1)}, bf16[512,2048]{1,0:T(8,128)(2,1)}, u32[]{:S(2)}) copy-start(bf16[512,2048]{1,0:T(8,128)(2,1)} %param.18) | copy-start | bytes 6291460
  133.2 8.1 %copy-start.1 = (s32[4]{0:T(128)S(1)}, s32[4]{0:T(128)}, u32[]{:S(2)}) copy-start(s32[4]{0:T(128)} %param.25) | copy-start | bytes 52
  133.3 9.3 %copy-start.16 = (s32[6]{0:T(128)S(1)}, s32[6]{0:T(128)}, u32[]{:S(2)}) copy-start(s32[6]{0:T(128)} %param.26) | copy-start | bytes 76
  133.3 12.0 %copy-start.17 = (s32[8]{0:T(128)S(1)}, s32[8]{0:T(128)}, u32[]{:S(2)}) copy-start(s32[8]{0:T(128)} %param.27) | copy-start | bytes 100
  133.3 12.0 %copy-start.18 = (s32[8]{0:T(128)S(1)}, s32[8]{0:T(128)}, u32[]{:S(2)}) copy-start(s32[8]{0:T(128)} %param.23) | copy-start | bytes 100
  133.3 13.9 %copy-start.3 = (bf16[1,512,512]{2,1,0:T(8,128)(2,1)S(1)}, bf16[1,512,512]{2,1,0:T(8,128)(2,1)}, u32[]{:S(2)}) copy-start(bf16[1,512,512]{2,1,0:T(8,128)(2,1)} %param.19) | copy-start | bytes 1572868
  133.3 13.9 %copy-start.4 = (bf16[192,512]{1,0:T(8,128)(2,1)S(1)}, bf16[192,512]{1,0:T(8,128)(2,1)}, u32[]{:S(2)}) copy-start(bf16[192,512]{1,0:T(8,128)(2,1)} %param.15) | copy-start | bytes 589828
  133.3 13.9 %copy-start.12 = (bf16[192,512]{1,0:T(8,128)(2,1)S(1)}, bf16[192,512]{1,0:T(8,128)(2,1)}, u32[]{:S(2)}) copy-start(bf16[192,512]{1,0:T(8,128)(2,1)} %param.14) | copy-start | bytes 589828
  133.3 100.7 %all-to-all-start = ((bf16[8,4,128,512]{3,2,1,0:T(8,128)(2,1)}), bf16[8,4,128,512]{3,2,1,0:T(8,128)(2,1)}, u32[]{:S(2)}, u32[]{:S(2)}) async-start(bf16[8,4,128,512]{3,2,1,0:T(8,128)(2,1)} %shard_map.136), calls=%async_computation | async-start | bytes 8388608 | tf_op jit(solution)/shard_map/all_to_all | solution.py:146
  147.6 1.9 copy-start.9
  147.9 1.6 copy-start.7
  148.3 1.2 copy-start.5
  150.3 86.2 %copy-start.13 = (bf16[192,512]{1,0:T(8,128)(2,1)S(1)}, bf16[192,512]{1,0:T(8,128)(2,1)}, u32[]{:S(2)}) copy-start(bf16[192,512]{1,0:T(8,128)(2,1)} %param.14) | copy-start | bytes 589828
  238.4 1.3 copy-start.10
  238.4 1.3 copy-start.11
  238.4 1.3 copy-start.14
  238.4 1.6 copy-start.8
  239.6 1.1 copy-start.6
  243.9 1.2 copy-start.2
  245.1 9.8 %collective-permute-start = (bf16[192,1024]{1,0:T(8,128)(2,1)S(1)}, bf16[192,1024]{1,0:T(8,128)(2,1)S(1)}, u32[]{:S(2)}, u32[]{:S(2)}) collective-permute-start(bf16[192,1024]{1,0:T(8,128)(2,1)S(1)} %select_convert_fusion), channel_id=1, source_target_pairs={{0,2},{1,3},{2,0},{3,1},{4,6},{5,7},{6,4},{7,5},{8,10},{9,11},{10,... | collective-permute-start | bytes 1179656 | tf_op jit(solution)/shard_map/ppermute | solution.py:111
  246.7 11.6 %copy-start.15 = (bf16[192,512]{1,0:T(8,128)(2,1)S(1)}, bf16[192,512]{1,0:T(8,128)(2,1)}, u32[]{:S(2)}) copy-start(bf16[192,512]{1,0:T(8,128)(2,1)} %param.17) | copy-start | bytes 589828
  256.5 1.8 collective-permute-start.1

commit v5 on v2

--- a/solution.py
+++ b/solution.py
@@ -45,6 +45,25 @@
     return merged
 
 
+def sum_over_grp(projected):
+    size = lax.axis_size("grp")
+    index = lax.axis_index("grp")
+    block = projected.shape[1] // size
+    kept = projected
+    step = size // 2
+    while step >= 1:
+        width = step * block
+        lower = (index & step) == 0
+        keep = jnp.where(lower, kept[:, :width], kept[:, width:])
+        give = jnp.where(lower, kept[:, width:], kept[:, :width])
+        if step == size // 2:
+            give = give.astype(jnp.bfloat16)
+        pairs = [(g, g ^ step) for g in range(size)]
+        kept = keep + lax.ppermute(give, "grp", pairs).astype(jnp.float32)
+        step //= 2
+    return kept
+
+
 def shards(
     queries,
     new_keys,
@@ -74,12 +93,9 @@
     dest_mid = leaf_mid.astype(jnp.int32)
     dest_root = jnp.take(mid_root, dest_mid).astype(jnp.int32)
     dest_nodes = jnp.stack([dest_root, root_count + dest_mid], axis=1)
-    send = jnp.concatenate(
-        [
-            upper_keys.at[dest_nodes].get(mode="promise_in_bounds"),
-            upper_values.at[dest_nodes].get(mode="promise_in_bounds"),
-        ],
-        axis=1,
+    both = jnp.concatenate([upper_keys, upper_values], axis=0)
+    send = both.at[jnp.concatenate([dest_nodes, node_count + dest_nodes], axis=1)].get(
+        mode="promise_in_bounds"
     )
     received = lax.all_to_all(send, "tok", 0, 0, tiled=True)
     recv_keys = received[:, :2]
@@ -127,9 +143,7 @@
     attended = jnp.concatenate([part[2] / part[1] for part in merged], axis=1)
     attention = jnp.where(is_live[:, None], attended, 0.0).astype(jnp.bfloat16)
     projected = jnp.dot(attention, w_out, preferred_element_type=jnp.float32)
-    mixed = lax.psum_scatter(
-        projected.astype(jnp.bfloat16), "grp", scatter_dimension=1, tiled=True
-    ).astype(jnp.float32)
+    mixed = sum_over_grp(projected)
     return (residual.astype(jnp.float32) + mixed).astype(jnp.bfloat16)
 
 

time: 163 us -> 137 us (0.84)
  between operations: 14.4 us -> 1.04 us
  waiting for transfers between devices: 106 us -> 93.5 us
    reduce_scatter x1 -> x0, waiting for transfers between devices: 22.5 us -> none  [shards(): lax.psum_scatter(projected.astype(jnp.bfloat16), 'grp', scatter_dimension...]
    ppermute x0 -> x2, waiting for transfers between devices: none -> 9.9 us  [sum_over_grp(): kept = keep + lax.ppermute(give, 'grp', pairs).astype(jnp.float32)]
    ppermute x0 -> x2, starting transfers between devices: none -> 1.65 us  [sum_over_grp(): kept = keep + lax.ppermute(give, 'grp', pairs).astype(jnp.float32)]
    gather x2 -> x1, local copies, waits for them, and re-layouts: 5.24 us -> 4.15 us  [shards(): both.at[jnp.concatenate([dest_nodes, node_count + dest_nodes], axis=1)]]
    concatenate x1 -> x3, other arithmetic: 4.51 us -> 3.99 us  [the longest x1 2.68 us: shards(): both = jnp.concatenate([upper_keys, upper_values], axis=0)]
  transfers between devices with their start and end apart: 2 -> 3, of which waited for: 2 -> 3; matrix products, arithmetic and copies ran while one was open for 5% -> 7% of each run, Pallas kernels for 0% -> 0%
where the time goes in v5:
time: 137 us; the launch traced here: 136 us
  waiting for transfers between devices  93.5 us (68%)
  other arithmetic  15.1 us (11%)
  local copies, waits for them, and re-layouts  9.71 us (7%)
  starting transfers between devices  9.05 us (7%)
  matrix products  7.84 us (6%)
    all_to_all x1, waiting for transfers between devices, shards(): received = lax.all_to_all(send, 'tok', 0, 0, tiled=True)  83.6 us
    ppermute x2, waiting for transfers between devices, sum_over_grp(): kept = keep + lax.ppermute(give, 'grp', pairs).astype(jnp.float32)  9.9 us
    all_to_all x1, starting transfers between devices, shards(): received = lax.all_to_all(send, 'tok', 0, 0, tiled=True)  7.4 us
    gather x1, local copies, waits for them, and re-layouts, shards(): both.at[jnp.concatenate([dest_nodes, node_count + dest_nodes], axis=1)]  4.15 us
    dot_general x8, matrix products, partial_attention(): lax.dot_general(query_rows[:, cols], key_rows[:, cols], (((1,), (1,)), ((...  4.13 us
    dot_general x8, matrix products, partial_attention(): jnp.dot(exp_scores.astype(jnp.bfloat16), values[:, cols], preferred_eleme...  3.07 us
  transfers between devices with their start and end apart: 3, of which 3 were waited for; matrix products, arithmetic and copies ran while one was open for 7% of the time, Pallas kernels for 0%

profile of v5, /device:TPU:0, one launch (start us, length us, event | category | flops | bytes accessed | tf_op | source)
XLA Modules:
  0.0 136.3 jit_solution(11142142348195653161)
XLA Ops:
  0.0 0.0 copy-start
  0.0 0.8 compare_select_fusion.1
  0.8 1.3 gather_fusion
  2.1 1.3 add_bitcast_fusion.1
  3.4 0.1 copy.20
  3.5 0.1 reshape.366
  3.6 2.7 %pad_maximum_fusion = bf16[12,128,512]{2,1,0:T(8,128)(2,1)} fusion(bf16[6,128,512]{2,1,0:T(8,128)(2,1)} %param.22, bf16[6,128,512]{2,1,0:T(8,128)(2,1)} %param.21), kind=kLoop, calls=%fused_computation.10 | loop fusion | flops 786432 | bytes 3145728 | tf_op jit(solution)/shard_map/concatenate | solution.py:96
  6.3 4.1 %gather_fusion.1 = bf16[32,128,512]{2,1,0:T(8,128)(2,1)} fusion(bf16[12,128,512]{2,1,0:T(8,128)(2,1)} %pad_maximum_fusion, s32[1024]{0:T(1024)S(1)} %pad_clamp_fusion), kind=kCustom, calls=%fused_computation.1 | custom fusion | bytes 8388736 | tf_op jit(solution)/shard_map/gather | solution.py:97
  10.5 0.0 copy-start.3
  10.5 0.0 copy-start.4
  10.5 0.0 copy-start.12
  10.5 7.4 %all-to-all-start = ((bf16[8,4,128,512]{3,2,1,0:T(8,128)(2,1)}), bf16[8,4,128,512]{3,2,1,0:T(8,128)(2,1)}, u32[]{:S(2)}, u32[]{:S(2)}) async-start(bf16[8,4,128,512]{3,2,1,0:T(8,128)(2,1)} %bitcast.38), calls=%async_computation | async-start | bytes 8388608 | tf_op jit(solution)/shard_map/all_to_all | solution.py:100
  18.6 0.0 copy-done.1
  18.6 1.3 fusion.109
  19.8 0.0 copy-done.16
  19.8 1.2 fusion.110
  21.0 1.3 pad_add_fusion.1
  22.4 0.1 iota_add_fusion
  22.4 0.1 broadcast_compare_fusion
  22.5 0.0 copy-done.17
  22.6 0.0 copy-done.18
  22.6 0.6 select_reduce_fusion.1
  23.2 0.6 iota_compare_fusion.1
  23.9 0.6 iota_compare_fusion.2
  24.5 0.0 copy-done.3
  24.5 0.0 copy-done.4
  24.5 0.3 fusion.144
  24.9 0.3 fusion.145
  25.2 0.3 fusion.146
  25.6 1.2 fusion.139
  26.8 0.8 fusion.52
  27.6 83.6 %all-to-all-done = bf16[8,4,128,512]{3,2,1,0:T(8,128)(2,1)} async-done(((bf16[8,4,128,512]{3,2,1,0:T(8,128)(2,1)}), bf16[8,4,128,512]{3,2,1,0:T(8,128)(2,1)}, u32[]{:S(2)}, u32[]{:S(2)}) %all-to-all-start) | async-done | bytes 4194336 | tf_op jit(solution)/shard_map/all_to_all | solution.py:100
  111.2 2.5 %fusion.138 = (bf16[8,2,128,512]{3,2,1,0:T(8,128)(2,1)S(1)}, bf16[8,2,128,512]{3,2,1,0:T(8,128)(2,1)S(1)}) fusion(bf16[8,4,128,512]{3,2,1,0:T(8,128)(2,1)} %all-to-all-done), kind=kLoop, calls=%fused_computation.196 | loop fusion | bytes 8388608 | tf_op jit(solution)/shard_map/slice | solution.py:102
  113.7 0.0 copy-done.13
  113.7 0.5 fusion.140
  114.2 0.5 fusion.141
  114.6 0.5 fusion.142
  115.1 0.5 fusion.143
  115.6 0.0 copy-start.11
  115.6 0.0 copy-start.14
  115.6 1.2 fusion.4
  116.8 0.0 copy-done.10
  116.8 0.0 copy-done.11
  116.9 0.0 copy-done.14
  116.9 0.3 convolution_multiply_fusion.15
  117.2 0.3 convolution_multiply_fusion.13
  117.6 0.4 copy-done.6
  117.9 0.3 convolution_multiply_fusion.11
  118.3 0.3 convolution_multiply_fusion.9
  118.6 0.4 fusion.27
  119.1 0.4 fusion.25
  119.5 0.4 fusion.23
  119.9 0.4 fusion.21
  120.4 0.6 fusion.73
  121.1 1.1 copy-done.2
  122.2 0.1 select_convert_fusion
  122.3 1.6 %collective-permute-start = (bf16[192,1024]{1,0:T(8,128)(2,1)S(1)}, bf16[192,1024]{1,0:T(8,128)(2,1)S(1)}, u32[]{:S(2)}, u32[]{:S(2)}) collective-permute-start(bf16[192,1024]{1,0:T(8,128)(2,1)S(1)} %select_convert_fusion), channel_id=1, source_target_pairs={{0,2},{1,3},{2,0},{3,1},{4,6},{5,7},{6,4},{7,5},{8,10},{9,11},{10,... | collective-permute-start | bytes 1179656 | tf_op jit(solution)/shard_map/ppermute | solution.py:62
  123.9 8.2 %collective-permute-done = bf16[192,1024]{1,0:T(8,128)(2,1)S(1)} collective-permute-done((bf16[192,1024]{1,0:T(8,128)(2,1)S(1)}, bf16[192,1024]{1,0:T(8,128)(2,1)S(1)}, u32[]{:S(2)}, u32[]{:S(2)}) %collective-permute-start) | collective-permute-done | bytes 393248 | tf_op jit(solution)/shard_map/ppermute | solution.py:62
  132.0 1.5 %convert_add_fusion = f32[192,1024]{1,0:T(8,128)S(1)} fusion(bf16[192,1024]{1,0:T(8,128)(2,1)S(1)} %collective-permute-done, f32[192,2048]{1,0:T(8,128)} %copy-done.2, pred[]{:T(512)S(6)} %eq.31), kind=kLoop, calls=%fused_computation.61 | loop fusion | flops 589824 | bytes 2752513 | tf_op jit(solution)/shard_map/add | solution.py:62
  133.6 0.1 slice_select_fusion
  133.6 0.1 collective-permute-start.1
  133.7 1.7 %collective-permute-done.1 = f32[192,512]{1,0:T(8,128)S(1)} collective-permute-done((f32[192,512]{1,0:T(8,128)S(1)}, f32[192,512]{1,0:T(8,128)S(1)}, u32[]{:S(2)}, u32[]{:S(2)}) %collective-permute-start.1) | collective-permute-done | bytes 393248 | tf_op jit(solution)/shard_map/ppermute | solution.py:62
  135.4 0.0 copy-done.15
  135.4 0.8 add_convert_fusion
  (31 shorter events, 0.2 us)
Async XLA Ops:
  0.0 120.4 %copy-start = (bf16[512,2048]{1,0:T(8,128)(2,1)S(1)}, bf16[512,2048]{1,0:T(8,128)(2,1)}, u32[]{:S(2)}) copy-start(bf16[512,2048]{1,0:T(8,128)(2,1)} %param.18) | copy-start | bytes 6291460
  10.4 8.1 %copy-start.1 = (s32[4]{0:T(128)S(1)}, s32[4]{0:T(128)}, u32[]{:S(2)}) copy-start(s32[4]{0:T(128)} %param.25) | copy-start | bytes 52
  10.4 9.4 %copy-start.16 = (s32[6]{0:T(128)S(1)}, s32[6]{0:T(128)}, u32[]{:S(2)}) copy-start(s32[6]{0:T(128)} %param.26) | copy-start | bytes 76
  10.4 12.1 %copy-start.17 = (s32[8]{0:T(128)S(1)}, s32[8]{0:T(128)}, u32[]{:S(2)}) copy-start(s32[8]{0:T(128)} %param.27) | copy-start | bytes 100
  10.5 12.1 %copy-start.18 = (s32[8]{0:T(128)S(1)}, s32[8]{0:T(128)}, u32[]{:S(2)}) copy-start(s32[8]{0:T(128)} %param.23) | copy-start | bytes 100
  10.5 14.0 %copy-start.3 = (bf16[1,512,512]{2,1,0:T(8,128)(2,1)S(1)}, bf16[1,512,512]{2,1,0:T(8,128)(2,1)}, u32[]{:S(2)}) copy-start(bf16[1,512,512]{2,1,0:T(8,128)(2,1)} %param.19) | copy-start | bytes 1572868
  10.5 14.0 %copy-start.4 = (bf16[192,512]{1,0:T(8,128)(2,1)S(1)}, bf16[192,512]{1,0:T(8,128)(2,1)}, u32[]{:S(2)}) copy-start(bf16[192,512]{1,0:T(8,128)(2,1)} %param.15) | copy-start | bytes 589828
  10.5 14.0 %copy-start.12 = (bf16[192,512]{1,0:T(8,128)(2,1)S(1)}, bf16[192,512]{1,0:T(8,128)(2,1)}, u32[]{:S(2)}) copy-start(bf16[192,512]{1,0:T(8,128)(2,1)} %param.14) | copy-start | bytes 589828
  10.5 100.7 %all-to-all-start = ((bf16[8,4,128,512]{3,2,1,0:T(8,128)(2,1)}), bf16[8,4,128,512]{3,2,1,0:T(8,128)(2,1)}, u32[]{:S(2)}, u32[]{:S(2)}) async-start(bf16[8,4,128,512]{3,2,1,0:T(8,128)(2,1)} %bitcast.38), calls=%async_computation | async-start | bytes 8388608 | tf_op jit(solution)/shard_map/all_to_all | solution.py:100
  24.9 1.9 %copy-start.9 = (f32[192,704]{1,0:T(8,128)}, f32[192,704]{1,0:T(8,128)S(1)}, u32[]{:S(2)}) copy-start(f32[192,704]{1,0:T(8,128)S(1)} %get-tuple-element.44) | copy-start | bytes 1622020
  25.2 1.6 %copy-start.7 = (f32[192,704]{1,0:T(8,128)}, f32[192,704]{1,0:T(8,128)S(1)}, u32[]{:S(2)}) copy-start(f32[192,704]{1,0:T(8,128)S(1)} %get-tuple-element.46) | copy-start | bytes 1622020
  25.6 1.2 copy-start.5
  27.6 86.1 %copy-start.13 = (bf16[192,512]{1,0:T(8,128)(2,1)S(1)}, bf16[192,512]{1,0:T(8,128)(2,1)}, u32[]{:S(2)}) copy-start(bf16[192,512]{1,0:T(8,128)(2,1)} %param.14) | copy-start | bytes 589828
  115.6 1.3 copy-start.10
  115.6 1.3 copy-start.11
  115.6 1.3 copy-start.14
  115.6 1.6 %copy-start.8 = (f32[192,704]{1,0:T(8,128)S(1)}, f32[192,704]{1,0:T(8,128)}, u32[]{:S(2)}) copy-start(f32[192,704]{1,0:T(8,128)} %copy-done.7) | copy-start | bytes 1622020
  116.8 1.1 copy-start.6
  121.0 1.2 copy-start.2
  122.3 9.8 %collective-permute-start = (bf16[192,1024]{1,0:T(8,128)(2,1)S(1)}, bf16[192,1024]{1,0:T(8,128)(2,1)S(1)}, u32[]{:S(2)}, u32[]{:S(2)}) collective-permute-start(bf16[192,1024]{1,0:T(8,128)(2,1)S(1)} %select_convert_fusion), channel_id=1, source_target_pairs={{0,2},{1,3},{2,0},{3,1},{4,6},{5,7},{6,4},{7,5},{8,10},{9,11},{10,... | collective-permute-start | bytes 1179656 | tf_op jit(solution)/shard_map/ppermute | solution.py:62
  123.9 11.6 %copy-start.15 = (bf16[192,512]{1,0:T(8,128)(2,1)S(1)}, bf16[192,512]{1,0:T(8,128)(2,1)}, u32[]{:S(2)}) copy-start(bf16[192,512]{1,0:T(8,128)(2,1)} %param.17) | copy-start | bytes 589828
  133.6 1.8 %collective-permute-start.1 = (f32[192,512]{1,0:T(8,128)S(1)}, f32[192,512]{1,0:T(8,128)S(1)}, u32[]{:S(2)}, u32[]{:S(2)}) collective-permute-start(f32[192,512]{1,0:T(8,128)S(1)} %slice_select_fusion), channel_id=1, source_target_pairs={{0,1},{1,0},{2,3},{3,2},{4,5},{5,4},{6,7},{7,6},{8,9},{9,8},{10,11... | collective-permute-start | bytes 1179656 | tf_op jit(solution)/shard_map/ppermute | solution.py:62

commit v6 on v5

--- a/solution.py
+++ b/solution.py
@@ -48,20 +48,26 @@
 def sum_over_grp(projected):
     size = lax.axis_size("grp")
     index = lax.axis_index("grp")
+    rows = projected.shape[0]
     block = projected.shape[1] // size
-    kept = projected
-    step = size // 2
-    while step >= 1:
-        width = step * block
-        lower = (index & step) == 0
-        keep = jnp.where(lower, kept[:, :width], kept[:, width:])
-        give = jnp.where(lower, kept[:, width:], kept[:, :width])
-        if step == size // 2:
+    kept = projected.reshape(rows, size, block)
+    step = 1
+    while step < size:
+        pairs = kept.reshape(rows, kept.shape[1] // 2, 2, block)
+        high = (index & step) != 0
+        keep = jnp.where(high, pairs[:, :, 1], pairs[:, :, 0])
+        give = jnp.where(high, pairs[:, :, 0], pairs[:, :, 1])
+        if step * 2 == size:
             give = give.astype(jnp.bfloat16)
-        pairs = [(g, g ^ step) for g in range(size)]
-        kept = keep + lax.ppermute(give, "grp", pairs).astype(jnp.float32)
-        step //= 2
-    return kept
+        moved = lax.ppermute(give, "grp", [(g, g ^ step) for g in range(size)])
+        kept = keep + moved.astype(jnp.float32)
+        step *= 2
+    return kept.reshape(rows, block)
+
+
+def pick(table, index):
+    ids = jnp.arange(table.shape[0], dtype=jnp.int32)
+    return jnp.sum(jnp.where(ids == index, table, 0))
 
 
 def shards(
@@ -90,25 +96,21 @@
     root_count = node_count - mid_count
     chunk = upper_keys.shape[1]
 
-    dest_mid = leaf_mid.astype(jnp.int32)
-    dest_root = jnp.take(mid_root, dest_mid).astype(jnp.int32)
-    dest_nodes = jnp.stack([dest_root, root_count + dest_mid], axis=1)
-    both = jnp.concatenate([upper_keys, upper_values], axis=0)
-    send = both.at[jnp.concatenate([dest_nodes, node_count + dest_nodes], axis=1)].get(
+    root_rows = jnp.stack([upper_keys[:root_count], upper_values[:root_count]], axis=1)
+    roots = lax.all_gather(root_rows[None], "tok", axis=0, tiled=True)
+    dest_mid = root_count + leaf_mid.astype(jnp.int32)
+    mid_rows = jnp.concatenate([upper_keys, upper_values], axis=0)
+    send = mid_rows.at[jnp.stack([dest_mid, node_count + dest_mid], axis=1)].get(
         mode="promise_in_bounds"
     )
-    received = lax.all_to_all(send, "tok", 0, 0, tiled=True)
-    recv_keys = received[:, :2]
-    recv_values = received[:, 2:]
+    mids = lax.all_to_all(send, "tok", 0, 0, tiled=True)
 
-    owned = (jnp.arange(dev_count, dtype=jnp.int32) == my_index).astype(jnp.int32)
-    my_length = jnp.sum(owned * req_len)
-    my_mid = jnp.sum(owned * leaf_mid)
-    my_leaf_len = jnp.sum(owned * leaf_len)
-    my_root = jnp.sum((jnp.arange(mid_count) == my_mid).astype(jnp.int32) * mid_root)
-    node_ids = jnp.arange(node_count)
-    root_len = jnp.sum((node_ids == my_root).astype(jnp.int32) * upper_len)
-    mid_len = jnp.sum((node_ids == root_count + my_mid).astype(jnp.int32) * upper_len)
+    my_length = pick(req_len, my_index)
+    my_mid = pick(leaf_mid, my_index)
+    my_leaf_len = pick(leaf_len, my_index)
+    my_root = pick(mid_root, my_mid)
+    root_len = pick(upper_len, my_root)
+    mid_len = pick(upper_len, root_count + my_mid)
     position = jnp.arange(row_count, dtype=jnp.int32)
     is_live = position < my_length
     leaf_count = leaf_keys.shape[1]
@@ -118,7 +120,7 @@
         (jnp.arange(leaf_count) < my_leaf_len)[None, :], (row_count, leaf_count)
     )
     new_allowed = (position[None, :] <= position[:, None]) & is_live[None, :]
-    local_part = partial_attention(
+    merged = partial_attention(
         queries,
         local_keys,
         local_values,
@@ -127,19 +129,26 @@
     )
 
     upper_pos = (
-        jnp.arange(dev_count, dtype=jnp.int32)[:, None, None] * chunk
-        + jnp.arange(chunk, dtype=jnp.int32)[None, None, :]
-    )
-    upper_limit = jnp.stack([root_len, mid_len])[None, :, None]
-    upper_ok = (upper_pos < upper_limit).reshape(-1)
-    upper_part = partial_attention(
+        jnp.arange(dev_count, dtype=jnp.int32)[:, None] * chunk
+        + jnp.arange(chunk, dtype=jnp.int32)[None, :]
+    ).reshape(-1)
+    my_roots = lax.dynamic_index_in_dim(roots, my_root, axis=1, keepdims=False)
+    root_part = partial_attention(
         queries,
-        recv_keys.reshape(-1, col_count),
-        recv_values.reshape(-1, col_count),
-        upper_ok[None, :],
+        my_roots[:, 0].reshape(-1, col_count),
+        my_roots[:, 1].reshape(-1, col_count),
+        (upper_pos < root_len)[None, :],
         head_count,
     )
-    merged = combine(local_part, upper_part)
+    merged = combine(merged, root_part)
+    mid_part = partial_attention(
+        queries,
+        mids[:, 0].reshape(-1, col_count),
+        mids[:, 1].reshape(-1, col_count),
+        (upper_pos < mid_len)[None, :],
+        head_count,
+    )
+    merged = combine(merged, mid_part)
     attended = jnp.concatenate([part[2] / part[1] for part in merged], axis=1)
     attention = jnp.where(is_live[:, None], attended, 0.0).astype(jnp.bfloat16)
     projected = jnp.dot(attention, w_out, preferred_element_type=jnp.float32)

time: 137 us -> 162 us (1.18)
  between operations: 1.04 us -> 16.5 us
  local copies, waits for them, and re-layouts: 9.71 us -> 19 us
  waiting for transfers between devices: 93.5 us -> 90 us
  matrix products: 7.84 us -> 10.9 us
    all_to_all x1, waiting for transfers between devices: 83.6 us -> 78.3 us  [shards(): mids = lax.all_to_all(send, 'tok', 0, 0, tiled=True)]
    another operation x0 -> x2, local copies, waits for them, and re-layouts: none -> 4.64 us  [the longest x1 3.43 us: sum_over_grp(): pairs = kept.reshape(rows, kept.shape[1] // 2, 2, block)]
    slice x1 -> x3, local copies, waits for them, and re-layouts: 2.49 us -> 6.18 us  [the longest x1 3.25 us: sum_over_grp(): keep = jnp.where(high, pairs[:, :, 1], pairs[:, :, 0])]
    all_gather x0 -> x1, waiting for transfers between devices: none -> 3.57 us  [shards(): roots = lax.all_gather(root_rows[None], 'tok', axis=0, tiled=True)]
    gather x2 -> x1, local copies, waits for them, and re-layouts: 5.44 us -> 3.43 us  [shards(): mid_rows.at[jnp.stack([dest_mid, node_count + dest_mid], axis=1)]]
    ppermute x2, waiting for transfers between devices: 9.9 us -> 8.09 us  [sum_over_grp(): moved = lax.ppermute(give, 'grp', [(g, g ^ step) for g in range(size)])]
    squeeze x0 -> x1, local copies, waits for them, and re-layouts: none -> 1.79 us  [shards(): my_roots = lax.dynamic_index_in_dim(roots, my_root, axis=1, keepdims=False)]
    reshape x0 -> x1, other arithmetic: none -> 1.71 us  [sum_over_grp(): pairs = kept.reshape(rows, kept.shape[1] // 2, 2, block)]
  transfers between devices with their start and end apart: 3 -> 4, of which waited for: 3 -> 4; matrix products, arithmetic and copies ran while one was open for 7% -> 13% of each run, Pallas kernels for 0% -> 0%
where the time goes in v6:
time: 162 us; the launch traced here: 161 us
  waiting for transfers between devices  90 us (56%)
  local copies, waits for them, and re-layouts  19 us (12%)
  between operations  16.5 us (10%)
  other arithmetic  15.7 us (10%)
  matrix products  10.9 us (7%)
  starting transfers between devices  8.98 us (6%)
    all_to_all x1, waiting for transfers between devices, shards(): mids = lax.all_to_all(send, 'tok', 0, 0, tiled=True)  78.3 us
    ppermute x2, waiting for transfers between devices, sum_over_grp(): moved = lax.ppermute(give, 'grp', [(g, g ^ step) for g in range(size)])  8.09 us
    all_to_all x1, starting transfers between devices, shards(): mids = lax.all_to_all(send, 'tok', 0, 0, tiled=True)  7.4 us
    dot_general x12, matrix products, partial_attention(): lax.dot_general(query_rows[:, cols], key_rows[:, cols], (((1,), (1,)), ((...  5.11 us
    dot_general x12, matrix products, partial_attention(): jnp.dot(exp_scores.astype(jnp.bfloat16), values[:, cols], preferred_eleme...  3.96 us
    all_gather x1, waiting for transfers between devices, shards(): roots = lax.all_gather(root_rows[None], 'tok', axis=0, tiled=True)  3.57 us
    gather x1, local copies, waits for them, and re-layouts, shards(): mid_rows.at[jnp.stack([dest_mid, node_count + dest_mid], axis=1)]  3.43 us
    another operation x1, local copies, waits for them, and re-layouts, sum_over_grp(): pairs = kept.reshape(rows, kept.shape[1] // 2, 2, block)  3.43 us
  transfers between devices with their start and end apart: 4, of which 4 were waited for; matrix products, arithmetic and copies ran while one was open for 13% of the time, Pallas kernels for 0%

profile of v6, /device:TPU:0, one launch (start us, length us, event | category | flops | bytes accessed | tf_op | source)
XLA Modules:
  0.0 161.0 jit_solution(16900303664565731567)
XLA Ops:
  6.6 1.2 slice_bitcast_fusion
  7.8 0.9 pad_maximum_fusion.1
  8.7 0.6 add_bitcast_fusion.1
  9.3 0.1 copy.18
  9.4 0.1 reshape.458
  9.5 2.4 %pad_maximum_fusion = bf16[12,128,512]{2,1,0:T(8,128)(2,1)} fusion(bf16[6,128,512]{2,1,0:T(8,128)(2,1)S(1)} %copy-done.10, bf16[6,128,512]{2,1,0:T(8,128)(2,1)} %param.21), kind=kLoop, calls=%fused_computation.2 | loop fusion | flops 786432 | bytes 3145728 | tf_op jit(solution)/shard_map/concatenate | solution.py:102
  12.0 3.4 %gather_fusion = bf16[16,128,512]{2,1,0:T(8,128)(2,1)} fusion(bf16[12,128,512]{2,1,0:T(8,128)(2,1)} %pad_maximum_fusion, s32[1024]{0:T(1024)S(1)} %pad_clamp_fusion), kind=kCustom, calls=%fused_computation | custom fusion | bytes 4194368 | tf_op jit(solution)/shard_map/gather | solution.py:103
  15.4 7.4 %all-to-all-start = ((bf16[8,2,128,512]{3,2,1,0:T(8,128)(2,1)}), bf16[8,2,128,512]{3,2,1,0:T(8,128)(2,1)}, u32[]{:S(2)}, u32[]{:S(2)}) async-start(bf16[8,2,128,512]{3,2,1,0:T(8,128)(2,1)} %bitcast.59), calls=%async_computation | async-start | bytes 4194304 | tf_op jit(solution)/shard_map/all_to_all | solution.py:106
  23.5 1.3 fusion.163
  26.7 0.6 iota_compare_fusion.1
  27.3 0.6 select_reduce_fusion.2
  27.9 0.6 iota_compare_fusion.2
  28.6 1.3 fusion.165
  29.8 1.3 fusion.153
  31.2 0.3 fusion.208
  31.6 0.3 fusion.209
  31.9 0.3 fusion.210
  32.3 1.2 fusion.199
  33.5 0.8 fusion.49
  34.3 78.3 %all-to-all-done = bf16[8,2,128,512]{3,2,1,0:T(8,128)(2,1)} async-done(((bf16[8,2,128,512]{3,2,1,0:T(8,128)(2,1)}), bf16[8,2,128,512]{3,2,1,0:T(8,128)(2,1)}, u32[]{:S(2)}, u32[]{:S(2)}) %all-to-all-start) | async-done | bytes 2097184 | tf_op jit(solution)/shard_map/all_to_all | solution.py:106
  112.6 2.7 %fusion.196 = (bf16[8,1,128,512]{3,2,1,0:T(8,128)(2,1)}, bf16[8,1,128,512]{3,2,1,0:T(8,128)(2,1)S(1)}) fusion(bf16[8,2,128,512]{3,2,1,0:T(8,128)(2,1)} %all-to-all-done), kind=kLoop, calls=%fused_computation.268 | loop fusion | bytes 4194304 | tf_op jit(solution)/shard_map/slice | solution.py:147
  115.3 0.4 fusion.200
  115.7 0.4 fusion.201
  116.1 0.4 fusion.202
  116.4 0.4 fusion.203
  116.8 0.1 copy-done.16
  116.9 0.4 copy-done.14
  117.3 0.3 copy-done.12
  117.7 0.7 fusion.35
  118.4 3.6 %all-gather.3.cloned.1.call-done = bf16[16,2,128,512]{3,2,0,1:T(8,128)(2,1)} async-done(((bf16[2,2,128,512]{3,2,0,1:T(8,128)(2,1)}), bf16[16,2,128,512]{3,2,0,1:T(8,128)(2,1)}) %all-gather.3.cloned.1.call-update) | async-done | bytes 4194320 | tf_op jit(solution)/shard_map/all_gather | solution.py:100
  122.0 1.8 %dynamic-slice_bitcast_fusion = bf16[8,2,128,512]{3,2,0,1:T(8,128)(2,1)S(1)} fusion(bf16[8,2,2,128,512]{4,3,1,0,2:T(8,128)(2,1)} %bitcast.64, s32[]{:T(128)S(6)} %select_n.180), kind=kLoop, calls=%fused_computation.1 | loop fusion | bytes 4194308 | tf_op jit(solution)/shard_map/jit(dynamic_index_in_dim)/squeeze | solution.py:135
  123.8 0.2 fusion.197
  124.0 0.4 fusion.204
  124.3 0.4 fusion.205
  124.7 0.4 fusion.206
  125.1 0.4 fusion.207
  125.5 0.8 fusion.33
  126.3 0.0 copy-done.23
  126.3 0.3 convolution_multiply_fusion.23
  126.7 0.3 convolution_multiply_fusion.22
  127.1 0.3 copy-done.5
  127.4 0.3 convolution_multiply_fusion.21
  127.8 0.3 convolution_multiply_fusion.20
  128.1 0.3 fusion.31
  128.4 0.3 fusion.27
  128.8 0.2 copy-done.11
  129.0 0.2 copy-done.19
  129.2 0.3 fusion.29
  129.5 0.3 fusion.25
  129.9 0.3 fusion.23
  130.2 0.2 copy-done.15
  130.4 0.3 fusion.21
  130.7 0.3 fusion.19
  131.1 0.3 fusion.17
  131.4 1.8 %fusion.120 = f32[192,2048]{1,0:T(8,128)} fusion(bf16[512,2048]{1,0:T(8,128)(2,1)S(1)} %copy-done, bf16[192,128]{1,0:T(8,128)(2,1)S(1)} %fusion.17, bf16[192,128]{1,0:T(8,128)(2,1)S(1)} %fusion.21, bf16[192,128]{1,0:T(8,128)(2,1)S(1)} %fusion.25, bf16[192,128]{1,0:T(8,128)(2,1)S(1)} %fusion.29, pred[192]{0:T(512)(128)(4,1)S(1)} %iota_compare_fusion.2), kind=kOutput, calls=%fused_computation.169 | convolution fusion | flops 403537920 | bytes 3866816 | tf_op jit(solution)/shard_map/dot_general | solution.py:154
  133.2 3.4 %reshape_reshape.3 = f32[192,2,2,512]{3,2,1,0:T(2,128)} reshape(f32[192,2048]{1,0:T(8,128)} %fusion.120) | data formatting | bytes 3145728 | tf_op jit(solution)/shard_map/reshape;reshape | solution.py:56
  136.6 3.3 %fusion.198 = (f32[192,2,1,512]{3,2,1,0:T(1,128)S(1)}, f32[192,2,1,512]{3,2,1,0:T(1,128)S(1)}) fusion(f32[192,2,2,512]{3,2,1,0:T(2,128)} %reshape_reshape.3), kind=kLoop, calls=%fused_computation.270 | loop fusion | bytes 3145728 | tf_op jit(solution)/shard_map/slice | solution.py:58
  139.9 0.9 copy-done.2
  140.8 1.1 select_bitcast_fusion
  141.9 2.6 %collective-permute-done = f32[192,2,512]{2,0,1:T(8,128)} collective-permute-done((f32[192,2,512]{2,0,1:T(8,128)}, f32[192,2,512]{2,0,1:T(8,128)}, u32[]{:S(2)}, u32[]{:S(2)}) %collective-permute-start) | collective-permute-done | bytes 786464 | tf_op jit(solution)/shard_map/ppermute | solution.py:62
  144.6 1.7 %fusion.32 = f32[192,1,2,512]{3,0,2,1:T(8,128)S(1)} fusion(f32[192,2,512]{2,0,1:T(8,128)} %collective-permute-done, f32[192,2,1,512]{3,2,1,0:T(1,128)} %copy-done.2, f32[192,2,1,512]{3,2,1,0:T(1,128)S(1)} %get-tuple-element.43, pred[]{:T(512)S(6)} %ne.7), kind=kLoop, calls=%fused_computation.66 | loop fusion | flops 393216 | bytes 3145729 | tf_op jit(solution)/shard_map/reshape | solution.py:56
  146.3 1.5 collective-permute-start.1
  147.9 5.5 %collective-permute-done.1 = bf16[192,1,512]{2,0,1:T(8,128)(2,1)S(1)} collective-permute-done((bf16[192,1,512]{2,0,1:T(8,128)(2,1)S(1)}, bf16[192,1,512]{2,0,1:T(8,128)(2,1)S(1)}, u32[]{:S(2)}, u32[]{:S(2)}) %collective-permute-start.1) | collective-permute-done | bytes 196640 | tf_op jit(solution)/shard_map/ppermute | solution.py:62
  153.3 0.8 fusion.66
  (64 shorter events, 0.3 us)
Async XLA Ops:
  6.5 124.9 %copy-start = (bf16[512,2048]{1,0:T(8,128)(2,1)S(1)}, bf16[512,2048]{1,0:T(8,128)(2,1)}, u32[]{:S(2)}) copy-start(bf16[512,2048]{1,0:T(8,128)(2,1)} %param.18) | copy-start | bytes 6291460
  6.5 3.0 %copy-start.10 = (bf16[6,128,512]{2,1,0:T(8,128)(2,1)S(1)}, bf16[6,128,512]{2,1,0:T(8,128)(2,1)}, u32[]{:S(2)}) copy-start(bf16[6,128,512]{2,1,0:T(8,128)(2,1)} %param.22) | copy-start | bytes 2359300
  6.5 2.1 %copy-start.25 = (s32[8]{0:T(128)S(1)}, s32[8]{0:T(128)}, u32[]{:S(2)}) copy-start(s32[8]{0:T(128)} %param.24) | copy-start | bytes 100
  6.5 2.2 %copy-start.26 = (s32[8]{0:T(128)S(1)}, s32[8]{0:T(128)}, u32[]{:S(2)}) copy-start(s32[8]{0:T(128)} %param.27) | copy-start | bytes 100
  6.5 115.4 %all-gather.3.cloned.1.call-start = ((), (), s32[]{:S(2)}) async-start(), calls=%async_computation.1 | async-start | bytes 4718592 | tf_op jit(solution)/shard_map/all_gather | solution.py:100
  15.4 8.1 %copy-start.28 = (s32[4]{0:T(128)S(1)}, s32[4]{0:T(128)}, u32[]{:S(2)}) copy-start(s32[4]{0:T(128)} %param.25) | copy-start | bytes 52
  15.4 11.9 %copy-start.29 = (s32[8]{0:T(128)S(1)}, s32[8]{0:T(128)}, u32[]{:S(2)}) copy-start(s32[8]{0:T(128)} %param.23) | copy-start | bytes 100
  15.4 13.2 %copy-start.27 = (s32[6]{0:T(128)S(1)}, s32[6]{0:T(128)}, u32[]{:S(2)}) copy-start(s32[6]{0:T(128)} %param.26) | copy-start | bytes 76
  15.4 15.8 %copy-start.1 = (bf16[1,512,512]{2,1,0:T(8,128)(2,1)S(1)}, bf16[1,512,512]{2,1,0:T(8,128)(2,1)}, u32[]{:S(2)}) copy-start(bf16[1,512,512]{2,1,0:T(8,128)(2,1)} %param.19) | copy-start | bytes 1572868
  15.4 15.8 %copy-start.3 = (bf16[192,512]{1,0:T(8,128)(2,1)S(1)}, bf16[192,512]{1,0:T(8,128)(2,1)}, u32[]{:S(2)}) copy-start(bf16[192,512]{1,0:T(8,128)(2,1)} %param.15) | copy-start | bytes 589828
  15.4 15.8 %copy-start.21 = (bf16[192,512]{1,0:T(8,128)(2,1)S(1)}, bf16[192,512]{1,0:T(8,128)(2,1)}, u32[]{:S(2)}) copy-start(bf16[192,512]{1,0:T(8,128)(2,1)} %param.14) | copy-start | bytes 589828
  15.4 97.1 %all-to-all-start = ((bf16[8,2,128,512]{3,2,1,0:T(8,128)(2,1)}), bf16[8,2,128,512]{3,2,1,0:T(8,128)(2,1)}, u32[]{:S(2)}, u32[]{:S(2)}) async-start(bf16[8,2,128,512]{3,2,1,0:T(8,128)(2,1)} %bitcast.59), calls=%async_computation | async-start | bytes 4194304 | tf_op jit(solution)/shard_map/all_to_all | solution.py:106
  31.5 1.9 %copy-start.8 = (f32[192,704]{1,0:T(8,128)}, f32[192,704]{1,0:T(8,128)S(1)}, u32[]{:S(2)}) copy-start(f32[192,704]{1,0:T(8,128)S(1)} %get-tuple-element.69) | copy-start | bytes 1622020
  31.9 1.6 copy-start.6
  32.3 1.2 copy-start.4
  34.3 81.1 %copy-start.22 = (bf16[192,512]{1,0:T(8,128)(2,1)S(1)}, bf16[192,512]{1,0:T(8,128)(2,1)}, u32[]{:S(2)}) copy-start(bf16[192,512]{1,0:T(8,128)(2,1)} %param.14) | copy-start | bytes 589828
  115.7 1.1 copy-start.18
  116.0 0.9 copy-start.16
  116.4 0.9 copy-start.14
  116.8 0.9 copy-start.12
  125.1 1.2 copy-start.9
  125.1 1.2 copy-start.20
  125.1 1.2 copy-start.23
  125.5 1.2 copy-start.7
  126.2 1.1 copy-start.5
  127.7 1.2 copy-start.11
  127.7 1.4 copy-start.19
  128.1 1.4 copy-start.17
  129.2 1.2 copy-start.15
  129.9 1.2 copy-start.13
  139.9 0.9 copy-start.2
  141.9 11.4 %copy-start.24 = (bf16[192,512]{1,0:T(8,128)(2,1)S(1)}, bf16[192,512]{1,0:T(8,128)(2,1)}, u32[]{:S(2)}) copy-start(bf16[192,512]{1,0:T(8,128)(2,1)} %param.17) | copy-start | bytes 589828
  141.9 2.6 %collective-permute-start = (f32[192,2,512]{2,0,1:T(8,128)}, f32[192,2,512]{2,0,1:T(8,128)}, u32[]{:S(2)}, u32[]{:S(2)}) collective-permute-start(f32[192,2,512]{2,0,1:T(8,128)} %select_bitcast_fusion), channel_id=1, source_target_pairs={{0,1},{1,0},{2,3},{3,2},{4,5},{5,4},{6,7},{7,6},{8,9},{9,8},{10,11... | collective-permute-start | bytes 2359304 | tf_op jit(solution)/shard_map/ppermute | solution.py:62
  146.3 7.0 %collective-permute-start.1 = (bf16[192,1,512]{2,0,1:T(8,128)(2,1)S(1)}, bf16[192,1,512]{2,0,1:T(8,128)(2,1)S(1)}, u32[]{:S(2)}, u32[]{:S(2)}) collective-permute-start(bf16[192,1,512]{2,0,1:T(8,128)(2,1)S(1)} %fusion.119), channel_id=1, source_target_pairs={{0,2},{1,3},{2,0},{3,1},{4,6},{5,7},{6,4},{7,5},{8,10},{9,11},{10,... | collective-permute-start | bytes 589832 | tf_op jit(solution)/shard_map/ppermute | solution.py:62
Sparse Core Ops, SparseCore 0:
  9.6 112.3 all-gather.2

commit v7 on v6

--- a/solution.py
+++ b/solution.py
@@ -96,14 +96,19 @@
     root_count = node_count - mid_count
     chunk = upper_keys.shape[1]
 
-    root_rows = jnp.stack([upper_keys[:root_count], upper_values[:root_count]], axis=1)
-    roots = lax.all_gather(root_rows[None], "tok", axis=0, tiled=True)
-    dest_mid = root_count + leaf_mid.astype(jnp.int32)
-    mid_rows = jnp.concatenate([upper_keys, upper_values], axis=0)
-    send = mid_rows.at[jnp.stack([dest_mid, node_count + dest_mid], axis=1)].get(
+    dest_mid = leaf_mid.astype(jnp.int32)
+    mid_ids = jnp.arange(mid_count, dtype=jnp.int32)
+    dest_root = jnp.sum(
+        jnp.where(dest_mid[:, None] == mid_ids[None, :], mid_root[None, :], 0), axis=1
+    )
+    dest_nodes = jnp.stack([dest_root, root_count + dest_mid], axis=1)
+    both = jnp.concatenate([upper_keys, upper_values], axis=0)
+    send = both.at[jnp.concatenate([dest_nodes, node_count + dest_nodes], axis=1)].get(
         mode="promise_in_bounds"
     )
-    mids = lax.all_to_all(send, "tok", 0, 0, tiled=True)
+    received = lax.all_to_all(send, "tok", 0, 0, tiled=True)
+    recv_keys = received[:, :2]
+    recv_values = received[:, 2:]
 
     my_length = pick(req_len, my_index)
     my_mid = pick(leaf_mid, my_index)
@@ -120,7 +125,7 @@
         (jnp.arange(leaf_count) < my_leaf_len)[None, :], (row_count, leaf_count)
     )
     new_allowed = (position[None, :] <= position[:, None]) & is_live[None, :]
-    merged = partial_attention(
+    local_part = partial_attention(
         queries,
         local_keys,
         local_values,
@@ -129,26 +134,19 @@
     )
 
     upper_pos = (
-        jnp.arange(dev_count, dtype=jnp.int32)[:, None] * chunk
-        + jnp.arange(chunk, dtype=jnp.int32)[None, :]
-    ).reshape(-1)
-    my_roots = lax.dynamic_index_in_dim(roots, my_root, axis=1, keepdims=False)
-    root_part = partial_attention(
+        jnp.arange(dev_count, dtype=jnp.int32)[:, None, None] * chunk
+        + jnp.arange(chunk, dtype=jnp.int32)[None, None, :]
+    )
+    upper_limit = jnp.stack([root_len, mid_len])[None, :, None]
+    upper_ok = (upper_pos < upper_limit).reshape(-1)
+    upper_part = partial_attention(
         queries,
-        my_roots[:, 0].reshape(-1, col_count),
-        my_roots[:, 1].reshape(-1, col_count),
-        (upper_pos < root_len)[None, :],
+        recv_keys.reshape(-1, col_count),
+        recv_values.reshape(-1, col_count),
+        upper_ok[None, :],
         head_count,
     )
-    merged = combine(merged, root_part)
-    mid_part = partial_attention(
-        queries,
-        mids[:, 0].reshape(-1, col_count),
-        mids[:, 1].reshape(-1, col_count),
-        (upper_pos < mid_len)[None, :],
-        head_count,
-    )
-    merged = combine(merged, mid_part)
+    merged = combine(local_part, upper_part)
     attended = jnp.concatenate([part[2] / part[1] for part in merged], axis=1)
     attention = jnp.where(is_live[:, None], attended, 0.0).astype(jnp.bfloat16)
     projected = jnp.dot(attention, w_out, preferred_element_type=jnp.float32)

time: 162 us -> 142 us (0.88)
  between operations: 16.5 us -> 1.02 us
  local copies, waits for them, and re-layouts: 19 us -> 14.8 us
  matrix products: 10.9 us -> 8.98 us
    all_to_all x1, waiting for transfers between devices: 78.3 us -> 83.6 us  [shards(): received = lax.all_to_all(send, 'tok', 0, 0, tiled=True)]
    all_gather x1 -> x0, waiting for transfers between devices: 3.57 us -> none  [shards(): roots = lax.all_gather(root_rows[None], 'tok', axis=0, tiled=True)]
    squeeze x1 -> x0, local copies, waits for them, and re-layouts: 1.79 us -> none  [shards(): my_roots = lax.dynamic_index_in_dim(roots, my_root, axis=1, keepdims=False)]
    concatenate x1 -> x3, other arithmetic: 2.45 us -> 4.14 us  [the longest x1 2.68 us: shards(): both = jnp.concatenate([upper_keys, upper_values], axis=0)]
    dot_general x12 -> x8, matrix products: 5.11 us -> 4.12 us  [partial_attention(): lax.dot_general(query_rows[:, cols], key_rows[:, cols], (((1,), (1,)), ((...]
    dot_general x12 -> x8, matrix products: 3.96 us -> 3.06 us  [partial_attention(): jnp.dot(exp_scores.astype(jnp.bfloat16), values[:, cols], preferred_eleme...]
  transfers between devices with their start and end apart: 4 -> 3, of which waited for: 4 -> 3; matrix products, arithmetic and copies ran while one was open for 13% -> 6% of each run, Pallas kernels for 0% -> 0%
where the time goes in v7:
time: 142 us
  waiting for transfers between devices  91.6 us (65%)
  other arithmetic  16.4 us (12%)
  local copies, waits for them, and re-layouts  14.8 us (10%)
  starting transfers between devices  8.98 us (6%)
  matrix products  8.98 us (6%)
    all_to_all x1, waiting for transfers between devices, shards(): received = lax.all_to_all(send, 'tok', 0, 0, tiled=True)  83.6 us
    ppermute x2, waiting for transfers between devices, sum_over_grp(): moved = lax.ppermute(give, 'grp', [(g, g ^ step) for g in range(size)])  8.05 us
    all_to_all x1, starting transfers between devices, shards(): received = lax.all_to_all(send, 'tok', 0, 0, tiled=True)  7.4 us
    gather x1, local copies, waits for them, and re-layouts, shards(): both.at[jnp.concatenate([dest_nodes, node_count + dest_nodes], axis=1)]  4.15 us
    dot_general x8, matrix products, partial_attention(): lax.dot_general(query_rows[:, cols], key_rows[:, cols], (((1,), (1,)), ((...  4.12 us
    another operation x1, local copies, waits for them, and re-layouts, sum_over_grp(): pairs = kept.reshape(rows, kept.shape[1] // 2, 2, block)  3.43 us
    slice x1, local copies, waits for them, and re-layouts, sum_over_grp(): keep = jnp.where(high, pairs[:, :, 1], pairs[:, :, 0])  3.25 us
    reduce_sum x3, other arithmetic, pick(): return jnp.sum(jnp.where(ids == index, table, 0))  3.1 us
  transfers between devices with their start and end apart: 3, of which 3 were waited for; matrix products, arithmetic and copies ran while one was open for 6% of the time, Pallas kernels for 0%

profile of v7, /device:TPU:0, one launch (start us, length us, event | category | flops | bytes accessed | tf_op | source)
XLA Modules:
  0.0 141.9 jit_solution(17718200087161461476)
XLA Ops:
  0.0 1.4 %add_bitcast_fusion.1 = (s32[8,1,1]{0,1,2:T(1,128)S(1)}, s32[8,1]{0,1:T(1,128)S(1)}, s32[]{:T(128)}) fusion(s32[8]{0:T(128)} %param.24, s32[]{:T(128)S(6)} %axis_index.25), kind=kLoop, calls=%fused_computation.179 | loop fusion | flops 31 | bytes 104 | tf_op jit(solution)/shard_map/concatenate | solution.py:106
  1.4 0.8 select_reduce_fusion
  2.2 0.1 copy.27
  2.3 0.1 reshape.415
  2.4 2.7 %pad_maximum_fusion = bf16[12,128,512]{2,1,0:T(8,128)(2,1)} fusion(bf16[6,128,512]{2,1,0:T(8,128)(2,1)} %param.22, bf16[6,128,512]{2,1,0:T(8,128)(2,1)} %param.21), kind=kLoop, calls=%fused_computation.9 | loop fusion | flops 786432 | bytes 3145728 | tf_op jit(solution)/shard_map/concatenate | solution.py:105
  5.1 4.1 %gather_fusion = bf16[32,128,512]{2,1,0:T(8,128)(2,1)} fusion(bf16[12,128,512]{2,1,0:T(8,128)(2,1)} %pad_maximum_fusion, s32[1024]{0:T(1024)S(1)} %pad_clamp_fusion), kind=kCustom, calls=%fused_computation | custom fusion | bytes 8388736 | tf_op jit(solution)/shard_map/gather | solution.py:106
  9.2 0.0 copy-start.1
  9.3 0.0 copy-start.3
  9.3 0.0 copy-start.11
  9.3 7.4 %all-to-all-start = ((bf16[8,4,128,512]{3,2,1,0:T(8,128)(2,1)}), bf16[8,4,128,512]{3,2,1,0:T(8,128)(2,1)}, u32[]{:S(2)}, u32[]{:S(2)}) async-start(bf16[8,4,128,512]{3,2,1,0:T(8,128)(2,1)} %bitcast.56), calls=%async_computation | async-start | bytes 8388608 | tf_op jit(solution)/shard_map/all_to_all | solution.py:109
  17.4 1.3 fusion.112
  18.6 0.0 copy-done.15
  18.6 1.2 fusion.113
  19.8 1.3 pad_add_fusion.1
  21.2 0.1 iota_add_fusion
  21.2 0.1 broadcast_compare_fusion
  21.3 0.6 select_reduce_fusion.2
  22.0 0.6 iota_compare_fusion.2
  22.7 0.6 iota_compare_fusion.3
  23.3 0.0 copy-done.1
  23.3 0.0 copy-done.3
  23.3 0.0 copy-done.11
  23.3 0.3 fusion.148
  23.6 0.0 copy-start.8
  23.7 0.3 fusion.149
  24.0 0.3 fusion.150
  24.4 1.2 fusion.143
  25.6 0.0 copy-done.8
  25.6 0.0 copy-done.6
  25.6 0.0 copy-done.4
  25.6 0.8 fusion.53
  26.4 83.6 %all-to-all-done = bf16[8,4,128,512]{3,2,1,0:T(8,128)(2,1)} async-done(((bf16[8,4,128,512]{3,2,1,0:T(8,128)(2,1)}), bf16[8,4,128,512]{3,2,1,0:T(8,128)(2,1)}, u32[]{:S(2)}, u32[]{:S(2)}) %all-to-all-start) | async-done | bytes 4194336 | tf_op jit(solution)/shard_map/all_to_all | solution.py:109
  110.0 2.5 %fusion.141 = (bf16[8,2,128,512]{3,2,1,0:T(8,128)(2,1)S(1)}, bf16[8,2,128,512]{3,2,1,0:T(8,128)(2,1)S(1)}) fusion(bf16[8,4,128,512]{3,2,1,0:T(8,128)(2,1)} %all-to-all-done), kind=kLoop, calls=%fused_computation.198 | loop fusion | bytes 8388608 | tf_op jit(solution)/shard_map/slice | solution.py:111
  112.5 0.0 copy-done.12
  112.5 0.5 fusion.144
  112.9 0.5 fusion.145
  113.4 0.5 fusion.146
  113.9 0.5 fusion.147
  114.4 0.0 copy-start.10
  114.4 0.0 copy-start.13
  114.4 0.0 copy-start.7
  114.4 1.2 fusion.4
  115.7 0.3 convolution_multiply_fusion.15
  116.0 0.0 copy-done.7
  116.0 0.3 convolution_multiply_fusion.13
  116.3 0.4 copy-done.5
  116.7 0.3 convolution_multiply_fusion.11
  117.1 0.3 convolution_multiply_fusion.9
  117.4 0.4 fusion.27
  117.8 0.4 fusion.25
  118.3 0.4 fusion.23
  118.7 0.4 fusion.21
  119.2 0.0 copy-done
  119.2 1.8 %fusion.76 = f32[192,2048]{1,0:T(8,128)} fusion(bf16[512,2048]{1,0:T(8,128)(2,1)S(1)} %copy-done, bf16[192,128]{1,0:T(8,128)(2,1)S(1)} %fusion.21, bf16[192,128]{1,0:T(8,128)(2,1)S(1)} %fusion.23, bf16[192,128]{1,0:T(8,128)(2,1)S(1)} %fusion.25, bf16[192,128]{1,0:T(8,128)(2,1)S(1)} %fusion.27, pred[192]{0:T(512)(128)(4,1)S(1)} %iota_compare_fusion.3), kind=kOutput, calls=%fused_computation.113 | convolution fusion | flops 403537920 | bytes 3866816 | tf_op jit(solution)/shard_map/dot_general | solution.py:152
  121.0 3.4 %reshape_reshape.3 = f32[192,2,2,512]{3,2,1,0:T(2,128)} reshape(f32[192,2048]{1,0:T(8,128)} %fusion.76) | data formatting | bytes 3145728 | tf_op jit(solution)/shard_map/reshape;reshape | solution.py:56
  124.4 3.3 %fusion.142 = (f32[192,2,1,512]{3,2,1,0:T(1,128)S(1)}, f32[192,2,1,512]{3,2,1,0:T(1,128)S(1)}) fusion(f32[192,2,2,512]{3,2,1,0:T(2,128)} %reshape_reshape.3), kind=kLoop, calls=%fused_computation.199 | loop fusion | bytes 3145728 | tf_op jit(solution)/shard_map/slice | solution.py:58
  127.7 0.9 copy-done.2
  128.5 1.1 select_bitcast_fusion
  129.7 0.0 collective-permute-start
  129.7 2.6 %collective-permute-done = f32[192,2,512]{2,0,1:T(8,128)} collective-permute-done((f32[192,2,512]{2,0,1:T(8,128)}, f32[192,2,512]{2,0,1:T(8,128)}, u32[]{:S(2)}, u32[]{:S(2)}) %collective-permute-start) | collective-permute-done | bytes 786464 | tf_op jit(solution)/shard_map/ppermute | solution.py:62
  132.3 1.7 %fusion.32 = f32[192,1,2,512]{3,0,2,1:T(8,128)S(1)} fusion(f32[192,2,512]{2,0,1:T(8,128)} %collective-permute-done, f32[192,2,1,512]{3,2,1,0:T(1,128)} %copy-done.2, f32[192,2,1,512]{3,2,1,0:T(1,128)S(1)} %get-tuple-element.29, pred[]{:T(512)S(6)} %ne.7), kind=kLoop, calls=%fused_computation.57 | loop fusion | flops 393216 | bytes 3145729 | tf_op jit(solution)/shard_map/reshape | solution.py:56
  134.1 1.6 %collective-permute-start.1 = (bf16[192,1,512]{2,0,1:T(8,128)(2,1)S(1)}, bf16[192,1,512]{2,0,1:T(8,128)(2,1)S(1)}, u32[]{:S(2)}, u32[]{:S(2)}) collective-permute-start(bf16[192,1,512]{2,0,1:T(8,128)(2,1)S(1)} %fusion.75), channel_id=1, source_target_pairs={{0,2},{1,3},{2,0},{3,1},{4,6},{5,7},{6,4},{7,5},{8,10},{9,11},{10,... | collective-permute-start | bytes 589832 | tf_op jit(solution)/shard_map/ppermute | solution.py:62
  135.7 5.4 %collective-permute-done.1 = bf16[192,1,512]{2,0,1:T(8,128)(2,1)S(1)} collective-permute-done((bf16[192,1,512]{2,0,1:T(8,128)(2,1)S(1)}, bf16[192,1,512]{2,0,1:T(8,128)(2,1)S(1)}, u32[]{:S(2)}, u32[]{:S(2)}) %collective-permute-start.1) | collective-permute-done | bytes 196640 | tf_op jit(solution)/shard_map/ppermute | solution.py:62
  141.1 0.8 fusion.62
  (31 shorter events, 0.2 us)
Async XLA Ops:
  0.0 119.2 %copy-start = (bf16[512,2048]{1,0:T(8,128)(2,1)S(1)}, bf16[512,2048]{1,0:T(8,128)(2,1)}, u32[]{:S(2)}) copy-start(bf16[512,2048]{1,0:T(8,128)(2,1)} %param.18) | copy-start | bytes 6291460
  9.2 8.1 %copy-start.18 = (s32[4]{0:T(128)S(1)}, s32[4]{0:T(128)}, u32[]{:S(2)}) copy-start(s32[4]{0:T(128)} %param.25) | copy-start | bytes 52
  9.2 9.4 %copy-start.15 = (s32[6]{0:T(128)S(1)}, s32[6]{0:T(128)}, u32[]{:S(2)}) copy-start(s32[6]{0:T(128)} %param.26) | copy-start | bytes 76
  9.2 12.1 %copy-start.16 = (s32[8]{0:T(128)S(1)}, s32[8]{0:T(128)}, u32[]{:S(2)}) copy-start(s32[8]{0:T(128)} %param.27) | copy-start | bytes 100
  9.2 12.1 %copy-start.17 = (s32[8]{0:T(128)S(1)}, s32[8]{0:T(128)}, u32[]{:S(2)}) copy-start(s32[8]{0:T(128)} %param.23) | copy-start | bytes 100
  9.2 14.0 %copy-start.1 = (bf16[1,512,512]{2,1,0:T(8,128)(2,1)S(1)}, bf16[1,512,512]{2,1,0:T(8,128)(2,1)}, u32[]{:S(2)}) copy-start(bf16[1,512,512]{2,1,0:T(8,128)(2,1)} %param.19) | copy-start | bytes 1572868
  9.3 14.0 %copy-start.3 = (bf16[192,512]{1,0:T(8,128)(2,1)S(1)}, bf16[192,512]{1,0:T(8,128)(2,1)}, u32[]{:S(2)}) copy-start(bf16[192,512]{1,0:T(8,128)(2,1)} %param.15) | copy-start | bytes 589828
  9.3 14.0 %copy-start.11 = (bf16[192,512]{1,0:T(8,128)(2,1)S(1)}, bf16[192,512]{1,0:T(8,128)(2,1)}, u32[]{:S(2)}) copy-start(bf16[192,512]{1,0:T(8,128)(2,1)} %param.14) | copy-start | bytes 589828
  9.3 100.7 %all-to-all-start = ((bf16[8,4,128,512]{3,2,1,0:T(8,128)(2,1)}), bf16[8,4,128,512]{3,2,1,0:T(8,128)(2,1)}, u32[]{:S(2)}, u32[]{:S(2)}) async-start(bf16[8,4,128,512]{3,2,1,0:T(8,128)(2,1)} %bitcast.56), calls=%async_computation | async-start | bytes 8388608 | tf_op jit(solution)/shard_map/all_to_all | solution.py:109
  23.6 1.9 %copy-start.8 = (f32[192,704]{1,0:T(8,128)}, f32[192,704]{1,0:T(8,128)S(1)}, u32[]{:S(2)}) copy-start(f32[192,704]{1,0:T(8,128)S(1)} %get-tuple-element.45) | copy-start | bytes 1622020
  24.0 1.6 %copy-start.6 = (f32[192,704]{1,0:T(8,128)}, f32[192,704]{1,0:T(8,128)S(1)}, u32[]{:S(2)}) copy-start(f32[192,704]{1,0:T(8,128)S(1)} %get-tuple-element.47) | copy-start | bytes 1622020
  24.4 1.2 copy-start.4
  26.4 86.1 %copy-start.12 = (bf16[192,512]{1,0:T(8,128)(2,1)S(1)}, bf16[192,512]{1,0:T(8,128)(2,1)}, u32[]{:S(2)}) copy-start(bf16[192,512]{1,0:T(8,128)(2,1)} %param.14) | copy-start | bytes 589828
  114.4 1.3 copy-start.9
  114.4 1.3 copy-start.10
  114.4 1.3 copy-start.13
  114.4 1.6 %copy-start.7 = (f32[192,704]{1,0:T(8,128)S(1)}, f32[192,704]{1,0:T(8,128)}, u32[]{:S(2)}) copy-start(f32[192,704]{1,0:T(8,128)} %copy-done.6) | copy-start | bytes 1622020
  115.6 1.1 copy-start.5
  127.7 0.9 copy-start.2
  129.7 2.6 %collective-permute-start = (f32[192,2,512]{2,0,1:T(8,128)}, f32[192,2,512]{2,0,1:T(8,128)}, u32[]{:S(2)}, u32[]{:S(2)}) collective-permute-start(f32[192,2,512]{2,0,1:T(8,128)} %select_bitcast_fusion), channel_id=1, source_target_pairs={{0,1},{1,0},{2,3},{3,2},{4,5},{5,4},{6,7},{7,6},{8,9},{9,8},{10,11... | collective-permute-start | bytes 2359304 | tf_op jit(solution)/shard_map/ppermute | solution.py:62
  129.7 11.4 %copy-start.14 = (bf16[192,512]{1,0:T(8,128)(2,1)S(1)}, bf16[192,512]{1,0:T(8,128)(2,1)}, u32[]{:S(2)}) copy-start(bf16[192,512]{1,0:T(8,128)(2,1)} %param.17) | copy-start | bytes 589828
  134.1 7.0 %collective-permute-start.1 = (bf16[192,1,512]{2,0,1:T(8,128)(2,1)S(1)}, bf16[192,1,512]{2,0,1:T(8,128)(2,1)S(1)}, u32[]{:S(2)}, u32[]{:S(2)}) collective-permute-start(bf16[192,1,512]{2,0,1:T(8,128)(2,1)S(1)} %fusion.75), channel_id=1, source_target_pairs={{0,2},{1,3},{2,0},{3,1},{4,6},{5,7},{6,4},{7,5},{8,10},{9,11},{10,... | collective-permute-start | bytes 589832 | tf_op jit(solution)/shard_map/ppermute | solution.py:62

commit v8 on v7

--- a/solution.py
+++ b/solution.py
@@ -45,24 +45,27 @@
     return merged
 
 
-def sum_over_grp(projected):
+def project_over_grp(attention, w_out):
     size = lax.axis_size("grp")
     index = lax.axis_index("grp")
-    rows = projected.shape[0]
-    block = projected.shape[1] // size
-    kept = projected.reshape(rows, size, block)
+    block = w_out.shape[1] // size
+    kept = [
+        jnp.dot(attention, w_out[:, b * block : (b + 1) * block], preferred_element_type=jnp.float32)
+        for b in range(size)
+    ]
     step = 1
     while step < size:
-        pairs = kept.reshape(rows, kept.shape[1] // 2, 2, block)
         high = (index & step) != 0
-        keep = jnp.where(high, pairs[:, :, 1], pairs[:, :, 0])
-        give = jnp.where(high, pairs[:, :, 0], pairs[:, :, 1])
+        keep = [jnp.where(high, kept[k + 1], kept[k]) for k in range(0, len(kept), 2)]
+        give = jnp.concatenate(
+            [jnp.where(high, kept[k], kept[k + 1]) for k in range(0, len(kept), 2)], axis=1
+        )
         if step * 2 == size:
             give = give.astype(jnp.bfloat16)
-        moved = lax.ppermute(give, "grp", [(g, g ^ step) for g in range(size)])
-        kept = keep + moved.astype(jnp.float32)
+        moved = lax.ppermute(give, "grp", [(g, g ^ step) for g in range(size)]).astype(jnp.float32)
+        kept = [part + moved[:, k * block : (k + 1) * block] for k, part in enumerate(keep)]
         step *= 2
-    return kept.reshape(rows, block)
+    return kept[0]
 
 
 def pick(table, index):
@@ -149,8 +152,7 @@
     merged = combine(local_part, upper_part)
     attended = jnp.concatenate([part[2] / part[1] for part in merged], axis=1)
     attention = jnp.where(is_live[:, None], attended, 0.0).astype(jnp.bfloat16)
-    projected = jnp.dot(attention, w_out, preferred_element_type=jnp.float32)
-    mixed = sum_over_grp(projected)
+    mixed = project_over_grp(attention, w_out)
     return (residual.astype(jnp.float32) + mixed).astype(jnp.bfloat16)
 
 

time: 142 us -> 129 us (0.908)
  local copies, waits for them, and re-layouts: 14.8 us -> 6.56 us
  other arithmetic: 16.4 us -> 12.6 us
  matrix products: 8.98 us -> 7.45 us
    another operation x1 -> x0, local copies, waits for them, and re-layouts: 3.43 us -> none  [sum_over_grp(): pairs = kept.reshape(rows, kept.shape[1] // 2, 2, block)]
    slice x1 -> x0, local copies, waits for them, and re-layouts: 3.25 us -> none  [sum_over_grp(): keep = jnp.where(high, pairs[:, :, 1], pairs[:, :, 0])]
    reshape x1 -> x0, other arithmetic: 1.71 us -> none  [sum_over_grp(): pairs = kept.reshape(rows, kept.shape[1] // 2, 2, block)]
where the time goes in v8:
time: 129 us
  waiting for transfers between devices  92.2 us (71%)
  other arithmetic  12.6 us (10%)
  starting transfers between devices  9.06 us (7%)
  matrix products  7.45 us (6%)
  local copies, waits for them, and re-layouts  6.56 us (5%)
    all_to_all x1, waiting for transfers between devices, shards(): received = lax.all_to_all(send, 'tok', 0, 0, tiled=True)  84.5 us
    ppermute x2, waiting for transfers between devices, project_over_grp(): lax.ppermute(give, 'grp', [(g, g ^ step) for g in range(size)])  7.68 us
    all_to_all x1, starting transfers between devices, shards(): received = lax.all_to_all(send, 'tok', 0, 0, tiled=True)  7.4 us
    dot_general x8, matrix products, partial_attention(): lax.dot_general(query_rows[:, cols], key_rows[:, cols], (((1,), (1,)), ((...  3.29 us
    reduce_sum x3, other arithmetic, pick(): return jnp.sum(jnp.where(ids == index, table, 0))  3.1 us
    dot_general x8, matrix products, partial_attention(): jnp.dot(exp_scores.astype(jnp.bfloat16), values[:, cols], preferred_eleme...  3.06 us
    gather x1, local copies, waits for them, and re-layouts, shards(): both.at[jnp.concatenate([dest_nodes, node_count + dest_nodes], axis=1)]  2.79 us
  transfers between devices with their start and end apart: 3, of which 3 were waited for; matrix products, arithmetic and copies ran while one was open for 6% of the time, Pallas kernels for 0%

profile of v8, /device:TPU:0, one launch (start us, length us, event | category | flops | bytes accessed | tf_op | source)
XLA Modules:
  0.0 128.9 jit_solution(5286455712696549310)
XLA Ops:
  0.0 1.3 %add_bitcast_fusion.1 = (s32[8,1,1]{0,1,2:T(1,128)S(1)}, s32[8,1]{0,1:T(1,128)S(1)}, s32[]{:T(128)}) fusion(s32[8]{0:T(128)} %param.24, s32[]{:T(128)S(6)} %axis_index.25), kind=kLoop, calls=%fused_computation.183 | loop fusion | flops 31 | bytes 104 | tf_op jit(solution)/shard_map/concatenate | solution.py:109
  1.3 0.8 select_reduce_fusion
  2.1 0.1 copy.23
  2.2 0.1 reshape.354
  2.3 1.5 %pad_maximum_fusion = bf16[12,128,512]{2,1,0:T(8,128)(2,1)S(1)} fusion(bf16[6,128,512]{2,1,0:T(8,128)(2,1)} %param.22, bf16[6,128,512]{2,1,0:T(8,128)(2,1)} %param.21), kind=kLoop, calls=%fused_computation.9 | loop fusion | flops 786432 | bytes 3145728 | tf_op jit(solution)/shard_map/concatenate | solution.py:108
  3.8 2.8 %gather_fusion = bf16[32,128,512]{2,1,0:T(8,128)(2,1)} fusion(bf16[12,128,512]{2,1,0:T(8,128)(2,1)S(1)} %pad_maximum_fusion, s32[1024]{0:T(1024)S(1)} %pad_clamp_fusion), kind=kCustom, calls=%fused_computation | custom fusion | bytes 8388736 | tf_op jit(solution)/shard_map/gather | solution.py:109
  6.6 0.0 copy-start
  6.6 0.0 copy-start.1
  6.6 0.0 copy-start.4
  6.6 7.4 %all-to-all-start = ((bf16[8,4,128,512]{3,2,1,0:T(8,128)(2,1)}), bf16[8,4,128,512]{3,2,1,0:T(8,128)(2,1)}, u32[]{:S(2)}, u32[]{:S(2)}) async-start(bf16[8,4,128,512]{3,2,1,0:T(8,128)(2,1)} %bitcast.41), calls=%async_computation | async-start | bytes 8388608 | tf_op jit(solution)/shard_map/all_to_all | solution.py:112
  14.7 0.0 copy-done.10
  14.7 1.3 fusion.113
  15.9 0.0 copy-done.7
  15.9 1.2 fusion.114
  17.1 1.3 %pad_add_fusion.1 = s32[2]{0:T(128)S(1)} fusion(s32[1]{0:T(128)} %bitcast.4, s32[1]{0:T(128)} %bitcast.3), kind=kLoop, calls=%fused_computation.176 | loop fusion | flops 2 | bytes 16 | tf_op jit(solution)/shard_map/stack | solution.py:143
  18.5 0.1 iota_add_fusion
  18.6 0.1 broadcast_compare_fusion
  18.7 0.0 copy-done.8
  18.7 0.0 copy-done.9
  18.7 0.6 select_reduce_fusion.2
  19.3 0.6 iota_compare_fusion.2
  20.0 0.6 iota_compare_fusion.3
  20.6 0.0 copy-done
  20.6 0.0 copy-done.1
  20.6 0.0 copy-done.4
  20.6 0.3 fusion.146
  21.0 0.4 fusion.147
  21.3 0.4 fusion.148
  21.7 0.4 fusion.141
  22.0 0.7 fusion.60
  22.8 84.5 %all-to-all-done = bf16[8,4,128,512]{3,2,1,0:T(8,128)(2,1)} async-done(((bf16[8,4,128,512]{3,2,1,0:T(8,128)(2,1)}), bf16[8,4,128,512]{3,2,1,0:T(8,128)(2,1)}, u32[]{:S(2)}, u32[]{:S(2)}) %all-to-all-start) | async-done | bytes 4194336 | tf_op jit(solution)/shard_map/all_to_all | solution.py:112
  107.3 2.5 %fusion.140 = (bf16[8,2,128,512]{3,2,1,0:T(8,128)(2,1)S(1)}, bf16[8,2,128,512]{3,2,1,0:T(8,128)(2,1)S(1)}) fusion(bf16[8,4,128,512]{3,2,1,0:T(8,128)(2,1)} %all-to-all-done), kind=kLoop, calls=%fused_computation.200 | loop fusion | bytes 8388608 | tf_op jit(solution)/shard_map/slice | solution.py:114
  109.8 0.5 fusion.142
  110.2 0.5 fusion.143
  110.7 0.5 fusion.144
  111.2 0.5 fusion.145
  111.7 0.0 copy-start.3
  111.7 0.0 copy-start.5
  111.7 1.2 fusion.4
  112.9 0.0 copy-done.3
  112.9 0.0 copy-done.5
  112.9 0.3 convolution_multiply_fusion.15
  113.3 0.3 convolution_multiply_fusion.13
  113.6 0.3 convolution_multiply_fusion.11
  114.0 0.3 convolution_multiply_fusion.9
  114.3 0.4 fusion.27
  114.7 0.4 fusion.25
  115.2 0.4 fusion.23
  115.6 0.0 copy-start.2
  115.6 0.4 fusion.21
  116.1 0.1 fusion.68
  116.2 1.0 copy-done.2
  117.2 0.3 fusion.52
  117.5 0.3 fusion.58
  117.8 0.3 broadcast_select_fusion.1
  118.1 0.3 broadcast_select_fusion
  118.3 0.1 pad_maximum_fusion.1
  118.4 0.1 collective-permute-start
  118.5 2.3 %collective-permute-done = f32[192,1024]{1,0:T(8,128)S(1)} collective-permute-done((f32[192,1024]{1,0:T(8,128)S(1)}, f32[192,1024]{1,0:T(8,128)S(1)}, u32[]{:S(2)}, u32[]{:S(2)}) %collective-permute-start) | collective-permute-done | bytes 786464 | tf_op jit(solution)/shard_map/ppermute | solution.py:65
  120.8 0.3 select_convert_fusion
  121.0 1.6 %collective-permute-start.1 = (bf16[192,512]{1,0:T(8,128)(2,1)S(1)}, bf16[192,512]{1,0:T(8,128)(2,1)S(1)}, u32[]{:S(2)}, u32[]{:S(2)}) collective-permute-start(bf16[192,512]{1,0:T(8,128)(2,1)S(1)} %get-tuple-element.15), channel_id=1, source_target_pairs={{0,2},{1,3},{2,0},{3,1},{4,6},{5,7},{6,4},{7,5},{8,10},{9,11},{10,... | collective-permute-start | bytes 589832 | tf_op jit(solution)/shard_map/ppermute | solution.py:65
  122.6 5.4 %collective-permute-done.1 = bf16[192,512]{1,0:T(8,128)(2,1)S(1)} collective-permute-done((bf16[192,512]{1,0:T(8,128)(2,1)S(1)}, bf16[192,512]{1,0:T(8,128)(2,1)S(1)}, u32[]{:S(2)}, u32[]{:S(2)}) %collective-permute-start.1) | collective-permute-done | bytes 196640 | tf_op jit(solution)/shard_map/ppermute | solution.py:65
  128.0 0.0 copy-done.6
  128.0 0.8 add_convert_fusion
  (16 shorter events, 0.1 us)
Async XLA Ops:
  6.5 8.1 %copy-start.10 = (s32[4]{0:T(128)S(1)}, s32[4]{0:T(128)}, u32[]{:S(2)}) copy-start(s32[4]{0:T(128)} %param.25) | copy-start | bytes 52
  6.6 9.4 %copy-start.7 = (s32[6]{0:T(128)S(1)}, s32[6]{0:T(128)}, u32[]{:S(2)}) copy-start(s32[6]{0:T(128)} %param.26) | copy-start | bytes 76
  6.6 12.1 %copy-start.8 = (s32[8]{0:T(128)S(1)}, s32[8]{0:T(128)}, u32[]{:S(2)}) copy-start(s32[8]{0:T(128)} %param.27) | copy-start | bytes 100
  6.6 12.1 %copy-start.9 = (s32[8]{0:T(128)S(1)}, s32[8]{0:T(128)}, u32[]{:S(2)}) copy-start(s32[8]{0:T(128)} %param.23) | copy-start | bytes 100
  6.6 14.0 %copy-start = (bf16[1,512,512]{2,1,0:T(8,128)(2,1)S(1)}, bf16[1,512,512]{2,1,0:T(8,128)(2,1)}, u32[]{:S(2)}) copy-start(bf16[1,512,512]{2,1,0:T(8,128)(2,1)} %param.19) | copy-start | bytes 1572868
  6.6 14.0 %copy-start.1 = (bf16[192,512]{1,0:T(8,128)(2,1)S(1)}, bf16[192,512]{1,0:T(8,128)(2,1)}, u32[]{:S(2)}) copy-start(bf16[192,512]{1,0:T(8,128)(2,1)} %param.15) | copy-start | bytes 589828
  6.6 14.0 %copy-start.4 = (bf16[192,512]{1,0:T(8,128)(2,1)S(1)}, bf16[192,512]{1,0:T(8,128)(2,1)}, u32[]{:S(2)}) copy-start(bf16[192,512]{1,0:T(8,128)(2,1)} %param.14) | copy-start | bytes 589828
  6.6 100.7 %all-to-all-start = ((bf16[8,4,128,512]{3,2,1,0:T(8,128)(2,1)}), bf16[8,4,128,512]{3,2,1,0:T(8,128)(2,1)}, u32[]{:S(2)}, u32[]{:S(2)}) async-start(bf16[8,4,128,512]{3,2,1,0:T(8,128)(2,1)} %bitcast.41), calls=%async_computation | async-start | bytes 8388608 | tf_op jit(solution)/shard_map/all_to_all | solution.py:112
  111.7 1.2 copy-start.3
  111.7 1.2 copy-start.5
  115.6 1.6 %copy-start.2 = (bf16[512,2048]{1,0:T(8,128)(2,1)S(1)}, bf16[512,2048]{1,0:T(8,128)(2,1)}, u32[]{:S(2)}) copy-start(bf16[512,2048]{1,0:T(8,128)(2,1)} %param.18) | copy-start | bytes 6291460
  118.4 2.4 %collective-permute-start = (f32[192,1024]{1,0:T(8,128)S(1)}, f32[192,1024]{1,0:T(8,128)S(1)}, u32[]{:S(2)}, u32[]{:S(2)}) collective-permute-start(f32[192,1024]{1,0:T(8,128)S(1)} %pad_maximum_fusion.1), channel_id=1, source_target_pairs={{0,1},{1,0},{2,3},{3,2},{4,5},{5,4},{6,7},{7,6},{8,9},{9,8},{10,11... | collective-permute-start | bytes 2359304 | tf_op jit(solution)/shard_map/ppermute | solution.py:65
  120.8 7.3 %copy-start.6 = (bf16[192,512]{1,0:T(8,128)(2,1)S(1)}, bf16[192,512]{1,0:T(8,128)(2,1)}, u32[]{:S(2)}) copy-start(bf16[192,512]{1,0:T(8,128)(2,1)} %param.17) | copy-start | bytes 589828
  121.0 7.0 %collective-permute-start.1 = (bf16[192,512]{1,0:T(8,128)(2,1)S(1)}, bf16[192,512]{1,0:T(8,128)(2,1)S(1)}, u32[]{:S(2)}, u32[]{:S(2)}) collective-permute-start(bf16[192,512]{1,0:T(8,128)(2,1)S(1)} %get-tuple-element.15), channel_id=1, source_target_pairs={{0,2},{1,3},{2,0},{3,1},{4,6},{5,7},{6,4},{7,5},{8,10},{9,11},{10,... | collective-permute-start | bytes 589832 | tf_op jit(solution)/shard_map/ppermute | solution.py:65

commit v9 on v8

--- a/solution.py
+++ b/solution.py
@@ -106,10 +106,21 @@
     )
     dest_nodes = jnp.stack([dest_root, root_count + dest_mid], axis=1)
     both = jnp.concatenate([upper_keys, upper_values], axis=0)
-    send = both.at[jnp.concatenate([dest_nodes, node_count + dest_nodes], axis=1)].get(
-        mode="promise_in_bounds"
-    )
-    received = lax.all_to_all(send, "tok", 0, 0, tiled=True)
+    both_nodes = jnp.concatenate([dest_nodes, node_count + dest_nodes], axis=1)
+    if dev_count <= 8:
+        shift = jnp.arange(dev_count, dtype=jnp.int32)
+        order = (my_index + shift) % dev_count
+        slabs = both.at[both_nodes[order]].get(mode="promise_in_bounds")
+        received = [slabs[0]] + [
+            lax.ppermute(slabs[k], "tok", [(j, (j + k) % dev_count) for j in range(dev_count)])
+            for k in range(1, dev_count)
+        ]
+        received = jnp.stack(received)
+        sources = (my_index - shift) % dev_count
+    else:
+        send = both.at[both_nodes].get(mode="promise_in_bounds")
+        received = lax.all_to_all(send, "tok", 0, 0, tiled=True)
+        sources = jnp.arange(dev_count, dtype=jnp.int32)
     recv_keys = received[:, :2]
     recv_values = received[:, 2:]
 
@@ -137,7 +148,7 @@
     )
 
     upper_pos = (
-        jnp.arange(dev_count, dtype=jnp.int32)[:, None, None] * chunk
+        sources[:, None, None] * chunk
         + jnp.arange(chunk, dtype=jnp.int32)[None, None, :]
     )
     upper_limit = jnp.stack([root_len, mid_len])[None, :, None]

time: 129 us -> 131 us (1.016)
  the two profiles are of different devices: /device:TPU:0 before, /device:TPU:26 now
where the time goes in v9:
time: 131 us
  waiting for transfers between devices  75.9 us (58%)
  local copies, waits for them, and re-layouts  24.1 us (18%)
  other arithmetic  13 us (10%)
  starting transfers between devices  9.44 us (7%)
  matrix products  7.46 us (6%)
    ppermute x7, waiting for transfers between devices, shards(): lax.ppermute(slabs[k], 'tok', [(j, (j + k) % dev_count) for j in range(de...  68.2 us
    unnamed x31, local copies, waits for them, and re-layouts  13.2 us
    ppermute x7, starting transfers between devices, shards(): lax.ppermute(slabs[k], 'tok', [(j, (j + k) % dev_count) for j in range(de...  7.79 us
    ppermute x2, waiting for transfers between devices, project_over_grp(): lax.ppermute(give, 'grp', [(g, g ^ step) for g in range(size)])  7.69 us
    slice x1, local copies, waits for them, and re-layouts, shards(): slabs[k]  3.67 us
    gather x3, local copies, waits for them, and re-layouts, shards(): slabs = both.at[both_nodes[order]].get(mode='promise_in_bounds')  3.38 us
    dot_general x8, matrix products, partial_attention(): lax.dot_general(query_rows[:, cols], key_rows[:, cols], (((1,), (1,)), ((...  3.29 us
    reduce_sum x3, other arithmetic, pick(): return jnp.sum(jnp.where(ids == index, table, 0))  3.27 us
  transfers between devices with their start and end apart: 9, of which 5 were waited for; matrix products, arithmetic and copies ran while one was open for 16% of the time, Pallas kernels for 0%

profile of v9, /device:TPU:26, one launch (start us, length us, event | category | flops | bytes accessed | tf_op | source)
XLA Modules:
  0.0 130.8 jit_solution(14415677087057705568)
XLA Ops:
  0.0 1.3 add_bitcast_fusion
  1.3 0.8 select_reduce_fusion
  2.1 0.1 copy.34
  2.1 0.1 copy.33
  2.2 0.1 copy.32
  2.4 0.6 gather_fusion
  3.0 0.1 copy.35
  3.1 0.1 copy.36
  3.1 0.1 reshape.284
  3.2 1.5 %pad_maximum_fusion = bf16[12,128,512]{2,1,0:T(8,128)(2,1)S(1)} fusion(bf16[6,128,512]{2,1,0:T(8,128)(2,1)} %param.22, bf16[6,128,512]{2,1,0:T(8,128)(2,1)} %param.21), kind=kLoop, calls=%fused_computation.10 | loop fusion | flops 786432 | bytes 3145728 | tf_op jit(solution)/shard_map/concatenate | solution.py:108
  4.7 2.7 %gather_fusion.1 = bf16[32,128,512]{2,1,0:T(8,128)(2,1)} fusion(bf16[12,128,512]{2,1,0:T(8,128)(2,1)S(1)} %pad_maximum_fusion, s32[1024]{0:T(1024)S(1)} %pad_clamp_fusion), kind=kCustom, calls=%fused_computation.1 | custom fusion | bytes 8388736 | tf_op jit(solution)/shard_map/gather | solution.py:113
  7.5 3.7 %fusion.145 = (bf16[4,128,512]{2,1,0:T(8,128)(2,1)S(1)}, bf16[4,128,512]{2,1,0:T(8,128)(2,1)S(1)}, bf16[4,128,512]{2,1,0:T(8,128)(2,1)}, bf16[4,128,512]{2,1,0:T...) fusion(bf16[32,128,512]{2,1,0:T(8,128)(2,1)} %gather_fusion.1), kind=kLoop, calls=%fused_computation.222 | loop fusion | bytes 7340032 | tf_op jit(solution)/shard_map/slice | solution.py:115
  11.2 1.8 %collective-permute-start.1 = (bf16[4,128,512]{2,1,0:T(8,128)(2,1)}, bf16[4,128,512]{2,1,0:T(8,128)(2,1)}, u32[]{:S(2)}, u32[]{:S(2)}) collective-permute-start(bf16[4,128,512]{2,1,0:T(8,128)(2,1)} %get-tuple-element.37), channel_id=1, source_target_pairs={{0,8},{4,12},{8,16},{12,20},{16,24},{20,28},{24,0},{28,4},{1,9},{5... | collective-permute-start | bytes 1572872 | tf_op jit(solution)/shard_map/ppermute | solution.py:115
  12.9 1.6 %collective-permute-start.2 = (bf16[4,128,512]{2,1,0:T(8,128)(2,1)}, bf16[4,128,512]{2,1,0:T(8,128)(2,1)}, u32[]{:S(2)}, u32[]{:S(2)}) collective-permute-start(bf16[4,128,512]{2,1,0:T(8,128)(2,1)} %get-tuple-element.36), channel_id=1, source_target_pairs={{0,12},{4,16},{8,20},{12,24},{16,28},{20,0},{24,4},{28,8},{1,13},{... | collective-permute-start | bytes 1572872 | tf_op jit(solution)/shard_map/ppermute | solution.py:115
  14.6 1.2 collective-permute-start.3
  15.8 1.8 %collective-permute-start.4 = (bf16[4,128,512]{2,1,0:T(8,128)(2,1)}, bf16[4,128,512]{2,1,0:T(8,128)(2,1)}, u32[]{:S(2)}, u32[]{:S(2)}) collective-permute-start(bf16[4,128,512]{2,1,0:T(8,128)(2,1)} %get-tuple-element.34), channel_id=1, source_target_pairs={{0,20},{4,24},{8,28},{12,0},{16,4},{20,8},{24,12},{28,16},{1,21},{... | collective-permute-start | bytes 1572872 | tf_op jit(solution)/shard_map/ppermute | solution.py:115
  17.6 1.9 %fusion.52 = bf16[8,4,128,512]{3,2,1,0:T(8,128)(2,1)} fusion(bf16[32,128,512]{2,1,0:T(8,128)(2,1)} %gather_fusion.1), kind=kLoop, calls=%fused_computation.90 | loop fusion | bytes 1048576
  19.4 0.7 select_reduce_fusion.2
  20.2 0.7 iota_compare_fusion.3
  20.9 0.7 iota_compare_fusion.2
  21.6 0.3 fusion.151
  21.9 0.4 fusion.152
  22.3 0.3 fusion.153
  22.7 0.4 fusion.146
  23.0 1.2 fusion.114
  24.8 1.4 %fusion.115 = (s32[]{:T(128)}, s32[]{:T(128)}) fusion(s32[6]{0:T(128)S(1)} %copy-done.10, s32[]{:T(128)} %fusion.114, s32[]{:T(128)S(6)} %add.142), kind=kLoop, calls=%fused_computation.194 | loop fusion | flops 34 | bytes 40 | tf_op jit(solution)/shard_map/reduce_sum | solution.py:73
  26.2 0.7 fusion.61
  27.0 1.3 %pad_add_fusion.3 = s32[2]{0:T(128)S(1)} fusion(s32[1]{0:T(128)} %bitcast.4, s32[1]{0:T(128)} %bitcast.3), kind=kLoop, calls=%fused_computation.199 | loop fusion | flops 2 | bytes 16 | tf_op jit(solution)/shard_map/stack | solution.py:154
  28.4 1.4 %collective-permute-start.5 = (bf16[4,128,512]{2,1,0:T(8,128)(2,1)S(1)}, bf16[4,128,512]{2,1,0:T(8,128)(2,1)S(1)}, u32[]{:S(2)}, u32[]{:S(2)}) collective-permute-start(bf16[4,128,512]{2,1,0:T(8,128)(2,1)S(1)} %get-tuple-element.33), channel_id=1, source_target_pairs={{0,24},{4,28},{8,0},{12,4},{16,8},{20,12},{24,16},{28,20},{1,25},{... | collective-permute-start | bytes 1572872 | tf_op jit(solution)/shard_map/ppermute | solution.py:115
  29.8 1.9 %bitcast_dynamic-update-slice_fusion.6 = bf16[8,4,128,512]{3,2,1,0:T(8,128)(2,1)} fusion(bf16[8,4,128,512]{3,2,1,0:T(8,128)(2,1)} %fusion.52, bf16[4,128,512]{2,1,0:T(8,128)(2,1)} %collective-permute-done), kind=kLoop, calls=%fused_computation.97 | loop fusion | bytes 1048576
  31.7 5.0 %collective-permute-done.1 = bf16[4,128,512]{2,1,0:T(8,128)(2,1)} collective-permute-done((bf16[4,128,512]{2,1,0:T(8,128)(2,1)}, bf16[4,128,512]{2,1,0:T(8,128)(2,1)}, u32[]{:S(2)}, u32[]{:S(2)}) %collective-permute-start.1) | collective-permute-done | bytes 524320 | tf_op jit(solution)/shard_map/ppermute | solution.py:115
  36.8 1.9 %bitcast_dynamic-update-slice_fusion.5 = bf16[8,4,128,512]{3,2,1,0:T(8,128)(2,1)} fusion(bf16[8,4,128,512]{3,2,1,0:T(8,128)(2,1)} %bitcast_dynamic-update-slice_fusion.6, bf16[4,128,512]{2,1,0:T(8,128)(2,1)} %collective-permute-done.1), kind=kLoop, calls=%fused_computation.96 | loop fusion | bytes 1048576
  38.6 7.8 %collective-permute-done.2 = bf16[4,128,512]{2,1,0:T(8,128)(2,1)} collective-permute-done((bf16[4,128,512]{2,1,0:T(8,128)(2,1)}, bf16[4,128,512]{2,1,0:T(8,128)(2,1)}, u32[]{:S(2)}, u32[]{:S(2)}) %collective-permute-start.2) | collective-permute-done | bytes 524320 | tf_op jit(solution)/shard_map/ppermute | solution.py:115
  46.4 1.9 %bitcast_dynamic-update-slice_fusion.4 = bf16[8,4,128,512]{3,2,1,0:T(8,128)(2,1)} fusion(bf16[8,4,128,512]{3,2,1,0:T(8,128)(2,1)} %bitcast_dynamic-update-slice_fusion.5, bf16[4,128,512]{2,1,0:T(8,128)(2,1)} %collective-permute-done.2), kind=kLoop, calls=%fused_computation.95 | loop fusion | bytes 1048576
  48.3 55.4 %collective-permute-done.3 = bf16[4,128,512]{2,1,0:T(8,128)(2,1)} collective-permute-done((bf16[4,128,512]{2,1,0:T(8,128)(2,1)}, bf16[4,128,512]{2,1,0:T(8,128)(2,1)}, u32[]{:S(2)}, u32[]{:S(2)}) %collective-permute-start.3) | collective-permute-done | bytes 524320 | tf_op jit(solution)/shard_map/ppermute | solution.py:115
  103.7 1.9 %bitcast_dynamic-update-slice_fusion.3 = bf16[8,4,128,512]{3,2,1,0:T(8,128)(2,1)} fusion(bf16[8,4,128,512]{3,2,1,0:T(8,128)(2,1)} %bitcast_dynamic-update-slice_fusion.4, bf16[4,128,512]{2,1,0:T(8,128)(2,1)} %collective-permute-done.3), kind=kLoop, calls=%fused_computation.94 | loop fusion | bytes 1048576
  105.5 1.9 %bitcast_dynamic-update-slice_fusion.2 = bf16[8,4,128,512]{3,2,1,0:T(8,128)(2,1)} fusion(bf16[8,4,128,512]{3,2,1,0:T(8,128)(2,1)} %bitcast_dynamic-update-slice_fusion.3, bf16[4,128,512]{2,1,0:T(8,128)(2,1)} %collective-permute-done.4), kind=kLoop, calls=%fused_computation.93 | loop fusion | bytes 1048576
  107.4 0.8 bitcast_dynamic-update-slice_fusion.1
  108.3 0.8 bitcast_dynamic-update-slice_fusion
  109.1 2.5 %fusion.144 = (bf16[8,2,128,512]{3,2,1,0:T(8,128)(2,1)S(1)}, bf16[8,2,128,512]{3,2,1,0:T(8,128)(2,1)S(1)}) fusion(bf16[8,4,128,512]{3,2,1,0:T(8,128)(2,1)} %bitcast_dynamic-update-slice_fusion), kind=kLoop, calls=%fused_computation.221 | loop fusion | bytes 8388608 | tf_op jit(solution)/shard_map/slice | solution.py:125
  111.7 0.5 fusion.148
  112.1 0.5 fusion.149
  112.6 0.5 fusion.150
  113.1 0.5 fusion.147
  113.6 1.2 fusion.4
  114.8 0.3 convolution_multiply_fusion.15
  115.1 0.3 convolution_multiply_fusion.13
  115.5 0.3 convolution_multiply_fusion.11
  115.9 0.3 convolution_multiply_fusion.9
  116.2 0.4 fusion.27
  116.6 0.4 fusion.25
  117.1 0.4 fusion.23
  117.5 0.4 fusion.21
  118.0 0.1 fusion.69
  118.1 1.0 copy-done.2
  119.1 0.3 fusion.53
  119.4 0.3 fusion.59
  119.7 0.3 broadcast_select_fusion.1
  120.0 0.3 broadcast_select_fusion
  120.4 2.3 %collective-permute-done.7 = f32[192,1024]{1,0:T(8,128)S(1)} collective-permute-done((f32[192,1024]{1,0:T(8,128)S(1)}, f32[192,1024]{1,0:T(8,128)S(1)}, u32[]{:S(2)}, u32[]{:S(2)}) %collective-permute-start.7) | collective-permute-done | bytes 786464 | tf_op jit(solution)/shard_map/ppermute | solution.py:65
  122.7 0.3 select_convert_fusion
  122.9 1.6 %collective-permute-start.8 = (bf16[192,512]{1,0:T(8,128)(2,1)S(1)}, bf16[192,512]{1,0:T(8,128)(2,1)S(1)}, u32[]{:S(2)}, u32[]{:S(2)}) collective-permute-start(bf16[192,512]{1,0:T(8,128)(2,1)S(1)} %get-tuple-element.15), channel_id=1, source_target_pairs={{0,2},{1,3},{2,0},{3,1},{4,6},{5,7},{6,4},{7,5},{8,10},{9,11},{10,... | collective-permute-start | bytes 589832 | tf_op jit(solution)/shard_map/ppermute | solution.py:65
  124.5 5.4 %collective-permute-done.8 = bf16[192,512]{1,0:T(8,128)(2,1)S(1)} collective-permute-done((bf16[192,512]{1,0:T(8,128)(2,1)S(1)}, bf16[192,512]{1,0:T(8,128)(2,1)S(1)}, u32[]{:S(2)}, u32[]{:S(2)}) %collective-permute-start.8) | collective-permute-done | bytes 196640 | tf_op jit(solution)/shard_map/ppermute | solution.py:65
  130.0 0.8 add_convert_fusion
  (47 shorter events, 0.6 us)
Async XLA Ops:
  7.5 11.9 %copy-start.8 = (s32[8]{0:T(128)S(1)}, s32[8]{0:T(128)}, u32[]{:S(2)}) copy-start(s32[8]{0:T(128)} %param.27) | copy-start | bytes 100
  7.5 11.9 %copy-start.9 = (s32[8]{0:T(128)S(1)}, s32[8]{0:T(128)}, u32[]{:S(2)}) copy-start(s32[8]{0:T(128)} %param.23) | copy-start | bytes 100
  7.5 14.1 %copy-start = (bf16[1,512,512]{2,1,0:T(8,128)(2,1)S(1)}, bf16[1,512,512]{2,1,0:T(8,128)(2,1)}, u32[]{:S(2)}) copy-start(bf16[1,512,512]{2,1,0:T(8,128)(2,1)} %param.19) | copy-start | bytes 1572868
  7.5 14.1 %copy-start.1 = (bf16[192,512]{1,0:T(8,128)(2,1)S(1)}, bf16[192,512]{1,0:T(8,128)(2,1)}, u32[]{:S(2)}) copy-start(bf16[192,512]{1,0:T(8,128)(2,1)} %param.15) | copy-start | bytes 589828
  7.5 14.1 %copy-start.4 = (bf16[192,512]{1,0:T(8,128)(2,1)S(1)}, bf16[192,512]{1,0:T(8,128)(2,1)}, u32[]{:S(2)}) copy-start(bf16[192,512]{1,0:T(8,128)(2,1)} %param.14) | copy-start | bytes 589828
  11.2 17.2 %collective-permute-start = (bf16[4,128,512]{2,1,0:T(8,128)(2,1)}, bf16[4,128,512]{2,1,0:T(8,128)(2,1)}, u32[]{:S(2)}, u32[]{:S(2)}) collective-permute-start(bf16[4,128,512]{2,1,0:T(8,128)(2,1)} %get-tuple-element.38), channel_id=1, source_target_pairs={{0,4},{4,8},{8,12},{12,16},{16,20},{20,24},{24,28},{28,0},{1,5},{5... | collective-permute-start | bytes 1572872 | tf_op jit(solution)/shard_map/ppermute | solution.py:115
  11.2 25.6 %collective-permute-start.1 = (bf16[4,128,512]{2,1,0:T(8,128)(2,1)}, bf16[4,128,512]{2,1,0:T(8,128)(2,1)}, u32[]{:S(2)}, u32[]{:S(2)}) collective-permute-start(bf16[4,128,512]{2,1,0:T(8,128)(2,1)} %get-tuple-element.37), channel_id=1, source_target_pairs={{0,8},{4,12},{8,16},{12,20},{16,24},{20,28},{24,0},{28,4},{1,9},{5... | collective-permute-start | bytes 1572872 | tf_op jit(solution)/shard_map/ppermute | solution.py:115
  12.9 33.4 %collective-permute-start.2 = (bf16[4,128,512]{2,1,0:T(8,128)(2,1)}, bf16[4,128,512]{2,1,0:T(8,128)(2,1)}, u32[]{:S(2)}, u32[]{:S(2)}) collective-permute-start(bf16[4,128,512]{2,1,0:T(8,128)(2,1)} %get-tuple-element.36), channel_id=1, source_target_pairs={{0,12},{4,16},{8,20},{12,24},{16,28},{20,0},{24,4},{28,8},{1,13},{... | collective-permute-start | bytes 1572872 | tf_op jit(solution)/shard_map/ppermute | solution.py:115
  14.6 89.1 %collective-permute-start.3 = (bf16[4,128,512]{2,1,0:T(8,128)(2,1)}, bf16[4,128,512]{2,1,0:T(8,128)(2,1)}, u32[]{:S(2)}, u32[]{:S(2)}) collective-permute-start(bf16[4,128,512]{2,1,0:T(8,128)(2,1)} %get-tuple-element.35), channel_id=1, source_target_pairs={{0,16},{4,20},{8,24},{12,28},{16,0},{20,4},{24,8},{28,12},{1,17},{... | collective-permute-start | bytes 1572872 | tf_op jit(solution)/shard_map/ppermute | solution.py:115
  15.8 89.8 %collective-permute-start.4 = (bf16[4,128,512]{2,1,0:T(8,128)(2,1)}, bf16[4,128,512]{2,1,0:T(8,128)(2,1)}, u32[]{:S(2)}, u32[]{:S(2)}) collective-permute-start(bf16[4,128,512]{2,1,0:T(8,128)(2,1)} %get-tuple-element.34), channel_id=1, source_target_pairs={{0,20},{4,24},{8,28},{12,0},{16,4},{20,8},{24,12},{28,16},{1,21},{... | collective-permute-start | bytes 1572872 | tf_op jit(solution)/shard_map/ppermute | solution.py:115
  22.3 0.7 copy-start.11
  22.3 2.5 %copy-start.10 = (s32[6]{0:T(128)S(1)}, s32[6]{0:T(128)}, u32[]{:S(2)}) copy-start(s32[6]{0:T(128)} %param.26) | copy-start | bytes 76
  28.4 79.0 %collective-permute-start.5 = (bf16[4,128,512]{2,1,0:T(8,128)(2,1)S(1)}, bf16[4,128,512]{2,1,0:T(8,128)(2,1)S(1)}, u32[]{:S(2)}, u32[]{:S(2)}) collective-permute-start(bf16[4,128,512]{2,1,0:T(8,128)(2,1)S(1)} %get-tuple-element.33), channel_id=1, source_target_pairs={{0,24},{4,28},{8,0},{12,4},{16,8},{20,12},{24,16},{28,20},{1,25},{... | collective-permute-start | bytes 1572872 | tf_op jit(solution)/shard_map/ppermute | solution.py:115
  36.7 71.5 %collective-permute-start.6 = (bf16[4,128,512]{2,1,0:T(8,128)(2,1)S(1)}, bf16[4,128,512]{2,1,0:T(8,128)(2,1)S(1)}, u32[]{:S(2)}, u32[]{:S(2)}) collective-permute-start(bf16[4,128,512]{2,1,0:T(8,128)(2,1)S(1)} %get-tuple-element.32), channel_id=1, source_target_pairs={{0,28},{4,0},{8,4},{12,8},{16,12},{20,16},{24,20},{28,24},{1,29},{... | collective-permute-start | bytes 1572872 | tf_op jit(solution)/shard_map/ppermute | solution.py:115
  109.1 2.5 %copy-start.5 = (bf16[192,512]{1,0:T(8,128)(2,1)S(1)}, bf16[192,512]{1,0:T(8,128)(2,1)}, u32[]{:S(2)}) copy-start(bf16[192,512]{1,0:T(8,128)(2,1)} %param.14) | copy-start | bytes 589828
  113.6 1.2 copy-start.3
  113.6 1.2 copy-start.6
  117.5 1.6 %copy-start.2 = (bf16[512,2048]{1,0:T(8,128)(2,1)S(1)}, bf16[512,2048]{1,0:T(8,128)(2,1)}, u32[]{:S(2)}) copy-start(bf16[512,2048]{1,0:T(8,128)(2,1)} %param.18) | copy-start | bytes 6291460
  120.3 2.4 %collective-permute-start.7 = (f32[192,1024]{1,0:T(8,128)S(1)}, f32[192,1024]{1,0:T(8,128)S(1)}, u32[]{:S(2)}, u32[]{:S(2)}) collective-permute-start(f32[192,1024]{1,0:T(8,128)S(1)} %pad_maximum_fusion.1), channel_id=1, source_target_pairs={{0,1},{1,0},{2,3},{3,2},{4,5},{5,4},{6,7},{7,6},{8,9},{9,8},{10,11... | collective-permute-start | bytes 2359304 | tf_op jit(solution)/shard_map/ppermute | solution.py:65
  122.7 7.3 %copy-start.7 = (bf16[192,512]{1,0:T(8,128)(2,1)S(1)}, bf16[192,512]{1,0:T(8,128)(2,1)}, u32[]{:S(2)}) copy-start(bf16[192,512]{1,0:T(8,128)(2,1)} %param.17) | copy-start | bytes 589828
  122.9 7.0 %collective-permute-start.8 = (bf16[192,512]{1,0:T(8,128)(2,1)S(1)}, bf16[192,512]{1,0:T(8,128)(2,1)S(1)}, u32[]{:S(2)}, u32[]{:S(2)}) collective-permute-start(bf16[192,512]{1,0:T(8,128)(2,1)S(1)} %get-tuple-element.15), channel_id=1, source_target_pairs={{0,2},{1,3},{2,0},{3,1},{4,6},{5,7},{6,4},{7,5},{8,10},{9,11},{10,... | collective-permute-start | bytes 589832 | tf_op jit(solution)/shard_map/ppermute | solution.py:65

commit v10 on v9

--- a/solution.py
+++ b/solution.py
@@ -107,16 +107,15 @@
     dest_nodes = jnp.stack([dest_root, root_count + dest_mid], axis=1)
     both = jnp.concatenate([upper_keys, upper_values], axis=0)
     both_nodes = jnp.concatenate([dest_nodes, node_count + dest_nodes], axis=1)
-    if dev_count <= 8:
-        shift = jnp.arange(dev_count, dtype=jnp.int32)
-        order = (my_index + shift) % dev_count
-        slabs = both.at[both_nodes[order]].get(mode="promise_in_bounds")
-        received = [slabs[0]] + [
-            lax.ppermute(slabs[k], "tok", [(j, (j + k) % dev_count) for j in range(dev_count)])
-            for k in range(1, dev_count)
-        ]
+    if dev_count <= 8 and dev_count & (dev_count - 1) == 0:
+        flips = jnp.arange(dev_count, dtype=jnp.int32)
+        slabs = both.at[both_nodes[my_index ^ flips]].get(mode="promise_in_bounds")
+        received = [None] * dev_count
+        received[0] = slabs[0]
+        for k in sorted(range(1, dev_count), key=lambda k: (-bin(k).count("1"), -k)):
+            received[k] = lax.ppermute(slabs[k], "tok", [(j, j ^ k) for j in range(dev_count)])
         received = jnp.stack(received)
-        sources = (my_index - shift) % dev_count
+        sources = my_index ^ flips
     else:
         send = both.at[both_nodes].get(mode="promise_in_bounds")
         received = lax.all_to_all(send, "tok", 0, 0, tiled=True)

time: 131 us -> 131 us (level)
  the two profiles are of different devices: /device:TPU:26 before, /device:TPU:16 now
where the time goes in v10:
time: 131 us
  waiting for transfers between devices  75.9 us (58%)
  local copies, waits for them, and re-layouts  24.1 us (18%)
  other arithmetic  13 us (10%)
  starting transfers between devices  9.51 us (7%)
  matrix products  7.47 us (6%)
    ppermute x7, waiting for transfers between devices, shards(): lax.ppermute(slabs[k], 'tok', [(j, j ^ k) for j in range(dev_count)])  68.2 us
    unnamed x31, local copies, waits for them, and re-layouts  13.2 us
    ppermute x7, starting transfers between devices, shards(): lax.ppermute(slabs[k], 'tok', [(j, j ^ k) for j in range(dev_count)])  7.86 us
    ppermute x2, waiting for transfers between devices, project_over_grp(): lax.ppermute(give, 'grp', [(g, g ^ step) for g in range(size)])  7.69 us
    slice x1, local copies, waits for them, and re-layouts, shards(): slabs[k]  3.67 us
    gather x3, local copies, waits for them, and re-layouts, shards(): slabs = both.at[both_nodes[my_index ^ flips]].get(mode='promise_in_bounds')  3.38 us
    dot_general x8, matrix products, partial_attention(): lax.dot_general(query_rows[:, cols], key_rows[:, cols], (((1,), (1,)), ((...  3.29 us
    reduce_sum x3, other arithmetic, pick(): return jnp.sum(jnp.where(ids == index, table, 0))  3.27 us
  transfers between devices with their start and end apart: 9, of which 7 were waited for; matrix products, arithmetic and copies ran while one was open for 16% of the time, Pallas kernels for 0%

profile of v10, /device:TPU:16, one launch (start us, length us, event | category | flops | bytes accessed | tf_op | source)
XLA Modules:
  0.0 130.8 jit_solution(11557073482949386465)
XLA Ops:
  0.0 1.3 add_bitcast_fusion
  1.3 0.8 select_reduce_fusion
  2.1 0.1 copy.34
  2.4 0.6 gather_fusion
  3.0 0.1 copy.35
  3.0 0.1 copy.36
  3.1 0.1 reshape.240
  3.2 1.5 %pad_maximum_fusion = bf16[12,128,512]{2,1,0:T(8,128)(2,1)S(1)} fusion(bf16[6,128,512]{2,1,0:T(8,128)(2,1)} %param.22, bf16[6,128,512]{2,1,0:T(8,128)(2,1)} %param.21), kind=kLoop, calls=%fused_computation.10 | loop fusion | flops 786432 | bytes 3145728 | tf_op jit(solution)/shard_map/concatenate | solution.py:108
  4.7 2.7 %gather_fusion.1 = bf16[32,128,512]{2,1,0:T(8,128)(2,1)} fusion(bf16[12,128,512]{2,1,0:T(8,128)(2,1)S(1)} %pad_maximum_fusion, s32[1024]{0:T(1024)S(1)} %pad_clamp_fusion), kind=kCustom, calls=%fused_computation.1 | custom fusion | bytes 8388736 | tf_op jit(solution)/shard_map/gather | solution.py:112
  7.5 3.7 %fusion.142 = (bf16[4,128,512]{2,1,0:T(8,128)(2,1)S(1)}, bf16[4,128,512]{2,1,0:T(8,128)(2,1)S(1)}, bf16[4,128,512]{2,1,0:T(8,128)(2,1)}, bf16[4,128,512]{2,1,0:T...) fusion(bf16[32,128,512]{2,1,0:T(8,128)(2,1)} %gather_fusion.1), kind=kLoop, calls=%fused_computation.214 | loop fusion | bytes 7340032 | tf_op jit(solution)/shard_map/slice | solution.py:116
  11.2 1.5 %collective-permute-start = (bf16[4,128,512]{2,1,0:T(8,128)(2,1)}, bf16[4,128,512]{2,1,0:T(8,128)(2,1)}, u32[]{:S(2)}, u32[]{:S(2)}) collective-permute-start(bf16[4,128,512]{2,1,0:T(8,128)(2,1)} %get-tuple-element.38), channel_id=1, source_target_pairs={{0,4},{4,0},{8,12},{12,8},{16,20},{20,16},{24,28},{28,24},{1,5},{5... | collective-permute-start | bytes 1572872 | tf_op jit(solution)/shard_map/ppermute | solution.py:116
  12.7 1.6 %collective-permute-start.1 = (bf16[4,128,512]{2,1,0:T(8,128)(2,1)}, bf16[4,128,512]{2,1,0:T(8,128)(2,1)}, u32[]{:S(2)}, u32[]{:S(2)}) collective-permute-start(bf16[4,128,512]{2,1,0:T(8,128)(2,1)} %get-tuple-element.37), channel_id=1, source_target_pairs={{0,8},{4,12},{8,0},{12,4},{16,24},{20,28},{24,16},{28,20},{1,9},{5... | collective-permute-start | bytes 1572872 | tf_op jit(solution)/shard_map/ppermute | solution.py:116
  14.2 0.4 collective-permute-start.2
  14.7 3.9 %collective-permute-start.4 = (bf16[4,128,512]{2,1,0:T(8,128)(2,1)}, bf16[4,128,512]{2,1,0:T(8,128)(2,1)}, u32[]{:S(2)}, u32[]{:S(2)}) collective-permute-start(bf16[4,128,512]{2,1,0:T(8,128)(2,1)} %get-tuple-element.34), channel_id=1, source_target_pairs={{0,20},{4,16},{8,28},{12,24},{16,4},{20,0},{24,12},{28,8},{1,21},{... | collective-permute-start | bytes 1572872 | tf_op jit(solution)/shard_map/ppermute | solution.py:116
  18.5 1.9 %fusion.52 = bf16[8,4,128,512]{3,2,1,0:T(8,128)(2,1)} fusion(bf16[32,128,512]{2,1,0:T(8,128)(2,1)} %gather_fusion.1), kind=kLoop, calls=%fused_computation.90 | loop fusion | bytes 1048576
  20.4 0.7 select_reduce_fusion.2
  21.1 0.7 iota_compare_fusion.3
  21.8 0.7 iota_compare_fusion.2
  22.5 0.3 fusion.148
  22.9 0.4 fusion.149
  23.3 0.3 fusion.150
  23.6 0.4 fusion.143
  24.0 1.2 fusion.113
  25.8 1.4 %fusion.114 = (s32[]{:T(128)}, s32[]{:T(128)}) fusion(s32[6]{0:T(128)S(1)} %copy-done.10, s32[]{:T(128)} %fusion.113, s32[]{:T(128)S(6)} %add.109), kind=kLoop, calls=%fused_computation.187 | loop fusion | flops 34 | bytes 40 | tf_op jit(solution)/shard_map/reduce_sum | solution.py:73
  27.1 0.7 fusion.61
  27.9 1.3 %pad_add_fusion.3 = s32[2]{0:T(128)S(1)} fusion(s32[1]{0:T(128)} %bitcast.4, s32[1]{0:T(128)} %bitcast.3), kind=kLoop, calls=%fused_computation.190 | loop fusion | flops 2 | bytes 16 | tf_op jit(solution)/shard_map/stack | solution.py:153
  29.4 0.5 collective-permute-start.5
  29.9 1.9 %bitcast_dynamic-update-slice_fusion.6 = bf16[8,4,128,512]{3,2,1,0:T(8,128)(2,1)} fusion(bf16[8,4,128,512]{3,2,1,0:T(8,128)(2,1)} %fusion.52, bf16[4,128,512]{2,1,0:T(8,128)(2,1)} %collective-permute-done), kind=kLoop, calls=%fused_computation.97 | loop fusion | bytes 1048576
  31.8 15.1 %collective-permute-done.1 = bf16[4,128,512]{2,1,0:T(8,128)(2,1)} collective-permute-done((bf16[4,128,512]{2,1,0:T(8,128)(2,1)}, bf16[4,128,512]{2,1,0:T(8,128)(2,1)}, u32[]{:S(2)}, u32[]{:S(2)}) %collective-permute-start.1) | collective-permute-done | bytes 524320 | tf_op jit(solution)/shard_map/ppermute | solution.py:116
  46.9 1.9 %bitcast_dynamic-update-slice_fusion.5 = bf16[8,4,128,512]{3,2,1,0:T(8,128)(2,1)} fusion(bf16[8,4,128,512]{3,2,1,0:T(8,128)(2,1)} %bitcast_dynamic-update-slice_fusion.6, bf16[4,128,512]{2,1,0:T(8,128)(2,1)} %collective-permute-done.1), kind=kLoop, calls=%fused_computation.96 | loop fusion | bytes 1048576
  48.8 7.9 %collective-permute-done.2 = bf16[4,128,512]{2,1,0:T(8,128)(2,1)} collective-permute-done((bf16[4,128,512]{2,1,0:T(8,128)(2,1)}, bf16[4,128,512]{2,1,0:T(8,128)(2,1)}, u32[]{:S(2)}, u32[]{:S(2)}) %collective-permute-start.2) | collective-permute-done | bytes 524320 | tf_op jit(solution)/shard_map/ppermute | solution.py:116
  56.7 1.9 %bitcast_dynamic-update-slice_fusion.4 = bf16[8,4,128,512]{3,2,1,0:T(8,128)(2,1)} fusion(bf16[8,4,128,512]{3,2,1,0:T(8,128)(2,1)} %bitcast_dynamic-update-slice_fusion.5, bf16[4,128,512]{2,1,0:T(8,128)(2,1)} %collective-permute-done.2), kind=kLoop, calls=%fused_computation.95 | loop fusion | bytes 1048576
  58.5 1.9 %bitcast_dynamic-update-slice_fusion.3 = bf16[8,4,128,512]{3,2,1,0:T(8,128)(2,1)} fusion(bf16[8,4,128,512]{3,2,1,0:T(8,128)(2,1)} %bitcast_dynamic-update-slice_fusion.4, bf16[4,128,512]{2,1,0:T(8,128)(2,1)} %collective-permute-done.3), kind=kLoop, calls=%fused_computation.94 | loop fusion | bytes 1048576
  60.4 23.1 %collective-permute-done.4 = bf16[4,128,512]{2,1,0:T(8,128)(2,1)} collective-permute-done((bf16[4,128,512]{2,1,0:T(8,128)(2,1)}, bf16[4,128,512]{2,1,0:T(8,128)(2,1)}, u32[]{:S(2)}, u32[]{:S(2)}) %collective-permute-start.4) | collective-permute-done | bytes 524320 | tf_op jit(solution)/shard_map/ppermute | solution.py:116
  83.5 1.9 %bitcast_dynamic-update-slice_fusion.2 = bf16[8,4,128,512]{3,2,1,0:T(8,128)(2,1)} fusion(bf16[8,4,128,512]{3,2,1,0:T(8,128)(2,1)} %bitcast_dynamic-update-slice_fusion.3, bf16[4,128,512]{2,1,0:T(8,128)(2,1)} %collective-permute-done.4), kind=kLoop, calls=%fused_computation.93 | loop fusion | bytes 1048576
  85.4 12.7 %collective-permute-done.5 = bf16[4,128,512]{2,1,0:T(8,128)(2,1)S(1)} collective-permute-done((bf16[4,128,512]{2,1,0:T(8,128)(2,1)S(1)}, bf16[4,128,512]{2,1,0:T(8,128)(2,1)S(1)}, u32[]{:S(2)}, u32[]{:S(2)}) %collective-permute-start.5) | collective-permute-done | bytes 524320 | tf_op jit(solution)/shard_map/ppermute | solution.py:116
  98.2 0.8 bitcast_dynamic-update-slice_fusion.1
  99.0 9.3 %collective-permute-done.6 = bf16[4,128,512]{2,1,0:T(8,128)(2,1)S(1)} collective-permute-done((bf16[4,128,512]{2,1,0:T(8,128)(2,1)S(1)}, bf16[4,128,512]{2,1,0:T(8,128)(2,1)S(1)}, u32[]{:S(2)}, u32[]{:S(2)}) %collective-permute-start.6) | collective-permute-done | bytes 524320 | tf_op jit(solution)/shard_map/ppermute | solution.py:116
  108.3 0.8 bitcast_dynamic-update-slice_fusion
  109.2 2.5 %fusion.141 = (bf16[8,2,128,512]{3,2,1,0:T(8,128)(2,1)S(1)}, bf16[8,2,128,512]{3,2,1,0:T(8,128)(2,1)S(1)}) fusion(bf16[8,4,128,512]{3,2,1,0:T(8,128)(2,1)} %bitcast_dynamic-update-slice_fusion), kind=kLoop, calls=%fused_computation.213 | loop fusion | bytes 8388608 | tf_op jit(solution)/shard_map/slice | solution.py:124
  111.7 0.5 fusion.145
  112.2 0.5 fusion.146
  112.7 0.5 fusion.147
  113.1 0.5 fusion.144
  113.6 1.2 fusion.4
  114.9 0.3 convolution_multiply_fusion.15
  115.2 0.3 convolution_multiply_fusion.13
  115.6 0.3 convolution_multiply_fusion.11
  115.9 0.3 convolution_multiply_fusion.9
  116.2 0.4 fusion.27
  116.7 0.4 fusion.25
  117.1 0.4 fusion.23
  117.6 0.4 fusion.21
  118.0 0.1 fusion.69
  118.1 1.0 copy-done.2
  119.2 0.3 fusion.53
  119.5 0.3 fusion.59
  119.7 0.3 broadcast_select_fusion.1
  120.0 0.3 broadcast_select_fusion
  120.5 2.3 %collective-permute-done.7 = f32[192,1024]{1,0:T(8,128)S(1)} collective-permute-done((f32[192,1024]{1,0:T(8,128)S(1)}, f32[192,1024]{1,0:T(8,128)S(1)}, u32[]{:S(2)}, u32[]{:S(2)}) %collective-permute-start.7) | collective-permute-done | bytes 786464 | tf_op jit(solution)/shard_map/ppermute | solution.py:65
  122.7 0.3 select_convert_fusion
  123.0 1.6 %collective-permute-start.8 = (bf16[192,512]{1,0:T(8,128)(2,1)S(1)}, bf16[192,512]{1,0:T(8,128)(2,1)S(1)}, u32[]{:S(2)}, u32[]{:S(2)}) collective-permute-start(bf16[192,512]{1,0:T(8,128)(2,1)S(1)} %get-tuple-element.15), channel_id=1, source_target_pairs={{0,2},{1,3},{2,0},{3,1},{4,6},{5,7},{6,4},{7,5},{8,10},{9,11},{10,... | collective-permute-start | bytes 589832 | tf_op jit(solution)/shard_map/ppermute | solution.py:65
  124.6 5.4 %collective-permute-done.8 = bf16[192,512]{1,0:T(8,128)(2,1)S(1)} collective-permute-done((bf16[192,512]{1,0:T(8,128)(2,1)S(1)}, bf16[192,512]{1,0:T(8,128)(2,1)S(1)}, u32[]{:S(2)}, u32[]{:S(2)}) %collective-permute-start.8) | collective-permute-done | bytes 196640 | tf_op jit(solution)/shard_map/ppermute | solution.py:65
  130.0 0.8 add_convert_fusion
  (47 shorter events, 0.7 us)
Async XLA Ops:
  7.5 12.9 %copy-start.8 = (s32[8]{0:T(128)S(1)}, s32[8]{0:T(128)}, u32[]{:S(2)}) copy-start(s32[8]{0:T(128)} %param.27) | copy-start | bytes 100
  7.5 12.9 %copy-start.9 = (s32[8]{0:T(128)S(1)}, s32[8]{0:T(128)}, u32[]{:S(2)}) copy-start(s32[8]{0:T(128)} %param.23) | copy-start | bytes 100
  7.5 15.0 %copy-start = (bf16[1,512,512]{2,1,0:T(8,128)(2,1)S(1)}, bf16[1,512,512]{2,1,0:T(8,128)(2,1)}, u32[]{:S(2)}) copy-start(bf16[1,512,512]{2,1,0:T(8,128)(2,1)} %param.19) | copy-start | bytes 1572868
  7.5 15.0 %copy-start.1 = (bf16[192,512]{1,0:T(8,128)(2,1)S(1)}, bf16[192,512]{1,0:T(8,128)(2,1)}, u32[]{:S(2)}) copy-start(bf16[192,512]{1,0:T(8,128)(2,1)} %param.15) | copy-start | bytes 589828
  7.5 15.0 %copy-start.4 = (bf16[192,512]{1,0:T(8,128)(2,1)S(1)}, bf16[192,512]{1,0:T(8,128)(2,1)}, u32[]{:S(2)}) copy-start(bf16[192,512]{1,0:T(8,128)(2,1)} %param.14) | copy-start | bytes 589828
  11.2 18.2 %collective-permute-start = (bf16[4,128,512]{2,1,0:T(8,128)(2,1)}, bf16[4,128,512]{2,1,0:T(8,128)(2,1)}, u32[]{:S(2)}, u32[]{:S(2)}) collective-permute-start(bf16[4,128,512]{2,1,0:T(8,128)(2,1)} %get-tuple-element.38), channel_id=1, source_target_pairs={{0,4},{4,0},{8,12},{12,8},{16,20},{20,16},{24,28},{28,24},{1,5},{5... | collective-permute-start | bytes 1572872 | tf_op jit(solution)/shard_map/ppermute | solution.py:116
  12.7 34.2 %collective-permute-start.1 = (bf16[4,128,512]{2,1,0:T(8,128)(2,1)}, bf16[4,128,512]{2,1,0:T(8,128)(2,1)}, u32[]{:S(2)}, u32[]{:S(2)}) collective-permute-start(bf16[4,128,512]{2,1,0:T(8,128)(2,1)} %get-tuple-element.37), channel_id=1, source_target_pairs={{0,8},{4,12},{8,0},{12,4},{16,24},{20,28},{24,16},{28,20},{1,9},{5... | collective-permute-start | bytes 1572872 | tf_op jit(solution)/shard_map/ppermute | solution.py:116
  14.2 42.4 %collective-permute-start.2 = (bf16[4,128,512]{2,1,0:T(8,128)(2,1)}, bf16[4,128,512]{2,1,0:T(8,128)(2,1)}, u32[]{:S(2)}, u32[]{:S(2)}) collective-permute-start(bf16[4,128,512]{2,1,0:T(8,128)(2,1)} %get-tuple-element.36), channel_id=1, source_target_pairs={{0,12},{4,8},{8,4},{12,0},{16,28},{20,24},{24,20},{28,16},{1,13},{... | collective-permute-start | bytes 1572872 | tf_op jit(solution)/shard_map/ppermute | solution.py:116
  14.7 43.9 %collective-permute-start.3 = (bf16[4,128,512]{2,1,0:T(8,128)(2,1)}, bf16[4,128,512]{2,1,0:T(8,128)(2,1)}, u32[]{:S(2)}, u32[]{:S(2)}) collective-permute-start(bf16[4,128,512]{2,1,0:T(8,128)(2,1)} %get-tuple-element.35), channel_id=1, source_target_pairs={{0,16},{4,20},{8,24},{12,28},{16,0},{20,4},{24,8},{28,12},{1,17},{... | collective-permute-start | bytes 1572872 | tf_op jit(solution)/shard_map/ppermute | solution.py:116
  14.7 68.9 %collective-permute-start.4 = (bf16[4,128,512]{2,1,0:T(8,128)(2,1)}, bf16[4,128,512]{2,1,0:T(8,128)(2,1)}, u32[]{:S(2)}, u32[]{:S(2)}) collective-permute-start(bf16[4,128,512]{2,1,0:T(8,128)(2,1)} %get-tuple-element.34), channel_id=1, source_target_pairs={{0,20},{4,16},{8,28},{12,24},{16,4},{20,0},{24,12},{28,8},{1,21},{... | collective-permute-start | bytes 1572872 | tf_op jit(solution)/shard_map/ppermute | solution.py:116
  23.2 0.7 copy-start.11
  23.2 2.5 %copy-start.10 = (s32[6]{0:T(128)S(1)}, s32[6]{0:T(128)}, u32[]{:S(2)}) copy-start(s32[6]{0:T(128)} %param.26) | copy-start | bytes 76
  29.4 68.8 %collective-permute-start.5 = (bf16[4,128,512]{2,1,0:T(8,128)(2,1)S(1)}, bf16[4,128,512]{2,1,0:T(8,128)(2,1)S(1)}, u32[]{:S(2)}, u32[]{:S(2)}) collective-permute-start(bf16[4,128,512]{2,1,0:T(8,128)(2,1)S(1)} %get-tuple-element.33), channel_id=1, source_target_pairs={{0,24},{4,28},{8,16},{12,20},{16,8},{20,12},{24,0},{28,4},{1,25},{... | collective-permute-start | bytes 1572872 | tf_op jit(solution)/shard_map/ppermute | solution.py:116
  46.9 61.4 %collective-permute-start.6 = (bf16[4,128,512]{2,1,0:T(8,128)(2,1)S(1)}, bf16[4,128,512]{2,1,0:T(8,128)(2,1)S(1)}, u32[]{:S(2)}, u32[]{:S(2)}) collective-permute-start(bf16[4,128,512]{2,1,0:T(8,128)(2,1)S(1)} %get-tuple-element.32), channel_id=1, source_target_pairs={{0,28},{4,24},{8,20},{12,16},{16,12},{20,8},{24,4},{28,0},{1,29},{... | collective-permute-start | bytes 1572872 | tf_op jit(solution)/shard_map/ppermute | solution.py:116
  109.2 2.5 %copy-start.5 = (bf16[192,512]{1,0:T(8,128)(2,1)S(1)}, bf16[192,512]{1,0:T(8,128)(2,1)}, u32[]{:S(2)}) copy-start(bf16[192,512]{1,0:T(8,128)(2,1)} %param.14) | copy-start | bytes 589828
  113.6 1.2 copy-start.3
  113.6 1.2 copy-start.6
  117.6 1.6 %copy-start.2 = (bf16[512,2048]{1,0:T(8,128)(2,1)S(1)}, bf16[512,2048]{1,0:T(8,128)(2,1)}, u32[]{:S(2)}) copy-start(bf16[512,2048]{1,0:T(8,128)(2,1)} %param.18) | copy-start | bytes 6291460
  120.4 2.4 %collective-permute-start.7 = (f32[192,1024]{1,0:T(8,128)S(1)}, f32[192,1024]{1,0:T(8,128)S(1)}, u32[]{:S(2)}, u32[]{:S(2)}) collective-permute-start(f32[192,1024]{1,0:T(8,128)S(1)} %pad_maximum_fusion.1), channel_id=1, source_target_pairs={{0,1},{1,0},{2,3},{3,2},{4,5},{5,4},{6,7},{7,6},{8,9},{9,8},{10,11... | collective-permute-start | bytes 2359304 | tf_op jit(solution)/shard_map/ppermute | solution.py:65
  122.7 7.3 %copy-start.7 = (bf16[192,512]{1,0:T(8,128)(2,1)S(1)}, bf16[192,512]{1,0:T(8,128)(2,1)}, u32[]{:S(2)}) copy-start(bf16[192,512]{1,0:T(8,128)(2,1)} %param.17) | copy-start | bytes 589828
  123.0 7.0 %collective-permute-start.8 = (bf16[192,512]{1,0:T(8,128)(2,1)S(1)}, bf16[192,512]{1,0:T(8,128)(2,1)S(1)}, u32[]{:S(2)}, u32[]{:S(2)}) collective-permute-start(bf16[192,512]{1,0:T(8,128)(2,1)S(1)} %get-tuple-element.15), channel_id=1, source_target_pairs={{0,2},{1,3},{2,0},{3,1},{4,6},{5,7},{6,4},{7,5},{8,10},{9,11},{10,... | collective-permute-start | bytes 589832 | tf_op jit(solution)/shard_map/ppermute | solution.py:65

commit v11 on v8

--- a/solution.py
+++ b/solution.py
@@ -106,12 +106,11 @@
     )
     dest_nodes = jnp.stack([dest_root, root_count + dest_mid], axis=1)
     both = jnp.concatenate([upper_keys, upper_values], axis=0)
-    send = both.at[jnp.concatenate([dest_nodes, node_count + dest_nodes], axis=1)].get(
-        mode="promise_in_bounds"
-    )
-    received = lax.all_to_all(send, "tok", 0, 0, tiled=True)
-    recv_keys = received[:, :2]
-    recv_values = received[:, 2:]
+    slots = jnp.concatenate([dest_nodes, node_count + dest_nodes], axis=1).T
+    send = both.at[slots].get(mode="promise_in_bounds")
+    received = lax.all_to_all(send, "tok", 1, 1, tiled=True)
+    recv_keys = received[:2]
+    recv_values = received[2:]
 
     my_length = pick(req_len, my_index)
     my_mid = pick(leaf_mid, my_index)
@@ -137,10 +136,10 @@
     )
 
     upper_pos = (
-        jnp.arange(dev_count, dtype=jnp.int32)[:, None, None] * chunk
+        jnp.arange(dev_count, dtype=jnp.int32)[None, :, None] * chunk
         + jnp.arange(chunk, dtype=jnp.int32)[None, None, :]
     )
-    upper_limit = jnp.stack([root_len, mid_len])[None, :, None]
+    upper_limit = jnp.stack([root_len, mid_len])[:, None, None]
     upper_ok = (upper_pos < upper_limit).reshape(-1)
     upper_part = partial_attention(
         queries,

time: 129 us -> 134 us (1.039)
  local copies, waits for them, and re-layouts: 6.56 us -> 11.3 us
    gather x1 -> x2, local copies, waits for them, and re-layouts: 2.79 us -> 7.34 us  [shards(): send = both.at[slots].get(mode='promise_in_bounds')]
where the time goes in v11:
time: 134 us
  waiting for transfers between devices  92.3 us (69%)
  other arithmetic  12.7 us (9%)
  local copies, waits for them, and re-layouts  11.3 us (8%)
  starting transfers between devices  9.05 us (7%)
  matrix products  7.46 us (6%)
    all_to_all x1, waiting for transfers between devices, shards(): received = lax.all_to_all(send, 'tok', 1, 1, tiled=True)  84.6 us
    ppermute x2, waiting for transfers between devices, project_over_grp(): lax.ppermute(give, 'grp', [(g, g ^ step) for g in range(size)])  7.69 us
    all_to_all x1, starting transfers between devices, shards(): received = lax.all_to_all(send, 'tok', 1, 1, tiled=True)  7.4 us
    gather x2, local copies, waits for them, and re-layouts, shards(): send = both.at[slots].get(mode='promise_in_bounds')  7.34 us
    dot_general x8, matrix products, partial_attention(): lax.dot_general(query_rows[:, cols], key_rows[:, cols], (((1,), (1,)), ((...  3.29 us
    reduce_sum x3, other arithmetic, pick(): return jnp.sum(jnp.where(ids == index, table, 0))  3.12 us
    dot_general x8, matrix products, partial_attention(): jnp.dot(exp_scores.astype(jnp.bfloat16), values[:, cols], preferred_eleme...  3.06 us
  transfers between devices with their start and end apart: 3, of which 3 were waited for; matrix products, arithmetic and copies ran while one was open for 6% of the time, Pallas kernels for 0%

profile of v11, /device:TPU:0, one launch (start us, length us, event | category | flops | bytes accessed | tf_op | source)
XLA Modules:
  0.0 133.7 jit_solution(9079477138839112868)
XLA Ops:
  0.0 0.8 select_reduce_fusion
  0.8 1.3 add_bitcast_fusion.1
  2.1 0.1 reshape.203
  2.2 1.5 %pad_maximum_fusion = bf16[12,128,512]{2,1,0:T(8,128)(2,1)S(1)} fusion(bf16[6,128,512]{2,1,0:T(8,128)(2,1)} %param.22, bf16[6,128,512]{2,1,0:T(8,128)(2,1)} %param.21), kind=kLoop, calls=%fused_computation.9 | loop fusion | flops 786432 | bytes 3145728 | tf_op jit(solution)/shard_map/concatenate | solution.py:108
  3.7 2.8 %gather_fusion = bf16[32,128,512]{2,1,0:T(8,128)(2,1)} fusion(bf16[12,128,512]{2,1,0:T(8,128)(2,1)S(1)} %pad_maximum_fusion, s32[1024]{0:T(1024)S(1)} %pad_clamp_fusion), kind=kCustom, calls=%fused_computation | custom fusion | bytes 8388736 | tf_op jit(solution)/shard_map/gather | solution.py:110
  6.5 4.5 %copy.18 = bf16[4,8,128,512]{3,2,0,1:T(8,128)(2,1)} copy(bf16[4,8,128,512]{3,2,1,0:T(8,128)(2,1)} %bitcast.36) | data formatting | bytes 8388608 | tf_op jit(solution)/shard_map/gather | solution.py:110
  11.0 0.0 copy-start.1
  11.1 0.0 copy-start.4
  11.1 7.4 %all-to-all-start = ((bf16[4,8,128,512]{3,2,0,1:T(8,128)(2,1)}), bf16[4,8,128,512]{3,2,0,1:T(8,128)(2,1)}, u32[]{:S(2)}, u32[]{:S(2)}) async-start(bf16[4,8,128,512]{3,2,0,1:T(8,128)(2,1)} %copy.18), calls=%async_computation | async-start | bytes 8388608 | tf_op jit(solution)/shard_map/all_to_all | solution.py:111
  19.0 0.7 iota_compare_fusion.2
  19.7 0.0 copy-done.8
  19.7 0.6 select_reduce_fusion.3
  20.4 0.6 iota_compare_fusion.3
  21.0 0.0 copy-done.9
  21.0 1.2 fusion.112
  22.2 0.0 copy-done.7
  22.2 1.3 fusion.113
  23.5 1.3 pad_add_fusion.1
  24.8 0.1 iota_add_fusion
  24.9 0.1 compare_bitcast_fusion
  25.0 0.0 copy-done
  25.0 0.0 copy-done.1
  25.0 0.0 copy-done.4
  25.0 0.3 fusion.140
  25.4 0.4 fusion.145
  25.7 0.4 fusion.146
  26.1 0.4 fusion.147
  26.4 0.7 fusion.60
  27.2 84.6 %all-to-all-done = bf16[4,8,128,512]{3,2,0,1:T(8,128)(2,1)} async-done(((bf16[4,8,128,512]{3,2,0,1:T(8,128)(2,1)}), bf16[4,8,128,512]{3,2,0,1:T(8,128)(2,1)}, u32[]{:S(2)}, u32[]{:S(2)}) %all-to-all-start) | async-done | bytes 4194336 | tf_op jit(solution)/shard_map/all_to_all | solution.py:111
  111.8 2.5 %fusion.139 = (bf16[2,8,128,512]{3,2,0,1:T(8,128)(2,1)S(1)}, bf16[2,8,128,512]{3,2,0,1:T(8,128)(2,1)S(1)}) fusion(bf16[4,8,128,512]{3,2,0,1:T(8,128)(2,1)} %all-to-all-done), kind=kLoop, calls=%fused_computation.199 | loop fusion | bytes 8388608 | tf_op jit(solution)/shard_map/slice | solution.py:113
  114.3 0.1 copy.21
  114.4 0.5 fusion.141
  114.9 0.5 fusion.142
  115.3 0.5 fusion.143
  115.8 0.5 fusion.144
  116.3 0.2 copy.22
  116.5 0.0 copy-start.3
  116.5 0.0 copy-start.5
  116.5 1.2 fusion.4
  117.7 0.0 copy-done.3
  117.8 0.0 copy-done.5
  117.8 0.3 convolution_multiply_fusion.15
  118.1 0.3 convolution_multiply_fusion.13
  118.4 0.3 convolution_multiply_fusion.11
  118.8 0.3 convolution_multiply_fusion.9
  119.1 0.4 fusion.27
  119.6 0.4 fusion.25
  120.0 0.4 fusion.23
  120.5 0.0 copy-start.2
  120.5 0.4 fusion.21
  120.9 0.1 fusion.68
  121.0 1.0 copy-done.2
  122.1 0.3 fusion.52
  122.3 0.3 fusion.58
  122.6 0.3 broadcast_select_fusion.1
  122.9 0.3 broadcast_select_fusion
  123.2 0.1 pad_maximum_fusion.1
  123.3 0.1 collective-permute-start
  123.3 2.3 %collective-permute-done = f32[192,1024]{1,0:T(8,128)S(1)} collective-permute-done((f32[192,1024]{1,0:T(8,128)S(1)}, f32[192,1024]{1,0:T(8,128)S(1)}, u32[]{:S(2)}, u32[]{:S(2)}) %collective-permute-start) | collective-permute-done | bytes 786464 | tf_op jit(solution)/shard_map/ppermute | solution.py:65
  125.6 0.3 select_convert_fusion
  125.9 1.6 %collective-permute-start.1 = (bf16[192,512]{1,0:T(8,128)(2,1)S(1)}, bf16[192,512]{1,0:T(8,128)(2,1)S(1)}, u32[]{:S(2)}, u32[]{:S(2)}) collective-permute-start(bf16[192,512]{1,0:T(8,128)(2,1)S(1)} %get-tuple-element.15), channel_id=1, source_target_pairs={{0,2},{1,3},{2,0},{3,1},{4,6},{5,7},{6,4},{7,5},{8,10},{9,11},{10,... | collective-permute-start | bytes 589832 | tf_op jit(solution)/shard_map/ppermute | solution.py:65
  127.5 5.4 %collective-permute-done.1 = bf16[192,512]{1,0:T(8,128)(2,1)S(1)} collective-permute-done((bf16[192,512]{1,0:T(8,128)(2,1)S(1)}, bf16[192,512]{1,0:T(8,128)(2,1)S(1)}, u32[]{:S(2)}, u32[]{:S(2)}) %collective-permute-start.1) | collective-permute-done | bytes 196640 | tf_op jit(solution)/shard_map/ppermute | solution.py:65
  132.9 0.0 copy-done.6
  132.9 0.8 add_convert_fusion
  (15 shorter events, 0.1 us)
Async XLA Ops:
  11.0 8.7 %copy-start.8 = (s32[8]{0:T(128)S(1)}, s32[8]{0:T(128)}, u32[]{:S(2)}) copy-start(s32[8]{0:T(128)} %param.23) | copy-start | bytes 100
  11.0 10.0 %copy-start.9 = (s32[4]{0:T(128)S(1)}, s32[4]{0:T(128)}, u32[]{:S(2)}) copy-start(s32[4]{0:T(128)} %param.25) | copy-start | bytes 52
  11.0 11.2 %copy-start.7 = (s32[6]{0:T(128)S(1)}, s32[6]{0:T(128)}, u32[]{:S(2)}) copy-start(s32[6]{0:T(128)} %param.26) | copy-start | bytes 76
  11.0 13.9 %copy-start = (bf16[1,512,512]{2,1,0:T(8,128)(2,1)S(1)}, bf16[1,512,512]{2,1,0:T(8,128)(2,1)}, u32[]{:S(2)}) copy-start(bf16[1,512,512]{2,1,0:T(8,128)(2,1)} %param.19) | copy-start | bytes 1572868
  11.0 13.9 %copy-start.1 = (bf16[192,512]{1,0:T(8,128)(2,1)S(1)}, bf16[192,512]{1,0:T(8,128)(2,1)}, u32[]{:S(2)}) copy-start(bf16[192,512]{1,0:T(8,128)(2,1)} %param.15) | copy-start | bytes 589828
  11.1 13.9 %copy-start.4 = (bf16[192,512]{1,0:T(8,128)(2,1)S(1)}, bf16[192,512]{1,0:T(8,128)(2,1)}, u32[]{:S(2)}) copy-start(bf16[192,512]{1,0:T(8,128)(2,1)} %param.14) | copy-start | bytes 589828
  11.1 100.7 %all-to-all-start = ((bf16[4,8,128,512]{3,2,0,1:T(8,128)(2,1)}), bf16[4,8,128,512]{3,2,0,1:T(8,128)(2,1)}, u32[]{:S(2)}, u32[]{:S(2)}) async-start(bf16[4,8,128,512]{3,2,0,1:T(8,128)(2,1)} %copy.18), calls=%async_computation | async-start | bytes 8388608 | tf_op jit(solution)/shard_map/all_to_all | solution.py:111
  116.5 1.2 copy-start.3
  116.5 1.2 copy-start.5
  120.5 1.6 %copy-start.2 = (bf16[512,2048]{1,0:T(8,128)(2,1)S(1)}, bf16[512,2048]{1,0:T(8,128)(2,1)}, u32[]{:S(2)}) copy-start(bf16[512,2048]{1,0:T(8,128)(2,1)} %param.18) | copy-start | bytes 6291460
  123.3 2.4 %collective-permute-start = (f32[192,1024]{1,0:T(8,128)S(1)}, f32[192,1024]{1,0:T(8,128)S(1)}, u32[]{:S(2)}, u32[]{:S(2)}) collective-permute-start(f32[192,1024]{1,0:T(8,128)S(1)} %pad_maximum_fusion.1), channel_id=1, source_target_pairs={{0,1},{1,0},{2,3},{3,2},{4,5},{5,4},{6,7},{7,6},{8,9},{9,8},{10,11... | collective-permute-start | bytes 2359304 | tf_op jit(solution)/shard_map/ppermute | solution.py:65
  125.6 7.3 %copy-start.6 = (bf16[192,512]{1,0:T(8,128)(2,1)S(1)}, bf16[192,512]{1,0:T(8,128)(2,1)}, u32[]{:S(2)}) copy-start(bf16[192,512]{1,0:T(8,128)(2,1)} %param.17) | copy-start | bytes 589828
  125.9 7.0 %collective-permute-start.1 = (bf16[192,512]{1,0:T(8,128)(2,1)S(1)}, bf16[192,512]{1,0:T(8,128)(2,1)S(1)}, u32[]{:S(2)}, u32[]{:S(2)}) collective-permute-start(bf16[192,512]{1,0:T(8,128)(2,1)S(1)} %get-tuple-element.15), channel_id=1, source_target_pairs={{0,2},{1,3},{2,0},{3,1},{4,6},{5,7},{6,4},{7,5},{8,10},{9,11},{10,... | collective-permute-start | bytes 589832 | tf_op jit(solution)/shard_map/ppermute | solution.py:65

commit v12 on v8

--- a/solution.py
+++ b/solution.py
@@ -105,13 +105,9 @@
         jnp.where(dest_mid[:, None] == mid_ids[None, :], mid_root[None, :], 0), axis=1
     )
     dest_nodes = jnp.stack([dest_root, root_count + dest_mid], axis=1)
-    both = jnp.concatenate([upper_keys, upper_values], axis=0)
-    send = both.at[jnp.concatenate([dest_nodes, node_count + dest_nodes], axis=1)].get(
-        mode="promise_in_bounds"
-    )
-    received = lax.all_to_all(send, "tok", 0, 0, tiled=True)
-    recv_keys = received[:, :2]
-    recv_values = received[:, 2:]
+    both = jnp.concatenate([upper_keys, upper_values], axis=2)
+    send = both.at[dest_nodes].get(mode="promise_in_bounds")
+    received = lax.all_to_all(send, "tok", 0, 0, tiled=True).reshape(-1, 2 * col_count)
 
     my_length = pick(req_len, my_index)
     my_mid = pick(leaf_mid, my_index)
@@ -144,8 +140,8 @@
     upper_ok = (upper_pos < upper_limit).reshape(-1)
     upper_part = partial_attention(
         queries,
-        recv_keys.reshape(-1, col_count),
-        recv_values.reshape(-1, col_count),
+        received[:, :col_count],
+        received[:, col_count:],
         upper_ok[None, :],
         head_count,
     )

time: 129 us -> 135 us (1.047)
  matrix products: 7.45 us -> 16 us
  local copies, waits for them, and re-layouts: 6.56 us -> 3.03 us
    dot_general x8, matrix products: 3.06 us -> 7.44 us  [partial_attention(): jnp.dot(exp_scores.astype(jnp.bfloat16), values[:, cols], preferred_eleme...]
    dot_general x8, matrix products: 3.29 us -> 7.45 us  [partial_attention(): lax.dot_general(query_rows[:, cols], key_rows[:, cols], (((1,), (1,)), ((...]
    slice x1 -> x0, local copies, waits for them, and re-layouts: 2.49 us -> none  [shards(): recv_values = received[:, 2:]]
    concatenate x3 -> x1, other arithmetic: 2.81 us -> 1.55 us  [shards(): both = jnp.concatenate([upper_keys, upper_values], axis=2)]
where the time goes in v12:
time: 135 us; the launch traced here: 134 us
  waiting for transfers between devices  92.2 us (68%)
  matrix products  16 us (12%)
  other arithmetic  12.7 us (9%)
  starting transfers between devices  9.05 us (7%)
  local copies, waits for them, and re-layouts  3.03 us (2%)
    all_to_all x1, waiting for transfers between devices, shards(): lax.all_to_all(send, 'tok', 0, 0, tiled=True).reshape(-1, 2 * col_count)  84.5 us
    ppermute x2, waiting for transfers between devices, project_over_grp(): lax.ppermute(give, 'grp', [(g, g ^ step) for g in range(size)])  7.69 us
    dot_general x8, matrix products, partial_attention(): lax.dot_general(query_rows[:, cols], key_rows[:, cols], (((1,), (1,)), ((...  7.45 us
    dot_general x8, matrix products, partial_attention(): jnp.dot(exp_scores.astype(jnp.bfloat16), values[:, cols], preferred_eleme...  7.44 us
    all_to_all x1, starting transfers between devices, shards(): lax.all_to_all(send, 'tok', 0, 0, tiled=True).reshape(-1, 2 * col_count)  7.4 us
    reduce_sum x3, other arithmetic, pick(): return jnp.sum(jnp.where(ids == index, table, 0))  3.19 us
    gather x1, local copies, waits for them, and re-layouts, shards(): send = both.at[dest_nodes].get(mode='promise_in_bounds')  2.79 us
  transfers between devices with their start and end apart: 3, of which 3 were waited for; matrix products, arithmetic and copies ran while one was open for 6% of the time, Pallas kernels for 0%

profile of v12, /device:TPU:0, one launch (start us, length us, event | category | flops | bytes accessed | tf_op | source)
XLA Modules:
  0.0 133.9 jit_solution(365891184730536422)
XLA Ops:
  0.0 0.8 select_reduce_fusion
  0.8 1.3 add_bitcast_fusion
  2.1 0.1 copy.17
  2.2 0.1 reshape.283
  2.2 1.5 %pad_maximum_fusion = bf16[6,128,1024]{2,1,0:T(8,128)(2,1)S(1)} fusion(bf16[6,128,512]{2,1,0:T(8,128)(2,1)} %param.22, bf16[6,128,512]{2,1,0:T(8,128)(2,1)} %param.21), kind=kLoop, calls=%fused_computation.9 | loop fusion | flops 3145728 | bytes 3145728 | tf_op jit(solution)/shard_map/concatenate | solution.py:108
  3.8 2.8 %gather_fusion = bf16[16,128,1024]{2,1,0:T(8,128)(2,1)} fusion(bf16[6,128,1024]{2,1,0:T(8,128)(2,1)S(1)} %pad_maximum_fusion, s32[1024]{0:T(1024)S(1)} %pad_clamp_fusion), kind=kCustom, calls=%fused_computation | custom fusion | bytes 8388672 | tf_op jit(solution)/shard_map/gather | solution.py:109
  6.6 0.0 copy-start.8
  6.6 0.0 copy-start.7
  6.6 0.0 copy-start.9
  6.6 0.0 copy-start.1
  6.6 0.0 copy-start.4
  6.6 7.4 %all-to-all-start = ((bf16[8,2,128,1024]{3,2,1,0:T(8,128)(2,1)}), bf16[8,2,128,1024]{3,2,1,0:T(8,128)(2,1)}, u32[]{:S(2)}, u32[]{:S(2)}) async-start(bf16[8,2,128,1024]{3,2,1,0:T(8,128)(2,1)} %bitcast.31), calls=%async_computation | async-start | bytes 8388608 | tf_op jit(solution)/shard_map/all_to_all | solution.py:110
  14.7 0.0 copy-done.8
  14.7 1.3 fusion.112
  16.0 0.0 copy-done.7
  16.0 1.3 fusion.113
  17.3 1.3 pad_add_fusion.1
  18.5 0.1 iota_add_fusion
  18.6 0.1 broadcast_compare_fusion
  18.7 0.6 iota_compare_fusion.2
  19.3 0.0 copy-done.9
  19.3 0.6 select_reduce_fusion.3
  20.0 0.6 iota_compare_fusion.3
  20.6 0.0 copy-done
  20.7 0.0 copy-done.1
  20.7 0.0 copy-done.4
  20.7 0.3 fusion.139
  21.0 0.4 fusion.144
  21.4 0.4 fusion.145
  21.7 0.4 fusion.146
  22.1 0.7 fusion.60
  22.8 84.5 %all-to-all-done = bf16[8,2,128,1024]{3,2,1,0:T(8,128)(2,1)} async-done(((bf16[8,2,128,1024]{3,2,1,0:T(8,128)(2,1)}), bf16[8,2,128,1024]{3,2,1,0:T(8,128)(2,1)}, u32[]{:S(2)}, u32[]{:S(2)}) %all-to-all-start) | async-done | bytes 4194336 | tf_op jit(solution)/shard_map/all_to_all | solution.py:110
  107.3 1.5 %fusion.140 = (f32[192]{0:T(256)S(1)}, f32[2048,192]{0,1:T(8,128)S(1)}) fusion(bf16[192,512]{1,0:T(8,128)(2,1)S(1)} %copy-done.4, bf16[2048,1024]{1,0:T(8,128)(2,1)} %bitcast.8, pred[2048]{0:T(1024)(128)(4,1)S(1)} %lt.61), kind=kOutput, calls=%fused_computation.198 | convolution fusion | flops 101842752 | bytes 2149120 | tf_op jit(solution)/shard_map/dot_general | solution.py:17
  108.8 1.5 %fusion.141 = (f32[192]{0:T(256)S(1)}, f32[2048,192]{0,1:T(8,128)S(1)}) fusion(bf16[192,512]{1,0:T(8,128)(2,1)S(1)} %copy-done.4, bf16[2048,1024]{1,0:T(8,128)(2,1)} %bitcast.8, pred[2048]{0:T(1024)(128)(4,1)S(1)} %lt.61), kind=kOutput, calls=%fused_computation.199 | convolution fusion | flops 101842752 | bytes 2149120 | tf_op jit(solution)/shard_map/dot_general | solution.py:17
  110.3 1.5 %fusion.142 = (f32[192]{0:T(256)S(1)}, f32[2048,192]{0,1:T(8,128)S(1)}) fusion(bf16[192,512]{1,0:T(8,128)(2,1)S(1)} %copy-done.4, bf16[2048,1024]{1,0:T(8,128)(2,1)} %bitcast.8, pred[2048]{0:T(1024)(128)(4,1)S(1)} %lt.61), kind=kOutput, calls=%fused_computation.200 | convolution fusion | flops 101842752 | bytes 2149120 | tf_op jit(solution)/shard_map/dot_general | solution.py:17
  111.8 1.5 %fusion.143 = (f32[192]{0:T(256)S(1)}, f32[2048,192]{0,1:T(8,128)S(1)}) fusion(bf16[192,512]{1,0:T(8,128)(2,1)S(1)} %copy-done.4, bf16[2048,1024]{1,0:T(8,128)(2,1)} %bitcast.8, pred[2048]{0:T(1024)(128)(4,1)S(1)} %lt.61), kind=kOutput, calls=%fused_computation.201 | convolution fusion | flops 101842752 | bytes 2149120 | tf_op jit(solution)/shard_map/dot_general | solution.py:17
  113.4 0.0 copy-start.3
  113.4 0.0 copy-start.5
  113.4 1.2 fusion.4
  114.6 0.0 copy-done.3
  114.6 0.0 copy-done.5
  114.6 0.3 convolution_multiply_fusion.15
  114.9 0.3 convolution_multiply_fusion.13
  115.3 0.3 convolution_multiply_fusion.11
  115.6 0.3 convolution_multiply_fusion.9
  116.0 1.5 %fusion.27 = bf16[192,128]{1,0:T(8,128)(2,1)S(1)} fusion(f32[192,128]{1,0:T(8,128)S(1)} %convolution_multiply_fusion.15, f32[2048,192]{0,1:T(8,128)S(1)} %get-tuple-element.35, f32[192]{0:T(256)S(1)} %get-tuple-element.34, pred[2048]{0:T(1024)(128)(4,1)S(1)} %lt.61, bf16[2048,1024]{1,0:T(8,128)(2,1)} %bitcast.8, f32[192]{0:T(256)S(1)} %get-tuple-element.18, ...), kind=kOutput, calls=%fused_computation.48 | convolution fusion | flops 101941248 | bytes 2248960 | tf_op jit(solution)/shard_map/dot_general | solution.py:27
  117.5 1.5 %fusion.25 = bf16[192,128]{1,0:T(8,128)(2,1)S(1)} fusion(f32[192,128]{1,0:T(8,128)S(1)} %convolution_multiply_fusion.13, f32[2048,192]{0,1:T(8,128)S(1)} %get-tuple-element.37, f32[192]{0:T(256)S(1)} %get-tuple-element.36, pred[2048]{0:T(1024)(128)(4,1)S(1)} %lt.61, bf16[2048,1024]{1,0:T(8,128)(2,1)} %bitcast.8, f32[192]{0:T(256)S(1)} %get-tuple-element.21, ...), kind=kOutput, calls=%fused_computation.44 | convolution fusion | flops 101941248 | bytes 2248960 | tf_op jit(solution)/shard_map/dot_general | solution.py:27
  119.0 1.5 %fusion.23 = bf16[192,128]{1,0:T(8,128)(2,1)S(1)} fusion(f32[192,128]{1,0:T(8,128)S(1)} %convolution_multiply_fusion.11, f32[2048,192]{0,1:T(8,128)S(1)} %get-tuple-element.39, f32[192]{0:T(256)S(1)} %get-tuple-element.38, pred[2048]{0:T(1024)(128)(4,1)S(1)} %lt.61, bf16[2048,1024]{1,0:T(8,128)(2,1)} %bitcast.8, f32[192]{0:T(256)S(1)} %get-tuple-element.24, ...), kind=kOutput, calls=%fused_computation.40 | convolution fusion | flops 101941248 | bytes 2248960 | tf_op jit(solution)/shard_map/dot_general | solution.py:27
  120.5 0.0 copy-start.2
  120.5 1.6 %fusion.21 = bf16[192,128]{1,0:T(8,128)(2,1)S(1)} fusion(f32[192,128]{1,0:T(8,128)S(1)} %convolution_multiply_fusion.9, f32[2048,192]{0,1:T(8,128)S(1)} %get-tuple-element.41, f32[192]{0:T(256)S(1)} %get-tuple-element.40, pred[2048]{0:T(1024)(128)(4,1)S(1)} %lt.61, bf16[2048,1024]{1,0:T(8,128)(2,1)} %bitcast.8, f32[192]{0:T(256)S(1)} %get-tuple-element.27, ...), kind=kOutput, calls=%fused_computation.36 | convolution fusion | flops 101941248 | bytes 2248960 | tf_op jit(solution)/shard_map/dot_general | solution.py:27
  122.1 0.1 fusion.68
  122.2 0.0 copy-done.2
  122.3 0.3 fusion.52
  122.5 0.3 fusion.58
  122.8 0.3 broadcast_select_fusion.1
  123.1 0.3 broadcast_select_fusion
  123.4 0.1 pad_maximum_fusion.1
  123.5 0.1 collective-permute-start
  123.5 2.3 %collective-permute-done = f32[192,1024]{1,0:T(8,128)S(1)} collective-permute-done((f32[192,1024]{1,0:T(8,128)S(1)}, f32[192,1024]{1,0:T(8,128)S(1)}, u32[]{:S(2)}, u32[]{:S(2)}) %collective-permute-start) | collective-permute-done | bytes 786464 | tf_op jit(solution)/shard_map/ppermute | solution.py:65
  125.8 0.3 select_convert_fusion
  126.1 1.6 %collective-permute-start.1 = (bf16[192,512]{1,0:T(8,128)(2,1)S(1)}, bf16[192,512]{1,0:T(8,128)(2,1)S(1)}, u32[]{:S(2)}, u32[]{:S(2)}) collective-permute-start(bf16[192,512]{1,0:T(8,128)(2,1)S(1)} %get-tuple-element.15), channel_id=1, source_target_pairs={{0,2},{1,3},{2,0},{3,1},{4,6},{5,7},{6,4},{7,5},{8,10},{9,11},{10,... | collective-permute-start | bytes 589832 | tf_op jit(solution)/shard_map/ppermute | solution.py:65
  127.7 5.4 %collective-permute-done.1 = bf16[192,512]{1,0:T(8,128)(2,1)S(1)} collective-permute-done((bf16[192,512]{1,0:T(8,128)(2,1)S(1)}, bf16[192,512]{1,0:T(8,128)(2,1)S(1)}, u32[]{:S(2)}, u32[]{:S(2)}) %collective-permute-start.1) | collective-permute-done | bytes 196640 | tf_op jit(solution)/shard_map/ppermute | solution.py:65
  133.1 0.0 copy-done.6
  133.1 0.8 add_convert_fusion
  (12 shorter events, 0.1 us)
Async XLA Ops:
  6.6 8.1 %copy-start.8 = (s32[4]{0:T(128)S(1)}, s32[4]{0:T(128)}, u32[]{:S(2)}) copy-start(s32[4]{0:T(128)} %param.25) | copy-start | bytes 52
  6.6 9.4 %copy-start.7 = (s32[6]{0:T(128)S(1)}, s32[6]{0:T(128)}, u32[]{:S(2)}) copy-start(s32[6]{0:T(128)} %param.26) | copy-start | bytes 76
  6.6 12.7 %copy-start.9 = (s32[8]{0:T(128)S(1)}, s32[8]{0:T(128)}, u32[]{:S(2)}) copy-start(s32[8]{0:T(128)} %param.23) | copy-start | bytes 100
  6.6 14.1 %copy-start = (bf16[1,512,512]{2,1,0:T(8,128)(2,1)S(1)}, bf16[1,512,512]{2,1,0:T(8,128)(2,1)}, u32[]{:S(2)}) copy-start(bf16[1,512,512]{2,1,0:T(8,128)(2,1)} %param.19) | copy-start | bytes 1572868
  6.6 14.1 %copy-start.1 = (bf16[192,512]{1,0:T(8,128)(2,1)S(1)}, bf16[192,512]{1,0:T(8,128)(2,1)}, u32[]{:S(2)}) copy-start(bf16[192,512]{1,0:T(8,128)(2,1)} %param.15) | copy-start | bytes 589828
  6.6 14.1 %copy-start.4 = (bf16[192,512]{1,0:T(8,128)(2,1)S(1)}, bf16[192,512]{1,0:T(8,128)(2,1)}, u32[]{:S(2)}) copy-start(bf16[192,512]{1,0:T(8,128)(2,1)} %param.14) | copy-start | bytes 589828
  6.6 100.7 %all-to-all-start = ((bf16[8,2,128,1024]{3,2,1,0:T(8,128)(2,1)}), bf16[8,2,128,1024]{3,2,1,0:T(8,128)(2,1)}, u32[]{:S(2)}, u32[]{:S(2)}) async-start(bf16[8,2,128,1024]{3,2,1,0:T(8,128)(2,1)} %bitcast.31), calls=%async_computation | async-start | bytes 8388608 | tf_op jit(solution)/shard_map/all_to_all | solution.py:110
  113.4 1.2 copy-start.3
  113.4 1.2 copy-start.5
  120.5 1.8 %copy-start.2 = (bf16[512,2048]{1,0:T(8,128)(2,1)S(1)}, bf16[512,2048]{1,0:T(8,128)(2,1)}, u32[]{:S(2)}) copy-start(bf16[512,2048]{1,0:T(8,128)(2,1)} %param.18) | copy-start | bytes 6291460
  123.5 2.4 %collective-permute-start = (f32[192,1024]{1,0:T(8,128)S(1)}, f32[192,1024]{1,0:T(8,128)S(1)}, u32[]{:S(2)}, u32[]{:S(2)}) collective-permute-start(f32[192,1024]{1,0:T(8,128)S(1)} %pad_maximum_fusion.1), channel_id=1, source_target_pairs={{0,1},{1,0},{2,3},{3,2},{4,5},{5,4},{6,7},{7,6},{8,9},{9,8},{10,11... | collective-permute-start | bytes 2359304 | tf_op jit(solution)/shard_map/ppermute | solution.py:65
  125.8 7.3 %copy-start.6 = (bf16[192,512]{1,0:T(8,128)(2,1)S(1)}, bf16[192,512]{1,0:T(8,128)(2,1)}, u32[]{:S(2)}) copy-start(bf16[192,512]{1,0:T(8,128)(2,1)} %param.17) | copy-start | bytes 589828
  126.1 7.0 %collective-permute-start.1 = (bf16[192,512]{1,0:T(8,128)(2,1)S(1)}, bf16[192,512]{1,0:T(8,128)(2,1)S(1)}, u32[]{:S(2)}, u32[]{:S(2)}) collective-permute-start(bf16[192,512]{1,0:T(8,128)(2,1)S(1)} %get-tuple-element.15), channel_id=1, source_target_pairs={{0,2},{1,3},{2,0},{3,1},{4,6},{5,7},{6,4},{7,5},{8,10},{9,11},{10,... | collective-permute-start | bytes 589832 | tf_op jit(solution)/shard_map/ppermute | solution.py:65

commit v13 on v8

--- a/solution.py
+++ b/solution.py
@@ -1,6 +1,8 @@
 import jax
 import jax.numpy as jnp
 from jax import lax
+from jax.experimental import pallas as pl
+from jax.experimental.pallas import tpu as pltpu
 from jax.sharding import PartitionSpec as P
 
 HEAD_DIM = 128
@@ -44,6 +46,53 @@
         )
     return merged
 
+
+def upper_merge(queries, received, local_max, local_total, local_sum, lens, head_width):
+    rows, cols = queries.shape
+    srcs, _, chunk, _ = received.shape
+    heads = cols // head_width
+    keys = srcs * 2 * chunk
+    scale = head_width ** (-0.5)
+
+    def kernel(lens_ref, q_ref, k_ref, v_ref, m_ref, l_ref, o_ref, out_ref):
+        k = k_ref[...].reshape(keys, head_width)
+        v = v_ref[...].reshape(keys, head_width)
+        s = lax.dot_general(q_ref[...], k, (((1,), (1,)), ((), ())),
+                            preferred_element_type=jnp.float32) * scale
+        col = lax.broadcasted_iota(jnp.int32, (1, keys), 1)
+        src = col // (2 * chunk)
+        slot = (col // chunk) % 2
+        pos = src * chunk + col % chunk
+        allowed = pos < jnp.where(slot == 0, lens_ref[0], lens_ref[1])
+        s = jnp.where(allowed, s, NEG_FILL)
+        up_max = jnp.max(s, axis=1, keepdims=True)
+        p = jnp.where(allowed, jnp.exp(s - up_max), 0.0)
+        up_total = jnp.sum(p, axis=1, keepdims=True)
+        up_sum = jnp.dot(p.astype(jnp.bfloat16), v, preferred_element_type=jnp.float32)
+        lo_max = m_ref[0]
+        new_max = jnp.maximum(lo_max, up_max)
+        scale_a = jnp.exp(lo_max - new_max)
+        scale_b = jnp.exp(up_max - new_max)
+        total = l_ref[0] * scale_a + up_total * scale_b
+        out_ref[...] = (o_ref[...] * scale_a + up_sum * scale_b) / total
+
+    return pl.pallas_call(
+        kernel,
+        out_shape=jax.ShapeDtypeStruct((rows, cols), jnp.float32),
+        grid_spec=pltpu.PrefetchScalarGridSpec(
+            num_scalar_prefetch=1,
+            grid=(heads,),
+            in_specs=[
+                pl.BlockSpec((rows, head_width), lambda h, lens: (0, h)),
+                pl.BlockSpec((srcs, 2, chunk, head_width), lambda h, lens: (0, 0, 0, h)),
+                pl.BlockSpec((srcs, 2, chunk, head_width), lambda h, lens: (0, 1, 0, h)),
+                pl.BlockSpec((1, rows, 1), lambda h, lens: (h, 0, 0)),
+                pl.BlockSpec((1, rows, 1), lambda h, lens: (h, 0, 0)),
+                pl.BlockSpec((rows, head_width), lambda h, lens: (0, h)),
+            ],
+            out_specs=pl.BlockSpec((rows, head_width), lambda h, lens: (0, h)),
+        ),
+    )(lens, queries, received, received, local_max, local_total, local_sum)
 
 def project_over_grp(attention, w_out):
     size = lax.axis_size("grp")
@@ -110,8 +159,6 @@
         mode="promise_in_bounds"
     )
     received = lax.all_to_all(send, "tok", 0, 0, tiled=True)
-    recv_keys = received[:, :2]
-    recv_values = received[:, 2:]
 
     my_length = pick(req_len, my_index)
     my_mid = pick(leaf_mid, my_index)
@@ -136,21 +183,15 @@
         head_count,
     )
 
-    upper_pos = (
-        jnp.arange(dev_count, dtype=jnp.int32)[:, None, None] * chunk
-        + jnp.arange(chunk, dtype=jnp.int32)[None, None, :]
-    )
-    upper_limit = jnp.stack([root_len, mid_len])[None, :, None]
-    upper_ok = (upper_pos < upper_limit).reshape(-1)
-    upper_part = partial_attention(
+    attended = upper_merge(
         queries,
-        recv_keys.reshape(-1, col_count),
-        recv_values.reshape(-1, col_count),
-        upper_ok[None, :],
-        head_count,
-    )
-    merged = combine(local_part, upper_part)
-    attended = jnp.concatenate([part[2] / part[1] for part in merged], axis=1)
+        received,
+        jnp.stack([part[0] for part in local_part]),
+        jnp.stack([part[1] for part in local_part]),
+        jnp.concatenate([part[2] for part in local_part], axis=1),
+        jnp.stack([root_len, mid_len]).astype(jnp.int32),
+        col_count // head_count,
+    )
     attention = jnp.where(is_live[:, None], attended, 0.0).astype(jnp.bfloat16)
     mixed = project_over_grp(attention, w_out)
     return (residual.astype(jnp.float32) + mixed).astype(jnp.bfloat16)

time: 129 us -> 129 us (level)
  waiting for transfers between devices: 92.2 us -> 80 us
  Pallas kernels: 0 us -> 7.23 us
  other arithmetic: 12.6 us -> 19 us
  matrix products: 7.45 us -> 5.32 us
    all_to_all x1, waiting for transfers between devices: 84.5 us -> 73.3 us  [shards(): received = lax.all_to_all(send, 'tok', 0, 0, tiled=True)]
    pallas_call x0 -> x1, Pallas kernels: none -> 7.23 us  [upper_merge(): pl.pallas_call(kernel, out_shape=jax.ShapeDtypeStruct((rows, cols), jnp.f...]
    another operation x0 -> x8, local copies, waits for them, and re-layouts: none -> 3.58 us  [the longest x4 1.8 us: shards(): jnp.stack([part[0] for part in local_part])]
    another operation x1 -> x3, other arithmetic: 1.35 us -> 4.51 us  [the longest x1 1.94 us: shards(): jnp.stack([root_len, mid_len]).astype(jnp.int32)]
    slice x1 -> x0, local copies, waits for them, and re-layouts: 2.49 us -> none  [shards(): recv_values = received[:, 2:]]
    dot_general x8 -> x4, matrix products: 3.29 us -> 1.38 us  [partial_attention(): lax.dot_general(query_rows[:, cols], key_rows[:, cols], (((1,), (1,)), ((...]
    reduce_sum x3, other arithmetic: 3.1 us -> 4.7 us  [pick(): return jnp.sum(jnp.where(ids == index, table, 0))]
    dot_general x8 -> x4, matrix products: 3.06 us -> 2.08 us  [partial_attention(): jnp.dot(exp_scores.astype(jnp.bfloat16), values[:, cols], preferred_eleme...]
  transfers between devices with their start and end apart: 3 -> 3, of which waited for: 3 -> 3; matrix products, arithmetic and copies ran while one was open for 6% -> 15% of each run, Pallas kernels for 0% -> 0%
where the time goes in v13:
time: 129 us; the launch traced here: 128 us
  waiting for transfers between devices  80 us (62%)
  other arithmetic  19 us (15%)
  starting transfers between devices  9.05 us (7%)
  Pallas kernels  7.23 us (6%)
  local copies, waits for them, and re-layouts  6.59 us (5%)
  matrix products  5.32 us (4%)
    all_to_all x1, waiting for transfers between devices, shards(): received = lax.all_to_all(send, 'tok', 0, 0, tiled=True)  73.3 us
    all_to_all x1, starting transfers between devices, shards(): received = lax.all_to_all(send, 'tok', 0, 0, tiled=True)  7.4 us
    pallas_call x1, Pallas kernels, upper_merge(): pl.pallas_call(kernel, out_shape=jax.ShapeDtypeStruct((rows, cols), jnp.f...  7.23 us
    ppermute x2, waiting for transfers between devices, project_over_grp(): lax.ppermute(give, 'grp', [(g, g ^ step) for g in range(size)])  6.7 us
    reduce_sum x3, other arithmetic, pick(): return jnp.sum(jnp.where(ids == index, table, 0))  4.7 us
    gather x1, local copies, waits for them, and re-layouts, shards(): both.at[jnp.concatenate([dest_nodes, node_count + dest_nodes], axis=1)]  2.79 us
  transfers between devices with their start and end apart: 3, of which 3 were waited for; matrix products, arithmetic and copies ran while one was open for 15% of the time, Pallas kernels for 0%

profile of v13, /device:TPU:0, one launch (start us, length us, event | category | flops | bytes accessed | tf_op | source)
XLA Modules:
  0.0 128.1 jit_solution(6632120443796528038)
XLA Ops:
  0.0 0.8 select_reduce_fusion
  0.8 1.4 %add_bitcast_fusion.1 = (s32[8,1,1]{0,1,2:T(1,128)S(1)}, s32[8,1]{0,1:T(1,128)S(1)}, s32[]{:T(128)}, s32[]{:T(128)}) fusion(s32[8]{0:T(128)} %param.24, s32[]{:T(128)S(6)} %axis_index.25, s32[8]{0:T(128)} %param.27), kind=kLoop, calls=%fused_computation.106 | loop fusion | flops 46 | bytes 140 | tf_op jit(solution)/shard_map/concatenate | solution.py:158
  2.2 0.1 copy.44
  2.2 0.1 reshape.172
  2.3 1.5 %pad_maximum_fusion = bf16[12,128,512]{2,1,0:T(8,128)(2,1)S(1)} fusion(bf16[6,128,512]{2,1,0:T(8,128)(2,1)} %param.22, bf16[6,128,512]{2,1,0:T(8,128)(2,1)} %param.21), kind=kLoop, calls=%fused_computation.1 | loop fusion | flops 786432 | bytes 3145728 | tf_op jit(solution)/shard_map/concatenate | solution.py:157
  3.8 2.8 %gather_fusion = bf16[32,128,512]{2,1,0:T(8,128)(2,1)} fusion(bf16[12,128,512]{2,1,0:T(8,128)(2,1)S(1)} %pad_maximum_fusion, s32[1024]{0:T(1024)S(1)} %pad_clamp_fusion), kind=kCustom, calls=%fused_computation | custom fusion | bytes 8388736 | tf_op jit(solution)/shard_map/gather | solution.py:158
  6.6 7.4 %all-to-all-start = ((bf16[8,4,128,512]{3,2,1,0:T(8,128)(2,1)}), bf16[8,4,128,512]{3,2,1,0:T(8,128)(2,1)}, u32[]{:S(2)}, u32[]{:S(2)}) async-start(bf16[8,4,128,512]{3,2,1,0:T(8,128)(2,1)} %bitcast.47), calls=%async_computation | async-start | bytes 8388608 | tf_op jit(solution)/shard_map/all_to_all | solution.py:161
  14.0 0.6 iota_compare_fusion.1
  14.7 0.0 copy-done.11
  14.7 0.6 select_reduce_fusion.3
  15.3 0.6 iota_compare_fusion.3
  16.0 0.0 copy-start.9
  16.0 0.0 copy-done
  16.1 0.0 copy-done.1
  16.1 0.0 copy-done.3
  16.1 0.3 fusion.75
  16.4 0.1 copy.48
  16.6 0.4 fusion.76
  16.9 0.8 copy.47
  17.7 0.3 fusion.77
  18.0 0.0 copy-done.9
  18.0 0.8 copy.46
  18.8 0.3 fusion.78
  19.2 0.0 copy-start.5
  19.2 0.0 copy-start.6
  19.2 0.1 copy.45
  19.3 0.0 copy-start.4
  19.3 0.7 fusion.17
  20.1 0.1 copy.52
  20.2 0.1 copy.51
  20.3 0.8 copy.50
  21.1 0.8 copy.49
  22.5 0.0 copy-start.8
  22.5 2.0 %fusion.60 = s32[]{:T(128)} fusion(s32[4]{0:T(128)} %param.25, s32[]{:T(128)} %get-tuple-element.16), kind=kLoop, calls=%fused_computation.97 | loop fusion | flops 11 | bytes 24 | tf_op jit(solution)/shard_map/reduce_sum | solution.py:122
  24.6 2.0 %fusion.61 = (s32[]{:T(128)}, s32[]{:T(128)}) fusion(s32[6]{0:T(128)} %param.26, s32[]{:T(128)} %fusion.60, s32[]{:T(128)S(6)} %add.46), kind=kLoop, calls=%fused_computation.98 | loop fusion | flops 34 | bytes 40 | tf_op jit(solution)/shard_map/reduce_sum | solution.py:122
  26.6 1.9 %pad_add_fusion.1.lens_ref = s32[2]{0:T(128)} fusion(s32[1]{0:T(128)} %bitcast.1, s32[1]{0:T(128)} %bitcast), kind=kLoop, calls=%fused_computation.100 | loop fusion | flops 2 | bytes 16 | tf_op jit(solution)/shard_map/stack | solution.py:192
  28.5 0.0 copy-done.5
  28.5 0.0 copy-done.6
  28.5 0.8 pad_maximum_fusion.2.m_ref
  29.4 1.7 %pad_maximum_fusion.3.l_ref = f32[4,192,1]{2,1,0:T(8,128)} fusion(f32[1,192,1]{2,1,0:T(8,128)S(1)} %copy.52, f32[1,192,1]{2,1,0:T(8,128)S(1)} %copy.51, f32[1,192,1]{2,1,0:T(8,128)} %copy.50, f32[1,192,1]{2,1,0:T(8,128)} %copy.49), kind=kLoop, calls=%fused_computation.51 | loop fusion | flops 2304 | bytes 6144 | tf_op jit(solution)/shard_map/stack | solution.py:190
  31.1 0.0 copy-done.4
  31.1 1.1 fusion.24
  32.2 0.0 copy-done.8
  32.2 0.3 fusion.26
  32.6 0.3 fusion.28
  32.9 0.3 fusion.30
  33.2 0.8 pad_maximum_fusion.4.o_ref
  34.0 73.3 %all-to-all-done.k_ref.v_ref = bf16[8,4,128,512]{3,2,1,0:T(8,128)(2,1)} async-done(((bf16[8,4,128,512]{3,2,1,0:T(8,128)(2,1)}), bf16[8,4,128,512]{3,2,1,0:T(8,128)(2,1)}, u32[]{:S(2)}, u32[]{:S(2)}) %all-to-all-start) | async-done | bytes 4194336 | tf_op jit(solution)/shard_map/all_to_all | solution.py:161
  107.3 7.2 %shard_map.136 = f32[192,512]{1,0:T(8,128)} custom-call(s32[2]{0:T(128)} %pad_add_fusion.1.lens_ref, bf16[192,512]{1,0:T(8,128)(2,1)} %q_ref.1, bf16[8,4,128,512]{3,2,1,0:T(8,128)(2,1)} %all-to-all-done.k_ref.v_ref, bf16[8,4,128,512]{3,2,1,0:T(8,128)(2,1)} %all-to-all-done.k_ref.v_ref, f32[4,192,1]{2,1,0:T(8,128)} %pad_maximum_fusion.2.m_ref, ...), custom_call_target="tpu_custom_call" | custom-call | tf_op jit(solution)/shard_map/pallas_call | solution.py:79
  114.5 0.0 copy-done.10
  114.6 1.1 select_convert_fusion.1
  115.6 0.0 copy-done.2
  115.7 0.3 fusion.14
  115.9 0.3 fusion.8
  116.2 0.3 broadcast_select_fusion
  116.5 1.0 broadcast_select_fusion.1
  117.5 0.1 pad_maximum_fusion.1
  117.6 0.1 collective-permute-start
  117.7 2.3 %collective-permute-done = f32[192,1024]{1,0:T(8,128)S(1)} collective-permute-done((f32[192,1024]{1,0:T(8,128)S(1)}, f32[192,1024]{1,0:T(8,128)S(1)}, u32[]{:S(2)}, u32[]{:S(2)}) %collective-permute-start) | collective-permute-done | bytes 786464 | tf_op jit(solution)/shard_map/ppermute | solution.py:114
  120.0 1.3 select_convert_fusion
  121.2 1.6 %collective-permute-start.1 = (bf16[192,512]{1,0:T(8,128)(2,1)S(1)}, bf16[192,512]{1,0:T(8,128)(2,1)S(1)}, u32[]{:S(2)}, u32[]{:S(2)}) collective-permute-start(bf16[192,512]{1,0:T(8,128)(2,1)S(1)} %get-tuple-element.11), channel_id=1, source_target_pairs={{0,2},{1,3},{2,0},{3,1},{4,6},{5,7},{6,4},{7,5},{8,10},{9,11},{10,... | collective-permute-start | bytes 589832 | tf_op jit(solution)/shard_map/ppermute | solution.py:114
  122.8 4.4 %collective-permute-done.1 = bf16[192,512]{1,0:T(8,128)(2,1)S(1)} collective-permute-done((bf16[192,512]{1,0:T(8,128)(2,1)S(1)}, bf16[192,512]{1,0:T(8,128)(2,1)S(1)}, u32[]{:S(2)}, u32[]{:S(2)}) %collective-permute-start.1) | collective-permute-done | bytes 196640 | tf_op jit(solution)/shard_map/ppermute | solution.py:114
  127.2 0.0 copy-done.7
  127.2 0.8 add_convert_fusion
  (12 shorter events, 0.1 us)
Async XLA Ops:
  6.6 8.1 %copy-start.11 = (s32[8]{0:T(128)S(1)}, s32[8]{0:T(128)}, u32[]{:S(2)}) copy-start(s32[8]{0:T(128)} %param.23) | copy-start | bytes 100
  6.6 9.4 %copy-start = (bf16[1,512,512]{2,1,0:T(8,128)(2,1)S(1)}, bf16[1,512,512]{2,1,0:T(8,128)(2,1)}, u32[]{:S(2)}) copy-start(bf16[1,512,512]{2,1,0:T(8,128)(2,1)} %param.19) | copy-start | bytes 1572868
  6.6 9.4 %copy-start.1 = (bf16[192,512]{1,0:T(8,128)(2,1)S(1)}, bf16[192,512]{1,0:T(8,128)(2,1)}, u32[]{:S(2)}) copy-start(bf16[192,512]{1,0:T(8,128)(2,1)} %param.15) | copy-start | bytes 589828
  6.6 9.4 %copy-start.3 = (bf16[192,512]{1,0:T(8,128)(2,1)S(1)}, bf16[192,512]{1,0:T(8,128)(2,1)}, u32[]{:S(2)}) copy-start(bf16[192,512]{1,0:T(8,128)(2,1)} %q_ref.1) | copy-start | bytes 589828
  6.6 100.7 %all-to-all-start = ((bf16[8,4,128,512]{3,2,1,0:T(8,128)(2,1)}), bf16[8,4,128,512]{3,2,1,0:T(8,128)(2,1)}, u32[]{:S(2)}, u32[]{:S(2)}) async-start(bf16[8,4,128,512]{3,2,1,0:T(8,128)(2,1)} %bitcast.47), calls=%async_computation | async-start | bytes 8388608 | tf_op jit(solution)/shard_map/all_to_all | solution.py:161
  16.0 2.0 %copy-start.9 = (pred[192]{0:T(512)(128)(4,1)}, pred[192]{0:T(512)(128)(4,1)S(1)}, u32[]{:S(2)}) copy-start(pred[192]{0:T(512)(128)(4,1)S(1)} %iota_compare_fusion.3) | copy-start | bytes 580
  19.2 9.4 %copy-start.5 = (f32[1,192,1]{2,1,0:T(8,128)S(1)}, f32[1,192,1]{2,1,0:T(8,128)}, u32[]{:S(2)}) copy-start(f32[1,192,1]{2,1,0:T(8,128)} %copy.47) | copy-start | bytes 2308
  19.2 9.4 %copy-start.6 = (f32[1,192,1]{2,1,0:T(8,128)S(1)}, f32[1,192,1]{2,1,0:T(8,128)}, u32[]{:S(2)}) copy-start(f32[1,192,1]{2,1,0:T(8,128)} %copy.46) | copy-start | bytes 2308
  19.3 11.8 %copy-start.4 = (bf16[1,512,512]{2,1,0:T(8,128)(2,1)S(1)}, bf16[1,512,512]{2,1,0:T(8,128)(2,1)}, u32[]{:S(2)}) copy-start(bf16[1,512,512]{2,1,0:T(8,128)(2,1)} %param.20) | copy-start | bytes 1572868
  22.5 9.7 %copy-start.8 = (bf16[192,512]{1,0:T(8,128)(2,1)S(1)}, bf16[192,512]{1,0:T(8,128)(2,1)}, u32[]{:S(2)}) copy-start(bf16[192,512]{1,0:T(8,128)(2,1)} %param.16) | copy-start | bytes 589828
  34.0 80.5 %copy-start.10 = (pred[192]{0:T(512)(128)(4,1)S(1)}, pred[192]{0:T(512)(128)(4,1)}, u32[]{:S(2)}) copy-start(pred[192]{0:T(512)(128)(4,1)} %copy-done.9) | copy-start | bytes 580
  34.0 81.6 %copy-start.2 = (bf16[512,2048]{1,0:T(8,128)(2,1)S(1)}, bf16[512,2048]{1,0:T(8,128)(2,1)}, u32[]{:S(2)}) copy-start(bf16[512,2048]{1,0:T(8,128)(2,1)} %param.18) | copy-start | bytes 6291460
  117.5 9.7 %copy-start.7 = (bf16[192,512]{1,0:T(8,128)(2,1)S(1)}, bf16[192,512]{1,0:T(8,128)(2,1)}, u32[]{:S(2)}) copy-start(bf16[192,512]{1,0:T(8,128)(2,1)} %param.17) | copy-start | bytes 589828
  117.6 2.4 %collective-permute-start = (f32[192,1024]{1,0:T(8,128)S(1)}, f32[192,1024]{1,0:T(8,128)S(1)}, u32[]{:S(2)}, u32[]{:S(2)}) collective-permute-start(f32[192,1024]{1,0:T(8,128)S(1)} %pad_maximum_fusion.1), channel_id=1, source_target_pairs={{0,1},{1,0},{2,3},{3,2},{4,5},{5,4},{6,7},{7,6},{8,9},{9,8},{10,11... | collective-permute-start | bytes 2359304 | tf_op jit(solution)/shard_map/ppermute | solution.py:114
  121.2 6.0 %collective-permute-start.1 = (bf16[192,512]{1,0:T(8,128)(2,1)S(1)}, bf16[192,512]{1,0:T(8,128)(2,1)S(1)}, u32[]{:S(2)}, u32[]{:S(2)}) collective-permute-start(bf16[192,512]{1,0:T(8,128)(2,1)S(1)} %get-tuple-element.11), channel_id=1, source_target_pairs={{0,2},{1,3},{2,0},{3,1},{4,6},{5,7},{6,4},{7,5},{8,10},{9,11},{10,... | collective-permute-start | bytes 589832 | tf_op jit(solution)/shard_map/ppermute | solution.py:114

commit v14 on v13

--- a/solution.py
+++ b/solution.py
@@ -54,45 +54,47 @@
     keys = srcs * 2 * chunk
     scale = head_width ** (-0.5)
 
-    def kernel(lens_ref, q_ref, k_ref, v_ref, m_ref, l_ref, o_ref, out_ref):
-        k = k_ref[...].reshape(keys, head_width)
-        v = v_ref[...].reshape(keys, head_width)
-        s = lax.dot_general(q_ref[...], k, (((1,), (1,)), ((), ())),
-                            preferred_element_type=jnp.float32) * scale
+    def kernel(lens_ref, q_ref, r_ref, m_ref, l_ref, o_ref, out_ref):
         col = lax.broadcasted_iota(jnp.int32, (1, keys), 1)
         src = col // (2 * chunk)
         slot = (col // chunk) % 2
         pos = src * chunk + col % chunk
         allowed = pos < jnp.where(slot == 0, lens_ref[0], lens_ref[1])
-        s = jnp.where(allowed, s, NEG_FILL)
-        up_max = jnp.max(s, axis=1, keepdims=True)
-        p = jnp.where(allowed, jnp.exp(s - up_max), 0.0)
-        up_total = jnp.sum(p, axis=1, keepdims=True)
-        up_sum = jnp.dot(p.astype(jnp.bfloat16), v, preferred_element_type=jnp.float32)
-        lo_max = m_ref[0]
-        new_max = jnp.maximum(lo_max, up_max)
-        scale_a = jnp.exp(lo_max - new_max)
-        scale_b = jnp.exp(up_max - new_max)
-        total = l_ref[0] * scale_a + up_total * scale_b
-        out_ref[...] = (o_ref[...] * scale_a + up_sum * scale_b) / total
+        for head in range(heads):
+            cols_h = slice(head * head_width, (head + 1) * head_width)
+            k = r_ref[:, 0:2, :, cols_h].reshape(keys, head_width)
+            v = r_ref[:, 2:4, :, cols_h].reshape(keys, head_width)
+            s = lax.dot_general(q_ref[:, cols_h], k, (((1,), (1,)), ((), ())),
+                                preferred_element_type=jnp.float32) * scale
+            s = jnp.where(allowed, s, NEG_FILL)
+            up_max = jnp.max(s, axis=1, keepdims=True)
+            p = jnp.where(allowed, jnp.exp(s - up_max), 0.0)
+            up_total = jnp.sum(p, axis=1, keepdims=True)
+            up_sum = jnp.dot(p.astype(jnp.bfloat16), v, preferred_element_type=jnp.float32)
+            lo_max = m_ref[head]
+            new_max = jnp.maximum(lo_max, up_max)
+            scale_a = jnp.exp(lo_max - new_max)
+            scale_b = jnp.exp(up_max - new_max)
+            total = l_ref[head] * scale_a + up_total * scale_b
+            out_ref[:, cols_h] = (o_ref[:, cols_h] * scale_a + up_sum * scale_b) / total
 
     return pl.pallas_call(
         kernel,
         out_shape=jax.ShapeDtypeStruct((rows, cols), jnp.float32),
         grid_spec=pltpu.PrefetchScalarGridSpec(
             num_scalar_prefetch=1,
-            grid=(heads,),
+            grid=(1,),
             in_specs=[
-                pl.BlockSpec((rows, head_width), lambda h, lens: (0, h)),
-                pl.BlockSpec((srcs, 2, chunk, head_width), lambda h, lens: (0, 0, 0, h)),
-                pl.BlockSpec((srcs, 2, chunk, head_width), lambda h, lens: (0, 1, 0, h)),
-                pl.BlockSpec((1, rows, 1), lambda h, lens: (h, 0, 0)),
-                pl.BlockSpec((1, rows, 1), lambda h, lens: (h, 0, 0)),
-                pl.BlockSpec((rows, head_width), lambda h, lens: (0, h)),
+                pl.BlockSpec((rows, cols), lambda i, lens: (0, 0)),
+                pl.BlockSpec(received.shape, lambda i, lens: (0, 0, 0, 0)),
+                pl.BlockSpec(local_max.shape, lambda i, lens: (0, 0, 0)),
+                pl.BlockSpec(local_total.shape, lambda i, lens: (0, 0, 0)),
+                pl.BlockSpec((rows, cols), lambda i, lens: (0, 0)),
             ],
-            out_specs=pl.BlockSpec((rows, head_width), lambda h, lens: (0, h)),
+            out_specs=pl.BlockSpec((rows, cols), lambda i, lens: (0, 0)),
         ),
-    )(lens, queries, received, received, local_max, local_total, local_sum)
+    )(lens, queries, received, local_max, local_total, local_sum)
+
 
 def project_over_grp(attention, w_out):
     size = lax.axis_size("grp")

time: 129 us -> 129 us (level)
  no operation moved by 1% of the time
where the time goes in v14:
time: 129 us; the launch traced here: 128 us
  waiting for transfers between devices  80 us (62%)
  other arithmetic  19 us (15%)
  starting transfers between devices  9.05 us (7%)
  Pallas kernels  7.2 us (6%)
  local copies, waits for them, and re-layouts  6.59 us (5%)
  matrix products  5.32 us (4%)
    all_to_all x1, waiting for transfers between devices, shards(): received = lax.all_to_all(send, 'tok', 0, 0, tiled=True)  73.3 us
    all_to_all x1, starting transfers between devices, shards(): received = lax.all_to_all(send, 'tok', 0, 0, tiled=True)  7.4 us
    pallas_call x1, Pallas kernels, upper_merge(): pl.pallas_call(kernel, out_shape=jax.ShapeDtypeStruct((rows, cols), jnp.f...  7.2 us
    ppermute x2, waiting for transfers between devices, project_over_grp(): lax.ppermute(give, 'grp', [(g, g ^ step) for g in range(size)])  6.7 us
    reduce_sum x3, other arithmetic, pick(): return jnp.sum(jnp.where(ids == index, table, 0))  4.7 us
    gather x1, local copies, waits for them, and re-layouts, shards(): both.at[jnp.concatenate([dest_nodes, node_count + dest_nodes], axis=1)]  2.79 us
  transfers between devices with their start and end apart: 3, of which 3 were waited for; matrix products, arithmetic and copies ran while one was open for 15% of the time, Pallas kernels for 0%

profile of v14, /device:TPU:0, one launch (start us, length us, event | category | flops | bytes accessed | tf_op | source)
XLA Modules:
  0.0 128.0 jit_solution(7234555456981540630)
XLA Ops:
  0.0 0.8 select_reduce_fusion
  0.8 1.4 %add_bitcast_fusion.1 = (s32[8,1,1]{0,1,2:T(1,128)S(1)}, s32[8,1]{0,1:T(1,128)S(1)}, s32[]{:T(128)}, s32[]{:T(128)}) fusion(s32[8]{0:T(128)} %param.24, s32[]{:T(128)S(6)} %axis_index.25, s32[8]{0:T(128)} %param.27), kind=kLoop, calls=%fused_computation.106 | loop fusion | flops 46 | bytes 140 | tf_op jit(solution)/shard_map/concatenate | solution.py:160
  2.2 0.1 copy.44
  2.2 0.1 reshape.172
  2.3 1.5 %pad_maximum_fusion = bf16[12,128,512]{2,1,0:T(8,128)(2,1)S(1)} fusion(bf16[6,128,512]{2,1,0:T(8,128)(2,1)} %param.22, bf16[6,128,512]{2,1,0:T(8,128)(2,1)} %param.21), kind=kLoop, calls=%fused_computation.1 | loop fusion | flops 786432 | bytes 3145728 | tf_op jit(solution)/shard_map/concatenate | solution.py:159
  3.8 2.8 %gather_fusion = bf16[32,128,512]{2,1,0:T(8,128)(2,1)} fusion(bf16[12,128,512]{2,1,0:T(8,128)(2,1)S(1)} %pad_maximum_fusion, s32[1024]{0:T(1024)S(1)} %pad_clamp_fusion), kind=kCustom, calls=%fused_computation | custom fusion | bytes 8388736 | tf_op jit(solution)/shard_map/gather | solution.py:160
  6.6 7.4 %all-to-all-start = ((bf16[8,4,128,512]{3,2,1,0:T(8,128)(2,1)}), bf16[8,4,128,512]{3,2,1,0:T(8,128)(2,1)}, u32[]{:S(2)}, u32[]{:S(2)}) async-start(bf16[8,4,128,512]{3,2,1,0:T(8,128)(2,1)} %bitcast.47), calls=%async_computation | async-start | bytes 8388608 | tf_op jit(solution)/shard_map/all_to_all | solution.py:163
  14.0 0.6 iota_compare_fusion.1
  14.7 0.0 copy-done.11
  14.7 0.6 select_reduce_fusion.3
  15.3 0.6 iota_compare_fusion.3
  16.0 0.0 copy-start.9
  16.0 0.0 copy-done
  16.1 0.0 copy-done.1
  16.1 0.0 copy-done.3
  16.1 0.3 fusion.75
  16.4 0.1 copy.48
  16.6 0.4 fusion.76
  16.9 0.8 copy.47
  17.7 0.3 fusion.77
  18.0 0.0 copy-done.9
  18.0 0.8 copy.46
  18.8 0.3 fusion.78
  19.2 0.0 copy-start.5
  19.2 0.0 copy-start.6
  19.2 0.1 copy.45
  19.3 0.0 copy-start.4
  19.3 0.7 fusion.17
  20.1 0.1 copy.52
  20.2 0.1 copy.51
  20.3 0.8 copy.50
  21.1 0.8 copy.49
  22.5 0.0 copy-start.8
  22.5 2.0 %fusion.60 = s32[]{:T(128)} fusion(s32[4]{0:T(128)} %param.25, s32[]{:T(128)} %get-tuple-element.16), kind=kLoop, calls=%fused_computation.97 | loop fusion | flops 11 | bytes 24 | tf_op jit(solution)/shard_map/reduce_sum | solution.py:124
  24.6 2.0 %fusion.61 = (s32[]{:T(128)}, s32[]{:T(128)}) fusion(s32[6]{0:T(128)} %param.26, s32[]{:T(128)} %fusion.60, s32[]{:T(128)S(6)} %add.46), kind=kLoop, calls=%fused_computation.98 | loop fusion | flops 34 | bytes 40 | tf_op jit(solution)/shard_map/reduce_sum | solution.py:124
  26.6 1.9 %pad_add_fusion.1.lens_ref = s32[2]{0:T(128)} fusion(s32[1]{0:T(128)} %bitcast.1, s32[1]{0:T(128)} %bitcast), kind=kLoop, calls=%fused_computation.100 | loop fusion | flops 2 | bytes 16 | tf_op jit(solution)/shard_map/stack | solution.py:194
  28.5 0.0 copy-done.5
  28.5 0.0 copy-done.6
  28.5 0.8 pad_maximum_fusion.2.m_ref
  29.4 1.7 %pad_maximum_fusion.3.l_ref = f32[4,192,1]{2,1,0:T(8,128)} fusion(f32[1,192,1]{2,1,0:T(8,128)S(1)} %copy.52, f32[1,192,1]{2,1,0:T(8,128)S(1)} %copy.51, f32[1,192,1]{2,1,0:T(8,128)} %copy.50, f32[1,192,1]{2,1,0:T(8,128)} %copy.49), kind=kLoop, calls=%fused_computation.51 | loop fusion | flops 2304 | bytes 6144 | tf_op jit(solution)/shard_map/stack | solution.py:192
  31.1 0.0 copy-done.4
  31.1 1.1 fusion.24
  32.2 0.0 copy-done.8
  32.2 0.3 fusion.26
  32.6 0.3 fusion.28
  32.9 0.3 fusion.30
  33.2 0.8 pad_maximum_fusion.4.o_ref
  34.0 73.3 %all-to-all-done.r_ref = bf16[8,4,128,512]{3,2,1,0:T(8,128)(2,1)} async-done(((bf16[8,4,128,512]{3,2,1,0:T(8,128)(2,1)}), bf16[8,4,128,512]{3,2,1,0:T(8,128)(2,1)}, u32[]{:S(2)}, u32[]{:S(2)}) %all-to-all-start) | async-done | bytes 4194336 | tf_op jit(solution)/shard_map/all_to_all | solution.py:163
  107.3 7.2 %shard_map.136 = f32[192,512]{1,0:T(8,128)} custom-call(s32[2]{0:T(128)} %pad_add_fusion.1.lens_ref, bf16[192,512]{1,0:T(8,128)(2,1)} %q_ref.1, bf16[8,4,128,512]{3,2,1,0:T(8,128)(2,1)} %all-to-all-done.r_ref, f32[4,192,1]{2,1,0:T(8,128)} %pad_maximum_fusion.2.m_ref, f32[4,192,1]{2,1,0:T(8,128)} %pad_maximum_fusion.3.l_ref, f32[192,512]{1,0:T(8,128)} %pad_maximum_fusion.4.o_ref), custom_call_target="tpu_custom_call" | custom-call | tf_op jit(solution)/shard_map/pallas_call | solution.py:81
  114.5 0.0 copy-done.10
  114.5 1.1 select_convert_fusion.1
  115.6 0.0 copy-done.2
  115.6 0.3 fusion.14
  115.9 0.3 fusion.8
  116.2 0.3 broadcast_select_fusion
  116.5 1.0 broadcast_select_fusion.1
  117.5 0.1 pad_maximum_fusion.1
  117.6 0.1 collective-permute-start
  117.7 2.3 %collective-permute-done = f32[192,1024]{1,0:T(8,128)S(1)} collective-permute-done((f32[192,1024]{1,0:T(8,128)S(1)}, f32[192,1024]{1,0:T(8,128)S(1)}, u32[]{:S(2)}, u32[]{:S(2)}) %collective-permute-start) | collective-permute-done | bytes 786464 | tf_op jit(solution)/shard_map/ppermute | solution.py:116
  119.9 1.3 select_convert_fusion
  121.2 1.6 %collective-permute-start.1 = (bf16[192,512]{1,0:T(8,128)(2,1)S(1)}, bf16[192,512]{1,0:T(8,128)(2,1)S(1)}, u32[]{:S(2)}, u32[]{:S(2)}) collective-permute-start(bf16[192,512]{1,0:T(8,128)(2,1)S(1)} %get-tuple-element.11), channel_id=1, source_target_pairs={{0,2},{1,3},{2,0},{3,1},{4,6},{5,7},{6,4},{7,5},{8,10},{9,11},{10,... | collective-permute-start | bytes 589832 | tf_op jit(solution)/shard_map/ppermute | solution.py:116
  122.8 4.4 %collective-permute-done.1 = bf16[192,512]{1,0:T(8,128)(2,1)S(1)} collective-permute-done((bf16[192,512]{1,0:T(8,128)(2,1)S(1)}, bf16[192,512]{1,0:T(8,128)(2,1)S(1)}, u32[]{:S(2)}, u32[]{:S(2)}) %collective-permute-start.1) | collective-permute-done | bytes 196640 | tf_op jit(solution)/shard_map/ppermute | solution.py:116
  127.2 0.0 copy-done.7
  127.2 0.8 add_convert_fusion
  (12 shorter events, 0.1 us)
Async XLA Ops:
  6.6 8.1 %copy-start.11 = (s32[8]{0:T(128)S(1)}, s32[8]{0:T(128)}, u32[]{:S(2)}) copy-start(s32[8]{0:T(128)} %param.23) | copy-start | bytes 100
  6.6 9.4 %copy-start = (bf16[1,512,512]{2,1,0:T(8,128)(2,1)S(1)}, bf16[1,512,512]{2,1,0:T(8,128)(2,1)}, u32[]{:S(2)}) copy-start(bf16[1,512,512]{2,1,0:T(8,128)(2,1)} %param.19) | copy-start | bytes 1572868
  6.6 9.4 %copy-start.1 = (bf16[192,512]{1,0:T(8,128)(2,1)S(1)}, bf16[192,512]{1,0:T(8,128)(2,1)}, u32[]{:S(2)}) copy-start(bf16[192,512]{1,0:T(8,128)(2,1)} %param.15) | copy-start | bytes 589828
  6.6 9.4 %copy-start.3 = (bf16[192,512]{1,0:T(8,128)(2,1)S(1)}, bf16[192,512]{1,0:T(8,128)(2,1)}, u32[]{:S(2)}) copy-start(bf16[192,512]{1,0:T(8,128)(2,1)} %q_ref.1) | copy-start | bytes 589828
  6.6 100.7 %all-to-all-start = ((bf16[8,4,128,512]{3,2,1,0:T(8,128)(2,1)}), bf16[8,4,128,512]{3,2,1,0:T(8,128)(2,1)}, u32[]{:S(2)}, u32[]{:S(2)}) async-start(bf16[8,4,128,512]{3,2,1,0:T(8,128)(2,1)} %bitcast.47), calls=%async_computation | async-start | bytes 8388608 | tf_op jit(solution)/shard_map/all_to_all | solution.py:163
  16.0 2.0 %copy-start.9 = (pred[192]{0:T(512)(128)(4,1)}, pred[192]{0:T(512)(128)(4,1)S(1)}, u32[]{:S(2)}) copy-start(pred[192]{0:T(512)(128)(4,1)S(1)} %iota_compare_fusion.3) | copy-start | bytes 580
  19.2 9.4 %copy-start.5 = (f32[1,192,1]{2,1,0:T(8,128)S(1)}, f32[1,192,1]{2,1,0:T(8,128)}, u32[]{:S(2)}) copy-start(f32[1,192,1]{2,1,0:T(8,128)} %copy.47) | copy-start | bytes 2308
  19.2 9.4 %copy-start.6 = (f32[1,192,1]{2,1,0:T(8,128)S(1)}, f32[1,192,1]{2,1,0:T(8,128)}, u32[]{:S(2)}) copy-start(f32[1,192,1]{2,1,0:T(8,128)} %copy.46) | copy-start | bytes 2308
  19.3 11.8 %copy-start.4 = (bf16[1,512,512]{2,1,0:T(8,128)(2,1)S(1)}, bf16[1,512,512]{2,1,0:T(8,128)(2,1)}, u32[]{:S(2)}) copy-start(bf16[1,512,512]{2,1,0:T(8,128)(2,1)} %param.20) | copy-start | bytes 1572868
  22.5 9.7 %copy-start.8 = (bf16[192,512]{1,0:T(8,128)(2,1)S(1)}, bf16[192,512]{1,0:T(8,128)(2,1)}, u32[]{:S(2)}) copy-start(bf16[192,512]{1,0:T(8,128)(2,1)} %param.16) | copy-start | bytes 589828
  34.0 80.5 %copy-start.10 = (pred[192]{0:T(512)(128)(4,1)S(1)}, pred[192]{0:T(512)(128)(4,1)}, u32[]{:S(2)}) copy-start(pred[192]{0:T(512)(128)(4,1)} %copy-done.9) | copy-start | bytes 580
  34.0 81.6 %copy-start.2 = (bf16[512,2048]{1,0:T(8,128)(2,1)S(1)}, bf16[512,2048]{1,0:T(8,128)(2,1)}, u32[]{:S(2)}) copy-start(bf16[512,2048]{1,0:T(8,128)(2,1)} %param.18) | copy-start | bytes 6291460
  117.5 9.7 %copy-start.7 = (bf16[192,512]{1,0:T(8,128)(2,1)S(1)}, bf16[192,512]{1,0:T(8,128)(2,1)}, u32[]{:S(2)}) copy-start(bf16[192,512]{1,0:T(8,128)(2,1)} %param.17) | copy-start | bytes 589828
  117.6 2.4 %collective-permute-start = (f32[192,1024]{1,0:T(8,128)S(1)}, f32[192,1024]{1,0:T(8,128)S(1)}, u32[]{:S(2)}, u32[]{:S(2)}) collective-permute-start(f32[192,1024]{1,0:T(8,128)S(1)} %pad_maximum_fusion.1), channel_id=1, source_target_pairs={{0,1},{1,0},{2,3},{3,2},{4,5},{5,4},{6,7},{7,6},{8,9},{9,8},{10,11... | collective-permute-start | bytes 2359304 | tf_op jit(solution)/shard_map/ppermute | solution.py:116
  121.2 6.0 %collective-permute-start.1 = (bf16[192,512]{1,0:T(8,128)(2,1)S(1)}, bf16[192,512]{1,0:T(8,128)(2,1)S(1)}, u32[]{:S(2)}, u32[]{:S(2)}) collective-permute-start(bf16[192,512]{1,0:T(8,128)(2,1)S(1)} %get-tuple-element.11), channel_id=1, source_target_pairs={{0,2},{1,3},{2,0},{3,1},{4,6},{5,7},{6,4},{7,5},{8,10},{9,11},{10,... | collective-permute-start | bytes 589832 | tf_op jit(solution)/shard_map/ppermute | solution.py:116

commit v15 on v8

--- a/solution.py
+++ b/solution.py
@@ -60,8 +60,7 @@
         give = jnp.concatenate(
             [jnp.where(high, kept[k], kept[k + 1]) for k in range(0, len(kept), 2)], axis=1
         )
-        if step * 2 == size:
-            give = give.astype(jnp.bfloat16)
+        give = give.astype(jnp.bfloat16)
         moved = lax.ppermute(give, "grp", [(g, g ^ step) for g in range(size)]).astype(jnp.float32)
         kept = [part + moved[:, k * block : (k + 1) * block] for k, part in enumerate(keep)]
         step *= 2

time: 129 us -> 129 us (level)
  no operation moved by 1% of the time
where the time goes in v15:
time: 129 us; the launch traced here: 128 us
  waiting for transfers between devices  91.6 us (71%)
  other arithmetic  12.7 us (10%)
  starting transfers between devices  9.06 us (7%)
  matrix products  7.45 us (6%)
  local copies, waits for them, and re-layouts  6.56 us (5%)
    all_to_all x1, waiting for transfers between devices, shards(): received = lax.all_to_all(send, 'tok', 0, 0, tiled=True)  84.5 us
    all_to_all x1, starting transfers between devices, shards(): received = lax.all_to_all(send, 'tok', 0, 0, tiled=True)  7.4 us
    ppermute x2, waiting for transfers between devices, project_over_grp(): lax.ppermute(give, 'grp', [(g, g ^ step) for g in range(size)])  7.12 us
    dot_general x8, matrix products, partial_attention(): lax.dot_general(query_rows[:, cols], key_rows[:, cols], (((1,), (1,)), ((...  3.29 us
    reduce_sum x3, other arithmetic, pick(): return jnp.sum(jnp.where(ids == index, table, 0))  3.1 us
    dot_general x8, matrix products, partial_attention(): jnp.dot(exp_scores.astype(jnp.bfloat16), values[:, cols], preferred_eleme...  3.06 us
    gather x1, local copies, waits for them, and re-layouts, shards(): both.at[jnp.concatenate([dest_nodes, node_count + dest_nodes], axis=1)]  2.79 us
  transfers between devices with their start and end apart: 3, of which 3 were waited for; matrix products, arithmetic and copies ran while one was open for 6% of the time, Pallas kernels for 0%

profile of v15, /device:TPU:0, one launch (start us, length us, event | category | flops | bytes accessed | tf_op | source)
XLA Modules:
  0.0 128.4 jit_solution(11015355195976672580)
XLA Ops:
  0.0 1.3 %add_bitcast_fusion.1 = (s32[8,1,1]{0,1,2:T(1,128)S(1)}, s32[8,1]{0,1:T(1,128)S(1)}, s32[]{:T(128)}) fusion(s32[8]{0:T(128)} %param.24, s32[]{:T(128)S(6)} %axis_index.25), kind=kLoop, calls=%fused_computation.183 | loop fusion | flops 31 | bytes 104 | tf_op jit(solution)/shard_map/concatenate | solution.py:108
  1.3 0.8 select_reduce_fusion
  2.1 0.1 copy.23
  2.2 0.1 reshape.354
  2.3 1.5 %pad_maximum_fusion = bf16[12,128,512]{2,1,0:T(8,128)(2,1)S(1)} fusion(bf16[6,128,512]{2,1,0:T(8,128)(2,1)} %param.22, bf16[6,128,512]{2,1,0:T(8,128)(2,1)} %param.21), kind=kLoop, calls=%fused_computation.9 | loop fusion | flops 786432 | bytes 3145728 | tf_op jit(solution)/shard_map/concatenate | solution.py:107
  3.8 2.8 %gather_fusion = bf16[32,128,512]{2,1,0:T(8,128)(2,1)} fusion(bf16[12,128,512]{2,1,0:T(8,128)(2,1)S(1)} %pad_maximum_fusion, s32[1024]{0:T(1024)S(1)} %pad_clamp_fusion), kind=kCustom, calls=%fused_computation | custom fusion | bytes 8388736 | tf_op jit(solution)/shard_map/gather | solution.py:108
  6.6 0.0 copy-start
  6.6 0.0 copy-start.1
  6.6 0.0 copy-start.4
  6.6 7.4 %all-to-all-start = ((bf16[8,4,128,512]{3,2,1,0:T(8,128)(2,1)}), bf16[8,4,128,512]{3,2,1,0:T(8,128)(2,1)}, u32[]{:S(2)}, u32[]{:S(2)}) async-start(bf16[8,4,128,512]{3,2,1,0:T(8,128)(2,1)} %bitcast.41), calls=%async_computation | async-start | bytes 8388608 | tf_op jit(solution)/shard_map/all_to_all | solution.py:111
  14.7 0.0 copy-done.10
  14.7 1.3 fusion.113
  15.9 0.0 copy-done.7
  15.9 1.2 fusion.114
  17.1 1.3 %pad_add_fusion.1 = s32[2]{0:T(128)S(1)} fusion(s32[1]{0:T(128)} %bitcast.4, s32[1]{0:T(128)} %bitcast.3), kind=kLoop, calls=%fused_computation.176 | loop fusion | flops 2 | bytes 16 | tf_op jit(solution)/shard_map/stack | solution.py:142
  18.5 0.1 iota_add_fusion
  18.6 0.1 broadcast_compare_fusion
  18.7 0.0 copy-done.8
  18.7 0.0 copy-done.9
  18.7 0.6 select_reduce_fusion.2
  19.3 0.6 iota_compare_fusion.2
  20.0 0.6 iota_compare_fusion.3
  20.6 0.0 copy-done
  20.6 0.0 copy-done.1
  20.6 0.0 copy-done.4
  20.6 0.3 fusion.146
  21.0 0.4 fusion.147
  21.3 0.4 fusion.148
  21.7 0.4 fusion.141
  22.0 0.7 fusion.60
  22.8 84.5 %all-to-all-done = bf16[8,4,128,512]{3,2,1,0:T(8,128)(2,1)} async-done(((bf16[8,4,128,512]{3,2,1,0:T(8,128)(2,1)}), bf16[8,4,128,512]{3,2,1,0:T(8,128)(2,1)}, u32[]{:S(2)}, u32[]{:S(2)}) %all-to-all-start) | async-done | bytes 4194336 | tf_op jit(solution)/shard_map/all_to_all | solution.py:111
  107.3 2.5 %fusion.140 = (bf16[8,2,128,512]{3,2,1,0:T(8,128)(2,1)S(1)}, bf16[8,2,128,512]{3,2,1,0:T(8,128)(2,1)S(1)}) fusion(bf16[8,4,128,512]{3,2,1,0:T(8,128)(2,1)} %all-to-all-done), kind=kLoop, calls=%fused_computation.200 | loop fusion | bytes 8388608 | tf_op jit(solution)/shard_map/slice | solution.py:113
  109.8 0.5 fusion.142
  110.2 0.5 fusion.143
  110.7 0.5 fusion.144
  111.2 0.5 fusion.145
  111.7 0.0 copy-start.3
  111.7 0.0 copy-start.5
  111.7 1.2 fusion.4
  112.9 0.0 copy-done.3
  112.9 0.0 copy-done.5
  112.9 0.3 convolution_multiply_fusion.15
  113.3 0.3 convolution_multiply_fusion.13
  113.6 0.3 convolution_multiply_fusion.11
  114.0 0.3 convolution_multiply_fusion.9
  114.3 0.4 fusion.27
  114.7 0.4 fusion.25
  115.2 0.4 fusion.23
  115.6 0.0 copy-start.2
  115.6 0.4 fusion.21
  116.1 0.1 fusion.68
  116.2 1.0 copy-done.2
  117.2 0.3 fusion.52
  117.5 0.3 fusion.58
  117.8 0.3 select_convert_fusion.2
  118.1 0.3 select_convert_fusion.1
  118.4 0.1 collective-permute-start
  118.5 1.7 %collective-permute-done = bf16[192,1024]{1,0:T(8,128)(2,1)S(1)} collective-permute-done((bf16[192,1024]{1,0:T(8,128)(2,1)S(1)}, bf16[192,1024]{1,0:T(8,128)(2,1)S(1)}, u32[]{:S(2)}, u32[]{:S(2)}) %collective-permute-start) | collective-permute-done | bytes 393248 | tf_op jit(solution)/shard_map/ppermute | solution.py:64
  120.2 0.1 convert_element_type.53
  120.3 0.0 copy-start.6
  120.3 0.3 select_convert_fusion
  120.5 1.6 %collective-permute-start.1 = (bf16[192,512]{1,0:T(8,128)(2,1)S(1)}, bf16[192,512]{1,0:T(8,128)(2,1)S(1)}, u32[]{:S(2)}, u32[]{:S(2)}) collective-permute-start(bf16[192,512]{1,0:T(8,128)(2,1)S(1)} %get-tuple-element.15), channel_id=1, source_target_pairs={{0,2},{1,3},{2,0},{3,1},{4,6},{5,7},{6,4},{7,5},{8,10},{9,11},{10,... | collective-permute-start | bytes 589832 | tf_op jit(solution)/shard_map/ppermute | solution.py:64
  122.1 5.4 %collective-permute-done.1 = bf16[192,512]{1,0:T(8,128)(2,1)S(1)} collective-permute-done((bf16[192,512]{1,0:T(8,128)(2,1)S(1)}, bf16[192,512]{1,0:T(8,128)(2,1)S(1)}, u32[]{:S(2)}, u32[]{:S(2)}) %collective-permute-start.1) | collective-permute-done | bytes 196640 | tf_op jit(solution)/shard_map/ppermute | solution.py:64
  127.6 0.8 add_convert_fusion
  (17 shorter events, 0.2 us)
Async XLA Ops:
  6.5 8.1 %copy-start.10 = (s32[4]{0:T(128)S(1)}, s32[4]{0:T(128)}, u32[]{:S(2)}) copy-start(s32[4]{0:T(128)} %param.25) | copy-start | bytes 52
  6.6 9.4 %copy-start.7 = (s32[6]{0:T(128)S(1)}, s32[6]{0:T(128)}, u32[]{:S(2)}) copy-start(s32[6]{0:T(128)} %param.26) | copy-start | bytes 76
  6.6 12.1 %copy-start.8 = (s32[8]{0:T(128)S(1)}, s32[8]{0:T(128)}, u32[]{:S(2)}) copy-start(s32[8]{0:T(128)} %param.27) | copy-start | bytes 100
  6.6 12.1 %copy-start.9 = (s32[8]{0:T(128)S(1)}, s32[8]{0:T(128)}, u32[]{:S(2)}) copy-start(s32[8]{0:T(128)} %param.23) | copy-start | bytes 100
  6.6 14.0 %copy-start = (bf16[1,512,512]{2,1,0:T(8,128)(2,1)S(1)}, bf16[1,512,512]{2,1,0:T(8,128)(2,1)}, u32[]{:S(2)}) copy-start(bf16[1,512,512]{2,1,0:T(8,128)(2,1)} %param.19) | copy-start | bytes 1572868
  6.6 14.0 %copy-start.1 = (bf16[192,512]{1,0:T(8,128)(2,1)S(1)}, bf16[192,512]{1,0:T(8,128)(2,1)}, u32[]{:S(2)}) copy-start(bf16[192,512]{1,0:T(8,128)(2,1)} %param.15) | copy-start | bytes 589828
  6.6 14.0 %copy-start.4 = (bf16[192,512]{1,0:T(8,128)(2,1)S(1)}, bf16[192,512]{1,0:T(8,128)(2,1)}, u32[]{:S(2)}) copy-start(bf16[192,512]{1,0:T(8,128)(2,1)} %param.14) | copy-start | bytes 589828
  6.6 100.7 %all-to-all-start = ((bf16[8,4,128,512]{3,2,1,0:T(8,128)(2,1)}), bf16[8,4,128,512]{3,2,1,0:T(8,128)(2,1)}, u32[]{:S(2)}, u32[]{:S(2)}) async-start(bf16[8,4,128,512]{3,2,1,0:T(8,128)(2,1)} %bitcast.41), calls=%async_computation | async-start | bytes 8388608 | tf_op jit(solution)/shard_map/all_to_all | solution.py:111
  111.7 1.2 copy-start.3
  111.7 1.2 copy-start.5
  115.6 1.6 %copy-start.2 = (bf16[512,2048]{1,0:T(8,128)(2,1)S(1)}, bf16[512,2048]{1,0:T(8,128)(2,1)}, u32[]{:S(2)}) copy-start(bf16[512,2048]{1,0:T(8,128)(2,1)} %param.18) | copy-start | bytes 6291460
  118.4 1.8 %collective-permute-start = (bf16[192,1024]{1,0:T(8,128)(2,1)S(1)}, bf16[192,1024]{1,0:T(8,128)(2,1)S(1)}, u32[]{:S(2)}, u32[]{:S(2)}) collective-permute-start(bf16[192,1024]{1,0:T(8,128)(2,1)S(1)} %pad_maximum_fusion.1), channel_id=1, source_target_pairs={{0,1},{1,0},{2,3},{3,2},{4,5},{5,4},{6,7},{7,6},{8,9},{9,8},{10,11... | collective-permute-start | bytes 1179656 | tf_op jit(solution)/shard_map/ppermute | solution.py:64
  120.3 7.3 %copy-start.6 = (bf16[192,512]{1,0:T(8,128)(2,1)S(1)}, bf16[192,512]{1,0:T(8,128)(2,1)}, u32[]{:S(2)}) copy-start(bf16[192,512]{1,0:T(8,128)(2,1)} %param.17) | copy-start | bytes 589828
  120.5 7.0 %collective-permute-start.1 = (bf16[192,512]{1,0:T(8,128)(2,1)S(1)}, bf16[192,512]{1,0:T(8,128)(2,1)S(1)}, u32[]{:S(2)}, u32[]{:S(2)}) collective-permute-start(bf16[192,512]{1,0:T(8,128)(2,1)S(1)} %get-tuple-element.15), channel_id=1, source_target_pairs={{0,2},{1,3},{2,0},{3,1},{4,6},{5,7},{6,4},{7,5},{8,10},{9,11},{10,... | collective-permute-start | bytes 589832 | tf_op jit(solution)/shard_map/ppermute | solution.py:64

commit v16 on v15

--- a/solution.py
+++ b/solution.py
@@ -45,14 +45,11 @@
     return merged
 
 
-def project_over_grp(attention, w_out):
+def project_over_grp(attention, w_blocks, residual):
     size = lax.axis_size("grp")
     index = lax.axis_index("grp")
-    block = w_out.shape[1] // size
-    kept = [
-        jnp.dot(attention, w_out[:, b * block : (b + 1) * block], preferred_element_type=jnp.float32)
-        for b in range(size)
-    ]
+    block = w_blocks[0].shape[1]
+    kept = [jnp.dot(attention, w, preferred_element_type=jnp.float32) for w in w_blocks]
     step = 1
     while step < size:
         high = (index & step) != 0
@@ -62,6 +59,8 @@
         )
         give = give.astype(jnp.bfloat16)
         moved = lax.ppermute(give, "grp", [(g, g ^ step) for g in range(size)]).astype(jnp.float32)
+        if step * 2 == size:
+            keep = [part + residual.astype(jnp.float32) for part in keep]
         kept = [part + moved[:, k * block : (k + 1) * block] for k, part in enumerate(keep)]
         step *= 2
     return kept[0]
@@ -134,6 +133,10 @@
         jnp.concatenate([leaf_allowed, new_allowed], axis=1),
         head_count,
     )
+    grp_size = lax.axis_size("grp")
+    block = w_out.shape[1] // grp_size
+    w_blocks = [w_out[:, b * block : (b + 1) * block] for b in range(grp_size)]
+    w_blocks, local_part = lax.optimization_barrier((w_blocks, local_part))
 
     upper_pos = (
         jnp.arange(dev_count, dtype=jnp.int32)[:, None, None] * chunk
@@ -151,8 +154,7 @@
     merged = combine(local_part, upper_part)
     attended = jnp.concatenate([part[2] / part[1] for part in merged], axis=1)
     attention = jnp.where(is_live[:, None], attended, 0.0).astype(jnp.bfloat16)
-    mixed = project_over_grp(attention, w_out)
-    return (residual.astype(jnp.float32) + mixed).astype(jnp.bfloat16)
+    return project_over_grp(attention, w_blocks, residual).astype(jnp.bfloat16)
 
 
 def solution(mesh):

time: 129 us -> 126 us (0.977)
  waiting for transfers between devices: 91.6 us -> 88.9 us
    all_to_all x1, waiting for transfers between devices: 84.5 us -> 81.8 us  [shards(): received = lax.all_to_all(send, 'tok', 0, 0, tiled=True)]
  transfers between devices with their start and end apart: 3 -> 3, of which waited for: 3 -> 3; matrix products, arithmetic and copies ran while one was open for 6% -> 8% of each run, Pallas kernels for 0% -> 0%
where the time goes in v16:
time: 126 us
  waiting for transfers between devices  88.9 us (71%)
  other arithmetic  12.7 us (10%)
  starting transfers between devices  9.06 us (7%)
  matrix products  7.43 us (6%)
  local copies, waits for them, and re-layouts  6.87 us (5%)
    all_to_all x1, waiting for transfers between devices, shards(): received = lax.all_to_all(send, 'tok', 0, 0, tiled=True)  81.8 us
    all_to_all x1, starting transfers between devices, shards(): received = lax.all_to_all(send, 'tok', 0, 0, tiled=True)  7.4 us
    ppermute x2, waiting for transfers between devices, project_over_grp(): lax.ppermute(give, 'grp', [(g, g ^ step) for g in range(size)])  7.12 us
    dot_general x8, matrix products, partial_attention(): lax.dot_general(query_rows[:, cols], key_rows[:, cols], (((1,), (1,)), ((...  3.28 us
    reduce_sum x3, other arithmetic, pick(): return jnp.sum(jnp.where(ids == index, table, 0))  3.1 us
    dot_general x8, matrix products, partial_attention(): jnp.dot(exp_scores.astype(jnp.bfloat16), values[:, cols], preferred_eleme...  3.09 us
    gather x1, local copies, waits for them, and re-layouts, shards(): both.at[jnp.concatenate([dest_nodes, node_count + dest_nodes], axis=1)]  2.79 us
  transfers between devices with their start and end apart: 3, of which 3 were waited for; matrix products, arithmetic and copies ran while one was open for 8% of the time, Pallas kernels for 0%

profile of v16, /device:TPU:0, one launch (start us, length us, event | category | flops | bytes accessed | tf_op | source)
XLA Modules:
  0.0 126.0 jit_solution(13525196119134489658)
XLA Ops:
  0.0 1.3 %add_bitcast_fusion.1 = (s32[8,1,1]{0,1,2:T(1,128)S(1)}, s32[8,1]{0,1:T(1,128)S(1)}, s32[]{:T(128)}) fusion(s32[8]{0:T(128)} %param.24, s32[]{:T(128)S(6)} %axis_index.25), kind=kLoop, calls=%fused_computation.175 | loop fusion | flops 31 | bytes 104 | tf_op jit(solution)/shard_map/concatenate | solution.py:107
  1.3 0.8 select_reduce_fusion
  2.1 0.1 copy.23
  2.2 0.1 reshape.226
  2.3 1.5 %pad_maximum_fusion = bf16[12,128,512]{2,1,0:T(8,128)(2,1)S(1)} fusion(bf16[6,128,512]{2,1,0:T(8,128)(2,1)} %param.22, bf16[6,128,512]{2,1,0:T(8,128)(2,1)} %param.21), kind=kLoop, calls=%fused_computation.9 | loop fusion | flops 786432 | bytes 3145728 | tf_op jit(solution)/shard_map/concatenate | solution.py:106
  3.8 2.8 %gather_fusion = bf16[32,128,512]{2,1,0:T(8,128)(2,1)} fusion(bf16[12,128,512]{2,1,0:T(8,128)(2,1)S(1)} %pad_maximum_fusion, s32[1024]{0:T(1024)S(1)} %pad_clamp_fusion), kind=kCustom, calls=%fused_computation | custom fusion | bytes 8388736 | tf_op jit(solution)/shard_map/gather | solution.py:107
  6.6 0.0 copy-start
  6.6 0.0 copy-start.1
  6.6 0.0 copy-start.4
  6.6 7.4 %all-to-all-start = ((bf16[8,4,128,512]{3,2,1,0:T(8,128)(2,1)}), bf16[8,4,128,512]{3,2,1,0:T(8,128)(2,1)}, u32[]{:S(2)}, u32[]{:S(2)}) async-start(bf16[8,4,128,512]{3,2,1,0:T(8,128)(2,1)} %bitcast.73), calls=%async_computation | async-start | bytes 8388608 | tf_op jit(solution)/shard_map/all_to_all | solution.py:110
  14.7 0.0 copy-done.10
  14.7 1.3 fusion.109
  15.9 0.0 copy-done.7
  15.9 1.2 fusion.110
  17.1 1.3 %pad_add_fusion.1 = s32[2]{0:T(128)S(1)} fusion(s32[1]{0:T(128)} %bitcast.15, s32[1]{0:T(128)} %bitcast.14), kind=kLoop, calls=%fused_computation.168 | loop fusion | flops 2 | bytes 16 | tf_op jit(solution)/shard_map/stack | solution.py:145
  18.5 0.1 iota_add_fusion
  18.6 0.1 broadcast_compare_fusion
  18.7 0.0 copy-done.9
  18.7 0.6 select_reduce_fusion.2
  19.3 0.6 iota_compare_fusion.2
  20.0 0.6 iota_compare_fusion.3
  20.6 0.0 copy-done
  20.6 0.0 copy-done.1
  20.6 0.0 copy-done.4
  20.6 0.3 fusion.139
  21.0 0.4 fusion.140
  21.3 0.0 copy-start.3
  21.3 0.0 copy-start.6
  21.3 0.3 fusion.141
  21.7 0.4 fusion.142
  22.0 0.3 copy-done.3
  22.4 0.0 copy-done.6
  22.4 0.3 fusion.61
  22.7 0.3 fusion.63
  23.1 0.3 fusion.65
  23.4 0.3 fusion.67
  23.7 0.0 copy-start.2
  23.7 0.8 fusion.59
  24.5 0.8 copy-done.2
  25.3 0.2 fusion.137
  25.5 81.8 %all-to-all-done = bf16[8,4,128,512]{3,2,1,0:T(8,128)(2,1)} async-done(((bf16[8,4,128,512]{3,2,1,0:T(8,128)(2,1)}), bf16[8,4,128,512]{3,2,1,0:T(8,128)(2,1)}, u32[]{:S(2)}, u32[]{:S(2)}) %all-to-all-start) | async-done | bytes 4194336 | tf_op jit(solution)/shard_map/all_to_all | solution.py:110
  107.3 2.5 %fusion.136 = (bf16[8,2,128,512]{3,2,1,0:T(8,128)(2,1)S(1)}, bf16[8,2,128,512]{3,2,1,0:T(8,128)(2,1)S(1)}) fusion(bf16[8,4,128,512]{3,2,1,0:T(8,128)(2,1)} %all-to-all-done), kind=kLoop, calls=%fused_computation.192 | loop fusion | bytes 8388608 | tf_op jit(solution)/shard_map/slice | solution.py:112
  109.8 0.5 fusion.143
  110.2 0.5 fusion.144
  110.7 0.5 fusion.145
  111.2 0.5 fusion.138
  111.7 1.2 fusion.4
  112.9 0.4 fusion.27
  113.3 0.4 fusion.25
  113.8 0.5 fusion.23
  114.3 0.5 fusion.21
  114.7 0.1 fusion.60
  114.9 0.3 fusion.147
  115.1 0.3 fusion.146
  115.4 0.3 select_convert_fusion.2
  115.7 0.3 select_convert_fusion.1
  116.0 0.1 collective-permute-start
  116.1 1.7 %collective-permute-done = bf16[192,1024]{1,0:T(8,128)(2,1)S(1)} collective-permute-done((bf16[192,1024]{1,0:T(8,128)(2,1)S(1)}, bf16[192,1024]{1,0:T(8,128)(2,1)S(1)}, u32[]{:S(2)}, u32[]{:S(2)}) %collective-permute-start) | collective-permute-done | bytes 393248 | tf_op jit(solution)/shard_map/ppermute | solution.py:61
  117.8 0.1 convert_element_type.52
  117.9 0.0 copy-start.5
  117.9 0.3 select_convert_fusion
  118.1 1.6 %collective-permute-start.1 = (bf16[192,512]{1,0:T(8,128)(2,1)S(1)}, bf16[192,512]{1,0:T(8,128)(2,1)S(1)}, u32[]{:S(2)}, u32[]{:S(2)}) collective-permute-start(bf16[192,512]{1,0:T(8,128)(2,1)S(1)} %get-tuple-element.47), channel_id=1, source_target_pairs={{0,2},{1,3},{2,0},{3,1},{4,6},{5,7},{6,4},{7,5},{8,10},{9,11},{10,... | collective-permute-start | bytes 589832 | tf_op jit(solution)/shard_map/ppermute | solution.py:61
  119.7 5.4 %collective-permute-done.1 = bf16[192,512]{1,0:T(8,128)(2,1)S(1)} collective-permute-done((bf16[192,512]{1,0:T(8,128)(2,1)S(1)}, bf16[192,512]{1,0:T(8,128)(2,1)S(1)}, u32[]{:S(2)}, u32[]{:S(2)}) %collective-permute-start.1) | collective-permute-done | bytes 196640 | tf_op jit(solution)/shard_map/ppermute | solution.py:61
  125.2 0.8 add_convert_fusion
  (18 shorter events, 0.2 us)
Async XLA Ops:
  6.5 8.1 %copy-start.10 = (s32[4]{0:T(128)S(1)}, s32[4]{0:T(128)}, u32[]{:S(2)}) copy-start(s32[4]{0:T(128)} %param.25) | copy-start | bytes 52
  6.6 9.4 %copy-start.7 = (s32[6]{0:T(128)S(1)}, s32[6]{0:T(128)}, u32[]{:S(2)}) copy-start(s32[6]{0:T(128)} %param.26) | copy-start | bytes 76
  6.6 12.1 %copy-start.8 = (s32[8]{0:T(128)S(1)}, s32[8]{0:T(128)}, u32[]{:S(2)}) copy-start(s32[8]{0:T(128)} %param.27) | copy-start | bytes 100
  6.6 12.1 %copy-start.9 = (s32[8]{0:T(128)S(1)}, s32[8]{0:T(128)}, u32[]{:S(2)}) copy-start(s32[8]{0:T(128)} %param.23) | copy-start | bytes 100
  6.6 14.0 %copy-start = (bf16[1,512,512]{2,1,0:T(8,128)(2,1)S(1)}, bf16[1,512,512]{2,1,0:T(8,128)(2,1)}, u32[]{:S(2)}) copy-start(bf16[1,512,512]{2,1,0:T(8,128)(2,1)} %param.19) | copy-start | bytes 1572868
  6.6 14.0 %copy-start.1 = (bf16[192,512]{1,0:T(8,128)(2,1)S(1)}, bf16[192,512]{1,0:T(8,128)(2,1)}, u32[]{:S(2)}) copy-start(bf16[192,512]{1,0:T(8,128)(2,1)} %param.15) | copy-start | bytes 589828
  6.6 14.0 %copy-start.4 = (bf16[192,512]{1,0:T(8,128)(2,1)S(1)}, bf16[192,512]{1,0:T(8,128)(2,1)}, u32[]{:S(2)}) copy-start(bf16[192,512]{1,0:T(8,128)(2,1)} %param.14) | copy-start | bytes 589828
  6.6 100.7 %all-to-all-start = ((bf16[8,4,128,512]{3,2,1,0:T(8,128)(2,1)}), bf16[8,4,128,512]{3,2,1,0:T(8,128)(2,1)}, u32[]{:S(2)}, u32[]{:S(2)}) async-start(bf16[8,4,128,512]{3,2,1,0:T(8,128)(2,1)} %bitcast.73), calls=%async_computation | async-start | bytes 8388608 | tf_op jit(solution)/shard_map/all_to_all | solution.py:110
  21.3 1.0 copy-start.3
  21.3 1.1 copy-start.6
  23.7 1.6 %copy-start.2 = (bf16[512,2048]{1,0:T(8,128)(2,1)S(1)}, bf16[512,2048]{1,0:T(8,128)(2,1)}, u32[]{:S(2)}) copy-start(bf16[512,2048]{1,0:T(8,128)(2,1)} %param.18) | copy-start | bytes 6291460
  116.0 1.8 %collective-permute-start = (bf16[192,1024]{1,0:T(8,128)(2,1)S(1)}, bf16[192,1024]{1,0:T(8,128)(2,1)S(1)}, u32[]{:S(2)}, u32[]{:S(2)}) collective-permute-start(bf16[192,1024]{1,0:T(8,128)(2,1)S(1)} %pad_maximum_fusion.1), channel_id=1, source_target_pairs={{0,1},{1,0},{2,3},{3,2},{4,5},{5,4},{6,7},{7,6},{8,9},{9,8},{10,11... | collective-permute-start | bytes 1179656 | tf_op jit(solution)/shard_map/ppermute | solution.py:61
  117.9 7.3 %copy-start.5 = (bf16[192,512]{1,0:T(8,128)(2,1)S(1)}, bf16[192,512]{1,0:T(8,128)(2,1)}, u32[]{:S(2)}) copy-start(bf16[192,512]{1,0:T(8,128)(2,1)} %param.17) | copy-start | bytes 589828
  118.1 7.0 %collective-permute-start.1 = (bf16[192,512]{1,0:T(8,128)(2,1)S(1)}, bf16[192,512]{1,0:T(8,128)(2,1)S(1)}, u32[]{:S(2)}, u32[]{:S(2)}) collective-permute-start(bf16[192,512]{1,0:T(8,128)(2,1)S(1)} %get-tuple-element.47), channel_id=1, source_target_pairs={{0,2},{1,3},{2,0},{3,1},{4,6},{5,7},{6,4},{7,5},{8,10},{9,11},{10,... | collective-permute-start | bytes 589832 | tf_op jit(solution)/shard_map/ppermute | solution.py:61

commit v17 on v16

--- a/solution.py
+++ b/solution.py
@@ -28,6 +28,27 @@
             exp_scores.astype(jnp.bfloat16),
             values[:, cols],
             preferred_element_type=jnp.float32,
+        )
+        parts.append((row_max, row_total, weighted))
+    return parts
+
+
+def head_attention(query_rows, key_heads, value_heads, allowed):
+    head_width = key_heads[0].shape[1]
+    parts = []
+    for head, (keys, values) in enumerate(zip(key_heads, value_heads)):
+        scores = lax.dot_general(
+            query_rows[:, head * head_width : (head + 1) * head_width],
+            keys,
+            (((1,), (1,)), ((), ())),
+            preferred_element_type=jnp.float32,
+        ) * head_width ** (-0.5)
+        scores = jnp.where(allowed, scores, NEG_FILL)
+        row_max = jnp.max(scores, axis=1, keepdims=True)
+        exp_scores = jnp.where(allowed, jnp.exp(scores - row_max), 0.0)
+        row_total = jnp.sum(exp_scores, axis=1, keepdims=True)
+        weighted = jnp.dot(
+            exp_scores.astype(jnp.bfloat16), values, preferred_element_type=jnp.float32
         )
         parts.append((row_max, row_total, weighted))
     return parts
@@ -103,13 +124,13 @@
         jnp.where(dest_mid[:, None] == mid_ids[None, :], mid_root[None, :], 0), axis=1
     )
     dest_nodes = jnp.stack([dest_root, root_count + dest_mid], axis=1)
+    head_width = col_count // head_count
     both = jnp.concatenate([upper_keys, upper_values], axis=0)
+    both = both.reshape(2 * node_count, chunk, head_count, head_width).transpose(0, 2, 1, 3)
     send = both.at[jnp.concatenate([dest_nodes, node_count + dest_nodes], axis=1)].get(
         mode="promise_in_bounds"
     )
     received = lax.all_to_all(send, "tok", 0, 0, tiled=True)
-    recv_keys = received[:, :2]
-    recv_values = received[:, 2:]
 
     my_length = pick(req_len, my_index)
     my_mid = pick(leaf_mid, my_index)
@@ -144,12 +165,11 @@
     )
     upper_limit = jnp.stack([root_len, mid_len])[None, :, None]
     upper_ok = (upper_pos < upper_limit).reshape(-1)
-    upper_part = partial_attention(
+    upper_part = head_attention(
         queries,
-        recv_keys.reshape(-1, col_count),
-        recv_values.reshape(-1, col_count),
+        [received[:, :2, head].reshape(-1, head_width) for head in range(head_count)],
+        [received[:, 2:, head].reshape(-1, head_width) for head in range(head_count)],
         upper_ok[None, :],
-        head_count,
     )
     merged = combine(local_part, upper_part)
     attended = jnp.concatenate([part[2] / part[1] for part in merged], axis=1)

time: 126 us -> 133 us (1.056)
  local copies, waits for them, and re-layouts: 6.87 us -> 14.8 us
    gather x1 -> x2, local copies, waits for them, and re-layouts: 2.79 us -> 7.75 us  [shards(): both.at[jnp.concatenate([dest_nodes, node_count + dest_nodes], axis=1)]]
    dot_general x0 -> x8, matrix products: none -> 3.65 us  [the longest x4 1.9 us: head_attention(): lax.dot_general(query_rows[:, head * head_width:(head + 1) * head_width],...]
    dot_general x8 -> x4, matrix products: 3.28 us -> 1.4 us  [partial_attention(): lax.dot_general(query_rows[:, cols], key_rows[:, cols], (((1,), (1,)), ((...]
    unnamed x22 -> x24, local copies, waits for them, and re-layouts: 1.24 us -> 3.11 us
    dot_general x8 -> x4, matrix products: 3.09 us -> 1.32 us  [partial_attention(): jnp.dot(exp_scores.astype(jnp.bfloat16), values[:, cols], preferred_eleme...]
    reduce_sum x3 -> x4, other arithmetic: 3.1 us -> 4.5 us  [pick(): return jnp.sum(jnp.where(ids == index, table, 0))]
    concatenate x1, other arithmetic: 1.51 us -> 0.14 us  [shards(): both = jnp.concatenate([upper_keys, upper_values], axis=0)]
  transfers between devices with their start and end apart: 3 -> 3, of which waited for: 3 -> 3; matrix products, arithmetic and copies ran while one was open for 8% -> 7% of each run, Pallas kernels for 0% -> 0%
where the time goes in v17:
time: 133 us
  waiting for transfers between devices  88.9 us (67%)
  local copies, waits for them, and re-layouts  14.8 us (11%)
  other arithmetic  11.5 us (9%)
  starting transfers between devices  9.05 us (7%)
  matrix products  7.43 us (6%)
    all_to_all x1, waiting for transfers between devices, shards(): received = lax.all_to_all(send, 'tok', 0, 0, tiled=True)  81.7 us
    gather x2, local copies, waits for them, and re-layouts, shards(): both.at[jnp.concatenate([dest_nodes, node_count + dest_nodes], axis=1)]  7.75 us
    all_to_all x1, starting transfers between devices, shards(): received = lax.all_to_all(send, 'tok', 0, 0, tiled=True)  7.4 us
    ppermute x2, waiting for transfers between devices, project_over_grp(): lax.ppermute(give, 'grp', [(g, g ^ step) for g in range(size)])  7.13 us
    reduce_sum x4, other arithmetic, pick(): return jnp.sum(jnp.where(ids == index, table, 0))  4.5 us
    unnamed x24, local copies, waits for them, and re-layouts  3.11 us
    slice x1, local copies, waits for them, and re-layouts, shards(): received[:, 2:, head].reshape(-1, head_width)  2.67 us
  transfers between devices with their start and end apart: 3, of which 3 were waited for; matrix products, arithmetic and copies ran while one was open for 7% of the time, Pallas kernels for 0%

profile of v17, /device:TPU:0, one launch (start us, length us, event | category | flops | bytes accessed | tf_op | source)
XLA Modules:
  0.0 132.6 jit_solution(13920832711933965698)
XLA Ops:
  0.0 0.8 select_reduce_fusion
  0.8 1.3 select_reduce_fusion.1
  2.2 0.1 copy.52
  2.2 0.1 reshape.222
  2.3 1.5 %copy.47 = bf16[6,128,512]{1,2,0:T(8,128)(2,1)S(1)} copy(bf16[6,128,512]{2,1,0:T(8,128)(2,1)} %param.21) | data formatting | bytes 1572864 | tf_op args[7]
  3.9 0.0 copy-done.4
  3.9 0.4 copy.48
  4.2 0.1 pad_maximum_fusion
  4.4 0.9 copy.49
  5.3 3.1 %gather_fusion = bf16[32,4,128,128]{3,2,1,0:T(8,128)(2,1)} fusion(bf16[12,4,128,128]{3,2,1,0:T(8,128)(2,1)S(1)} %bitcast.105, s32[1024]{0:T(1024)S(1)} %pad_clamp_fusion), kind=kCustom, calls=%fused_computation | custom fusion | bytes 8388736 | tf_op jit(solution)/shard_map/gather | solution.py:130
  8.4 4.7 %copy.53 = bf16[8,4,4,128,128]{4,3,1,2,0:T(8,128)(2,1)} copy(bf16[8,4,4,128,128]{4,3,2,1,0:T(8,128)(2,1)} %bitcast.106) | data formatting | bytes 8388608 | tf_op jit(solution)/shard_map/gather | solution.py:130
  13.1 0.0 copy-start.1
  13.1 0.0 copy-start.3
  13.1 7.4 %all-to-all-start = ((bf16[8,4,4,128,128]{4,3,1,2,0:T(8,128)(2,1)}), bf16[8,4,4,128,128]{4,3,1,2,0:T(8,128)(2,1)}, u32[]{:S(2)}, u32[]{:S(2)}) async-start(bf16[8,4,4,128,128]{4,3,1,2,0:T(8,128)(2,1)} %copy.53), calls=%async_computation | async-start | bytes 8388608 | tf_op jit(solution)/shard_map/all_to_all | solution.py:133
  21.1 0.0 copy-done.9
  21.2 1.3 fusion.101
  22.4 0.0 copy-done.8
  22.5 1.3 fusion.102
  23.7 1.3 pad_add_fusion.1
  25.0 0.1 iota_add_fusion
  25.1 0.1 broadcast_compare_fusion
  25.2 0.6 iota_compare_fusion.2
  25.8 0.6 select_reduce_fusion.3
  26.4 0.6 iota_compare_fusion.3
  27.1 0.3 fusion.131
  27.5 0.4 fusion.132
  27.8 0.0 copy-start.5
  27.9 0.0 copy-start.7
  27.9 0.3 fusion.133
  28.2 0.4 fusion.134
  28.6 0.3 copy-done.5
  28.9 0.0 copy-done.7
  28.9 0.3 fusion.53
  29.3 0.3 fusion.55
  29.6 0.3 fusion.57
  29.9 0.3 fusion.59
  30.3 0.0 copy-start.2
  30.3 0.8 fusion.51
  31.0 0.8 copy-done.2
  31.9 0.2 fusion.129
  32.0 81.7 %all-to-all-done = bf16[8,4,4,128,128]{4,3,1,2,0:T(8,128)(2,1)} async-done(((bf16[8,4,4,128,128]{4,3,1,2,0:T(8,128)(2,1)}), bf16[8,4,4,128,128]{4,3,1,2,0:T(8,128)(2,1)}, u32[]{:S(2)}, u32[]{:S(2)}) %all-to-all-start) | async-done | bytes 4194336 | tf_op jit(solution)/shard_map/all_to_all | solution.py:133
  113.8 2.7 %fusion.128 = (bf16[8,2,1,128,128]{4,3,1,2,0:T(8,128)(2,1)S(1)}, bf16[8,2,1,128,128]{4,3,1,2,0:T(8,128)(2,1)S(1)}, bf16[8,2,1,128,128]{4,3,1,2,0:T(8,128)(2,1)S(...) fusion(bf16[8,4,4,128,128]{4,3,1,2,0:T(8,128)(2,1)} %all-to-all, ...), kind=kLoop, calls=%fused_computation.184 | loop fusion | bytes 8388608 | tf_op jit(solution)/shard_map/slice | solution.py:171
  116.5 0.5 fusion.135
  116.9 0.5 fusion.136
  117.4 0.5 fusion.137
  117.9 0.5 fusion.130
  118.3 1.2 fusion.4
  119.6 0.4 fusion.27
  120.1 0.4 fusion.25
  120.5 0.4 fusion.23
  120.9 0.4 fusion.21
  121.4 0.1 fusion.52
  121.5 0.3 fusion.139
  121.8 0.3 fusion.138
  122.0 0.3 select_convert_fusion.2
  122.3 0.3 select_convert_fusion.1
  122.6 0.1 collective-permute-start
  122.7 1.7 %collective-permute-done = bf16[192,1024]{1,0:T(8,128)(2,1)S(1)} collective-permute-done((bf16[192,1024]{1,0:T(8,128)(2,1)S(1)}, bf16[192,1024]{1,0:T(8,128)(2,1)S(1)}, u32[]{:S(2)}, u32[]{:S(2)}) %collective-permute-start) | collective-permute-done | bytes 393248 | tf_op jit(solution)/shard_map/ppermute | solution.py:82
  124.4 0.1 convert_element_type.52
  124.5 0.0 copy-start.6
  124.5 0.3 select_convert_fusion
  124.8 1.6 %collective-permute-start.1 = (bf16[192,512]{1,0:T(8,128)(2,1)S(1)}, bf16[192,512]{1,0:T(8,128)(2,1)S(1)}, u32[]{:S(2)}, u32[]{:S(2)}) collective-permute-start(bf16[192,512]{1,0:T(8,128)(2,1)S(1)} %get-tuple-element.47), channel_id=1, source_target_pairs={{0,2},{1,3},{2,0},{3,1},{4,6},{5,7},{6,4},{7,5},{8,10},{9,11},{10,... | collective-permute-start | bytes 589832 | tf_op jit(solution)/shard_map/ppermute | solution.py:82
  126.4 5.4 %collective-permute-done.1 = bf16[192,512]{1,0:T(8,128)(2,1)S(1)} collective-permute-done((bf16[192,512]{1,0:T(8,128)(2,1)S(1)}, bf16[192,512]{1,0:T(8,128)(2,1)S(1)}, u32[]{:S(2)}, u32[]{:S(2)}) %collective-permute-start.1) | collective-permute-done | bytes 196640 | tf_op jit(solution)/shard_map/ppermute | solution.py:82
  131.8 0.8 add_convert_fusion
  (22 shorter events, 0.2 us)
Async XLA Ops:
  0.0 3.9 %copy-start.4 = (bf16[6,128,512]{2,1,0:T(8,128)(2,1)S(1)}, bf16[6,128,512]{2,1,0:T(8,128)(2,1)}, u32[]{:S(2)}) copy-start(bf16[6,128,512]{2,1,0:T(8,128)(2,1)} %param.22) | copy-start | bytes 2359300
  13.1 8.1 %copy-start.9 = (s32[4]{0:T(128)S(1)}, s32[4]{0:T(128)}, u32[]{:S(2)}) copy-start(s32[4]{0:T(128)} %param.25) | copy-start | bytes 52
  13.1 9.4 %copy-start.8 = (s32[6]{0:T(128)S(1)}, s32[6]{0:T(128)}, u32[]{:S(2)}) copy-start(s32[6]{0:T(128)} %param.26) | copy-start | bytes 76
  13.1 12.7 %copy-start.10 = (s32[8]{0:T(128)S(1)}, s32[8]{0:T(128)}, u32[]{:S(2)}) copy-start(s32[8]{0:T(128)} %param.23) | copy-start | bytes 100
  13.1 14.0 %copy-start = (bf16[1,512,512]{2,1,0:T(8,128)(2,1)S(1)}, bf16[1,512,512]{2,1,0:T(8,128)(2,1)}, u32[]{:S(2)}) copy-start(bf16[1,512,512]{2,1,0:T(8,128)(2,1)} %param.19) | copy-start | bytes 1572868
  13.1 14.1 %copy-start.1 = (bf16[192,512]{1,0:T(8,128)(2,1)S(1)}, bf16[192,512]{1,0:T(8,128)(2,1)}, u32[]{:S(2)}) copy-start(bf16[192,512]{1,0:T(8,128)(2,1)} %param.15) | copy-start | bytes 589828
  13.1 14.1 %copy-start.3 = (bf16[192,512]{1,0:T(8,128)(2,1)S(1)}, bf16[192,512]{1,0:T(8,128)(2,1)}, u32[]{:S(2)}) copy-start(bf16[192,512]{1,0:T(8,128)(2,1)} %param.14) | copy-start | bytes 589828
  13.1 100.7 %all-to-all-start = ((bf16[8,4,4,128,128]{4,3,1,2,0:T(8,128)(2,1)}), bf16[8,4,4,128,128]{4,3,1,2,0:T(8,128)(2,1)}, u32[]{:S(2)}, u32[]{:S(2)}) async-start(bf16[8,4,4,128,128]{4,3,1,2,0:T(8,128)(2,1)} %copy.53), calls=%async_computation | async-start | bytes 8388608 | tf_op jit(solution)/shard_map/all_to_all | solution.py:133
  27.8 1.0 copy-start.5
  27.9 1.1 copy-start.7
  30.3 1.6 %copy-start.2 = (bf16[512,2048]{1,0:T(8,128)(2,1)S(1)}, bf16[512,2048]{1,0:T(8,128)(2,1)}, u32[]{:S(2)}) copy-start(bf16[512,2048]{1,0:T(8,128)(2,1)} %param.18) | copy-start | bytes 6291460
  122.6 1.8 %collective-permute-start = (bf16[192,1024]{1,0:T(8,128)(2,1)S(1)}, bf16[192,1024]{1,0:T(8,128)(2,1)S(1)}, u32[]{:S(2)}, u32[]{:S(2)}) collective-permute-start(bf16[192,1024]{1,0:T(8,128)(2,1)S(1)} %pad_maximum_fusion.1), channel_id=1, source_target_pairs={{0,1},{1,0},{2,3},{3,2},{4,5},{5,4},{6,7},{7,6},{8,9},{9,8},{10,11... | collective-permute-start | bytes 1179656 | tf_op jit(solution)/shard_map/ppermute | solution.py:82
  124.5 7.3 %copy-start.6 = (bf16[192,512]{1,0:T(8,128)(2,1)S(1)}, bf16[192,512]{1,0:T(8,128)(2,1)}, u32[]{:S(2)}) copy-start(bf16[192,512]{1,0:T(8,128)(2,1)} %param.17) | copy-start | bytes 589828
  124.8 7.0 %collective-permute-start.1 = (bf16[192,512]{1,0:T(8,128)(2,1)S(1)}, bf16[192,512]{1,0:T(8,128)(2,1)S(1)}, u32[]{:S(2)}, u32[]{:S(2)}) collective-permute-start(bf16[192,512]{1,0:T(8,128)(2,1)S(1)} %get-tuple-element.47), channel_id=1, source_target_pairs={{0,2},{1,3},{2,0},{3,1},{4,6},{5,7},{6,4},{7,5},{8,10},{9,11},{10,... | collective-permute-start | bytes 589832 | tf_op jit(solution)/shard_map/ppermute | solution.py:82

commit v18 on v16

--- a/solution.py
+++ b/solution.py
@@ -58,7 +58,15 @@
             [jnp.where(high, kept[k], kept[k + 1]) for k in range(0, len(kept), 2)], axis=1
         )
         give = give.astype(jnp.bfloat16)
-        moved = lax.ppermute(give, "grp", [(g, g ^ step) for g in range(size)]).astype(jnp.float32)
+        pairs = [(g, g ^ step) for g in range(size)]
+        if step * 2 == size:
+            half = give.shape[0] // 2
+            moved = jnp.concatenate(
+                [lax.ppermute(give[:half], "grp", pairs), lax.ppermute(give[half:], "grp", pairs)],
+                axis=0,
+            ).astype(jnp.float32)
+        else:
+            moved = lax.ppermute(give, "grp", pairs).astype(jnp.float32)
         if step * 2 == size:
             keep = [part + residual.astype(jnp.float32) for part in keep]
         kept = [part + moved[:, k * block : (k + 1) * block] for k, part in enumerate(keep)]

time: 126 us -> 126 us (level)
    ppermute x2 -> x3, waiting for transfers between devices: 7.12 us -> 6.62 us  [the longest x1 3.61 us: project_over_grp(): lax.ppermute(give[:half], 'grp', pairs)]
  transfers between devices with their start and end apart: 3 -> 4, of which waited for: 3 -> 4; matrix products, arithmetic and copies ran while one was open for 8% -> 8% of each run, Pallas kernels for 0% -> 0%
where the time goes in v18:
time: 126 us
  waiting for transfers between devices  88.4 us (70%)
  other arithmetic  12.7 us (10%)
  starting transfers between devices  9.56 us (8%)
  matrix products  7.43 us (6%)
  local copies, waits for them, and re-layouts  6.88 us (5%)
    all_to_all x1, waiting for transfers between devices, shards(): received = lax.all_to_all(send, 'tok', 0, 0, tiled=True)  81.8 us
    all_to_all x1, starting transfers between devices, shards(): received = lax.all_to_all(send, 'tok', 0, 0, tiled=True)  7.4 us
    ppermute x1, waiting for transfers between devices, project_over_grp(): lax.ppermute(give[:half], 'grp', pairs)  3.61 us
    dot_general x8, matrix products, partial_attention(): lax.dot_general(query_rows[:, cols], key_rows[:, cols], (((1,), (1,)), ((...  3.28 us
    reduce_sum x3, other arithmetic, pick(): return jnp.sum(jnp.where(ids == index, table, 0))  3.1 us
    dot_general x8, matrix products, partial_attention(): jnp.dot(exp_scores.astype(jnp.bfloat16), values[:, cols], preferred_eleme...  3.09 us
    gather x1, local copies, waits for them, and re-layouts, shards(): both.at[jnp.concatenate([dest_nodes, node_count + dest_nodes], axis=1)]  2.79 us
  transfers between devices with their start and end apart: 4, of which 4 were waited for; matrix products, arithmetic and copies ran while one was open for 8% of the time, Pallas kernels for 0%

profile of v18, /device:TPU:0, one launch (start us, length us, event | category | flops | bytes accessed | tf_op | source)
XLA Modules:
  0.0 126.0 jit_solution(13802477555806549180)
XLA Ops:
  0.0 1.3 %add_bitcast_fusion.1 = (s32[8,1,1]{0,1,2:T(1,128)S(1)}, s32[8,1]{0,1:T(1,128)S(1)}, s32[]{:T(128)}) fusion(s32[8]{0:T(128)} %param.24, s32[]{:T(128)S(6)} %axis_index.25), kind=kLoop, calls=%fused_computation.175 | loop fusion | flops 31 | bytes 104 | tf_op jit(solution)/shard_map/concatenate | solution.py:115
  1.3 0.8 select_reduce_fusion
  2.1 0.1 copy.23
  2.2 0.1 reshape.226
  2.3 1.5 %pad_maximum_fusion = bf16[12,128,512]{2,1,0:T(8,128)(2,1)S(1)} fusion(bf16[6,128,512]{2,1,0:T(8,128)(2,1)} %param.22, bf16[6,128,512]{2,1,0:T(8,128)(2,1)} %param.21), kind=kLoop, calls=%fused_computation.9 | loop fusion | flops 786432 | bytes 3145728 | tf_op jit(solution)/shard_map/concatenate | solution.py:114
  3.8 2.8 %gather_fusion = bf16[32,128,512]{2,1,0:T(8,128)(2,1)} fusion(bf16[12,128,512]{2,1,0:T(8,128)(2,1)S(1)} %pad_maximum_fusion, s32[1024]{0:T(1024)S(1)} %pad_clamp_fusion), kind=kCustom, calls=%fused_computation | custom fusion | bytes 8388736 | tf_op jit(solution)/shard_map/gather | solution.py:115
  6.6 0.0 copy-start
  6.6 0.0 copy-start.1
  6.6 0.0 copy-start.4
  6.6 7.4 %all-to-all-start = ((bf16[8,4,128,512]{3,2,1,0:T(8,128)(2,1)}), bf16[8,4,128,512]{3,2,1,0:T(8,128)(2,1)}, u32[]{:S(2)}, u32[]{:S(2)}) async-start(bf16[8,4,128,512]{3,2,1,0:T(8,128)(2,1)} %bitcast.73), calls=%async_computation | async-start | bytes 8388608 | tf_op jit(solution)/shard_map/all_to_all | solution.py:118
  14.7 0.0 copy-done.10
  14.7 1.3 fusion.109
  15.9 1.2 fusion.110
  17.1 1.3 %pad_add_fusion.1 = s32[2]{0:T(128)S(1)} fusion(s32[1]{0:T(128)} %bitcast.15, s32[1]{0:T(128)} %bitcast.14), kind=kLoop, calls=%fused_computation.168 | loop fusion | flops 2 | bytes 16 | tf_op jit(solution)/shard_map/stack | solution.py:153
  18.5 0.1 iota_add_fusion
  18.6 0.1 broadcast_compare_fusion
  18.7 0.0 copy-done.9
  18.7 0.6 select_reduce_fusion.2
  19.3 0.6 iota_compare_fusion.2
  20.0 0.6 iota_compare_fusion.3
  20.6 0.0 copy-done
  20.6 0.0 copy-done.1
  20.6 0.3 fusion.140
  21.0 0.4 fusion.141
  21.3 0.0 copy-start.3
  21.3 0.0 copy-start.6
  21.3 0.3 fusion.142
  21.7 0.4 fusion.143
  22.0 0.3 copy-done.3
  22.4 0.0 copy-done.6
  22.4 0.3 fusion.61
  22.7 0.3 fusion.63
  23.1 0.3 fusion.65
  23.4 0.3 fusion.67
  23.7 0.0 copy-start.2
  23.7 0.8 fusion.59
  24.5 0.8 copy-done.2
  25.3 0.2 fusion.137
  25.5 81.8 %all-to-all-done = bf16[8,4,128,512]{3,2,1,0:T(8,128)(2,1)} async-done(((bf16[8,4,128,512]{3,2,1,0:T(8,128)(2,1)}), bf16[8,4,128,512]{3,2,1,0:T(8,128)(2,1)}, u32[]{:S(2)}, u32[]{:S(2)}) %all-to-all-start) | async-done | bytes 4194336 | tf_op jit(solution)/shard_map/all_to_all | solution.py:118
  107.3 2.5 %fusion.136 = (bf16[8,2,128,512]{3,2,1,0:T(8,128)(2,1)S(1)}, bf16[8,2,128,512]{3,2,1,0:T(8,128)(2,1)S(1)}) fusion(bf16[8,4,128,512]{3,2,1,0:T(8,128)(2,1)} %all-to-all-done), kind=kLoop, calls=%fused_computation.192 | loop fusion | bytes 8388608 | tf_op jit(solution)/shard_map/slice | solution.py:120
  109.8 0.5 fusion.144
  110.2 0.5 fusion.145
  110.7 0.5 fusion.146
  111.2 0.5 fusion.139
  111.7 1.2 fusion.4
  112.9 0.4 fusion.27
  113.3 0.4 fusion.25
  113.8 0.5 fusion.23
  114.3 0.5 fusion.21
  114.7 0.1 fusion.60
  114.9 0.3 fusion.148
  115.1 0.3 fusion.147
  115.4 0.3 select_convert_fusion.2
  115.7 0.3 select_convert_fusion.1
  116.0 0.1 collective-permute-start
  116.1 1.7 %collective-permute-done = bf16[192,1024]{1,0:T(8,128)(2,1)S(1)} collective-permute-done((bf16[192,1024]{1,0:T(8,128)(2,1)S(1)}, bf16[192,1024]{1,0:T(8,128)(2,1)S(1)}, u32[]{:S(2)}, u32[]{:S(2)}) %collective-permute-start) | collective-permute-done | bytes 393248 | tf_op jit(solution)/shard_map/ppermute | solution.py:69
  117.8 0.1 convert_element_type.52
  117.9 0.0 copy-start.5
  117.9 0.3 select_convert_fusion
  118.2 1.6 %collective-permute-start.1 = (bf16[96,512]{1,0:T(8,128)(2,1)S(1)}, bf16[96,512]{1,0:T(8,128)(2,1)S(1)}, u32[]{:S(2)}, u32[]{:S(2)}) collective-permute-start(bf16[96,512]{1,0:T(8,128)(2,1)S(1)} %get-tuple-element.68), channel_id=1, source_target_pairs={{0,2},{1,3},{2,0},{3,1},{4,6},{5,7},{6,4},{7,5},{8,10},{9,11},{10,... | collective-permute-start | bytes 294920 | tf_op jit(solution)/shard_map/ppermute | solution.py:65
  119.8 0.5 collective-permute-start.2
  120.3 3.6 %collective-permute-done.1 = bf16[96,512]{1,0:T(8,128)(2,1)S(1)} collective-permute-done((bf16[96,512]{1,0:T(8,128)(2,1)S(1)}, bf16[96,512]{1,0:T(8,128)(2,1)S(1)}, u32[]{:S(2)}, u32[]{:S(2)}) %collective-permute-start.1) | collective-permute-done | bytes 98336 | tf_op jit(solution)/shard_map/ppermute | solution.py:65
  123.9 1.3 %collective-permute-done.2 = bf16[96,512]{1,0:T(8,128)(2,1)S(1)} collective-permute-done((bf16[96,512]{1,0:T(8,128)(2,1)S(1)}, bf16[96,512]{1,0:T(8,128)(2,1)S(1)}, u32[]{:S(2)}, u32[]{:S(2)}) %collective-permute-start.2) | collective-permute-done | bytes 98336 | tf_op jit(solution)/shard_map/ppermute | solution.py:65
  125.2 0.8 add_convert_fusion
  (21 shorter events, 0.2 us)
Async XLA Ops:
  6.5 8.1 %copy-start.10 = (s32[4]{0:T(128)S(1)}, s32[4]{0:T(128)}, u32[]{:S(2)}) copy-start(s32[4]{0:T(128)} %param.25) | copy-start | bytes 52
  6.6 9.4 %copy-start.7 = (s32[6]{0:T(128)S(1)}, s32[6]{0:T(128)}, u32[]{:S(2)}) copy-start(s32[6]{0:T(128)} %param.26) | copy-start | bytes 76
  6.6 12.1 %copy-start.8 = (s32[8]{0:T(128)S(1)}, s32[8]{0:T(128)}, u32[]{:S(2)}) copy-start(s32[8]{0:T(128)} %param.27) | copy-start | bytes 100
  6.6 12.1 %copy-start.9 = (s32[8]{0:T(128)S(1)}, s32[8]{0:T(128)}, u32[]{:S(2)}) copy-start(s32[8]{0:T(128)} %param.23) | copy-start | bytes 100
  6.6 14.0 %copy-start = (bf16[1,512,512]{2,1,0:T(8,128)(2,1)S(1)}, bf16[1,512,512]{2,1,0:T(8,128)(2,1)}, u32[]{:S(2)}) copy-start(bf16[1,512,512]{2,1,0:T(8,128)(2,1)} %param.19) | copy-start | bytes 1572868
  6.6 14.0 %copy-start.1 = (bf16[192,512]{1,0:T(8,128)(2,1)S(1)}, bf16[192,512]{1,0:T(8,128)(2,1)}, u32[]{:S(2)}) copy-start(bf16[192,512]{1,0:T(8,128)(2,1)} %param.15) | copy-start | bytes 589828
  6.6 14.0 %copy-start.4 = (bf16[192,512]{1,0:T(8,128)(2,1)S(1)}, bf16[192,512]{1,0:T(8,128)(2,1)}, u32[]{:S(2)}) copy-start(bf16[192,512]{1,0:T(8,128)(2,1)} %param.14) | copy-start | bytes 589828
  6.6 100.7 %all-to-all-start = ((bf16[8,4,128,512]{3,2,1,0:T(8,128)(2,1)}), bf16[8,4,128,512]{3,2,1,0:T(8,128)(2,1)}, u32[]{:S(2)}, u32[]{:S(2)}) async-start(bf16[8,4,128,512]{3,2,1,0:T(8,128)(2,1)} %bitcast.73), calls=%async_computation | async-start | bytes 8388608 | tf_op jit(solution)/shard_map/all_to_all | solution.py:118
  21.3 1.0 copy-start.3
  21.3 1.1 copy-start.6
  23.7 1.6 %copy-start.2 = (bf16[512,2048]{1,0:T(8,128)(2,1)S(1)}, bf16[512,2048]{1,0:T(8,128)(2,1)}, u32[]{:S(2)}) copy-start(bf16[512,2048]{1,0:T(8,128)(2,1)} %param.18) | copy-start | bytes 6291460
  116.0 1.8 %collective-permute-start = (bf16[192,1024]{1,0:T(8,128)(2,1)S(1)}, bf16[192,1024]{1,0:T(8,128)(2,1)S(1)}, u32[]{:S(2)}, u32[]{:S(2)}) collective-permute-start(bf16[192,1024]{1,0:T(8,128)(2,1)S(1)} %pad_maximum_fusion.1), channel_id=1, source_target_pairs={{0,1},{1,0},{2,3},{3,2},{4,5},{5,4},{6,7},{7,6},{8,9},{9,8},{10,11... | collective-permute-start | bytes 1179656 | tf_op jit(solution)/shard_map/ppermute | solution.py:69
  117.9 7.3 %copy-start.5 = (bf16[192,512]{1,0:T(8,128)(2,1)S(1)}, bf16[192,512]{1,0:T(8,128)(2,1)}, u32[]{:S(2)}) copy-start(bf16[192,512]{1,0:T(8,128)(2,1)} %param.17) | copy-start | bytes 589828
  118.2 5.7 %collective-permute-start.1 = (bf16[96,512]{1,0:T(8,128)(2,1)S(1)}, bf16[96,512]{1,0:T(8,128)(2,1)S(1)}, u32[]{:S(2)}, u32[]{:S(2)}) collective-permute-start(bf16[96,512]{1,0:T(8,128)(2,1)S(1)} %get-tuple-element.68), channel_id=1, source_target_pairs={{0,2},{1,3},{2,0},{3,1},{4,6},{5,7},{6,4},{7,5},{8,10},{9,11},{10,... | collective-permute-start | bytes 294920 | tf_op jit(solution)/shard_map/ppermute | solution.py:65
  119.8 5.4 %collective-permute-start.2 = (bf16[96,512]{1,0:T(8,128)(2,1)S(1)}, bf16[96,512]{1,0:T(8,128)(2,1)S(1)}, u32[]{:S(2)}, u32[]{:S(2)}) collective-permute-start(bf16[96,512]{1,0:T(8,128)(2,1)S(1)} %get-tuple-element.69), channel_id=1, source_target_pairs={{0,2},{1,3},{2,0},{3,1},{4,6},{5,7},{6,4},{7,5},{8,10},{9,11},{10,... | collective-permute-start | bytes 294920 | tf_op jit(solution)/shard_map/ppermute | solution.py:65

commit v19 on v16

--- a/solution.py
+++ b/solution.py
@@ -144,17 +144,22 @@
     )
     upper_limit = jnp.stack([root_len, mid_len])[None, :, None]
     upper_ok = (upper_pos < upper_limit).reshape(-1)
-    upper_part = partial_attention(
-        queries,
-        recv_keys.reshape(-1, col_count),
-        recv_values.reshape(-1, col_count),
-        upper_ok[None, :],
-        head_count,
-    )
-    merged = combine(local_part, upper_part)
-    attended = jnp.concatenate([part[2] / part[1] for part in merged], axis=1)
-    attention = jnp.where(is_live[:, None], attended, 0.0).astype(jnp.bfloat16)
-    return project_over_grp(attention, w_blocks, residual).astype(jnp.bfloat16)
+    half = row_count // 2 if row_count % 16 == 0 else row_count
+    outputs = []
+    for start in range(0, row_count, half):
+        rows = slice(start, start + half)
+        upper_part = partial_attention(
+            queries[rows],
+            recv_keys.reshape(-1, col_count),
+            recv_values.reshape(-1, col_count),
+            upper_ok[None, :],
+            head_count,
+        )
+        merged = combine([tuple(x[rows] for x in part) for part in local_part], upper_part)
+        attended = jnp.concatenate([part[2] / part[1] for part in merged], axis=1)
+        attention = jnp.where(is_live[rows, None], attended, 0.0).astype(jnp.bfloat16)
+        outputs.append(project_over_grp(attention, w_blocks, residual[rows]).astype(jnp.bfloat16))
+    return jnp.concatenate(outputs, axis=0)
 
 
 def solution(mesh):

time: 126 us -> 129 us (1.024)
  matrix products: 7.43 us -> 10.4 us
  waiting for transfers between devices: 88.9 us -> 87.4 us
    ppermute x2 -> x4, waiting for transfers between devices: 7.12 us -> 5.09 us  [project_over_grp(): lax.ppermute(give, 'grp', [(g, g ^ step) for g in range(size)])]
    reduce_sum x3 -> x4, other arithmetic: 3.1 us -> 4.5 us  [pick(): return jnp.sum(jnp.where(ids == index, table, 0))]
    dot_general x8 -> x12, matrix products: 3.28 us -> 4.61 us  [partial_attention(): lax.dot_general(query_rows[:, cols], key_rows[:, cols], (((1,), (1,)), ((...]
    concatenate x2 -> x1, other arithmetic: 1.3 us -> 0.01 us  [shards(): jnp.concatenate([dest_nodes, node_count + dest_nodes], axis=1)]
    ppermute x2 -> x4, starting transfers between devices: 1.66 us -> 2.79 us  [project_over_grp(): lax.ppermute(give, 'grp', [(g, g ^ step) for g in range(size)])]
    dot_general x8 -> x12, matrix products: 3.09 us -> 4.03 us  [partial_attention(): jnp.dot(exp_scores.astype(jnp.bfloat16), values[:, cols], preferred_eleme...]
  transfers between devices with their start and end apart: 3 -> 5, of which waited for: 3 -> 4; matrix products, arithmetic and copies ran while one was open for 8% -> 8% of each run, Pallas kernels for 0% -> 0%
where the time goes in v19:
time: 129 us; the launch traced here: 128 us
  waiting for transfers between devices  87.4 us (68%)
  other arithmetic  12.3 us (10%)
  matrix products  10.4 us (8%)
  starting transfers between devices  10.2 us (8%)
  local copies, waits for them, and re-layouts  6.92 us (5%)
    all_to_all x1, waiting for transfers between devices, shards(): received = lax.all_to_all(send, 'tok', 0, 0, tiled=True)  82.4 us
    all_to_all x1, starting transfers between devices, shards(): received = lax.all_to_all(send, 'tok', 0, 0, tiled=True)  7.4 us
    ppermute x4, waiting for transfers between devices, project_over_grp(): lax.ppermute(give, 'grp', [(g, g ^ step) for g in range(size)])  5.09 us
    dot_general x12, matrix products, partial_attention(): lax.dot_general(query_rows[:, cols], key_rows[:, cols], (((1,), (1,)), ((...  4.61 us
    reduce_sum x4, other arithmetic, pick(): return jnp.sum(jnp.where(ids == index, table, 0))  4.5 us
    dot_general x12, matrix products, partial_attention(): jnp.dot(exp_scores.astype(jnp.bfloat16), values[:, cols], preferred_eleme...  4.03 us
    ppermute x4, starting transfers between devices, project_over_grp(): lax.ppermute(give, 'grp', [(g, g ^ step) for g in range(size)])  2.79 us
    gather x1, local copies, waits for them, and re-layouts, shards(): both.at[jnp.concatenate([dest_nodes, node_count + dest_nodes], axis=1)]  2.79 us
  transfers between devices with their start and end apart: 5, of which 4 were waited for; matrix products, arithmetic and copies ran while one was open for 8% of the time, Pallas kernels for 0%

profile of v19, /device:TPU:0, one launch (start us, length us, event | category | flops | bytes accessed | tf_op | source)
XLA Modules:
  0.0 128.3 jit_solution(18278180045172095762)
XLA Ops:
  0.0 0.8 select_reduce_fusion
  0.8 1.3 %select_reduce_fusion.1 = (s32[]{:T(128)}, s32[8,1]{0,1:T(1,128)S(1)}, s32[8,1,1]{0,1,2:T(1,128)S(1)}, s32[]{:T(128)}) fusion(s32[8]{0:T(128)} %param.24, s32[]{:T(128)S(6)} %axis_index.29, s32[8]{0:T(128)} %param.27), kind=kLoop, calls=%fused_computation.271 | loop fusion | flops 46 | bytes 140 | tf_op jit(solution)/shard_map/reduce_sum | solution.py:71
  2.1 0.1 copy.23
  2.2 0.1 reshape.230
  2.3 1.5 %pad_maximum_fusion = bf16[12,128,512]{2,1,0:T(8,128)(2,1)S(1)} fusion(bf16[6,128,512]{2,1,0:T(8,128)(2,1)} %param.22, bf16[6,128,512]{2,1,0:T(8,128)(2,1)} %param.21), kind=kLoop, calls=%fused_computation.17 | loop fusion | flops 786432 | bytes 3145728 | tf_op jit(solution)/shard_map/concatenate | solution.py:106
  3.8 2.8 %gather_fusion = bf16[32,128,512]{2,1,0:T(8,128)(2,1)} fusion(bf16[12,128,512]{2,1,0:T(8,128)(2,1)S(1)} %pad_maximum_fusion, s32[1024]{0:T(1024)S(1)} %pad_clamp_fusion), kind=kCustom, calls=%fused_computation | custom fusion | bytes 8388736 | tf_op jit(solution)/shard_map/gather | solution.py:107
  6.6 7.4 %all-to-all-start = ((bf16[8,4,128,512]{3,2,1,0:T(8,128)(2,1)}), bf16[8,4,128,512]{3,2,1,0:T(8,128)(2,1)}, u32[]{:S(2)}, u32[]{:S(2)}) async-start(bf16[8,4,128,512]{3,2,1,0:T(8,128)(2,1)} %bitcast.245), calls=%async_computation | async-start | bytes 8388608 | tf_op jit(solution)/shard_map/all_to_all | solution.py:110
  14.7 1.3 %fusion.166 = s32[]{:T(128)} fusion(s32[4]{0:T(128)S(1)} %copy-done.9, s32[]{:T(128)} %get-tuple-element.91), kind=kLoop, calls=%fused_computation.243 | loop fusion | flops 11 | bytes 24 | tf_op jit(solution)/shard_map/reduce_sum | solution.py:71
  16.0 1.3 fusion.167
  17.2 1.3 %pad_add_fusion.1 = s32[2]{0:T(128)S(1)} fusion(s32[1]{0:T(128)} %bitcast.15, s32[1]{0:T(128)} %bitcast.14), kind=kLoop, calls=%fused_computation.246 | loop fusion | flops 2 | bytes 16 | tf_op jit(solution)/shard_map/stack | solution.py:145
  18.7 0.6 iota_compare_fusion.2
  19.3 0.6 select_reduce_fusion.3
  19.9 0.6 iota_compare_fusion.3
  20.6 0.3 fusion.227
  21.0 0.3 fusion.228
  21.4 0.4 fusion.225
  21.7 0.4 fusion.226
  22.1 0.3 fusion.104
  22.4 0.3 fusion.106
  22.8 0.3 fusion.108
  23.1 0.3 fusion.110
  23.4 0.8 fusion.71
  24.2 0.5 copy-done.2
  24.7 0.2 fusion.222
  24.9 82.4 %all-to-all-done = bf16[8,4,128,512]{3,2,1,0:T(8,128)(2,1)} async-done(((bf16[8,4,128,512]{3,2,1,0:T(8,128)(2,1)}), bf16[8,4,128,512]{3,2,1,0:T(8,128)(2,1)}, u32[]{:S(2)}, u32[]{:S(2)}) %all-to-all-start) | async-done | bytes 4194336 | tf_op jit(solution)/shard_map/all_to_all | solution.py:110
  107.3 2.5 %fusion.221 = (bf16[8,2,128,512]{3,2,1,0:T(8,128)(2,1)S(1)}, bf16[8,2,128,512]{3,2,1,0:T(8,128)(2,1)S(1)}) fusion(bf16[8,4,128,512]{3,2,1,0:T(8,128)(2,1)} %all-to-all-done), kind=kLoop, calls=%fused_computation.314 | loop fusion | bytes 8388608 | tf_op jit(solution)/shard_map/slice | solution.py:111
  109.8 0.4 fusion.229
  110.2 0.4 fusion.230
  110.6 0.4 fusion.231
  111.0 0.4 fusion.232
  111.4 0.4 fusion.233
  111.8 0.4 fusion.234
  112.2 0.4 fusion.235
  112.6 0.4 fusion.224
  113.0 1.2 fusion.32
  114.3 0.1 fusion.182
  114.3 0.3 fusion.23
  114.7 0.3 fusion.21
  115.1 0.3 fusion.19
  115.5 0.3 fusion.17
  115.9 0.1 fusion.121
  116.0 0.2 fusion.239
  116.2 0.2 fusion.238
  116.4 0.4 fusion.31
  116.8 0.3 fusion.29
  117.1 0.3 fusion.27
  117.5 0.3 fusion.25
  117.8 0.1 fusion.120
  117.9 0.2 fusion.237
  118.1 0.2 fusion.236
  118.3 0.2 select_convert_fusion.2
  118.6 0.2 select_convert_fusion.1
  118.9 0.2 select_convert_fusion.5
  119.1 0.2 select_convert_fusion.4
  119.4 0.6 collective-permute-start
  120.0 0.4 collective-permute-done.2
  120.4 0.1 select_convert_fusion
  120.5 1.6 %collective-permute-start.3 = (bf16[96,512]{1,0:T(8,128)(2,1)S(1)}, bf16[96,512]{1,0:T(8,128)(2,1)S(1)}, u32[]{:S(2)}, u32[]{:S(2)}) collective-permute-start(bf16[96,512]{1,0:T(8,128)(2,1)S(1)} %get-tuple-element.54), channel_id=1, source_target_pairs={{0,2},{1,3},{2,0},{3,1},{4,6},{5,7},{6,4},{7,5},{8,10},{9,11},{10,... | collective-permute-start | bytes 294920 | tf_op jit(solution)/shard_map/ppermute | solution.py:61
  122.1 0.1 select_convert_fusion.3
  122.3 0.6 collective-permute-start.1
  122.8 3.3 %collective-permute-done.3 = bf16[96,512]{1,0:T(8,128)(2,1)S(1)} collective-permute-done((bf16[96,512]{1,0:T(8,128)(2,1)S(1)}, bf16[96,512]{1,0:T(8,128)(2,1)S(1)}, u32[]{:S(2)}, u32[]{:S(2)}) %collective-permute-start.3) | collective-permute-done | bytes 98336 | tf_op jit(solution)/shard_map/ppermute | solution.py:61
  126.1 1.4 %collective-permute-done.1 = bf16[96,512]{1,0:T(8,128)(2,1)S(1)} collective-permute-done((bf16[96,512]{1,0:T(8,128)(2,1)S(1)}, bf16[96,512]{1,0:T(8,128)(2,1)S(1)}, u32[]{:S(2)}, u32[]{:S(2)}) %collective-permute-start.1) | collective-permute-done | bytes 98336 | tf_op jit(solution)/shard_map/ppermute | solution.py:61
  127.5 0.1 add_convert_fusion.1
  127.7 0.7 copy-done.8
  (40 shorter events, 0.8 us)
Async XLA Ops:
  6.6 8.1 %copy-start.9 = (s32[4]{0:T(128)S(1)}, s32[4]{0:T(128)}, u32[]{:S(2)}) copy-start(s32[4]{0:T(128)} %param.25) | copy-start | bytes 52
  6.6 9.4 %copy-start.7 = (s32[6]{0:T(128)S(1)}, s32[6]{0:T(128)}, u32[]{:S(2)}) copy-start(s32[6]{0:T(128)} %param.26) | copy-start | bytes 76
  6.6 12.7 %copy-start.10 = (s32[8]{0:T(128)S(1)}, s32[8]{0:T(128)}, u32[]{:S(2)}) copy-start(s32[8]{0:T(128)} %param.23) | copy-start | bytes 100
  6.6 14.0 %copy-start = (bf16[1,512,512]{2,1,0:T(8,128)(2,1)S(1)}, bf16[1,512,512]{2,1,0:T(8,128)(2,1)}, u32[]{:S(2)}) copy-start(bf16[1,512,512]{2,1,0:T(8,128)(2,1)} %param.19) | copy-start | bytes 1572868
  6.6 14.1 %copy-start.1 = (bf16[192,512]{1,0:T(8,128)(2,1)S(1)}, bf16[192,512]{1,0:T(8,128)(2,1)}, u32[]{:S(2)}) copy-start(bf16[192,512]{1,0:T(8,128)(2,1)} %param.15) | copy-start | bytes 589828
  6.6 14.1 %copy-start.4 = (bf16[192,512]{1,0:T(8,128)(2,1)S(1)}, bf16[192,512]{1,0:T(8,128)(2,1)}, u32[]{:S(2)}) copy-start(bf16[192,512]{1,0:T(8,128)(2,1)} %param.14) | copy-start | bytes 589828
  6.6 100.7 %all-to-all-start = ((bf16[8,4,128,512]{3,2,1,0:T(8,128)(2,1)}), bf16[8,4,128,512]{3,2,1,0:T(8,128)(2,1)}, u32[]{:S(2)}, u32[]{:S(2)}) async-start(bf16[8,4,128,512]{3,2,1,0:T(8,128)(2,1)} %bitcast.245), calls=%async_computation | async-start | bytes 8388608 | tf_op jit(solution)/shard_map/all_to_all | solution.py:110
  21.0 1.1 copy-start.3
  21.0 1.1 copy-start.6
  23.1 1.6 %copy-start.2 = (bf16[512,2048]{1,0:T(8,128)(2,1)S(1)}, bf16[512,2048]{1,0:T(8,128)(2,1)}, u32[]{:S(2)}) copy-start(bf16[512,2048]{1,0:T(8,128)(2,1)} %param.18) | copy-start | bytes 6291460
  118.8 1.5 %collective-permute-start.2 = (bf16[96,1024]{1,0:T(8,128)(2,1)S(1)}, bf16[96,1024]{1,0:T(8,128)(2,1)S(1)}, u32[]{:S(2)}, u32[]{:S(2)}) collective-permute-start(bf16[96,1024]{1,0:T(8,128)(2,1)S(1)} %pad_maximum_fusion.2), channel_id=1, source_target_pairs={{0,1},{1,0},{2,3},{3,2},{4,5},{5,4},{6,7},{7,6},{8,9},{9,8},{10,11... | collective-permute-start | bytes 589832 | tf_op jit(solution)/shard_map/ppermute | solution.py:61
  119.4 2.7 %collective-permute-start = (bf16[96,1024]{1,0:T(8,128)(2,1)S(1)}, bf16[96,1024]{1,0:T(8,128)(2,1)S(1)}, u32[]{:S(2)}, u32[]{:S(2)}) collective-permute-start(bf16[96,1024]{1,0:T(8,128)(2,1)S(1)} %pad_maximum_fusion.1), channel_id=1, source_target_pairs={{0,1},{1,0},{2,3},{3,2},{4,5},{5,4},{6,7},{7,6},{8,9},{9,8},{10,11... | collective-permute-start | bytes 589832 | tf_op jit(solution)/shard_map/ppermute | solution.py:61
  120.4 7.1 %copy-start.5 = (bf16[192,512]{1,0:T(8,128)(2,1)S(1)}, bf16[192,512]{1,0:T(8,128)(2,1)}, u32[]{:S(2)}) copy-start(bf16[192,512]{1,0:T(8,128)(2,1)} %param.17) | copy-start | bytes 589828
  120.5 5.6 %collective-permute-start.3 = (bf16[96,512]{1,0:T(8,128)(2,1)S(1)}, bf16[96,512]{1,0:T(8,128)(2,1)S(1)}, u32[]{:S(2)}, u32[]{:S(2)}) collective-permute-start(bf16[96,512]{1,0:T(8,128)(2,1)S(1)} %get-tuple-element.54), channel_id=1, source_target_pairs={{0,2},{1,3},{2,0},{3,1},{4,6},{5,7},{6,4},{7,5},{8,10},{9,11},{10,... | collective-permute-start | bytes 294920 | tf_op jit(solution)/shard_map/ppermute | solution.py:61
  122.3 5.3 %collective-permute-start.1 = (bf16[96,512]{1,0:T(8,128)(2,1)S(1)}, bf16[96,512]{1,0:T(8,128)(2,1)S(1)}, u32[]{:S(2)}, u32[]{:S(2)}) collective-permute-start(bf16[96,512]{1,0:T(8,128)(2,1)S(1)} %get-tuple-element.51), channel_id=1, source_target_pairs={{0,2},{1,3},{2,0},{3,1},{4,6},{5,7},{6,4},{7,5},{8,10},{9,11},{10,... | collective-permute-start | bytes 294920 | tf_op jit(solution)/shard_map/ppermute | solution.py:61
  127.6 0.7 copy-start.8

commit v20 on v16

--- a/solution.py
+++ b/solution.py
@@ -30,6 +30,34 @@
             preferred_element_type=jnp.float32,
         )
         parts.append((row_max, row_total, weighted))
+    return parts
+
+
+def blocked_attention(query_rows, key_rows, values, allowed, head_count):
+    rows, cols = query_rows.shape
+    head_width = cols // head_count
+    head_of_col = jnp.arange(cols, dtype=jnp.int32) // head_width
+    spread = jnp.where(
+        jnp.arange(head_count, dtype=jnp.int32)[:, None, None] == head_of_col[None, None, :],
+        query_rows[None],
+        jnp.zeros((), query_rows.dtype),
+    ).reshape(head_count * rows, cols)
+    scores = lax.dot_general(
+        spread, key_rows, (((1,), (1,)), ((), ())), preferred_element_type=jnp.float32
+    ) * head_width ** (-0.5)
+    scores = jnp.where(allowed, scores, NEG_FILL)
+    row_max = jnp.max(scores, axis=1, keepdims=True)
+    exp_scores = jnp.where(allowed, jnp.exp(scores - row_max), 0.0)
+    row_total = jnp.sum(exp_scores, axis=1, keepdims=True)
+    weighted = jnp.dot(exp_scores.astype(jnp.bfloat16), values, preferred_element_type=jnp.float32)
+    parts = []
+    for head in range(head_count):
+        block = slice(head * rows, (head + 1) * rows)
+        parts.append((
+            row_max[block],
+            row_total[block],
+            weighted[block, head * head_width : (head + 1) * head_width],
+        ))
     return parts
 
 
@@ -144,7 +172,7 @@
     )
     upper_limit = jnp.stack([root_len, mid_len])[None, :, None]
     upper_ok = (upper_pos < upper_limit).reshape(-1)
-    upper_part = partial_attention(
+    upper_part = blocked_attention(
         queries,
         recv_keys.reshape(-1, col_count),
         recv_values.reshape(-1, col_count),

time: 126 us -> 128 us (1.016)
    dot_general x0 -> x2, matrix products: none -> 3.97 us  [the longest x1 2.08 us: blocked_attention(): lax.dot_general(spread, key_rows, (((1,), (1,)), ((), ())), preferred_ele...]
    dot_general x8 -> x4, matrix products: 3.28 us -> 1.4 us  [partial_attention(): lax.dot_general(query_rows[:, cols], key_rows[:, cols], (((1,), (1,)), ((...]
    dot_general x8 -> x4, matrix products: 3.09 us -> 1.32 us  [partial_attention(): jnp.dot(exp_scores.astype(jnp.bfloat16), values[:, cols], preferred_eleme...]
    reduce_sum x0 -> x1, other arithmetic: none -> 1.58 us  [blocked_attention(): row_total = jnp.sum(exp_scores, axis=1, keepdims=True)]
    reduce_sum x3 -> x4, other arithmetic: 3.1 us -> 4.5 us  [pick(): return jnp.sum(jnp.where(ids == index, table, 0))]
    concatenate x2 -> x1, other arithmetic: 1.3 us -> 0.01 us  [shards(): jnp.concatenate([dest_nodes, node_count + dest_nodes], axis=1)]
    slice x1 -> x3, local copies, waits for them, and re-layouts: 2.49 us -> 2.64 us  [the longest x1 2.49 us: shards(): recv_keys = received[:, :2]]
where the time goes in v20:
time: 128 us; the launch traced here: 127 us
  waiting for transfers between devices  89.9 us (70%)
  other arithmetic  13.7 us (11%)
  starting transfers between devices  9.06 us (7%)
  matrix products  7.75 us (6%)
  local copies, waits for them, and re-layouts  5.83 us (5%)
    all_to_all x1, waiting for transfers between devices, shards(): received = lax.all_to_all(send, 'tok', 0, 0, tiled=True)  82.7 us
    all_to_all x1, starting transfers between devices, shards(): received = lax.all_to_all(send, 'tok', 0, 0, tiled=True)  7.4 us
    ppermute x2, waiting for transfers between devices, project_over_grp(): lax.ppermute(give, 'grp', [(g, g ^ step) for g in range(size)])  7.12 us
    reduce_sum x4, other arithmetic, pick(): return jnp.sum(jnp.where(ids == index, table, 0))  4.5 us
    gather x1, local copies, waits for them, and re-layouts, shards(): both.at[jnp.concatenate([dest_nodes, node_count + dest_nodes], axis=1)]  2.79 us
  transfers between devices with their start and end apart: 3, of which 3 were waited for; matrix products, arithmetic and copies ran while one was open for 8% of the time, Pallas kernels for 0%

profile of v20, /device:TPU:0, one launch (start us, length us, event | category | flops | bytes accessed | tf_op | source)
XLA Modules:
  0.0 127.2 jit_solution(12150259540906359946)
XLA Ops:
  0.0 0.8 select_reduce_fusion
  0.8 1.3 %select_reduce_fusion.1 = (s32[]{:T(128)}, s32[8,1]{0,1:T(1,128)S(1)}, s32[8,1,1]{0,1,2:T(1,128)S(1)}, s32[]{:T(128)}) fusion(s32[8]{0:T(128)} %param.24, s32[]{:T(128)S(6)} %axis_index.25, s32[8]{0:T(128)} %param.27), kind=kLoop, calls=%fused_computation.145 | loop fusion | flops 46 | bytes 140 | tf_op jit(solution)/shard_map/reduce_sum | solution.py:99
  2.1 0.1 copy.23
  2.2 0.1 reshape.280
  2.3 1.5 %pad_maximum_fusion = bf16[12,128,512]{2,1,0:T(8,128)(2,1)S(1)} fusion(bf16[6,128,512]{2,1,0:T(8,128)(2,1)} %param.22, bf16[6,128,512]{2,1,0:T(8,128)(2,1)} %param.21), kind=kLoop, calls=%fused_computation.12 | loop fusion | flops 786432 | bytes 3145728 | tf_op jit(solution)/shard_map/concatenate | solution.py:134
  3.8 2.8 %gather_fusion = bf16[32,128,512]{2,1,0:T(8,128)(2,1)} fusion(bf16[12,128,512]{2,1,0:T(8,128)(2,1)S(1)} %pad_maximum_fusion, s32[1024]{0:T(1024)S(1)} %pad_clamp_fusion), kind=kCustom, calls=%fused_computation | custom fusion | bytes 8388736 | tf_op jit(solution)/shard_map/gather | solution.py:135
  6.6 0.0 copy-start.8
  6.6 0.0 copy-start.7
  6.6 0.0 copy-start.1
  6.6 0.0 copy-start.3
  6.6 7.4 %all-to-all-start = ((bf16[8,4,128,512]{3,2,1,0:T(8,128)(2,1)}), bf16[8,4,128,512]{3,2,1,0:T(8,128)(2,1)}, u32[]{:S(2)}, u32[]{:S(2)}) async-start(bf16[8,4,128,512]{3,2,1,0:T(8,128)(2,1)} %bitcast.77), calls=%async_computation | async-start | bytes 8388608 | tf_op jit(solution)/shard_map/all_to_all | solution.py:138
  14.0 0.0 copy-start.6
  14.7 0.0 copy-done.8
  14.7 1.3 %fusion.82 = s32[]{:T(128)} fusion(s32[4]{0:T(128)S(1)} %copy-done.8, s32[]{:T(128)} %get-tuple-element.75), kind=kLoop, calls=%fused_computation.141 | loop fusion | flops 11 | bytes 24 | tf_op jit(solution)/shard_map/reduce_sum | solution.py:99
  16.0 0.0 copy-done.7
  16.0 1.3 fusion.83
  17.3 1.3 %pad_add_fusion.1 = s32[2]{0:T(128)S(1)} fusion(s32[1]{0:T(128)} %bitcast.15, s32[1]{0:T(128)} %bitcast.14), kind=kLoop, calls=%fused_computation.144 | loop fusion | flops 2 | bytes 16 | tf_op jit(solution)/shard_map/stack | solution.py:173
  18.6 0.1 iota_add_fusion
  18.7 0.1 broadcast_compare_fusion
  18.8 0.6 iota_compare_fusion.3
  19.4 0.0 copy-done.9
  19.4 0.6 select_reduce_fusion.3
  20.0 0.6 iota_compare_fusion.4
  20.7 0.0 copy-done
  20.7 0.0 copy-done.1
  20.7 0.0 copy-done.3
  20.7 0.3 fusion.112
  21.1 0.4 fusion.113
  21.4 0.4 fusion.114
  21.8 0.4 fusion.115
  22.1 0.0 copy-start.2
  22.2 0.0 copy-done.4
  22.2 0.0 copy-done.6
  22.2 0.3 fusion.33
  22.5 0.3 fusion.31
  22.8 0.3 fusion.29
  23.2 0.3 fusion.27
  23.5 0.8 fusion.25
  24.3 0.0 copy-done.2
  24.3 0.2 fusion.109
  24.5 0.1 broadcast_select_fusion
  24.5 82.7 %all-to-all-done = bf16[8,4,128,512]{3,2,1,0:T(8,128)(2,1)} async-done(((bf16[8,4,128,512]{3,2,1,0:T(8,128)(2,1)}), bf16[8,4,128,512]{3,2,1,0:T(8,128)(2,1)}, u32[]{:S(2)}, u32[]{:S(2)}) %all-to-all-start) | async-done | bytes 4194336 | tf_op jit(solution)/shard_map/all_to_all | solution.py:138
  107.3 2.5 %fusion.108 = (bf16[8,2,128,512]{3,2,1,0:T(8,128)(2,1)S(1)}, bf16[8,2,128,512]{3,2,1,0:T(8,128)(2,1)S(1)}) fusion(bf16[8,4,128,512]{3,2,1,0:T(8,128)(2,1)} %all-to-all-done), kind=kLoop, calls=%fused_computation.167 | loop fusion | bytes 8388608 | tf_op jit(solution)/shard_map/slice | solution.py:139
  109.8 2.1 %fusion = (f32[768]{0:T(1024)S(1)}, f32[768,2048]{1,0:T(8,128)S(1)}) fusion(pred[2048]{0:T(1024)(128)(4,1)S(1)} %lt.62, bf16[768,512]{1,0:T(8,128)(2,1)S(1)} %bitcast.84, bf16[2048,512]{1,0:T(8,128)(2,1)S(1)} %bitcast.83), kind=kOutput, calls=%fused_computation.3 | convolution fusion | flops 1615330560 | bytes 9180160 | tf_op jit(solution)/shard_map/dot_general | solution.py:45
  111.9 0.1 fusion.110
  111.9 1.6 %fusion.1 = f32[768]{0:T(1024)S(1)} fusion(f32[768,2048]{1,0:T(8,128)S(1)} %get-tuple-element.79, f32[768]{0:T(1024)S(1)} %get-tuple-element.78, pred[2048]{0:T(1024)(128)(4,1)S(1)} %lt.62), kind=kLoop, calls=%fused_computation.4 | loop fusion | flops 7863552 | bytes 6299648 | tf_op jit(solution)/shard_map/reduce_sum | solution.py:51
  113.5 1.9 %fusion.3 = f32[768,512]{1,0:T(8,128)S(1)} fusion(bf16[2048,512]{1,0:T(8,128)(2,1)S(1)} %bitcast.82, f32[768,2048]{1,0:T(8,128)S(1)} %get-tuple-element.79, f32[768]{0:T(1024)S(1)} %get-tuple-element.78, pred[2048]{0:T(1024)(128)(4,1)S(1)} %lt.62), kind=kOutput, calls=%fused_computation.6 | convolution fusion | flops 1618477056 | bytes 9966592 | tf_op jit(solution)/shard_map/dot_general | solution.py:52
  115.4 0.1 fusion.111
  115.6 0.1 fusion.63
  115.7 0.3 fusion.65
  116.0 0.1 fusion.26
  116.1 0.3 fusion.116
  116.4 0.3 fusion.117
  116.7 0.0 copy-start.5
  116.7 0.3 select_convert_fusion.1
  117.0 0.3 select_convert_fusion.2
  117.3 0.1 collective-permute-start
  117.4 1.7 %collective-permute-done = bf16[192,1024]{1,0:T(8,128)(2,1)S(1)} collective-permute-done((bf16[192,1024]{1,0:T(8,128)(2,1)S(1)}, bf16[192,1024]{1,0:T(8,128)(2,1)S(1)}, u32[]{:S(2)}, u32[]{:S(2)}) %collective-permute-start) | collective-permute-done | bytes 393248 | tf_op jit(solution)/shard_map/ppermute | solution.py:89
  119.1 0.1 convert_element_type.40
  119.1 0.3 select_convert_fusion
  119.4 1.6 %collective-permute-start.1 = (bf16[192,512]{1,0:T(8,128)(2,1)S(1)}, bf16[192,512]{1,0:T(8,128)(2,1)S(1)}, u32[]{:S(2)}, u32[]{:S(2)}) collective-permute-start(bf16[192,512]{1,0:T(8,128)(2,1)S(1)} %get-tuple-element.43), channel_id=1, source_target_pairs={{0,2},{1,3},{2,0},{3,1},{4,6},{5,7},{6,4},{7,5},{8,10},{9,11},{10,... | collective-permute-start | bytes 589832 | tf_op jit(solution)/shard_map/ppermute | solution.py:89
  121.0 5.4 %collective-permute-done.1 = bf16[192,512]{1,0:T(8,128)(2,1)S(1)} collective-permute-done((bf16[192,512]{1,0:T(8,128)(2,1)S(1)}, bf16[192,512]{1,0:T(8,128)(2,1)S(1)}, u32[]{:S(2)}, u32[]{:S(2)}) %collective-permute-start.1) | collective-permute-done | bytes 196640 | tf_op jit(solution)/shard_map/ppermute | solution.py:89
  126.4 0.0 copy-done.5
  126.4 0.8 add_convert_fusion
  (17 shorter events, 0.2 us)
Async XLA Ops:
  6.6 8.2 %copy-start.8 = (s32[4]{0:T(128)S(1)}, s32[4]{0:T(128)}, u32[]{:S(2)}) copy-start(s32[4]{0:T(128)} %param.25) | copy-start | bytes 52
  6.6 9.5 %copy-start.7 = (s32[6]{0:T(128)S(1)}, s32[6]{0:T(128)}, u32[]{:S(2)}) copy-start(s32[6]{0:T(128)} %param.26) | copy-start | bytes 76
  6.6 12.8 %copy-start.9 = (s32[8]{0:T(128)S(1)}, s32[8]{0:T(128)}, u32[]{:S(2)}) copy-start(s32[8]{0:T(128)} %param.23) | copy-start | bytes 100
  6.6 14.1 %copy-start = (bf16[1,512,512]{2,1,0:T(8,128)(2,1)S(1)}, bf16[1,512,512]{2,1,0:T(8,128)(2,1)}, u32[]{:S(2)}) copy-start(bf16[1,512,512]{2,1,0:T(8,128)(2,1)} %param.19) | copy-start | bytes 1572868
  6.6 14.1 %copy-start.1 = (bf16[192,512]{1,0:T(8,128)(2,1)S(1)}, bf16[192,512]{1,0:T(8,128)(2,1)}, u32[]{:S(2)}) copy-start(bf16[192,512]{1,0:T(8,128)(2,1)} %param.15) | copy-start | bytes 589828
  6.6 14.1 %copy-start.3 = (bf16[192,512]{1,0:T(8,128)(2,1)S(1)}, bf16[192,512]{1,0:T(8,128)(2,1)}, u32[]{:S(2)}) copy-start(bf16[192,512]{1,0:T(8,128)(2,1)} %param.14) | copy-start | bytes 589828
  6.6 100.7 %all-to-all-start = ((bf16[8,4,128,512]{3,2,1,0:T(8,128)(2,1)}), bf16[8,4,128,512]{3,2,1,0:T(8,128)(2,1)}, u32[]{:S(2)}, u32[]{:S(2)}) async-start(bf16[8,4,128,512]{3,2,1,0:T(8,128)(2,1)} %bitcast.77), calls=%async_computation | async-start | bytes 8388608 | tf_op jit(solution)/shard_map/all_to_all | solution.py:138
  14.0 8.2 %copy-start.4 = (bf16[1,512,512]{2,1,0:T(8,128)(2,1)S(1)}, bf16[1,512,512]{2,1,0:T(8,128)(2,1)}, u32[]{:S(2)}) copy-start(bf16[1,512,512]{2,1,0:T(8,128)(2,1)} %param.20) | copy-start | bytes 1572868
  14.0 8.2 %copy-start.6 = (bf16[192,512]{1,0:T(8,128)(2,1)S(1)}, bf16[192,512]{1,0:T(8,128)(2,1)}, u32[]{:S(2)}) copy-start(bf16[192,512]{1,0:T(8,128)(2,1)} %param.16) | copy-start | bytes 589828
  22.1 2.1 %copy-start.2 = (bf16[512,2048]{1,0:T(8,128)(2,1)S(1)}, bf16[512,2048]{1,0:T(8,128)(2,1)}, u32[]{:S(2)}) copy-start(bf16[512,2048]{1,0:T(8,128)(2,1)} %param.18) | copy-start | bytes 6291460
  116.7 9.8 %copy-start.5 = (bf16[192,512]{1,0:T(8,128)(2,1)S(1)}, bf16[192,512]{1,0:T(8,128)(2,1)}, u32[]{:S(2)}) copy-start(bf16[192,512]{1,0:T(8,128)(2,1)} %param.17) | copy-start | bytes 589828
  117.3 1.8 %collective-permute-start = (bf16[192,1024]{1,0:T(8,128)(2,1)S(1)}, bf16[192,1024]{1,0:T(8,128)(2,1)S(1)}, u32[]{:S(2)}, u32[]{:S(2)}) collective-permute-start(bf16[192,1024]{1,0:T(8,128)(2,1)S(1)} %pad_maximum_fusion.1), channel_id=1, source_target_pairs={{0,1},{1,0},{2,3},{3,2},{4,5},{5,4},{6,7},{7,6},{8,9},{9,8},{10,11... | collective-permute-start | bytes 1179656 | tf_op jit(solution)/shard_map/ppermute | solution.py:89
  119.4 7.0 %collective-permute-start.1 = (bf16[192,512]{1,0:T(8,128)(2,1)S(1)}, bf16[192,512]{1,0:T(8,128)(2,1)S(1)}, u32[]{:S(2)}, u32[]{:S(2)}) collective-permute-start(bf16[192,512]{1,0:T(8,128)(2,1)S(1)} %get-tuple-element.43), channel_id=1, source_target_pairs={{0,2},{1,3},{2,0},{3,1},{4,6},{5,7},{6,4},{7,5},{8,10},{9,11},{10,... | collective-permute-start | bytes 589832 | tf_op jit(solution)/shard_map/ppermute | solution.py:89

commit v21 on v16

--- a/solution.py
+++ b/solution.py
@@ -103,13 +103,12 @@
         jnp.where(dest_mid[:, None] == mid_ids[None, :], mid_root[None, :], 0), axis=1
     )
     dest_nodes = jnp.stack([dest_root, root_count + dest_mid], axis=1)
-    both = jnp.concatenate([upper_keys, upper_values], axis=0)
-    send = both.at[jnp.concatenate([dest_nodes, node_count + dest_nodes], axis=1)].get(
-        mode="promise_in_bounds"
+    recv_keys = lax.all_to_all(
+        upper_keys.at[dest_nodes].get(mode="promise_in_bounds"), "tok", 0, 0, tiled=True
     )
-    received = lax.all_to_all(send, "tok", 0, 0, tiled=True)
-    recv_keys = received[:, :2]
-    recv_values = received[:, 2:]
+    recv_values = lax.all_to_all(
+        upper_values.at[dest_nodes].get(mode="promise_in_bounds"), "tok", 0, 0, tiled=True
+    )
 
     my_length = pick(req_len, my_index)
     my_mid = pick(leaf_mid, my_index)

time: 126 us -> 131 us (1.040)
  matrix products: 7.43 us -> 18.7 us
  waiting for transfers between devices: 88.9 us -> 79.7 us
  starting transfers between devices: 9.06 us -> 13.4 us
    all_to_all x1 -> x2, waiting for transfers between devices: 81.8 us -> 72.6 us  [the longest x1 38.5 us: shards(): lax.all_to_all(upper_keys.at[dest_nodes].get(mode='promise_in_bounds'), '...]
    dot_general x8, matrix products: 3.09 us -> 8.99 us  [partial_attention(): jnp.dot(exp_scores.astype(jnp.bfloat16), values[:, cols], preferred_eleme...]
    dot_general x8, matrix products: 3.28 us -> 8.63 us  [partial_attention(): lax.dot_general(query_rows[:, cols], key_rows[:, cols], (((1,), (1,)), ((...]
    all_to_all x1 -> x2, starting transfers between devices: 7.4 us -> 11.8 us  [the longest x1 7.38 us: shards(): lax.all_to_all(upper_keys.at[dest_nodes].get(mode='promise_in_bounds'), '...]
    concatenate x3 -> x0, other arithmetic: 2.81 us -> none  [the longest x1 1.51 us: shards(): both = jnp.concatenate([upper_keys, upper_values], axis=0)]
    slice x1 -> x0, local copies, waits for them, and re-layouts: 2.49 us -> none  [shards(): recv_values = received[:, 2:]]
    another operation x0 -> x1, other arithmetic: none -> 1.32 us  [shards(): dest_nodes = jnp.stack([dest_root, root_count + dest_mid], axis=1)]
    gather x1 -> x2, local copies, waits for them, and re-layouts: 2.79 us -> 3.99 us  [the longest x1 2.01 us: shards(): upper_values.at[dest_nodes].get(mode='promise_in_bounds')]
  transfers between devices with their start and end apart: 3 -> 4, of which waited for: 3 -> 4; matrix products, arithmetic and copies ran while one was open for 8% -> 17% of each run, Pallas kernels for 0% -> 0%
where the time goes in v21:
time: 131 us; the launch traced here: 130 us
  waiting for transfers between devices  79.7 us (61%)
  matrix products  18.7 us (14%)
  starting transfers between devices  13.4 us (10%)
  other arithmetic  11.4 us (9%)
  local copies, waits for them, and re-layouts  6.07 us (5%)
    all_to_all x1, waiting for transfers between devices, shards(): lax.all_to_all(upper_keys.at[dest_nodes].get(mode='promise_in_bounds'), '...  38.5 us
    all_to_all x1, waiting for transfers between devices, shards(): lax.all_to_all(upper_values.at[dest_nodes].get(mode='promise_in_bounds'),...  34.1 us
    dot_general x8, matrix products, partial_attention(): jnp.dot(exp_scores.astype(jnp.bfloat16), values[:, cols], preferred_eleme...  8.99 us
    dot_general x8, matrix products, partial_attention(): lax.dot_general(query_rows[:, cols], key_rows[:, cols], (((1,), (1,)), ((...  8.63 us
    all_to_all x1, starting transfers between devices, shards(): lax.all_to_all(upper_keys.at[dest_nodes].get(mode='promise_in_bounds'), '...  7.38 us
    ppermute x2, waiting for transfers between devices, project_over_grp(): lax.ppermute(give, 'grp', [(g, g ^ step) for g in range(size)])  7.13 us
    all_to_all x1, starting transfers between devices, shards(): lax.all_to_all(upper_values.at[dest_nodes].get(mode='promise_in_bounds'),...  4.37 us
    reduce_sum x3, other arithmetic, pick(): return jnp.sum(jnp.where(ids == index, table, 0))  3.2 us
  transfers between devices with their start and end apart: 4, of which 4 were waited for; matrix products, arithmetic and copies ran while one was open for 17% of the time, Pallas kernels for 0%

profile of v21, /device:TPU:0, one launch (start us, length us, event | category | flops | bytes accessed | tf_op | source)
XLA Modules:
  0.0 130.3 jit_solution(523486770334978539)
XLA Ops:
  0.0 0.0 copy-start
  0.0 0.8 select_reduce_fusion
  0.8 1.3 %add_bitcast_fusion = (s32[8,1,1]{0,2,1:T(1,128)S(1)}, s32[]{:T(128)}, s32[]{:T(128)}) fusion(s32[8]{0:T(128)} %param.24, s32[]{:T(128)S(6)} %axis_index.25, s32[8]{0:T(128)} %param.27), kind=kLoop, calls=%fused_computation.167 | loop fusion | flops 46 | bytes 108 | tf_op jit(solution)/shard_map/stack | solution.py:105
  2.2 0.1 copy.17
  2.2 0.1 reshape.159
  2.3 2.0 %gather_fusion = bf16[16,128,512]{2,1,0:T(8,128)(2,1)} fusion(bf16[6,128,512]{2,1,0:T(8,128)(2,1)S(1)} %copy-done, s32[1024]{0:T(1024)S(1)} %pad_clamp_fusion), kind=kCustom, calls=%fused_computation | custom fusion | bytes 4194368 | tf_op jit(solution)/shard_map/gather | solution.py:107
  4.3 7.4 %all-to-all-start = ((bf16[8,2,128,512]{3,2,1,0:T(8,128)(2,1)}), bf16[8,2,128,512]{3,2,1,0:T(8,128)(2,1)}, u32[]{:S(2)}, u32[]{:S(2)}) async-start(bf16[8,2,128,512]{3,2,1,0:T(8,128)(2,1)} %bitcast.18), calls=%async_computation | async-start | bytes 4194304 | tf_op jit(solution)/shard_map/all_to_all | solution.py:106
  12.4 1.3 fusion.108
  13.7 1.3 fusion.109
  14.9 1.3 %pad_add_fusion.1 = s32[2]{0:T(128)S(1)} fusion(s32[1]{0:T(128)} %bitcast.15, s32[1]{0:T(128)} %bitcast.14), kind=kLoop, calls=%fused_computation.166 | loop fusion | flops 2 | bytes 16 | tf_op jit(solution)/shard_map/stack | solution.py:144
  16.3 0.1 iota_add_fusion
  16.3 0.1 broadcast_compare_fusion
  16.4 0.0 copy-start.19
  16.5 0.0 copy-start.1
  16.5 0.0 copy-start.3
  16.5 0.0 copy-start.14
  16.5 2.0 %gather_fusion.1 = bf16[16,128,512]{2,1,0:T(8,128)(2,1)} fusion(bf16[6,128,512]{2,1,0:T(8,128)(2,1)S(1)} %copy-done.2, s32[1024]{0:T(1024)S(1)} %pad_clamp_fusion), kind=kCustom, calls=%fused_computation.1 | custom fusion | bytes 4194368 | tf_op jit(solution)/shard_map/gather | solution.py:110
  18.5 0.6 iota_compare_fusion.2
  19.1 0.0 copy-done.19
  19.1 0.6 select_reduce_fusion.3
  19.7 0.6 iota_compare_fusion.3
  20.5 0.3 fusion.140
  20.8 0.4 fusion.139
  21.2 0.4 fusion.138
  21.5 38.5 %all-to-all-done = bf16[8,2,128,512]{3,2,1,0:T(8,128)(2,1)} async-done(((bf16[8,2,128,512]{3,2,1,0:T(8,128)(2,1)}), bf16[8,2,128,512]{3,2,1,0:T(8,128)(2,1)}, u32[]{:S(2)}, u32[]{:S(2)}) %all-to-all-start) | async-done | bytes 2097184 | tf_op jit(solution)/shard_map/all_to_all | solution.py:106
  60.0 4.4 %all-to-all-start.1 = ((bf16[8,2,128,512]{3,2,1,0:T(8,128)(2,1)}), bf16[8,2,128,512]{3,2,1,0:T(8,128)(2,1)}, u32[]{:S(2)}, u32[]{:S(2)}) async-start(bf16[8,2,128,512]{3,2,1,0:T(8,128)(2,1)} %bitcast.22), calls=%async_computation.1 | async-start | bytes 4194304 | tf_op jit(solution)/shard_map/all_to_all | solution.py:109
  64.4 0.0 copy-start.13
  64.4 0.0 copy-start.16
  64.5 0.3 fusion.137
  64.8 1.2 fusion.63
  66.1 0.3 fusion.65
  66.4 0.3 fusion.61
  66.7 0.3 fusion.67
  67.1 0.0 copy-start.4
  67.1 0.8 fusion.59
  67.8 0.8 copy-done.4
  68.6 1.0 fusion.135
  69.6 1.5 %fusion.136 = (f32[192]{0:T(256)S(1)}, f32[2048,192]{0,1:T(8,128)S(1)}) fusion(bf16[192,512]{1,0:T(8,128)(2,1)S(1)} %copy-done.14, bf16[2048,512]{1,0:T(8,128)(2,1)} %bitcast.19, pred[2048]{0:T(1024)(128)(4,1)S(1)} %lt.62), kind=kOutput, calls=%fused_computation.190 | convolution fusion | flops 101842752 | bytes 2149120 | tf_op jit(solution)/shard_map/dot_general | solution.py:17
  71.1 1.9 %fusion.143 = (f32[192]{0:T(256)S(1)}, f32[2048,192]{0,1:T(8,128)S(1)}) fusion(bf16[192,512]{1,0:T(8,128)(2,1)S(1)} %copy-done.14, bf16[2048,512]{1,0:T(8,128)(2,1)} %bitcast.19, pred[2048]{0:T(1024)(128)(4,1)S(1)} %lt.62), kind=kOutput, calls=%fused_computation.197 | convolution fusion | flops 101842752 | bytes 2149120 | tf_op jit(solution)/shard_map/dot_general | solution.py:17
  73.1 1.9 %fusion.142 = (f32[192]{0:T(256)S(1)}, f32[2048,192]{0,1:T(8,128)S(1)}) fusion(bf16[192,512]{1,0:T(8,128)(2,1)S(1)} %copy-done.14, bf16[2048,512]{1,0:T(8,128)(2,1)} %bitcast.19, pred[2048]{0:T(1024)(128)(4,1)S(1)} %lt.62), kind=kOutput, calls=%fused_computation.196 | convolution fusion | flops 101842752 | bytes 2149120 | tf_op jit(solution)/shard_map/dot_general | solution.py:17
  75.0 1.9 %fusion.141 = (f32[192]{0:T(256)S(1)}, f32[2048,192]{0,1:T(8,128)S(1)}) fusion(bf16[192,512]{1,0:T(8,128)(2,1)S(1)} %copy-done.14, bf16[2048,512]{1,0:T(8,128)(2,1)} %bitcast.19, pred[2048]{0:T(1024)(128)(4,1)S(1)} %lt.62), kind=kOutput, calls=%fused_computation.195 | convolution fusion | flops 101842752 | bytes 2149120 | tf_op jit(solution)/shard_map/dot_general | solution.py:17
  76.9 1.2 fusion.4
  78.1 0.0 copy-done.10
  78.1 0.0 copy-done.12
  78.1 34.1 %all-to-all-done.1 = bf16[8,2,128,512]{3,2,1,0:T(8,128)(2,1)} async-done(((bf16[8,2,128,512]{3,2,1,0:T(8,128)(2,1)}), bf16[8,2,128,512]{3,2,1,0:T(8,128)(2,1)}, u32[]{:S(2)}, u32[]{:S(2)}) %all-to-all-start.1) | async-done | bytes 2097184 | tf_op jit(solution)/shard_map/all_to_all | solution.py:109
  112.2 2.1 %fusion.27 = bf16[192,128]{1,0:T(8,128)(2,1)S(1)} fusion(f32[2048,192]{0,1:T(8,128)} %copy-done.12, f32[192]{0:T(256)S(1)} %get-tuple-element.78, pred[2048]{0:T(1024)(128)(4,1)S(1)} %lt.62, bf16[2048,512]{1,0:T(8,128)(2,1)} %bitcast.23, f32[192,128]{1,0:T(8,128)S(1)} %fusion.67, f32[192]{0:T(256)S(1)} %bitcast.92, f32[192]{0:T(256)S(1)} %bitcast.94, ...), kind=kOutput, calls=%fused_computation.45 | convolution fusion | flops 101965824 | bytes 2249728 | tf_op jit(solution)/shard_map/dot_general | solution.py:27
  114.3 0.0 copy-start.9
  114.3 0.0 copy-done.11
  114.3 1.6 %fusion.25 = bf16[192,128]{1,0:T(8,128)(2,1)S(1)} fusion(f32[2048,192]{0,1:T(8,128)S(1)} %copy-done.11, f32[192]{0:T(256)S(1)} %get-tuple-element.80, pred[2048]{0:T(1024)(128)(4,1)S(1)} %lt.62, bf16[2048,512]{1,0:T(8,128)(2,1)} %bitcast.23, f32[192,128]{1,0:T(8,128)S(1)} %fusion.65, f32[192]{0:T(256)S(1)} %bitcast.89, f32[192]{0:T(256)S(1)} %bitcast.91, ...), kind=kOutput, calls=%fused_computation.42 | convolution fusion | flops 101965824 | bytes 2249728 | tf_op jit(solution)/shard_map/dot_general | solution.py:27
  116.0 1.6 %fusion.23 = bf16[192,128]{1,0:T(8,128)(2,1)S(1)} fusion(f32[2048,192]{0,1:T(8,128)S(1)} %copy-done.9, f32[192]{0:T(256)S(1)} %get-tuple-element.82, pred[2048]{0:T(1024)(128)(4,1)S(1)} %lt.62, bf16[2048,512]{1,0:T(8,128)(2,1)} %bitcast.23, f32[192,128]{1,0:T(8,128)S(1)} %fusion.63, f32[192]{0:T(256)S(1)} %bitcast.98, f32[192]{0:T(256)S(1)} %bitcast.100, ...), kind=kOutput, calls=%fused_computation.39 | convolution fusion | flops 101965824 | bytes 2249728 | tf_op jit(solution)/shard_map/dot_general | solution.py:27
  117.6 1.5 %fusion.21 = bf16[192,128]{1,0:T(8,128)(2,1)S(1)} fusion(f32[2048,192]{0,1:T(8,128)S(1)} %copy-done.7, f32[192]{0:T(256)S(1)} %get-tuple-element.68, pred[2048]{0:T(1024)(128)(4,1)S(1)} %lt.62, bf16[2048,512]{1,0:T(8,128)(2,1)} %bitcast.23, f32[192,128]{1,0:T(8,128)S(1)} %fusion.61, f32[192]{0:T(256)S(1)} %bitcast.95, f32[192]{0:T(256)S(1)} %bitcast.97, ...), kind=kOutput, calls=%fused_computation.36 | convolution fusion | flops 101965824 | bytes 2249728 | tf_op jit(solution)/shard_map/dot_general | solution.py:27
  119.1 0.1 fusion.60
  119.2 0.3 fusion.145
  119.5 0.3 fusion.144
  119.8 0.3 select_convert_fusion.1
  120.1 0.3 select_convert_fusion.2
  120.4 0.1 collective-permute-start
  120.5 1.7 %collective-permute-done = bf16[192,1024]{1,0:T(8,128)(2,1)S(1)} collective-permute-done((bf16[192,1024]{1,0:T(8,128)(2,1)S(1)}, bf16[192,1024]{1,0:T(8,128)(2,1)S(1)}, u32[]{:S(2)}, u32[]{:S(2)}) %collective-permute-start) | collective-permute-done | bytes 393248 | tf_op jit(solution)/shard_map/ppermute | solution.py:61
  122.2 0.1 convert_element_type.52
  122.2 0.0 copy-start.15
  122.3 0.3 select_convert_fusion
  122.5 1.6 %collective-permute-start.1 = (bf16[192,512]{1,0:T(8,128)(2,1)S(1)}, bf16[192,512]{1,0:T(8,128)(2,1)S(1)}, u32[]{:S(2)}, u32[]{:S(2)}) collective-permute-start(bf16[192,512]{1,0:T(8,128)(2,1)S(1)} %get-tuple-element.47), channel_id=1, source_target_pairs={{0,2},{1,3},{2,0},{3,1},{4,6},{5,7},{6,4},{7,5},{8,10},{9,11},{10,... | collective-permute-start | bytes 589832 | tf_op jit(solution)/shard_map/ppermute | solution.py:61
  124.1 5.4 %collective-permute-done.1 = bf16[192,512]{1,0:T(8,128)(2,1)S(1)} collective-permute-done((bf16[192,512]{1,0:T(8,128)(2,1)S(1)}, bf16[192,512]{1,0:T(8,128)(2,1)S(1)}, u32[]{:S(2)}, u32[]{:S(2)}) %collective-permute-start.1) | collective-permute-done | bytes 196640 | tf_op jit(solution)/shard_map/ppermute | solution.py:61
  129.6 0.8 add_convert_fusion
  (36 shorter events, 0.2 us)
Async XLA Ops:
  0.0 2.3 %copy-start = (bf16[6,128,512]{2,1,0:T(8,128)(2,1)S(1)}, bf16[6,128,512]{2,1,0:T(8,128)(2,1)}, u32[]{:S(2)}) copy-start(bf16[6,128,512]{2,1,0:T(8,128)(2,1)} %param.21) | copy-start | bytes 2359300
  4.3 8.1 %copy-start.18 = (s32[4]{0:T(128)S(1)}, s32[4]{0:T(128)}, u32[]{:S(2)}) copy-start(s32[4]{0:T(128)} %param.25) | copy-start | bytes 52
  4.3 9.3 %copy-start.17 = (s32[6]{0:T(128)S(1)}, s32[6]{0:T(128)}, u32[]{:S(2)}) copy-start(s32[6]{0:T(128)} %param.26) | copy-start | bytes 76
  4.3 12.1 %copy-start.2 = (bf16[6,128,512]{2,1,0:T(8,128)(2,1)S(1)}, bf16[6,128,512]{2,1,0:T(8,128)(2,1)}, u32[]{:S(2)}) copy-start(bf16[6,128,512]{2,1,0:T(8,128)(2,1)} %param.22) | copy-start | bytes 2359300
  4.3 55.7 %all-to-all-start = ((bf16[8,2,128,512]{3,2,1,0:T(8,128)(2,1)}), bf16[8,2,128,512]{3,2,1,0:T(8,128)(2,1)}, u32[]{:S(2)}, u32[]{:S(2)}) async-start(bf16[8,2,128,512]{3,2,1,0:T(8,128)(2,1)} %bitcast.18), calls=%async_computation | async-start | bytes 4194304 | tf_op jit(solution)/shard_map/all_to_all | solution.py:106
  16.4 2.7 %copy-start.19 = (s32[8]{0:T(128)S(1)}, s32[8]{0:T(128)}, u32[]{:S(2)}) copy-start(s32[8]{0:T(128)} %param.23) | copy-start | bytes 100
  16.5 4.0 %copy-start.1 = (bf16[1,512,512]{2,1,0:T(8,128)(2,1)S(1)}, bf16[1,512,512]{2,1,0:T(8,128)(2,1)}, u32[]{:S(2)}) copy-start(bf16[1,512,512]{2,1,0:T(8,128)(2,1)} %param.19) | copy-start | bytes 1572868
  16.5 4.0 %copy-start.3 = (bf16[192,512]{1,0:T(8,128)(2,1)S(1)}, bf16[192,512]{1,0:T(8,128)(2,1)}, u32[]{:S(2)}) copy-start(bf16[192,512]{1,0:T(8,128)(2,1)} %param.15) | copy-start | bytes 589828
  16.5 4.0 %copy-start.14 = (bf16[192,512]{1,0:T(8,128)(2,1)S(1)}, bf16[192,512]{1,0:T(8,128)(2,1)}, u32[]{:S(2)}) copy-start(bf16[192,512]{1,0:T(8,128)(2,1)} %param.14) | copy-start | bytes 589828
  60.0 52.2 %all-to-all-start.1 = ((bf16[8,2,128,512]{3,2,1,0:T(8,128)(2,1)}), bf16[8,2,128,512]{3,2,1,0:T(8,128)(2,1)}, u32[]{:S(2)}, u32[]{:S(2)}) async-start(bf16[8,2,128,512]{3,2,1,0:T(8,128)(2,1)} %bitcast.22), calls=%async_computation.1 | async-start | bytes 4194304 | tf_op jit(solution)/shard_map/all_to_all | solution.py:109
  64.4 1.6 %copy-start.13 = (bf16[1,512,512]{2,1,0:T(8,128)(2,1)S(1)}, bf16[1,512,512]{2,1,0:T(8,128)(2,1)}, u32[]{:S(2)}) copy-start(bf16[1,512,512]{2,1,0:T(8,128)(2,1)} %param.20) | copy-start | bytes 1572868
  64.4 1.6 %copy-start.16 = (bf16[192,512]{1,0:T(8,128)(2,1)S(1)}, bf16[192,512]{1,0:T(8,128)(2,1)}, u32[]{:S(2)}) copy-start(bf16[192,512]{1,0:T(8,128)(2,1)} %param.16) | copy-start | bytes 589828
  67.1 1.6 %copy-start.4 = (bf16[512,2048]{1,0:T(8,128)(2,1)S(1)}, bf16[512,2048]{1,0:T(8,128)(2,1)}, u32[]{:S(2)}) copy-start(bf16[512,2048]{1,0:T(8,128)(2,1)} %param.18) | copy-start | bytes 6291460
  71.1 5.8 %copy-start.6 = (f32[2048,192]{0,1:T(8,128)}, f32[2048,192]{0,1:T(8,128)S(1)}, u32[]{:S(2)}) copy-start(f32[2048,192]{0,1:T(8,128)S(1)} %get-tuple-element.69) | copy-start | bytes 4718596
  73.0 3.9 %copy-start.8 = (f32[2048,192]{0,1:T(8,128)}, f32[2048,192]{0,1:T(8,128)S(1)}, u32[]{:S(2)}) copy-start(f32[2048,192]{0,1:T(8,128)S(1)} %get-tuple-element.83) | copy-start | bytes 4718596
  75.0 3.1 %copy-start.10 = (f32[2048,192]{0,1:T(8,128)}, f32[2048,192]{0,1:T(8,128)S(1)}, u32[]{:S(2)}) copy-start(f32[2048,192]{0,1:T(8,128)S(1)} %get-tuple-element.81) | copy-start | bytes 4718596
  76.9 1.2 copy-start.12
  112.2 2.1 %copy-start.11 = (f32[2048,192]{0,1:T(8,128)S(1)}, f32[2048,192]{0,1:T(8,128)}, u32[]{:S(2)}) copy-start(f32[2048,192]{0,1:T(8,128)} %copy-done.10) | copy-start | bytes 4718596
  114.3 1.6 %copy-start.9 = (f32[2048,192]{0,1:T(8,128)S(1)}, f32[2048,192]{0,1:T(8,128)}, u32[]{:S(2)}) copy-start(f32[2048,192]{0,1:T(8,128)} %copy-done.8) | copy-start | bytes 4718596
  115.9 1.7 %copy-start.7 = (f32[2048,192]{0,1:T(8,128)S(1)}, f32[2048,192]{0,1:T(8,128)}, u32[]{:S(2)}) copy-start(f32[2048,192]{0,1:T(8,128)} %copy-done.6) | copy-start | bytes 4718596
  117.6 1.7 %copy-start.5 = (bf16[512,512]{1,0:T(8,128)(2,1)S(1)}, bf16[512,512]{1,0:T(8,128)(2,1)}, u32[]{:S(2)}) copy-start(bf16[512,512]{1,0:T(8,128)(2,1)} %get-tuple-element.36) | copy-start | bytes 1572868
  120.4 1.8 %collective-permute-start = (bf16[192,1024]{1,0:T(8,128)(2,1)S(1)}, bf16[192,1024]{1,0:T(8,128)(2,1)S(1)}, u32[]{:S(2)}, u32[]{:S(2)}) collective-permute-start(bf16[192,1024]{1,0:T(8,128)(2,1)S(1)} %pad_maximum_fusion), channel_id=1, source_target_pairs={{0,1},{1,0},{2,3},{3,2},{4,5},{5,4},{6,7},{7,6},{8,9},{9,8},{10,11... | collective-permute-start | bytes 1179656 | tf_op jit(solution)/shard_map/ppermute | solution.py:61
  122.2 7.3 %copy-start.15 = (bf16[192,512]{1,0:T(8,128)(2,1)S(1)}, bf16[192,512]{1,0:T(8,128)(2,1)}, u32[]{:S(2)}) copy-start(bf16[192,512]{1,0:T(8,128)(2,1)} %param.17) | copy-start | bytes 589828
  122.5 7.0 %collective-permute-start.1 = (bf16[192,512]{1,0:T(8,128)(2,1)S(1)}, bf16[192,512]{1,0:T(8,128)(2,1)S(1)}, u32[]{:S(2)}, u32[]{:S(2)}) collective-permute-start(bf16[192,512]{1,0:T(8,128)(2,1)S(1)} %get-tuple-element.47), channel_id=1, source_target_pairs={{0,2},{1,3},{2,0},{3,1},{4,6},{5,7},{6,4},{7,5},{8,10},{9,11},{10,... | collective-permute-start | bytes 589832 | tf_op jit(solution)/shard_map/ppermute | solution.py:61

commit v22 on v16

--- a/solution.py
+++ b/solution.py
@@ -9,7 +9,7 @@
 NEG_FILL = -1e30
 
 
-def partial_attention(query_rows, key_rows, values, allowed, head_count):
+def partial_attention(query_rows, key_rows, values, allowed, head_count, some_allowed=False):
     head_width = query_rows.shape[1] // head_count
     parts = []
     for head in range(head_count):
@@ -22,7 +22,9 @@
         ) * head_width ** (-0.5)
         scores = jnp.where(allowed, scores, NEG_FILL)
         row_max = jnp.max(scores, axis=1, keepdims=True)
-        exp_scores = jnp.where(allowed, jnp.exp(scores - row_max), 0.0)
+        exp_scores = jnp.exp(scores - row_max)
+        if not some_allowed:
+            exp_scores = jnp.where(allowed, exp_scores, 0.0)
         row_total = jnp.sum(exp_scores, axis=1, keepdims=True)
         weighted = jnp.dot(
             exp_scores.astype(jnp.bfloat16),
@@ -150,6 +152,7 @@
         recv_values.reshape(-1, col_count),
         upper_ok[None, :],
         head_count,
+        some_allowed=True,
     )
     merged = combine(local_part, upper_part)
     attended = jnp.concatenate([part[2] / part[1] for part in merged], axis=1)

time: 126 us -> 127 us (level)
  no operation moved by 1% of the time
where the time goes in v22:
time: 127 us; the launch traced here: 126 us
  waiting for transfers between devices  88.9 us (70%)
  other arithmetic  13 us (10%)
  starting transfers between devices  9.05 us (7%)
  matrix products  7.47 us (6%)
  local copies, waits for them, and re-layouts  6.87 us (5%)
    all_to_all x1, waiting for transfers between devices, shards(): received = lax.all_to_all(send, 'tok', 0, 0, tiled=True)  81.8 us
    all_to_all x1, starting transfers between devices, shards(): received = lax.all_to_all(send, 'tok', 0, 0, tiled=True)  7.4 us
    ppermute x2, waiting for transfers between devices, project_over_grp(): lax.ppermute(give, 'grp', [(g, g ^ step) for g in range(size)])  7.12 us
    dot_general x8, matrix products, partial_attention(): lax.dot_general(query_rows[:, cols], key_rows[:, cols], (((1,), (1,)), ((...  3.28 us
    dot_general x8, matrix products, partial_attention(): jnp.dot(exp_scores.astype(jnp.bfloat16), values[:, cols], preferred_eleme...  3.12 us
    reduce_sum x3, other arithmetic, pick(): return jnp.sum(jnp.where(ids == index, table, 0))  3.1 us
    gather x1, local copies, waits for them, and re-layouts, shards(): both.at[jnp.concatenate([dest_nodes, node_count + dest_nodes], axis=1)]  2.79 us
  transfers between devices with their start and end apart: 3, of which 3 were waited for; matrix products, arithmetic and copies ran while one was open for 8% of the time, Pallas kernels for 0%

profile of v22, /device:TPU:0, one launch (start us, length us, event | category | flops | bytes accessed | tf_op | source)
XLA Modules:
  0.0 126.3 jit_solution(8775269126962975062)
XLA Ops:
  0.0 1.3 %add_bitcast_fusion.1 = (s32[8,1,1]{0,1,2:T(1,128)S(1)}, s32[8,1]{0,1:T(1,128)S(1)}, s32[]{:T(128)}) fusion(s32[8]{0:T(128)} %param.24, s32[]{:T(128)S(6)} %axis_index.25), kind=kLoop, calls=%fused_computation.167 | loop fusion | flops 31 | bytes 104 | tf_op jit(solution)/shard_map/concatenate | solution.py:109
  1.3 0.8 select_reduce_fusion
  2.1 0.1 copy.23
  2.2 0.1 reshape.226
  2.3 1.5 %pad_maximum_fusion = bf16[12,128,512]{2,1,0:T(8,128)(2,1)S(1)} fusion(bf16[6,128,512]{2,1,0:T(8,128)(2,1)} %param.22, bf16[6,128,512]{2,1,0:T(8,128)(2,1)} %param.21), kind=kLoop, calls=%fused_computation.9 | loop fusion | flops 786432 | bytes 3145728 | tf_op jit(solution)/shard_map/concatenate | solution.py:108
  3.8 2.8 %gather_fusion = bf16[32,128,512]{2,1,0:T(8,128)(2,1)} fusion(bf16[12,128,512]{2,1,0:T(8,128)(2,1)S(1)} %pad_maximum_fusion, s32[1024]{0:T(1024)S(1)} %pad_clamp_fusion), kind=kCustom, calls=%fused_computation | custom fusion | bytes 8388736 | tf_op jit(solution)/shard_map/gather | solution.py:109
  6.6 0.0 copy-start
  6.6 0.0 copy-start.1
  6.6 0.0 copy-start.4
  6.6 7.4 %all-to-all-start = ((bf16[8,4,128,512]{3,2,1,0:T(8,128)(2,1)}), bf16[8,4,128,512]{3,2,1,0:T(8,128)(2,1)}, u32[]{:S(2)}, u32[]{:S(2)}) async-start(bf16[8,4,128,512]{3,2,1,0:T(8,128)(2,1)} %bitcast.73), calls=%async_computation | async-start | bytes 8388608 | tf_op jit(solution)/shard_map/all_to_all | solution.py:112
  14.7 0.0 copy-done.10
  14.7 1.3 fusion.101
  15.9 1.2 fusion.102
  17.1 1.3 %pad_add_fusion.1 = s32[2]{0:T(128)S(1)} fusion(s32[1]{0:T(128)} %bitcast.15, s32[1]{0:T(128)} %bitcast.14), kind=kLoop, calls=%fused_computation.160 | loop fusion | flops 2 | bytes 16 | tf_op jit(solution)/shard_map/stack | solution.py:147
  18.5 0.1 iota_add_fusion
  18.6 0.1 broadcast_compare_fusion
  18.7 0.0 copy-done.9
  18.7 0.6 select_reduce_fusion.2
  19.3 0.6 iota_compare_fusion.2
  20.0 0.6 iota_compare_fusion.3
  20.6 0.0 copy-done
  20.6 0.3 fusion.127
  21.0 0.4 fusion.128
  21.3 0.0 copy-start.3
  21.3 0.0 copy-start.6
  21.3 0.3 fusion.129
  21.7 0.4 fusion.130
  22.0 0.3 copy-done.3
  22.4 0.0 copy-done.6
  22.4 0.3 fusion.59
  22.7 0.3 fusion.57
  23.1 0.3 fusion.55
  23.4 0.3 fusion.53
  23.7 0.0 copy-start.2
  23.7 0.8 fusion.51
  24.5 0.8 copy-done.2
  25.3 0.2 fusion.125
  25.5 81.8 %all-to-all-done = bf16[8,4,128,512]{3,2,1,0:T(8,128)(2,1)} async-done(((bf16[8,4,128,512]{3,2,1,0:T(8,128)(2,1)}), bf16[8,4,128,512]{3,2,1,0:T(8,128)(2,1)}, u32[]{:S(2)}, u32[]{:S(2)}) %all-to-all-start) | async-done | bytes 4194336 | tf_op jit(solution)/shard_map/all_to_all | solution.py:112
  107.3 2.5 %fusion.124 = (bf16[8,2,128,512]{3,2,1,0:T(8,128)(2,1)S(1)}, bf16[8,2,128,512]{3,2,1,0:T(8,128)(2,1)S(1)}) fusion(bf16[8,4,128,512]{3,2,1,0:T(8,128)(2,1)} %all-to-all-done), kind=kLoop, calls=%fused_computation.180 | loop fusion | bytes 8388608 | tf_op jit(solution)/shard_map/slice | solution.py:114
  109.8 0.5 fusion.126
  110.2 0.5 fusion.131
  110.7 0.5 fusion.132
  111.2 0.5 fusion.133
  111.7 0.4 fusion.10
  112.0 0.4 fusion.8
  112.4 0.4 fusion.6
  112.8 0.4 fusion.4
  113.2 0.5 fusion.21
  113.6 0.5 fusion.23
  114.1 0.5 fusion.25
  114.6 0.5 fusion.27
  115.1 0.1 fusion.52
  115.2 0.3 fusion.134
  115.4 0.3 fusion.135
  115.7 0.3 select_convert_fusion.1
  116.0 0.3 select_convert_fusion.2
  116.3 0.1 collective-permute-start
  116.4 1.7 %collective-permute-done = bf16[192,1024]{1,0:T(8,128)(2,1)S(1)} collective-permute-done((bf16[192,1024]{1,0:T(8,128)(2,1)S(1)}, bf16[192,1024]{1,0:T(8,128)(2,1)S(1)}, u32[]{:S(2)}, u32[]{:S(2)}) %collective-permute-start) | collective-permute-done | bytes 393248 | tf_op jit(solution)/shard_map/ppermute | solution.py:63
  118.1 0.1 convert_element_type.40
  118.2 0.0 copy-start.5
  118.2 0.3 select_convert_fusion
  118.5 1.6 %collective-permute-start.1 = (bf16[192,512]{1,0:T(8,128)(2,1)S(1)}, bf16[192,512]{1,0:T(8,128)(2,1)S(1)}, u32[]{:S(2)}, u32[]{:S(2)}) collective-permute-start(bf16[192,512]{1,0:T(8,128)(2,1)S(1)} %get-tuple-element.43), channel_id=1, source_target_pairs={{0,2},{1,3},{2,0},{3,1},{4,6},{5,7},{6,4},{7,5},{8,10},{9,11},{10,... | collective-permute-start | bytes 589832 | tf_op jit(solution)/shard_map/ppermute | solution.py:63
  120.1 5.4 %collective-permute-done.1 = bf16[192,512]{1,0:T(8,128)(2,1)S(1)} collective-permute-done((bf16[192,512]{1,0:T(8,128)(2,1)S(1)}, bf16[192,512]{1,0:T(8,128)(2,1)S(1)}, u32[]{:S(2)}, u32[]{:S(2)}) %collective-permute-start.1) | collective-permute-done | bytes 196640 | tf_op jit(solution)/shard_map/ppermute | solution.py:63
  125.5 0.8 add_convert_fusion
  (21 shorter events, 0.2 us)
Async XLA Ops:
  6.5 8.1 %copy-start.10 = (s32[4]{0:T(128)S(1)}, s32[4]{0:T(128)}, u32[]{:S(2)}) copy-start(s32[4]{0:T(128)} %param.25) | copy-start | bytes 52
  6.6 9.4 %copy-start.7 = (s32[6]{0:T(128)S(1)}, s32[6]{0:T(128)}, u32[]{:S(2)}) copy-start(s32[6]{0:T(128)} %param.26) | copy-start | bytes 76
  6.6 12.1 %copy-start.8 = (s32[8]{0:T(128)S(1)}, s32[8]{0:T(128)}, u32[]{:S(2)}) copy-start(s32[8]{0:T(128)} %param.27) | copy-start | bytes 100
  6.6 12.1 %copy-start.9 = (s32[8]{0:T(128)S(1)}, s32[8]{0:T(128)}, u32[]{:S(2)}) copy-start(s32[8]{0:T(128)} %param.23) | copy-start | bytes 100
  6.6 14.0 %copy-start = (bf16[1,512,512]{2,1,0:T(8,128)(2,1)S(1)}, bf16[1,512,512]{2,1,0:T(8,128)(2,1)}, u32[]{:S(2)}) copy-start(bf16[1,512,512]{2,1,0:T(8,128)(2,1)} %param.19) | copy-start | bytes 1572868
  6.6 14.0 %copy-start.1 = (bf16[192,512]{1,0:T(8,128)(2,1)S(1)}, bf16[192,512]{1,0:T(8,128)(2,1)}, u32[]{:S(2)}) copy-start(bf16[192,512]{1,0:T(8,128)(2,1)} %param.15) | copy-start | bytes 589828
  6.6 14.0 %copy-start.4 = (bf16[192,512]{1,0:T(8,128)(2,1)S(1)}, bf16[192,512]{1,0:T(8,128)(2,1)}, u32[]{:S(2)}) copy-start(bf16[192,512]{1,0:T(8,128)(2,1)} %param.14) | copy-start | bytes 589828
  6.6 100.7 %all-to-all-start = ((bf16[8,4,128,512]{3,2,1,0:T(8,128)(2,1)}), bf16[8,4,128,512]{3,2,1,0:T(8,128)(2,1)}, u32[]{:S(2)}, u32[]{:S(2)}) async-start(bf16[8,4,128,512]{3,2,1,0:T(8,128)(2,1)} %bitcast.73), calls=%async_computation | async-start | bytes 8388608 | tf_op jit(solution)/shard_map/all_to_all | solution.py:112
  21.3 1.0 copy-start.3
  21.3 1.1 copy-start.6
  23.7 1.6 %copy-start.2 = (bf16[512,2048]{1,0:T(8,128)(2,1)S(1)}, bf16[512,2048]{1,0:T(8,128)(2,1)}, u32[]{:S(2)}) copy-start(bf16[512,2048]{1,0:T(8,128)(2,1)} %param.18) | copy-start | bytes 6291460
  116.3 1.8 %collective-permute-start = (bf16[192,1024]{1,0:T(8,128)(2,1)S(1)}, bf16[192,1024]{1,0:T(8,128)(2,1)S(1)}, u32[]{:S(2)}, u32[]{:S(2)}) collective-permute-start(bf16[192,1024]{1,0:T(8,128)(2,1)S(1)} %pad_maximum_fusion.1), channel_id=1, source_target_pairs={{0,1},{1,0},{2,3},{3,2},{4,5},{5,4},{6,7},{7,6},{8,9},{9,8},{10,11... | collective-permute-start | bytes 1179656 | tf_op jit(solution)/shard_map/ppermute | solution.py:63
  118.2 7.3 %copy-start.5 = (bf16[192,512]{1,0:T(8,128)(2,1)S(1)}, bf16[192,512]{1,0:T(8,128)(2,1)}, u32[]{:S(2)}) copy-start(bf16[192,512]{1,0:T(8,128)(2,1)} %param.17) | copy-start | bytes 589828
  118.5 7.0 %collective-permute-start.1 = (bf16[192,512]{1,0:T(8,128)(2,1)S(1)}, bf16[192,512]{1,0:T(8,128)(2,1)S(1)}, u32[]{:S(2)}, u32[]{:S(2)}) collective-permute-start(bf16[192,512]{1,0:T(8,128)(2,1)S(1)} %get-tuple-element.43), channel_id=1, source_target_pairs={{0,2},{1,3},{2,0},{3,1},{4,6},{5,7},{6,4},{7,5},{8,10},{9,11},{10,... | collective-permute-start | bytes 589832 | tf_op jit(solution)/shard_map/ppermute | solution.py:63

commit v23 on v16

--- a/solution.py
+++ b/solution.py
@@ -49,7 +49,10 @@
     size = lax.axis_size("grp")
     index = lax.axis_index("grp")
     block = w_blocks[0].shape[1]
-    kept = [jnp.dot(attention, w, preferred_element_type=jnp.float32) for w in w_blocks]
+    projected = jnp.dot(
+        attention, jnp.concatenate(w_blocks, axis=1), preferred_element_type=jnp.float32
+    )
+    kept = [projected[:, b * block : (b + 1) * block] for b in range(size)]
     step = 1
     while step < size:
         high = (index & step) != 0

time: 126 us -> 126 us (level)
  local copies, waits for them, and re-layouts: 6.87 us -> 8.28 us
where the time goes in v23:
time: 126 us
  waiting for transfers between devices  88.1 us (70%)
  other arithmetic  12.7 us (10%)
  starting transfers between devices  9.06 us (7%)
  local copies, waits for them, and re-layouts  8.28 us (7%)
  matrix products  7.01 us (6%)
    all_to_all x1, waiting for transfers between devices, shards(): received = lax.all_to_all(send, 'tok', 0, 0, tiled=True)  81 us
    all_to_all x1, starting transfers between devices, shards(): received = lax.all_to_all(send, 'tok', 0, 0, tiled=True)  7.4 us
    ppermute x2, waiting for transfers between devices, project_over_grp(): lax.ppermute(give, 'grp', [(g, g ^ step) for g in range(size)])  7.12 us
    dot_general x8, matrix products, partial_attention(): lax.dot_general(query_rows[:, cols], key_rows[:, cols], (((1,), (1,)), ((...  3.28 us
    dot_general x8, matrix products, partial_attention(): jnp.dot(exp_scores.astype(jnp.bfloat16), values[:, cols], preferred_eleme...  3.1 us
    reduce_sum x3, other arithmetic, pick(): return jnp.sum(jnp.where(ids == index, table, 0))  3.1 us
    gather x1, local copies, waits for them, and re-layouts, shards(): both.at[jnp.concatenate([dest_nodes, node_count + dest_nodes], axis=1)]  2.79 us
  transfers between devices with their start and end apart: 3, of which 3 were waited for; matrix products, arithmetic and copies ran while one was open for 8% of the time, Pallas kernels for 0%

profile of v23, /device:TPU:0, one launch (start us, length us, event | category | flops | bytes accessed | tf_op | source)
XLA Modules:
  0.0 126.0 jit_solution(7266349905085196397)
XLA Ops:
  0.0 1.3 %add_bitcast_fusion.1 = (s32[8,1,1]{0,1,2:T(1,128)S(1)}, s32[8,1]{0,1:T(1,128)S(1)}, s32[]{:T(128)}) fusion(s32[8]{0:T(128)} %param.24, s32[]{:T(128)S(6)} %axis_index.25), kind=kLoop, calls=%fused_computation.185 | loop fusion | flops 31 | bytes 104 | tf_op jit(solution)/shard_map/concatenate | solution.py:110
  1.3 0.8 select_reduce_fusion
  2.1 0.1 copy.23
  2.2 0.1 reshape.226
  2.3 1.5 %pad_maximum_fusion = bf16[12,128,512]{2,1,0:T(8,128)(2,1)S(1)} fusion(bf16[6,128,512]{2,1,0:T(8,128)(2,1)} %param.22, bf16[6,128,512]{2,1,0:T(8,128)(2,1)} %param.21), kind=kLoop, calls=%fused_computation.17 | loop fusion | flops 786432 | bytes 3145728 | tf_op jit(solution)/shard_map/concatenate | solution.py:109
  3.8 2.8 %gather_fusion = bf16[32,128,512]{2,1,0:T(8,128)(2,1)} fusion(bf16[12,128,512]{2,1,0:T(8,128)(2,1)S(1)} %pad_maximum_fusion, s32[1024]{0:T(1024)S(1)} %pad_clamp_fusion), kind=kCustom, calls=%fused_computation | custom fusion | bytes 8388736 | tf_op jit(solution)/shard_map/gather | solution.py:110
  6.6 0.0 copy-start
  6.6 0.0 copy-start.1
  6.6 0.0 copy-start.5
  6.6 7.4 %all-to-all-start = ((bf16[8,4,128,512]{3,2,1,0:T(8,128)(2,1)}), bf16[8,4,128,512]{3,2,1,0:T(8,128)(2,1)}, u32[]{:S(2)}, u32[]{:S(2)}) async-start(bf16[8,4,128,512]{3,2,1,0:T(8,128)(2,1)} %bitcast.65), calls=%async_computation | async-start | bytes 8388608 | tf_op jit(solution)/shard_map/all_to_all | solution.py:113
  14.7 0.0 copy-done.11
  14.7 1.3 fusion.120
  15.9 0.0 copy-done.8
  15.9 1.2 fusion.121
  17.1 1.3 %pad_add_fusion.1 = s32[2]{0:T(128)S(1)} fusion(s32[1]{0:T(128)} %bitcast.15, s32[1]{0:T(128)} %bitcast.14), kind=kLoop, calls=%fused_computation.178 | loop fusion | flops 2 | bytes 16 | tf_op jit(solution)/shard_map/stack | solution.py:148
  18.5 0.1 iota_add_fusion
  18.6 0.1 broadcast_compare_fusion
  18.7 0.0 copy-done.10
  18.7 0.6 select_reduce_fusion.2
  19.3 0.6 iota_compare_fusion.2
  20.0 0.6 iota_compare_fusion.3
  20.6 0.0 copy-done
  20.6 0.0 copy-done.1
  20.6 0.0 copy-done.5
  20.6 0.3 fusion.152
  21.0 0.4 fusion.153
  21.3 0.0 copy-start.3
  21.3 0.0 copy-start.7
  21.3 0.3 fusion.154
  21.7 0.4 fusion.155
  22.0 0.3 copy-done.3
  22.4 0.0 copy-done.7
  22.4 0.3 fusion.69
  22.7 0.3 fusion.71
  23.1 0.3 fusion.73
  23.4 0.3 fusion.75
  23.7 0.0 copy-start.2
  23.7 0.8 fusion.67
  24.5 0.8 copy-done.2
  25.3 1.0 fusion.151
  26.3 81.0 %all-to-all-done = bf16[8,4,128,512]{3,2,1,0:T(8,128)(2,1)} async-done(((bf16[8,4,128,512]{3,2,1,0:T(8,128)(2,1)}), bf16[8,4,128,512]{3,2,1,0:T(8,128)(2,1)}, u32[]{:S(2)}, u32[]{:S(2)}) %all-to-all-start) | async-done | bytes 4194336 | tf_op jit(solution)/shard_map/all_to_all | solution.py:113
  107.3 2.5 %fusion.150 = (bf16[8,2,128,512]{3,2,1,0:T(8,128)(2,1)S(1)}, bf16[8,2,128,512]{3,2,1,0:T(8,128)(2,1)S(1)}) fusion(bf16[8,4,128,512]{3,2,1,0:T(8,128)(2,1)} %all-to-all-done), kind=kLoop, calls=%fused_computation.205 | loop fusion | bytes 8388608 | tf_op jit(solution)/shard_map/slice | solution.py:115
  109.8 0.5 fusion.156
  110.2 0.5 fusion.157
  110.7 0.5 fusion.158
  111.2 0.5 fusion.159
  111.7 1.2 fusion.12
  112.9 0.5 fusion.35
  113.3 0.4 fusion.33
  113.8 0.5 fusion.31
  114.3 0.0 copy-start.4
  114.3 0.5 fusion.29
  114.8 0.6 copy-done.4
  115.3 0.6 fusion.4
  115.9 0.1 select_convert_fusion.2
  116.1 0.1 collective-permute-start
  116.2 1.7 %collective-permute-done = bf16[192,1024]{1,0:T(8,128)(2,1)S(1)} collective-permute-done((bf16[192,1024]{1,0:T(8,128)(2,1)S(1)}, bf16[192,1024]{1,0:T(8,128)(2,1)S(1)}, u32[]{:S(2)}, u32[]{:S(2)}) %collective-permute-start) | collective-permute-done | bytes 393248 | tf_op jit(solution)/shard_map/ppermute | solution.py:64
  117.9 0.1 convert_element_type.52
  117.9 0.0 copy-start.6
  118.0 0.3 select_convert_fusion
  118.2 1.6 %collective-permute-start.1 = (bf16[192,512]{1,0:T(8,128)(2,1)S(1)}, bf16[192,512]{1,0:T(8,128)(2,1)S(1)}, u32[]{:S(2)}, u32[]{:S(2)}) collective-permute-start(bf16[192,512]{1,0:T(8,128)(2,1)S(1)} %get-tuple-element.47), channel_id=1, source_target_pairs={{0,2},{1,3},{2,0},{3,1},{4,6},{5,7},{6,4},{7,5},{8,10},{9,11},{10,... | collective-permute-start | bytes 589832 | tf_op jit(solution)/shard_map/ppermute | solution.py:64
  119.8 5.4 %collective-permute-done.1 = bf16[192,512]{1,0:T(8,128)(2,1)S(1)} collective-permute-done((bf16[192,512]{1,0:T(8,128)(2,1)S(1)}, bf16[192,512]{1,0:T(8,128)(2,1)S(1)}, u32[]{:S(2)}, u32[]{:S(2)}) %collective-permute-start.1) | collective-permute-done | bytes 196640 | tf_op jit(solution)/shard_map/ppermute | solution.py:64
  125.2 0.0 copy-done.6
  125.2 0.8 add_convert_fusion
  (17 shorter events, 0.2 us)
Async XLA Ops:
  6.5 8.1 %copy-start.11 = (s32[4]{0:T(128)S(1)}, s32[4]{0:T(128)}, u32[]{:S(2)}) copy-start(s32[4]{0:T(128)} %param.25) | copy-start | bytes 52
  6.6 9.4 %copy-start.8 = (s32[6]{0:T(128)S(1)}, s32[6]{0:T(128)}, u32[]{:S(2)}) copy-start(s32[6]{0:T(128)} %param.26) | copy-start | bytes 76
  6.6 12.1 %copy-start.9 = (s32[8]{0:T(128)S(1)}, s32[8]{0:T(128)}, u32[]{:S(2)}) copy-start(s32[8]{0:T(128)} %param.27) | copy-start | bytes 100
  6.6 12.1 %copy-start.10 = (s32[8]{0:T(128)S(1)}, s32[8]{0:T(128)}, u32[]{:S(2)}) copy-start(s32[8]{0:T(128)} %param.23) | copy-start | bytes 100
  6.6 14.0 %copy-start = (bf16[1,512,512]{2,1,0:T(8,128)(2,1)S(1)}, bf16[1,512,512]{2,1,0:T(8,128)(2,1)}, u32[]{:S(2)}) copy-start(bf16[1,512,512]{2,1,0:T(8,128)(2,1)} %param.19) | copy-start | bytes 1572868
  6.6 14.0 %copy-start.1 = (bf16[192,512]{1,0:T(8,128)(2,1)S(1)}, bf16[192,512]{1,0:T(8,128)(2,1)}, u32[]{:S(2)}) copy-start(bf16[192,512]{1,0:T(8,128)(2,1)} %param.15) | copy-start | bytes 589828
  6.6 14.0 %copy-start.5 = (bf16[192,512]{1,0:T(8,128)(2,1)S(1)}, bf16[192,512]{1,0:T(8,128)(2,1)}, u32[]{:S(2)}) copy-start(bf16[192,512]{1,0:T(8,128)(2,1)} %param.14) | copy-start | bytes 589828
  6.6 100.7 %all-to-all-start = ((bf16[8,4,128,512]{3,2,1,0:T(8,128)(2,1)}), bf16[8,4,128,512]{3,2,1,0:T(8,128)(2,1)}, u32[]{:S(2)}, u32[]{:S(2)}) async-start(bf16[8,4,128,512]{3,2,1,0:T(8,128)(2,1)} %bitcast.65), calls=%async_computation | async-start | bytes 8388608 | tf_op jit(solution)/shard_map/all_to_all | solution.py:113
  21.3 1.0 copy-start.3
  21.3 1.1 copy-start.7
  23.7 1.6 %copy-start.2 = (bf16[512,2048]{1,0:T(8,128)(2,1)S(1)}, bf16[512,2048]{1,0:T(8,128)(2,1)}, u32[]{:S(2)}) copy-start(bf16[512,2048]{1,0:T(8,128)(2,1)} %param.18) | copy-start | bytes 6291460
  114.3 1.0 copy-start.4
  116.1 1.8 %collective-permute-start = (bf16[192,1024]{1,0:T(8,128)(2,1)S(1)}, bf16[192,1024]{1,0:T(8,128)(2,1)S(1)}, u32[]{:S(2)}, u32[]{:S(2)}) collective-permute-start(bf16[192,1024]{1,0:T(8,128)(2,1)S(1)} %pad_maximum_fusion.1), channel_id=1, source_target_pairs={{0,1},{1,0},{2,3},{3,2},{4,5},{5,4},{6,7},{7,6},{8,9},{9,8},{10,11... | collective-permute-start | bytes 1179656 | tf_op jit(solution)/shard_map/ppermute | solution.py:64
  117.9 7.3 %copy-start.6 = (bf16[192,512]{1,0:T(8,128)(2,1)S(1)}, bf16[192,512]{1,0:T(8,128)(2,1)}, u32[]{:S(2)}) copy-start(bf16[192,512]{1,0:T(8,128)(2,1)} %param.17) | copy-start | bytes 589828
  118.2 7.0 %collective-permute-start.1 = (bf16[192,512]{1,0:T(8,128)(2,1)S(1)}, bf16[192,512]{1,0:T(8,128)(2,1)S(1)}, u32[]{:S(2)}, u32[]{:S(2)}) collective-permute-start(bf16[192,512]{1,0:T(8,128)(2,1)S(1)} %get-tuple-element.47), channel_id=1, source_target_pairs={{0,2},{1,3},{2,0},{3,1},{4,6},{5,7},{6,4},{7,5},{8,10},{9,11},{10,... | collective-permute-start | bytes 589832 | tf_op jit(solution)/shard_map/ppermute | solution.py:64
